TPU v7x, 32 devices: a whole 2x2x4 slice. The times are simulated.
32 devices in a mesh: group: 2 (over y), seq: 4 (over z), batch: 2 (over x), mp: 2 (over core).
Axes of the slice: x: 2, y: 2, z: 4, core: 2. Of those that a mesh axis runs over, the one named last changes fastest.
Arguments:
- features: bfloat16 [4, 512, 384], P(('group', 'batch'), 'seq'), parts along dimension 0, may hold values from -6 to 6
- noise: float32 [4, 512, 384], P(('group', 'batch'), 'seq'), parts along dimension 0, may hold values from -3 to 3
- conv_weight: bfloat16 [5, 384, 768], P(None, 'seq', 'mp'), may hold values from -0.125 to 0.125
- conv_bias: float32 [768], P('mp'), may hold values from -3 to 3
- norm_gain: float32 [768], replicated, may hold values from 0.25 to 1.75
- qkv_weight: bfloat16 [3, 768, 768], P(None, 'seq', 'mp'), may hold values from -1.010363 to 1.010363
- out_weight: bfloat16 [768, 768], P('mp', 'seq'), may hold values from -0.21875 to 0.21875
Outputs:
- block_out: bfloat16 [4, 256, 768], P(('group', 'batch'), 'seq', 'mp'), parts along dimension 0
- new_noise: float32 [4, 512, 384], P(('group', 'batch'), 'seq'), parts along dimension 0
There are 2 independent parts, one for each index of `group`. A program takes and returns all parts, laid end to end along the dimension named above; an argument that names none is the same for every part. Nothing has to cross between parts.
All inputs are finite; a program needn't handle non-finite values.
Results may differ from a plain program's by a relative error of at most 0.014.
Values may be sent and summed in bfloat16 or wider, within the bound.
No kernel may reach another device: no remote copies, remote signals or barrier semaphores. Data moves between devices by JAX's collectives and lax.ppermute only.
A program may use at most 64 MiB of HBM per device.

v0:
```python
import jax
import jax.numpy as jnp
from jax import lax
from jax.sharding import PartitionSpec as P

F = 768
HD = 96
KW = 5


step_size = 0.5
epsilon = 1e-06


def with_halo(cells, sides, width):
    for axis, dim in sides:
        count = lax.axis_size(axis)
        ends = count - 1
        head = lax.slice_in_dim(cells, 0, width, axis=dim)
        tail = lax.slice_in_dim(cells, cells.shape[dim] - width, cells.shape[dim], axis=dim)
        cells = jnp.concatenate(
            [
                lax.ppermute(tail, axis, [(i, (i + 1) % count) for i in range(ends)]),
                cells,
                lax.ppermute(head, axis, [((i + 1) % count, i) for i in range(ends)]),
            ],
            axis=dim,
        )
    return cells


def attend_rows(query, keys, values):
    key_total = keys.shape[0]
    block_len = min(512, key_total)
    head_size = keys.shape[1]
    score_scale = head_size ** (-0.5)
    key_blocks = keys.reshape(key_total // block_len, block_len, head_size)
    value_blocks = values.reshape(key_total // block_len, block_len, head_size)
    query_count = query.shape[0]

    def find_top(carry, key_block):
        row_top, row_mass = carry
        scores = jnp.dot(query, key_block.T, preferred_element_type=jnp.float32) * score_scale
        new_top = jnp.maximum(row_top, jnp.max(scores, axis=1))
        row_mass = row_mass * jnp.exp(row_top - new_top) + jnp.sum(
            jnp.exp(scores - new_top[:, None]), axis=1
        )
        return ((new_top, row_mass), None)

    start_top = jnp.full((query_count,), -1e30, jnp.float32)
    (row_top, row_mass), _ = lax.scan(
        find_top, (start_top, jnp.zeros((query_count,), jnp.float32)), key_blocks
    )
    log_mass = row_top + jnp.log(row_mass)

    def collect(running, blocks):
        key_block, value_block = blocks
        scores = jnp.dot(query, key_block.T, preferred_element_type=jnp.float32) * score_scale
        soft_weights = jnp.exp(scores - log_mass[:, None]).astype(jnp.bfloat16)
        return (
            running + jnp.dot(soft_weights, value_block, preferred_element_type=jnp.float32),
            None,
        )

    running, _ = lax.scan(
        collect, jnp.zeros((query_count, head_size), jnp.float32), (key_blocks, value_blocks)
    )
    return (running.astype(jnp.bfloat16), log_mass)


def attend_back(query, keys, values, attended, log_mass, out_grad):
    key_total = keys.shape[0]
    block_len = min(512, key_total)
    head_size = keys.shape[1]
    score_scale = head_size ** (-0.5)
    key_blocks = keys.reshape(key_total // block_len, block_len, head_size)
    value_blocks = values.reshape(key_total // block_len, block_len, head_size)
    row_dot = jnp.sum(out_grad.astype(jnp.float32) * attended.astype(jnp.float32), axis=1)

    def step_back(query_acc, blocks):
        key_block, value_block = blocks
        scores = jnp.dot(query, key_block.T, preferred_element_type=jnp.float32) * score_scale
        exp_weights = jnp.exp(scores - log_mass[:, None])
        value_part = jnp.einsum(
            "qk,qd->kd",
            exp_weights.astype(jnp.bfloat16),
            out_grad,
            preferred_element_type=jnp.float32,
        )
        prob_grad = jnp.dot(out_grad, value_block.T, preferred_element_type=jnp.float32)
        score_grad = (exp_weights * (prob_grad - row_dot[:, None])).astype(jnp.bfloat16)
        query_acc = (
            query_acc
            + jnp.dot(score_grad, key_block, preferred_element_type=jnp.float32) * score_scale
        )
        key_part = (
            jnp.einsum("qk,qd->kd", score_grad, query, preferred_element_type=jnp.float32)
            * score_scale
        )
        return (query_acc, jnp.concatenate([key_part, value_part], axis=1))

    query_grad, keyval_parts = lax.scan(
        step_back, jnp.zeros((query.shape[0], head_size), jnp.float32), (key_blocks, value_blocks)
    )
    return (query_grad, keyval_parts.reshape(key_total, 2 * head_size))


def forward(stack, conv_weight, conv_bias, norm_gain, qkv_weight, out_weight):
    pass_count, positions, channels = stack.shape
    reach = KW // 2
    half_width = conv_weight.shape[2]
    padded_input = with_halo(stack, (("seq", 1),), reach)
    running = jnp.zeros((pass_count, positions, half_width), jnp.float32)
    piece = lax.all_gather(conv_weight, "seq", axis=1, tiled=True)
    for offset in range(piece.shape[0]):
        running = running + jnp.einsum(
            "ptc,cf->ptf",
            padded_input[:, offset : offset + positions],
            piece[offset],
            preferred_element_type=jnp.float32,
        )
    pre_act = running + conv_bias
    paired = jax.nn.gelu(pre_act).reshape(pass_count, positions // 2, 2, half_width)
    pooled = (0.5 * (paired[:, :, 0] + paired[:, :, 1])).astype(jnp.bfloat16)
    pooled_wide = lax.optimization_barrier(pooled).astype(jnp.float32)
    whole = lax.all_gather(pooled, "mp", axis=2, tiled=True)
    whole_wide = whole.astype(jnp.float32)
    row_scale = lax.rsqrt(jnp.mean(whole_wide * whole_wide, axis=2, keepdims=True) + epsilon)
    normed = (whole_wide * row_scale * norm_gain).astype(jnp.bfloat16)
    rows = positions // 2
    proj_width = qkv_weight.shape[2]
    projected = jnp.einsum(
        "prf,jfh->jprh",
        normed,
        lax.all_gather(qkv_weight, "seq", axis=1, tiled=True),
        preferred_element_type=jnp.float32,
    ).astype(jnp.bfloat16)
    head_size = HD
    head_count = proj_width // head_size
    devices = lax.axis_size("seq")
    query_groups = devices // head_count
    sub_rows = rows // query_groups
    query_send = (
        projected[0]
        .reshape(pass_count, query_groups, sub_rows, head_count, head_size)
        .transpose(3, 1, 0, 2, 4)
        .reshape(devices, pass_count, sub_rows * head_size)
    )
    keyval = jnp.concatenate(
        [
            projected[1].reshape(pass_count, rows, head_count, head_size),
            projected[2].reshape(pass_count, rows, head_count, head_size),
        ],
        axis=3,
    )
    keyval_flat = keyval.transpose(2, 0, 1, 3).reshape(
        head_count, 1, pass_count, rows * 2 * head_size
    )
    keyval_send = jnp.broadcast_to(
        keyval_flat, (head_count, query_groups, pass_count, rows * 2 * head_size)
    ).reshape(devices, pass_count, rows * 2 * head_size)
    query_in, keyval_in = (
        lax.all_to_all(query_send, "seq", split_axis=0, concat_axis=2, tiled=True),
        lax.all_to_all(keyval_send, "seq", split_axis=0, concat_axis=2, tiled=True),
    )
    query_heads = query_in.reshape(pass_count, devices * sub_rows, head_size)
    keyval_heads = keyval_in.reshape(pass_count, devices * rows, 2 * head_size)
    outputs = []
    masses = []
    for index in range(pass_count):
        out_now, mass_now = attend_rows(
            query_heads[index],
            keyval_heads[index, :, :head_size],
            keyval_heads[index, :, head_size:],
        )
        outputs.append(out_now)
        masses.append(mass_now)
    attended_heads = jnp.stack(outputs)
    log_mass = jnp.stack(masses)
    out_send = attended_heads.reshape(pass_count, devices, sub_rows * head_size).transpose(1, 0, 2)
    out_back = lax.all_to_all(out_send, "seq", split_axis=0, concat_axis=0, tiled=True)
    attended = (
        out_back.reshape(head_count, query_groups, pass_count, sub_rows, head_size)
        .transpose(2, 1, 3, 0, 4)
        .reshape(pass_count, rows, proj_width)
    )
    terms = jnp.einsum(
        "prh,hf->prf",
        attended,
        lax.all_gather(out_weight, "seq", axis=1, tiled=True),
        preferred_element_type=jnp.float32,
    )
    mixed = (
        lax.psum_scatter(terms.astype(jnp.bfloat16), "mp", scatter_dimension=2, tiled=True).astype(
            jnp.float32
        )
        + pooled_wide
    )
    return (
        pre_act,
        pooled_wide,
        whole_wide,
        row_scale,
        query_heads,
        keyval_heads,
        attended_heads,
        log_mass,
        mixed,
    )


def shards(features, noise, conv_weight, conv_bias, norm_gain, qkv_weight, out_weight):
    clean = features[0]
    moved = (clean.astype(jnp.float32) + noise[0]).astype(jnp.bfloat16)
    joint = forward(
        jnp.stack([clean, moved]), conv_weight, conv_bias, norm_gain, qkv_weight, out_weight
    )
    clean_run = [item[0:1] for item in joint]
    moved_run = [item[1:2] for item in joint]
    (
        pre_act,
        pooled_wide,
        whole_wide,
        row_scale,
        query_heads,
        keyval_heads,
        attended_heads,
        log_mass,
        mixed,
    ) = [item[0] for item in moved_run]
    clean_mixed = clean_run[8][0]
    rows, half_width = pooled_wide.shape
    positions = pre_act.shape[0]
    proj_width = qkv_weight.shape[2]
    head_size = HD
    head_count = proj_width // head_size
    devices = lax.axis_size("seq")
    query_groups = devices // head_count
    sub_rows = rows // query_groups
    difference = mixed - clean_mixed
    difference_half = difference.astype(jnp.bfloat16)
    difference_whole = lax.all_gather(difference_half, "mp", axis=1, tiled=True)
    out_grad = jnp.einsum(
        "rf,hf->rh",
        difference_whole,
        lax.all_gather(out_weight, "seq", axis=1, tiled=True),
        preferred_element_type=jnp.float32,
    ).astype(jnp.bfloat16)
    grad_send = (
        out_grad.reshape(query_groups, sub_rows, head_count, head_size)
        .transpose(2, 0, 1, 3)
        .reshape(devices, sub_rows * head_size)
    )
    grad_in = lax.all_to_all(grad_send, "seq", split_axis=0, concat_axis=1, tiled=True)
    grad_heads = grad_in.reshape(devices * sub_rows, head_size)
    query_grad, keyval_grad = attend_back(
        query_heads,
        keyval_heads[:, :head_size],
        keyval_heads[:, head_size:],
        attended_heads,
        log_mass,
        grad_heads,
    )
    query_back, keyval_back = (
        lax.all_to_all(
            query_grad.reshape(devices, sub_rows * head_size).astype(jnp.bfloat16),
            "seq",
            split_axis=0,
            concat_axis=0,
            tiled=True,
        ).astype(jnp.float32),
        lax.all_to_all(
            keyval_grad.reshape(devices, rows * 2 * head_size).astype(jnp.bfloat16),
            "seq",
            split_axis=0,
            concat_axis=0,
            tiled=True,
        ).astype(jnp.float32),
    )
    query_rows = (
        query_back.reshape(head_count, query_groups, sub_rows, head_size)
        .transpose(1, 2, 0, 3)
        .reshape(rows, proj_width)
        .astype(jnp.bfloat16)
    )
    keyval_rows = jnp.sum(keyval_back.reshape(head_count, query_groups, rows, 2, head_size), axis=1)
    key_rows = (
        keyval_rows[:, :, 0].transpose(1, 0, 2).reshape(rows, proj_width).astype(jnp.bfloat16)
    )
    value_rows = (
        keyval_rows[:, :, 1].transpose(1, 0, 2).reshape(rows, proj_width).astype(jnp.bfloat16)
    )
    grads = jnp.stack([query_rows, key_rows, value_rows])
    normed_terms = jnp.einsum(
        "jrh,jfh->rf",
        grads,
        lax.all_gather(qkv_weight, "seq", axis=1, tiled=True),
        preferred_element_type=jnp.float32,
    )
    offset_mp = lax.axis_index("mp") * half_width
    gain_own = lax.dynamic_slice_in_dim(norm_gain, offset_mp, half_width, 0)
    normed_grad = lax.psum_scatter(
        normed_terms.astype(jnp.bfloat16), "mp", scatter_dimension=1, tiled=True
    ).astype(jnp.float32)
    weighted = lax.psum(jnp.sum(normed_grad * gain_own * pooled_wide, axis=1, keepdims=True), "mp")
    pooled_grad = (
        difference + row_scale * gain_own * normed_grad - pooled_wide * row_scale**3 * weighted / F
    )
    spread = jnp.broadcast_to((0.5 * pooled_grad)[:, None, :], (rows, 2, half_width)).reshape(
        positions, half_width
    )
    gelu_back = jax.vjp(jax.nn.gelu, pre_act)[1]
    pre_grad = gelu_back(spread)[0].astype(jnp.bfloat16)
    reach = KW // 2
    padded = with_halo(pre_grad, (("seq", 0),), reach)
    piece = lax.all_gather(conv_weight, "seq", axis=1, tiled=True)
    running = jnp.zeros((positions, piece.shape[1]), jnp.float32)
    for offset in range(piece.shape[0]):
        lower = 2 * reach - offset
        running = running + jnp.einsum(
            "tf,cf->tc",
            padded[lower : lower + positions],
            piece[offset],
            preferred_element_type=jnp.float32,
        )
    input_grad = lax.psum(running.astype(jnp.bfloat16), "mp").astype(jnp.float32)
    new_noise = noise[0] + step_size * input_grad * lax.rsqrt(
        jnp.mean(input_grad * input_grad, axis=1, keepdims=True) + epsilon
    )
    return (clean_mixed.astype(jnp.bfloat16)[None], new_noise[None])


def solution(mesh):
    return jax.shard_map(
        shards,
        mesh=mesh,
        in_specs=(
            P(("group", "batch"), "seq", None),
            P(("group", "batch"), "seq", None),
            P(None, "seq", "mp"),
            P("mp"),
            P(),
            P(None, "seq", "mp"),
            P("mp", "seq"),
        ),
        out_specs=(P(("group", "batch"), "seq", "mp"), P(("group", "batch"), "seq", None)),
        check_vma=False,
    )
```

profile of v0, /device:TPU:0, one launch (start us, length us, event | category | flops | bytes accessed | tf_op | source)
XLA Modules:
  0.0 244.7 jit_solution(5682853137255914638)
XLA Ops:
  8.7 1.0 add_convert_fusion
  10.4 4.9 %collective-permute-start = (bf16[2,2,384]{2,1,0:T(2,128)(2,1)S(1)}, bf16[2,2,384]{2,1,0:T(2,128)(2,1)S(1)}, u32[]{:S(2)}, u32[]{:S(2)}) collective-permute-start(bf16[2,2,384]{2,1,0:T(2,128)(2,1)S(1)} %get-tuple-element.88), channel_id=1, source_target_pairs={{0,4},{4,8},{8,12},{1,5},{5,9},{9,13},{2,6},{6,10},{10,14},{3,7},{... | collective-permute-start | bytes 9224 | tf_op jit(solution)/shard_map/ppermute | solution.py:23
  15.4 1.3 collective-permute-start.1
  16.7 4.2 %collective-permute-done.1 = bf16[2,2,384]{2,1,0:T(2,128)(2,1)S(1)} collective-permute-done((bf16[2,2,384]{2,1,0:T(2,128)(2,1)S(1)}, bf16[2,2,384]{2,1,0:T(2,128)(2,1)S(1)}, u32[]{:S(2)}, u32[]{:S(2)}) %collective-permute-start.1) | collective-permute-done | bytes 3104 | tf_op jit(solution)/shard_map/ppermute | solution.py:25
  20.9 26.7 %all-gather.4.cloned.1.call-done = bf16[5,384,384]{2,1,0:T(8,128)(2,1)} async-done(((bf16[5,96,384]{2,1,0:T(8,128)(2,1)}), bf16[5,384,384]{2,1,0:T(8,128)(2,1)}) %all-gather.4.cloned.1.call-update) | async-done | bytes 1474576 | tf_op jit(solution)/shard_map/all_gather | solution.py:114
  47.6 1.3 fusion.38
  49.0 1.2 fusion.42
  51.9 1.9 all-gather
  54.0 34.5 %all-gather.6.cloned.1.call-done = bf16[3,768,384]{2,1,0:T(8,128)(2,1)} async-done(((bf16[3,192,384]{2,1,0:T(8,128)(2,1)}), bf16[3,768,384]{2,1,0:T(8,128)(2,1)}) %all-gather.6.cloned.1.call-update) | async-done | bytes 1769488 | tf_op jit(solution)/shard_map/all_gather | solution.py:135
  88.5 2.0 fusion.8
  91.5 3.3 %all-to-all-start = ((bf16[4,2,6144]{2,1,0:T(2,128)(2,1)}), bf16[4,2,6144]{2,1,0:T(2,128)(2,1)S(1)}, u32[]{:S(2)}, u32[]{:S(2)}) async-start(bf16[4,2,6144]{2,1,0:T(2,128)(2,1)} %reshape.242), calls=%async_computation | async-start | bytes 196608 | tf_op jit(solution)/shard_map/all_to_all | solution.py:163
  95.3 1.0 reshape_reshape.4
  96.3 4.3 %all-to-all-done = bf16[4,2,6144]{2,1,0:T(2,128)(2,1)S(1)} async-done(((bf16[4,2,6144]{2,1,0:T(2,128)(2,1)}), bf16[4,2,6144]{2,1,0:T(2,128)(2,1)S(1)}, u32[]{:S(2)}, u32[]{:S(2)}) %all-to-all-start) | async-done | bytes 98336 | tf_op jit(solution)/shard_map/all_to_all | solution.py:163
  100.6 3.4 %all-to-all-start.1 = ((bf16[4,2,12288]{2,1,0:T(2,128)(2,1)}), bf16[4,2,12288]{2,1,0:T(2,128)(2,1)S(1)}, u32[]{:S(2)}, u32[]{:S(2)}) async-start(bf16[4,2,12288]{2,1,0:T(2,128)(2,1)} %reshape_reshape.4), calls=%async_computation.1 | async-start | bytes 393216 | tf_op jit(solution)/shard_map/all_to_all | solution.py:164
  104.6 5.5 %all-to-all-done.1 = bf16[4,2,12288]{2,1,0:T(2,128)(2,1)S(1)} async-done(((bf16[4,2,12288]{2,1,0:T(2,128)(2,1)}), bf16[4,2,12288]{2,1,0:T(2,128)(2,1)S(1)}, u32[]{:S(2)}, u32[]{:S(2)}) %all-to-all-start.1) | async-done | bytes 196640 | tf_op jit(solution)/shard_map/all_to_all | solution.py:164
  113.2 3.3 %all-to-all-start.2 = ((bf16[4,2,6144]{2,1,0:T(2,128)(2,1)}), bf16[4,2,6144]{2,1,0:T(2,128)(2,1)S(1)}, u32[]{:S(2)}, u32[]{:S(2)}) async-start(bf16[4,2,6144]{2,1,0:T(2,128)(2,1)} %copy.103), calls=%async_computation.2 | async-start | bytes 196608 | tf_op jit(solution)/shard_map/all_to_all | solution.py:181
  116.6 16.8 %all_gather.21 = bf16[384,768]{0,1:T(8,128)(2,1)S(1)} all-gather(bf16[384,192]{0,1:T(8,128)(2,1)S(1)} %copy-done.8), channel_id=1, replica_groups=mesh['group'=2,'seq'=4,'batch'=2,'mp'=2] {'seq'}, dimensions={1}, use_global_device_ids=true | all-gather | bytes 737280 | tf_op jit(solution)/shard_map/all_gather | solution.py:190
  134.5 0.9 reshape.261
  137.8 5.3 %reduce-scatter.7.cloned.1.call-done = bf16[384,128]{1,0:T(8,128)(2,1)} async-done(((bf16[768,128]{1,0:T(8,128)(2,1)}), bf16[384,128]{1,0:T(8,128)(2,1)}) %reduce-scatter.7.cloned.1.call-update) | async-done | bytes 98320
  143.0 1.0 reshape.262
  144.3 1.9 all_gather.22
  147.1 0.9 reduce.9
  148.7 4.8 %all-to-all-start.3 = ((bf16[4,2,3072]{2,1,0:T(2,128)(2,1)}), bf16[4,2,3072]{2,1,0:T(2,128)(2,1)S(1)}, u32[]{:S(2)}, u32[]{:S(2)}) async-start(bf16[4,2,3072]{2,1,0:T(2,128)(2,1)} %reshape.271), calls=%async_computation.3 | async-start | bytes 98304 | tf_op jit(solution)/shard_map/all_to_all | solution.py:254
  153.7 5.5 %all-to-all-done.3 = bf16[4,2,3072]{2,1,0:T(2,128)(2,1)S(1)} async-done(((bf16[4,2,3072]{2,1,0:T(2,128)(2,1)}), bf16[4,2,3072]{2,1,0:T(2,128)(2,1)S(1)}, u32[]{:S(2)}, u32[]{:S(2)}) %all-to-all-start.3) | async-done | bytes 49184 | tf_op jit(solution)/shard_map/all_to_all | solution.py:254
  161.0 0.9 reduce.11
  162.6 3.5 %all-to-all-start.4 = ((bf16[4,2,3072]{2,1,0:T(2,128)(2,1)}), bf16[4,2,3072]{2,1,0:T(2,128)(2,1)S(1)}, u32[]{:S(2)}, u32[]{:S(2)}) async-start(bf16[4,2,3072]{2,1,0:T(2,128)(2,1)} %reshape.275), calls=%async_computation.4 | async-start | bytes 98304 | tf_op jit(solution)/shard_map/all_to_all | solution.py:265
  166.3 1.2 reduce.10
  168.3 3.2 %all-to-all-done.4 = bf16[4,2,3072]{2,1,0:T(2,128)(2,1)S(1)} async-done(((bf16[4,2,3072]{2,1,0:T(2,128)(2,1)}), bf16[4,2,3072]{2,1,0:T(2,128)(2,1)S(1)}, u32[]{:S(2)}, u32[]{:S(2)}) %all-to-all-start.4) | async-done | bytes 49184 | tf_op jit(solution)/shard_map/all_to_all | solution.py:265
  172.1 3.9 %all-to-all-start.5 = ((bf16[4,2,6144]{2,1,0:T(2,128)(2,1)}), bf16[4,2,6144]{2,1,0:T(2,128)(2,1)}, u32[]{:S(2)}, u32[]{:S(2)}) async-start(bf16[4,2,6144]{2,1,0:T(2,128)(2,1)} %reshape.273), calls=%async_computation.5 | async-start | bytes 196608 | tf_op jit(solution)/shard_map/all_to_all | solution.py:272
  176.1 1.0 reshape.276
  177.1 0.9 reduce.4
  178.0 0.9 convert_element_type.211
  179.6 1.6 convert_element_type.213
  181.9 1.7 reshape.274
  183.6 1.5 reduce.5
  185.9 1.2 fusion.123
  188.6 0.9 copy.116
  190.2 1.5 fusion.17
  192.6 8.3 %reduce-scatter.9.cloned.1.call-done = bf16[384,64]{1,0:T(8,128)(2,1)} async-done(((bf16[768,64]{1,0:T(8,128)(2,1)}), bf16[384,64]{1,0:T(8,128)(2,1)}) %reduce-scatter.9.cloned.1.call-update) | async-done | bytes 49168
  200.9 1.0 copy.130
  201.9 1.0 fusion.106
  202.9 2.5 %psum.14 = f32[64]{0:T(128)S(1)} all-reduce(f32[64]{0:T(128)S(1)} %fusion.106), channel_id=1, replica_groups=mesh['group'=2,'seq'=4,'batch'=2,'mp'=2] {'mp'}, use_global_device_ids=true, to_apply=%region_9.0 | all-reduce | flops 64 | bytes 512 | tf_op jit(solution)/shard_map/psum | solution.py:305
  205.4 1.0 broadcast_multiply_fusion
  206.8 1.3 collective-permute-start.2
  208.4 4.5 %collective-permute-start.3 = (bf16[2,384]{1,0:T(2,128)(2,1)S(1)}, bf16[2,384]{1,0:T(2,128)(2,1)S(1)}, u32[]{:S(2)}, u32[]{:S(2)}) collective-permute-start(bf16[2,384]{1,0:T(2,128)(2,1)S(1)} %get-tuple-element.93), channel_id=1, source_target_pairs={{0,4},{4,8},{8,12},{1,5},{5,9},{9,13},{2,6},{6,10},{10,14},{3,7},{... | collective-permute-start | bytes 4616 | tf_op jit(solution)/shard_map/ppermute | solution.py:23
  216.2 19.2 %all-reduce.2.cloned.1.call-done = bf16[128,384]{1,0:T(8,128)(2,1)} async-done(((bf16[128,384]{1,0:T(8,128)(2,1)}), bf16[128,384]{1,0:T(8,128)(2,1)}) %all-reduce.2.cloned.1.call-update) | async-done | bytes 98320 | tf_op jit(solution)/shard_map/psum | solution.py:326
  235.5 1.0 fusion.58
  236.5 1.7 fusion.60
  (138 shorter events, 27.9 us)
Async XLA Ops:
  7.2 13.7 %copy-start.4 = (bf16[1,128,384]{2,1,0:T(8,128)(2,1)S(1)}, bf16[1,128,384]{2,1,0:T(8,128)(2,1)}, u32[]{:S(2)}) copy-start(bf16[1,128,384]{2,1,0:T(8,128)(2,1)} %param.7) | copy-start | bytes 294916
  7.2 40.5 %all-gather.4.cloned.1.call-start = ((), (), s32[]{:S(2)}) async-start(), calls=%async_computation.8 | async-start | bytes 1843200 | tf_op jit(solution)/shard_map/all_gather | solution.py:114
  7.9 80.5 %all-gather.6.cloned.1.call-start = ((), (), s32[]{:S(2)}) async-start(), calls=%async_computation.9 | async-start | bytes 2211840 | tf_op jit(solution)/shard_map/all_gather | solution.py:135
  10.4 6.3 %collective-permute-start = (bf16[2,2,384]{2,1,0:T(2,128)(2,1)S(1)}, bf16[2,2,384]{2,1,0:T(2,128)(2,1)S(1)}, u32[]{:S(2)}, u32[]{:S(2)}) collective-permute-start(bf16[2,2,384]{2,1,0:T(2,128)(2,1)S(1)} %get-tuple-element.88), channel_id=1, source_target_pairs={{0,4},{4,8},{8,12},{1,5},{5,9},{9,13},{2,6},{6,10},{10,14},{3,7},{... | collective-permute-start | bytes 9224 | tf_op jit(solution)/shard_map/ppermute | solution.py:23
  15.4 5.5 %collective-permute-start.1 = (bf16[2,2,384]{2,1,0:T(2,128)(2,1)S(1)}, bf16[2,2,384]{2,1,0:T(2,128)(2,1)S(1)}, u32[]{:S(2)}, u32[]{:S(2)}) collective-permute-start(bf16[2,2,384]{2,1,0:T(2,128)(2,1)S(1)} %get-tuple-element.89), channel_id=1, source_target_pairs={{4,0},{8,4},{12,8},{5,1},{9,5},{13,9},{6,2},{10,6},{14,10},{7,3},{... | collective-permute-start | bytes 9224 | tf_op jit(solution)/shard_map/ppermute | solution.py:25
  47.6 2.6 %copy-start.1 = (bf16[5,384,384]{2,1,0:T(8,128)(2,1)S(1)}, bf16[5,384,384]{2,1,0:T(8,128)(2,1)}, u32[]{:S(2)}) copy-start(bf16[5,384,384]{2,1,0:T(8,128)(2,1)} %all-gather.4.cloned.1.call-done) | copy-start | bytes 4423684
  50.2 0.7 copy-start.10
  51.3 84.9 %copy-start.2 = (f32[2,128,384]{2,1,0:T(8,128)}, f32[2,128,384]{2,1,0:T(8,128)S(1)}, u32[]{:S(2)}) copy-start(f32[2,128,384]{2,1,0:T(8,128)S(1)} %get-tuple-element.95) | copy-start | bytes 1179652
  51.3 37.1 %copy-start.9 = (f32[768]{0:T(1024)S(1)}, f32[768]{0:T(1024)}, u32[]{:S(2)}) copy-start(f32[768]{0:T(1024)} %param.11) | copy-start | bytes 9220
  91.5 9.1 %all-to-all-start = ((bf16[4,2,6144]{2,1,0:T(2,128)(2,1)}), bf16[4,2,6144]{2,1,0:T(2,128)(2,1)S(1)}, u32[]{:S(2)}, u32[]{:S(2)}) async-start(bf16[4,2,6144]{2,1,0:T(2,128)(2,1)} %reshape.242), calls=%async_computation | async-start | bytes 196608 | tf_op jit(solution)/shard_map/all_to_all | solution.py:163
  100.6 9.6 %all-to-all-start.1 = ((bf16[4,2,12288]{2,1,0:T(2,128)(2,1)}), bf16[4,2,12288]{2,1,0:T(2,128)(2,1)S(1)}, u32[]{:S(2)}, u32[]{:S(2)}) async-start(bf16[4,2,12288]{2,1,0:T(2,128)(2,1)} %reshape_reshape.4), calls=%async_computation.1 | async-start | bytes 393216 | tf_op jit(solution)/shard_map/all_to_all | solution.py:164
  110.6 6.0 %copy-start.8 = (bf16[384,192]{0,1:T(8,128)(2,1)S(1)}, bf16[384,192]{0,1:T(8,128)(2,1)}, u32[]{:S(2)}) copy-start(bf16[384,192]{0,1:T(8,128)(2,1)} %param.13) | copy-start | bytes 442372
  113.2 20.2 %all-to-all-start.2 = ((bf16[4,2,6144]{2,1,0:T(2,128)(2,1)}), bf16[4,2,6144]{2,1,0:T(2,128)(2,1)S(1)}, u32[]{:S(2)}, u32[]{:S(2)}) async-start(bf16[4,2,6144]{2,1,0:T(2,128)(2,1)} %copy.103), calls=%async_computation.2 | async-start | bytes 196608 | tf_op jit(solution)/shard_map/all_to_all | solution.py:181
  116.6 26.5 %reduce-scatter.7.cloned.1.call-start = ((), (), s32[]{:S(2)}) async-start(), calls=%async_computation.11 | async-start | bytes 294912
  148.7 10.5 %all-to-all-start.3 = ((bf16[4,2,3072]{2,1,0:T(2,128)(2,1)}), bf16[4,2,3072]{2,1,0:T(2,128)(2,1)S(1)}, u32[]{:S(2)}, u32[]{:S(2)}) async-start(bf16[4,2,3072]{2,1,0:T(2,128)(2,1)} %reshape.271), calls=%async_computation.3 | async-start | bytes 98304 | tf_op jit(solution)/shard_map/all_to_all | solution.py:254
  162.6 8.9 %all-to-all-start.4 = ((bf16[4,2,3072]{2,1,0:T(2,128)(2,1)}), bf16[4,2,3072]{2,1,0:T(2,128)(2,1)S(1)}, u32[]{:S(2)}, u32[]{:S(2)}) async-start(bf16[4,2,3072]{2,1,0:T(2,128)(2,1)} %reshape.275), calls=%async_computation.4 | async-start | bytes 98304 | tf_op jit(solution)/shard_map/all_to_all | solution.py:265
  171.5 0.6 copy-start.7
  172.1 9.8 %all-to-all-start.5 = ((bf16[4,2,6144]{2,1,0:T(2,128)(2,1)}), bf16[4,2,6144]{2,1,0:T(2,128)(2,1)}, u32[]{:S(2)}, u32[]{:S(2)}) async-start(bf16[4,2,6144]{2,1,0:T(2,128)(2,1)} %reshape.273), calls=%async_computation.5 | async-start | bytes 196608 | tf_op jit(solution)/shard_map/all_to_all | solution.py:272
  176.0 14.2 %copy-start = (bf16[3,768,384]{2,1,0:T(8,128)(2,1)S(1)}, bf16[3,768,384]{2,1,0:T(8,128)(2,1)}, u32[]{:S(2)}) copy-start(bf16[3,768,384]{2,1,0:T(8,128)(2,1)} %all-gather.6.cloned.1.call-done) | copy-start | bytes 5308420
  176.1 24.8 %reduce-scatter.9.cloned.1.call-start = ((), (), s32[]{:S(2)}) async-start(), calls=%async_computation.12 | async-start | bytes 294912
  191.7 14.9 %copy-start.3 = (f32[2,128,384]{2,1,0:T(8,128)S(1)}, f32[2,128,384]{2,1,0:T(8,128)}, u32[]{:S(2)}) copy-start(f32[2,128,384]{2,1,0:T(8,128)} %copy-done.2) | copy-start | bytes 1179652
  191.7 16.4 %copy-start.6 = (f32[64,2,384]{2,1,0:T(2,128)S(1)}, f32[64,2,384]{2,1,0:T(2,128)}, u32[]{:S(2)}) copy-start(f32[64,2,384]{2,1,0:T(2,128)} %squeeze.90) | copy-start | bytes 589828
  192.6 42.9 %all-reduce.2.cloned.1.call-start = ((), (), s32[]{:S(2)}) async-start(), calls=%async_computation.10 | async-start | bytes 196608 | tf_op jit(solution)/shard_map/psum | solution.py:326
  206.8 6.4 %collective-permute-start.2 = (bf16[2,384]{1,0:T(2,128)(2,1)S(1)}, bf16[2,384]{1,0:T(2,128)(2,1)S(1)}, u32[]{:S(2)}, u32[]{:S(2)}) collective-permute-start(bf16[2,384]{1,0:T(2,128)(2,1)S(1)} %get-tuple-element.92), channel_id=1, source_target_pairs={{4,0},{8,4},{12,8},{5,1},{9,5},{13,9},{6,2},{10,6},{14,10},{7,3},{... | collective-permute-start | bytes 4616 | tf_op jit(solution)/shard_map/ppermute | solution.py:25
  208.4 5.8 %collective-permute-start.3 = (bf16[2,384]{1,0:T(2,128)(2,1)S(1)}, bf16[2,384]{1,0:T(2,128)(2,1)S(1)}, u32[]{:S(2)}, u32[]{:S(2)}) collective-permute-start(bf16[2,384]{1,0:T(2,128)(2,1)S(1)} %get-tuple-element.93), channel_id=1, source_target_pairs={{0,4},{4,8},{8,12},{1,5},{5,9},{9,13},{2,6},{6,10},{10,14},{3,7},{... | collective-permute-start | bytes 4616 | tf_op jit(solution)/shard_map/ppermute | solution.py:23
  213.4 23.1 %copy-start.5 = (f32[1,128,384]{2,1,0:T(8,128)S(1)}, f32[1,128,384]{2,1,0:T(8,128)}, u32[]{:S(2)}) copy-start(f32[1,128,384]{2,1,0:T(8,128)} %param.8) | copy-start | bytes 589828
Sparse Core Ops, SparseCore 0:
  9.6 38.0 all-gather.3
  49.2 39.1 all-gather.5
  135.6 7.4 reduce-scatter.6
  192.7 8.1 reduce-scatter.8
  215.7 19.7 all-reduce.1
where the time goes:
time: 246 us; the launch traced here: 245 us
  waiting for transfers between devices  120 us (49%)
  starting transfers between devices  34.4 us (14%)
  local copies, waits for them, and re-layouts  27.7 us (11%)
  blocking collectives  23.1 us (9%)
  between operations  14.6 us (6%)
  other arithmetic  13.9 us (6%)
  matrix products  11.3 us (5%)
    all_gather x1, waiting for transfers between devices, forward(): lax.all_gather(qkv_weight, 'seq', axis=1, tiled=True)  34.5 us
    all_gather x1, waiting for transfers between devices, forward(): piece = lax.all_gather(conv_weight, 'seq', axis=1, tiled=True)  26.7 us
    psum x1, waiting for transfers between devices, shards(): lax.psum(running.astype(jnp.bfloat16), 'mp').astype(jnp.float32)  19.2 us
    all_gather x1, blocking collectives, forward(): lax.all_gather(out_weight, 'seq', axis=1, tiled=True)  16.8 us
    unnamed x7, waiting for transfers between devices  14.9 us
    unnamed x34, local copies, waits for them, and re-layouts  9.74 us
    ppermute x2, starting transfers between devices, with_halo(): lax.ppermute(tail, axis, [(i, (i + 1) % count) for i in range(ends)])  9.49 us
    all_to_all x1, waiting for transfers between devices, forward(): lax.all_to_all(keyval_send, 'seq', split_axis=0, concat_axis=2, tiled=True)  5.54 us
  transfers between devices with their start and end apart: 15, of which 12 were waited for; matrix products, arithmetic and copies ran while one was open for 8% of the time, Pallas kernels for 0%

commit v1 on v0

--- a/solution.py
+++ b/solution.py
@@ -29,6 +29,39 @@
     return cells
 
 
+def gather_seq(cells, dim):
+    spread = ("group", "batch")
+    count = lax.axis_size("group") * lax.axis_size("batch")
+    ring = lax.axis_size("seq")
+    flat = cells.reshape(-1, cells.shape[-1])
+    rows = flat.shape[0]
+    size = -(-rows // count)
+    if size * count != rows:
+        flat = jnp.pad(flat, ((0, size * count - rows), (0, 0)))
+    piece = lax.dynamic_slice_in_dim(flat, lax.axis_index(spread) * size, size, 0)
+    along = lax.all_gather(piece, "seq", axis=0, tiled=False)
+    whole = lax.all_gather(along, spread, axis=0, tiled=False)
+    whole = whole.transpose(1, 0, 2, 3).reshape(ring, count * size, flat.shape[1])[:, :rows]
+    whole = jnp.moveaxis(whole.reshape((ring,) + cells.shape), 0, dim)
+    shape = list(cells.shape)
+    shape[dim] = shape[dim] * ring
+    return whole.reshape(shape)
+
+
+def swap_mp(cells):
+    return lax.ppermute(cells, "mp", [(0, 1), (1, 0)])
+
+
+def add_halves(cells, dim):
+    half = cells.shape[dim] // 2
+    index = lax.axis_index("mp")
+    own = lax.dynamic_slice_in_dim(cells, index * half, half, dim)
+    other = lax.dynamic_slice_in_dim(cells, (1 - index) * half, half, dim)
+    return (own.astype(jnp.float32) + swap_mp(other).astype(jnp.float32)).astype(
+        jnp.bfloat16
+    ).astype(jnp.float32)
+
+
 def attend_rows(query, keys, values):
     key_total = keys.shape[0]
     block_len = min(512, key_total)
@@ -111,7 +144,7 @@
     half_width = conv_weight.shape[2]
     padded_input = with_halo(stack, (("seq", 1),), reach)
     running = jnp.zeros((pass_count, positions, half_width), jnp.float32)
-    piece = lax.all_gather(conv_weight, "seq", axis=1, tiled=True)
+    piece = conv_weight
     for offset in range(piece.shape[0]):
         running = running + jnp.einsum(
             "ptc,cf->ptf",
@@ -132,7 +165,7 @@
     projected = jnp.einsum(
         "prf,jfh->jprh",
         normed,
-        lax.all_gather(qkv_weight, "seq", axis=1, tiled=True),
+        qkv_weight,
         preferred_element_type=jnp.float32,
     ).astype(jnp.bfloat16)
     head_size = HD
@@ -187,14 +220,11 @@
     terms = jnp.einsum(
         "prh,hf->prf",
         attended,
-        lax.all_gather(out_weight, "seq", axis=1, tiled=True),
+        out_weight,
         preferred_element_type=jnp.float32,
     )
     mixed = (
-        lax.psum_scatter(terms.astype(jnp.bfloat16), "mp", scatter_dimension=2, tiled=True).astype(
-            jnp.float32
-        )
-        + pooled_wide
+        add_halves(terms.astype(jnp.bfloat16), 2) + pooled_wide
     )
     return (
         pre_act,
@@ -210,6 +240,9 @@
 
 
 def shards(features, noise, conv_weight, conv_bias, norm_gain, qkv_weight, out_weight):
+    conv_weight = gather_seq(conv_weight, 1)
+    qkv_weight = gather_seq(qkv_weight, 1)
+    out_weight = gather_seq(out_weight, 1)
     clean = features[0]
     moved = (clean.astype(jnp.float32) + noise[0]).astype(jnp.bfloat16)
     joint = forward(
@@ -243,7 +276,7 @@
     out_grad = jnp.einsum(
         "rf,hf->rh",
         difference_whole,
-        lax.all_gather(out_weight, "seq", axis=1, tiled=True),
+        out_weight,
         preferred_element_type=jnp.float32,
     ).astype(jnp.bfloat16)
     grad_send = (
@@ -294,14 +327,12 @@
     normed_terms = jnp.einsum(
         "jrh,jfh->rf",
         grads,
-        lax.all_gather(qkv_weight, "seq", axis=1, tiled=True),
+        qkv_weight,
         preferred_element_type=jnp.float32,
     )
     offset_mp = lax.axis_index("mp") * half_width
     gain_own = lax.dynamic_slice_in_dim(norm_gain, offset_mp, half_width, 0)
-    normed_grad = lax.psum_scatter(
-        normed_terms.astype(jnp.bfloat16), "mp", scatter_dimension=1, tiled=True
-    ).astype(jnp.float32)
+    normed_grad = add_halves(normed_terms.astype(jnp.bfloat16), 1)
     weighted = lax.psum(jnp.sum(normed_grad * gain_own * pooled_wide, axis=1, keepdims=True), "mp")
     pooled_grad = (
         difference + row_scale * gain_own * normed_grad - pooled_wide * row_scale**3 * weighted / F
@@ -313,7 +344,7 @@
     pre_grad = gelu_back(spread)[0].astype(jnp.bfloat16)
     reach = KW // 2
     padded = with_halo(pre_grad, (("seq", 0),), reach)
-    piece = lax.all_gather(conv_weight, "seq", axis=1, tiled=True)
+    piece = conv_weight
     running = jnp.zeros((positions, piece.shape[1]), jnp.float32)
     for offset in range(piece.shape[0]):
         lower = 2 * reach - offset
@@ -323,7 +354,10 @@
             piece[offset],
             preferred_element_type=jnp.float32,
         )
-    input_grad = lax.psum(running.astype(jnp.bfloat16), "mp").astype(jnp.float32)
+    own_grad = running.astype(jnp.bfloat16)
+    input_grad = (own_grad.astype(jnp.float32) + swap_mp(own_grad).astype(jnp.float32)).astype(
+        jnp.bfloat16
+    ).astype(jnp.float32)
     new_noise = noise[0] + step_size * input_grad * lax.rsqrt(
         jnp.mean(input_grad * input_grad, axis=1, keepdims=True) + epsilon
     )

time: 246 us -> 225 us (0.915)
  waiting for transfers between devices: 120 us -> 63 us
  blocking collectives: 23.1 us -> 65.3 us
  other arithmetic: 13.9 us -> 7.35 us
  local copies, waits for them, and re-layouts: 27.7 us -> 30.6 us
  matrix products: 11.3 us -> 8.59 us
    all_gather x1 -> x4, blocking collectives: 16.8 us -> 58.7 us  [the longest x3 47.7 us: gather_seq(): along = lax.all_gather(piece, 'seq', axis=0, tiled=False)]
    all_gather x2, waiting for transfers between devices: 61.2 us -> 34.4 us  [gather_seq(): whole = lax.all_gather(along, spread, axis=0, tiled=False)]
    psum x1 -> x0, waiting for transfers between devices: 19.2 us -> none  [shards(): lax.psum(running.astype(jnp.bfloat16), 'mp').astype(jnp.float32)]
    unnamed x7 -> x2, waiting for transfers between devices: 14.9 us -> 0.04 us
    unnamed x34 -> x59, local copies, waits for them, and re-layouts: 9.74 us -> 2.94 us
    transpose x0 -> x4, local copies, waits for them, and re-layouts: none -> 4.64 us  [the longest x3 4.46 us: gather_seq(): whole.transpose(1, 0, 2, 3).reshape(ring, count * size, flat.shape[1])]
    all_to_all x1, waiting for transfers between devices: 0.81 us -> 5.16 us  [shards(): lax.all_to_all(keyval_grad.reshape(devices, rows * 2 * head_size).astype(...]
    dynamic_slice x0 -> x5, local copies, waits for them, and re-layouts: none -> 3.54 us  [the longest x3 1.96 us: gather_seq(): lax.dynamic_slice_in_dim(flat, lax.axis_index(spread) * size, size, 0)]
  transfers between devices with their start and end apart: 15 -> 15, of which waited for: 12 -> 11; matrix products, arithmetic and copies ran while one was open for 8% -> 9% of each run, Pallas kernels for 0% -> 0%
where the time goes in v1:
time: 225 us; the launch traced here: 223 us
  blocking collectives  65.3 us (29%)
  waiting for transfers between devices  63 us (28%)
  starting transfers between devices  33.2 us (15%)
  local copies, waits for them, and re-layouts  30.6 us (14%)
  between operations  15.2 us (7%)
  matrix products  8.59 us (4%)
  other arithmetic  7.35 us (3%)
    all_gather x3, blocking collectives, gather_seq(): along = lax.all_gather(piece, 'seq', axis=0, tiled=False)  47.7 us
    all_gather x2, waiting for transfers between devices, gather_seq(): whole = lax.all_gather(along, spread, axis=0, tiled=False)  34.4 us
    all_gather x1, blocking collectives, gather_seq(): whole = lax.all_gather(along, spread, axis=0, tiled=False)  11 us
    ppermute x2, starting transfers between devices, with_halo(): lax.ppermute(tail, axis, [(i, (i + 1) % count) for i in range(ends)])  7.57 us
    all_to_all x1, waiting for transfers between devices, shards(): lax.all_to_all(keyval_grad.reshape(devices, rows * 2 * head_size).astype(...  5.16 us
    all_to_all x1, waiting for transfers between devices, shards(): lax.all_to_all(grad_send, 'seq', split_axis=0, concat_axis=1, tiled=True)  4.66 us
    all_to_all x1, starting transfers between devices, forward(): lax.all_to_all(query_send, 'seq', split_axis=0, concat_axis=2, tiled=True)  4.6 us
  transfers between devices with their start and end apart: 15, of which 11 were waited for; matrix products, arithmetic and copies ran while one was open for 9% of the time, Pallas kernels for 0%

profile of v1, /device:TPU:0, one launch (start us, length us, event | category | flops | bytes accessed | tf_op | source)
XLA Modules:
  0.0 223.2 jit_solution(12056121577806178305)
XLA Ops:
  7.3 1.0 constant_dynamic-slice_fusion.3
  8.2 16.7 %all-gather.2 = bf16[480,384]{1,0:T(8,128)(2,1)} all-gather(bf16[120,384]{1,0:T(8,128)(2,1)S(1)} %constant_dynamic-slice_fusion.3), channel_id=4, replica_groups=mesh['group'=2,'seq'=4,'batch'=2,'mp'=2] {'seq'}, dimensions={0}, use_global_device_ids=true | all-gather | bytes 460800 | tf_op jit(solution)/shard_map/all_gather | solution.py:42
  25.0 16.6 %all-gather = bf16[576,384]{1,0:T(8,128)(2,1)} all-gather(bf16[144,384]{1,0:T(8,128)(2,1)S(1)} %constant_dynamic-slice_fusion.4), channel_id=2, replica_groups=mesh['group'=2,'seq'=4,'batch'=2,'mp'=2] {'seq'}, dimensions={0}, use_global_device_ids=true | all-gather | bytes 552960 | tf_op jit(solution)/shard_map/all_gather | solution.py:42
  41.7 3.0 %collective-permute-start = (bf16[2,2,384]{2,1,0:T(2,128)(2,1)S(1)}, bf16[2,2,384]{2,1,0:T(2,128)(2,1)S(1)}, u32[]{:S(2)}, u32[]{:S(2)}) collective-permute-start(bf16[2,2,384]{2,1,0:T(2,128)(2,1)S(1)} %get-tuple-element.93), channel_id=1, source_target_pairs={{0,4},{4,8},{8,12},{1,5},{5,9},{9,13},{2,6},{6,10},{10,14},{3,7},{... | collective-permute-start | bytes 9224 | tf_op jit(solution)/shard_map/ppermute | solution.py:23
  44.7 1.3 collective-permute-start.1
  46.0 4.2 %collective-permute-done.1 = bf16[2,2,384]{2,1,0:T(2,128)(2,1)S(1)} collective-permute-done((bf16[2,2,384]{2,1,0:T(2,128)(2,1)S(1)}, bf16[2,2,384]{2,1,0:T(2,128)(2,1)S(1)}, u32[]{:S(2)}, u32[]{:S(2)}) %collective-permute-start.1) | collective-permute-done | bytes 3104 | tf_op jit(solution)/shard_map/ppermute | solution.py:25
  50.3 6.7 %all-gather.12.cloned.1.call-done = bf16[16,120,384]{2,1,0:T(8,128)(2,1)} async-done(((bf16[4,120,384]{2,1,0:T(8,128)(2,1)}), bf16[16,120,384]{2,1,0:T(8,128)(2,1)}) %all-gather.12.cloned.1.call-update) | async-done | bytes 1474576 | tf_op jit(solution)/shard_map/all_gather | solution.py:43
  57.0 1.5 copy.142
  59.9 1.1 fusion.23
  61.6 1.9 all-gather.4
  63.7 27.6 %all-gather.10.cloned.1.call-done = bf16[16,144,384]{2,1,0:T(8,128)(2,1)} async-done(((bf16[4,144,384]{2,1,0:T(8,128)(2,1)}), bf16[16,144,384]{2,1,0:T(8,128)(2,1)}) %all-gather.10.cloned.1.call-update) | async-done | bytes 1769488 | tf_op jit(solution)/shard_map/all_gather | solution.py:43
  91.4 1.7 copy.140
  94.4 0.9 reshape.271
  95.3 4.6 %all-to-all-start = ((bf16[4,2,6144]{2,1,0:T(2,128)(2,1)}), bf16[4,2,6144]{2,1,0:T(2,128)(2,1)S(1)}, u32[]{:S(2)}, u32[]{:S(2)}) async-start(bf16[4,2,6144]{2,1,0:T(2,128)(2,1)} %reshape.271), calls=%async_computation | async-start | bytes 196608 | tf_op jit(solution)/shard_map/all_to_all | solution.py:196
  100.3 1.0 reshape_reshape.12
  101.3 4.4 %all-to-all-done = bf16[4,2,6144]{2,1,0:T(2,128)(2,1)S(1)} async-done(((bf16[4,2,6144]{2,1,0:T(2,128)(2,1)}), bf16[4,2,6144]{2,1,0:T(2,128)(2,1)S(1)}, u32[]{:S(2)}, u32[]{:S(2)}) %all-to-all-start) | async-done | bytes 98336 | tf_op jit(solution)/shard_map/all_to_all | solution.py:196
  105.7 3.4 %all-to-all-start.1 = ((bf16[4,2,12288]{2,1,0:T(2,128)(2,1)}), bf16[4,2,12288]{2,1,0:T(2,128)(2,1)S(1)}, u32[]{:S(2)}, u32[]{:S(2)}) async-start(bf16[4,2,12288]{2,1,0:T(2,128)(2,1)} %reshape_reshape.12), calls=%async_computation.1 | async-start | bytes 393216 | tf_op jit(solution)/shard_map/all_to_all | solution.py:197
  109.1 1.0 constant_dynamic-slice_fusion.2
  110.8 4.4 %all-to-all-done.1 = bf16[4,2,12288]{2,1,0:T(2,128)(2,1)S(1)} async-done(((bf16[4,2,12288]{2,1,0:T(2,128)(2,1)}), bf16[4,2,12288]{2,1,0:T(2,128)(2,1)S(1)}, u32[]{:S(2)}, u32[]{:S(2)}) %all-to-all-start.1) | async-done | bytes 196640 | tf_op jit(solution)/shard_map/all_to_all | solution.py:197
  118.3 3.9 %all-to-all-start.2 = ((bf16[4,2,6144]{2,1,0:T(2,128)(2,1)}), bf16[4,2,6144]{2,1,0:T(2,128)(2,1)}, u32[]{:S(2)}, u32[]{:S(2)}) async-start(bf16[4,2,6144]{2,1,0:T(2,128)(2,1)} %copy.151), calls=%async_computation.2 | async-start | bytes 196608 | tf_op jit(solution)/shard_map/all_to_all | solution.py:214
  122.3 14.4 %all-gather.5 = bf16[384,192]{1,0:T(8,128)(2,1)S(1)} all-gather(bf16[96,192]{1,0:T(8,128)(2,1)S(1)} %copy.184), channel_id=7, replica_groups=mesh['group'=2,'seq'=4,'batch'=2,'mp'=2] {'seq'}, dimensions={0}, use_global_device_ids=true | all-gather | bytes 184320 | tf_op jit(solution)/shard_map/all_gather | solution.py:42
  136.7 11.0 %all-gather.6 = bf16[16,96,192]{2,1,0:T(8,128)(2,1)S(1)} all-gather(bf16[4,96,192]{2,1,0:T(8,128)(2,1)S(1)} %bitcast.210), channel_id=8, replica_groups=mesh['group'=2,'seq'=4,'batch'=2,'mp'=2] {'group','batch'}, dimensions={0}, use_global_device_ids=true | all-gather | bytes 737280 | tf_op jit(solution)/shard_map/all_gather | solution.py:43
  147.7 1.3 copy.154
  149.0 1.8 reshape.275
  150.9 1.3 dynamic_slice.46
  152.2 1.7 reshape.273
  153.9 1.7 copy.152
  155.6 1.1 reshape.274
  156.6 1.0 convolution_convert_fusion.1
  157.6 1.6 constant_dynamic-slice_fusion.1
  159.2 1.3 slice_reduce_fusion
  160.5 1.7 squeeze.87
  162.2 1.0 convert_add_fusion
  163.2 2.0 all_gather.55
  166.2 0.9 reduce.9
  167.8 4.3 %all-to-all-start.3 = ((bf16[4,2,3072]{2,1,0:T(2,128)(2,1)}), bf16[4,2,3072]{2,1,0:T(2,128)(2,1)S(1)}, u32[]{:S(2)}, u32[]{:S(2)}) async-start(bf16[4,2,3072]{2,1,0:T(2,128)(2,1)} %reshape.304), calls=%async_computation.3 | async-start | bytes 98304 | tf_op jit(solution)/shard_map/all_to_all | solution.py:287
  172.1 1.0 fusion.6
  173.2 4.7 %all-to-all-done.3 = bf16[4,2,3072]{2,1,0:T(2,128)(2,1)S(1)} async-done(((bf16[4,2,3072]{2,1,0:T(2,128)(2,1)}), bf16[4,2,3072]{2,1,0:T(2,128)(2,1)S(1)}, u32[]{:S(2)}, u32[]{:S(2)}) %all-to-all-start.3) | async-done | bytes 49184 | tf_op jit(solution)/shard_map/all_to_all | solution.py:287
  179.6 0.9 reduce.11
  181.2 3.3 %all-to-all-start.4 = ((bf16[4,2,3072]{2,1,0:T(2,128)(2,1)}), bf16[4,2,3072]{2,1,0:T(2,128)(2,1)S(1)}, u32[]{:S(2)}, u32[]{:S(2)}) async-start(bf16[4,2,3072]{2,1,0:T(2,128)(2,1)} %reshape.308), calls=%async_computation.4 | async-start | bytes 98304 | tf_op jit(solution)/shard_map/all_to_all | solution.py:298
  184.8 1.2 reduce.10
  186.8 3.3 %all-to-all-done.4 = bf16[4,2,3072]{2,1,0:T(2,128)(2,1)S(1)} async-done(((bf16[4,2,3072]{2,1,0:T(2,128)(2,1)}), bf16[4,2,3072]{2,1,0:T(2,128)(2,1)S(1)}, u32[]{:S(2)}, u32[]{:S(2)}) %all-to-all-start.4) | async-done | bytes 49184 | tf_op jit(solution)/shard_map/all_to_all | solution.py:298
  190.1 3.3 %all-to-all-start.5 = ((bf16[4,2,6144]{2,1,0:T(2,128)(2,1)}), bf16[4,2,6144]{2,1,0:T(2,128)(2,1)S(1)}, u32[]{:S(2)}, u32[]{:S(2)}) async-start(bf16[4,2,6144]{2,1,0:T(2,128)(2,1)} %reshape.306), calls=%async_computation.5 | async-start | bytes 196608 | tf_op jit(solution)/shard_map/all_to_all | solution.py:305
  194.1 5.2 %all-to-all-done.5 = bf16[4,2,6144]{2,1,0:T(2,128)(2,1)S(1)} async-done(((bf16[4,2,6144]{2,1,0:T(2,128)(2,1)}), bf16[4,2,6144]{2,1,0:T(2,128)(2,1)S(1)}, u32[]{:S(2)}, u32[]{:S(2)}) %all-to-all-start.5) | async-done | bytes 98336 | tf_op jit(solution)/shard_map/all_to_all | solution.py:305
  201.7 1.0 collective-permute-done.3
  202.8 2.6 %psum.7 = f32[64]{0:T(128)S(1)} all-reduce(f32[64]{0:T(128)S(1)} %fusion.75), channel_id=1, replica_groups=mesh['group'=2,'seq'=4,'batch'=2,'mp'=2] {'mp'}, use_global_device_ids=true, to_apply=%region_7.8 | all-reduce | flops 64 | bytes 512 | tf_op jit(solution)/shard_map/psum | solution.py:336
  205.9 1.3 collective-permute-start.4
  207.5 4.5 %collective-permute-start.5 = (bf16[2,384]{1,0:T(2,128)(2,1)S(1)}, bf16[2,384]{1,0:T(2,128)(2,1)S(1)}, u32[]{:S(2)}, u32[]{:S(2)}) collective-permute-start(bf16[2,384]{1,0:T(2,128)(2,1)S(1)} %get-tuple-element.107), channel_id=1, source_target_pairs={{0,4},{4,8},{8,12},{1,5},{5,9},{9,13},{2,6},{6,10},{10,14},{3,7},{... | collective-permute-start | bytes 4616 | tf_op jit(solution)/shard_map/ppermute | solution.py:23
  (174 shorter events, 20.6 us)
Async XLA Ops:
  7.2 17.8 %copy-start = (bf16[3,192,384]{2,1,0:T(8,128)(2,1)S(1)}, bf16[3,192,384]{2,1,0:T(8,128)(2,1)}, u32[]{:S(2)}) copy-start(bf16[3,192,384]{2,1,0:T(8,128)(2,1)} %param.12) | copy-start | bytes 1327108
  7.2 34.4 %copy-start.11 = (bf16[1,128,384]{2,1,0:T(8,128)(2,1)S(1)}, bf16[1,128,384]{2,1,0:T(8,128)(2,1)}, u32[]{:S(2)}) copy-start(bf16[1,128,384]{2,1,0:T(8,128)(2,1)} %param.7) | copy-start | bytes 294916
  7.2 34.4 %copy-start.15 = (f32[1,128,384]{2,1,0:T(8,128)S(1)}, f32[1,128,384]{2,1,0:T(8,128)}, u32[]{:S(2)}) copy-start(f32[1,128,384]{2,1,0:T(8,128)} %param.8) | copy-start | bytes 589828
  7.2 49.8 %all-gather.12.cloned.1.call-start = ((), (), s32[]{:S(2)}) async-start(), calls=%async_computation.7 | async-start | bytes 1843200 | tf_op jit(solution)/shard_map/all_gather | solution.py:43
  24.9 66.4 %all-gather.10.cloned.1.call-start = ((), (), s32[]{:S(2)}) async-start(), calls=%async_computation.6 | async-start | bytes 2211840 | tf_op jit(solution)/shard_map/all_gather | solution.py:43
  41.7 4.3 %collective-permute-start = (bf16[2,2,384]{2,1,0:T(2,128)(2,1)S(1)}, bf16[2,2,384]{2,1,0:T(2,128)(2,1)S(1)}, u32[]{:S(2)}, u32[]{:S(2)}) collective-permute-start(bf16[2,2,384]{2,1,0:T(2,128)(2,1)S(1)} %get-tuple-element.93), channel_id=1, source_target_pairs={{0,4},{4,8},{8,12},{1,5},{5,9},{9,13},{2,6},{6,10},{10,14},{3,7},{... | collective-permute-start | bytes 9224 | tf_op jit(solution)/shard_map/ppermute | solution.py:23
  44.7 5.5 %collective-permute-start.1 = (bf16[2,2,384]{2,1,0:T(2,128)(2,1)S(1)}, bf16[2,2,384]{2,1,0:T(2,128)(2,1)S(1)}, u32[]{:S(2)}, u32[]{:S(2)}) collective-permute-start(bf16[2,2,384]{2,1,0:T(2,128)(2,1)S(1)} %get-tuple-element.94), channel_id=1, source_target_pairs={{4,0},{8,4},{12,8},{5,1},{9,5},{13,9},{6,2},{10,6},{14,10},{7,3},{... | collective-permute-start | bytes 9224 | tf_op jit(solution)/shard_map/ppermute | solution.py:25
  58.7 1.2 copy-start.1
  58.7 1.2 copy-start.3
  58.7 1.2 copy-start.5
  58.7 1.2 copy-start.7
  59.0 0.9 copy-start.21
  61.6 31.4 %copy-start.12 = (bf16[2,64,1,384]{3,1,0,2:T(8,128)(2,1)}, bf16[2,64,1,384]{3,1,0,2:T(8,128)(2,1)S(1)}, u32[]{:S(2)}) copy-start(bf16[2,64,1,384]{3,1,0,2:T(8,128)(2,1)S(1)} %fusion.54) | copy-start | bytes 294916
  63.7 29.5 %copy-start.23 = (f32[2,64]{1,0:T(2,128)}, f32[2,64]{1,0:T(2,128)S(1)}, u32[]{:S(2)}) copy-start(f32[2,64]{1,0:T(2,128)S(1)} %add_rsqrt_fusion) | copy-start | bytes 1540
  93.0 0.7 copy-start.22
  95.3 10.4 %all-to-all-start = ((bf16[4,2,6144]{2,1,0:T(2,128)(2,1)}), bf16[4,2,6144]{2,1,0:T(2,128)(2,1)S(1)}, u32[]{:S(2)}, u32[]{:S(2)}) async-start(bf16[4,2,6144]{2,1,0:T(2,128)(2,1)} %reshape.271), calls=%async_computation | async-start | bytes 196608 | tf_op jit(solution)/shard_map/all_to_all | solution.py:196
  105.7 9.6 %all-to-all-start.1 = ((bf16[4,2,12288]{2,1,0:T(2,128)(2,1)}), bf16[4,2,12288]{2,1,0:T(2,128)(2,1)S(1)}, u32[]{:S(2)}, u32[]{:S(2)}) async-start(bf16[4,2,12288]{2,1,0:T(2,128)(2,1)} %reshape_reshape.12), calls=%async_computation.1 | async-start | bytes 393216 | tf_op jit(solution)/shard_map/all_to_all | solution.py:197
  116.9 19.8 %copy-start.20 = (f32[256]{0:T(256)}, f32[256]{0:T(256)S(1)}, u32[]{:S(2)}) copy-start(f32[256]{0:T(256)S(1)} %log_add_fusion) | copy-start | bytes 3076
  117.2 19.5 %copy-start.17 = (bf16[256,96]{0,1:T(8,128)(2,1)}, bf16[256,96]{0,1:T(8,128)(2,1)S(1)}, u32[]{:S(2)}) copy-start(bf16[256,96]{0,1:T(8,128)(2,1)S(1)} %convolution_convert_fusion.4) | copy-start | bytes 147460
  118.3 33.9 %all-to-all-start.2 = ((bf16[4,2,6144]{2,1,0:T(2,128)(2,1)}), bf16[4,2,6144]{2,1,0:T(2,128)(2,1)}, u32[]{:S(2)}, u32[]{:S(2)}) async-start(bf16[4,2,6144]{2,1,0:T(2,128)(2,1)} %copy.151), calls=%async_computation.2 | async-start | bytes 196608 | tf_op jit(solution)/shard_map/all_to_all | solution.py:214
  149.0 13.2 %copy-start.13 = (bf16[2,64,1,384]{3,1,0,2:T(8,128)(2,1)S(1)}, bf16[2,64,1,384]{3,1,0,2:T(8,128)(2,1)}, u32[]{:S(2)}) copy-start(bf16[2,64,1,384]{3,1,0,2:T(8,128)(2,1)} %copy-done.12) | copy-start | bytes 294916
  159.2 3.0 %collective-permute-start.2 = (bf16[2,64,384]{2,1,0:T(8,128)(2,1)}, bf16[2,64,384]{2,1,0:T(8,128)(2,1)}, u32[]{:S(2)}, u32[]{:S(2)}) collective-permute-start(bf16[2,64,384]{2,1,0:T(8,128)(2,1)} %constant_dynamic-slice_fusion.1), channel_id=1, source_target_pairs={{0,1},{1,0},{2,3},{3,2},{4,5},{5,4},{6,7},{7,6},{8,9},{9,8},{10,11... | collective-permute-start | bytes 294920 | tf_op jit(solution)/shard_map/ppermute | solution.py:52
  160.5 17.9 %copy-start.18 = (bf16[256,96]{0,1:T(8,128)(2,1)S(1)}, bf16[256,96]{0,1:T(8,128)(2,1)}, u32[]{:S(2)}) copy-start(bf16[256,96]{0,1:T(8,128)(2,1)} %copy-done.17) | copy-start | bytes 147460
  165.5 13.0 %copy-start.14 = (bf16[256,192]{1,0:T(8,128)(2,1)S(1)}, bf16[256,192]{1,0:T(8,128)(2,1)}, u32[]{:S(2)}) copy-start(bf16[256,192]{1,0:T(8,128)(2,1)} %squeeze.87) | copy-start | bytes 294916
  167.8 10.0 %all-to-all-start.3 = ((bf16[4,2,3072]{2,1,0:T(2,128)(2,1)}), bf16[4,2,3072]{2,1,0:T(2,128)(2,1)S(1)}, u32[]{:S(2)}, u32[]{:S(2)}) async-start(bf16[4,2,3072]{2,1,0:T(2,128)(2,1)} %reshape.304), calls=%async_computation.3 | async-start | bytes 98304 | tf_op jit(solution)/shard_map/all_to_all | solution.py:287
  178.4 15.1 %copy-start.24 = (f32[2,64]{1,0:T(2,128)S(1)}, f32[2,64]{1,0:T(2,128)}, u32[]{:S(2)}) copy-start(f32[2,64]{1,0:T(2,128)} %copy-done.23) | copy-start | bytes 1540
  181.2 8.9 %all-to-all-start.4 = ((bf16[4,2,3072]{2,1,0:T(2,128)(2,1)}), bf16[4,2,3072]{2,1,0:T(2,128)(2,1)S(1)}, u32[]{:S(2)}, u32[]{:S(2)}) async-start(bf16[4,2,3072]{2,1,0:T(2,128)(2,1)} %reshape.308), calls=%async_computation.4 | async-start | bytes 98304 | tf_op jit(solution)/shard_map/all_to_all | solution.py:298
  190.1 9.1 %all-to-all-start.5 = ((bf16[4,2,6144]{2,1,0:T(2,128)(2,1)}), bf16[4,2,6144]{2,1,0:T(2,128)(2,1)S(1)}, u32[]{:S(2)}, u32[]{:S(2)}) async-start(bf16[4,2,6144]{2,1,0:T(2,128)(2,1)} %reshape.306), calls=%async_computation.5 | async-start | bytes 196608 | tf_op jit(solution)/shard_map/all_to_all | solution.py:305
  200.1 1.4 copy-start.25
  200.3 1.2 copy-start.9
  200.4 2.3 %copy-start.19 = (f32[384]{0:T(512)S(1)}, f32[384]{0:T(512)}, u32[]{:S(2)}) copy-start(f32[384]{0:T(512)} %dynamic_slice.46) | copy-start | bytes 4612
  201.3 4.4 %copy-start.10 = (f32[2,128,384]{2,1,0:T(8,128)S(1)}, f32[2,128,384]{2,1,0:T(8,128)}, u32[]{:S(2)}) copy-start(f32[2,128,384]{2,1,0:T(8,128)} %get-tuple-element.109) | copy-start | bytes 1179652
  201.4 1.3 collective-permute-start.3
  201.5 10.6 %copy-start.8 = (bf16[1,4,96,384]{3,2,0,1:T(8,128)(2,1)S(1)}, bf16[1,4,96,384]{3,2,0,1:T(8,128)(2,1)}, u32[]{:S(2)}) copy-start(bf16[1,4,96,384]{3,2,0,1:T(8,128)(2,1)} %copy-done.7) | copy-start | bytes 884740
  202.8 9.6 %copy-start.6 = (bf16[1,4,96,384]{3,2,0,1:T(8,128)(2,1)S(1)}, bf16[1,4,96,384]{3,2,0,1:T(8,128)(2,1)}, u32[]{:S(2)}) copy-start(bf16[1,4,96,384]{3,2,0,1:T(8,128)(2,1)} %copy-done.5) | copy-start | bytes 884740
  205.5 7.9 %copy-start.4 = (bf16[1,4,96,384]{3,2,0,1:T(8,128)(2,1)S(1)}, bf16[1,4,96,384]{3,2,0,1:T(8,128)(2,1)}, u32[]{:S(2)}) copy-start(bf16[1,4,96,384]{3,2,0,1:T(8,128)(2,1)} %copy-done.3) | copy-start | bytes 884740
  205.6 8.0 %copy-start.2 = (bf16[1,4,96,384]{3,2,0,1:T(8,128)(2,1)S(1)}, bf16[1,4,96,384]{3,2,0,1:T(8,128)(2,1)}, u32[]{:S(2)}) copy-start(bf16[1,4,96,384]{3,2,0,1:T(8,128)(2,1)} %copy-done.1) | copy-start | bytes 884740
  205.9 6.4 %collective-permute-start.4 = (bf16[2,384]{1,0:T(2,128)(2,1)S(1)}, bf16[2,384]{1,0:T(2,128)(2,1)S(1)}, u32[]{:S(2)}, u32[]{:S(2)}) collective-permute-start(bf16[2,384]{1,0:T(2,128)(2,1)S(1)} %get-tuple-element.106), channel_id=1, source_target_pairs={{4,0},{8,4},{12,8},{5,1},{9,5},{13,9},{6,2},{10,6},{14,10},{7,3},{... | collective-permute-start | bytes 4616 | tf_op jit(solution)/shard_map/ppermute | solution.py:25
  207.5 5.8 %collective-permute-start.5 = (bf16[2,384]{1,0:T(2,128)(2,1)S(1)}, bf16[2,384]{1,0:T(2,128)(2,1)S(1)}, u32[]{:S(2)}, u32[]{:S(2)}) collective-permute-start(bf16[2,384]{1,0:T(2,128)(2,1)S(1)} %get-tuple-element.107), channel_id=1, source_target_pairs={{0,4},{4,8},{8,12},{1,5},{5,9},{9,13},{2,6},{6,10},{10,14},{3,7},{... | collective-permute-start | bytes 4616 | tf_op jit(solution)/shard_map/ppermute | solution.py:23
  212.3 3.3 %copy-start.16 = (f32[1,128,384]{2,1,0:T(8,128)S(1)}, f32[1,128,384]{2,1,0:T(8,128)}, u32[]{:S(2)}) copy-start(f32[1,128,384]{2,1,0:T(8,128)} %param.8) | copy-start | bytes 589828
  214.1 1.4 collective-permute-start.6
Sparse Core Ops, SparseCore 0:
  25.0 31.9 all-gather.11
  58.9 32.4 all-gather.9

commit v2 on v1

--- a/solution.py
+++ b/solution.py
@@ -39,7 +39,17 @@
     if size * count != rows:
         flat = jnp.pad(flat, ((0, size * count - rows), (0, 0)))
     piece = lax.dynamic_slice_in_dim(flat, lax.axis_index(spread) * size, size, 0)
-    along = lax.all_gather(piece, "seq", axis=0, tiled=False)
+    if ring <= 8:
+        place = lax.axis_index("seq")
+        along = jnp.zeros((ring,) + piece.shape, piece.dtype)
+        along = lax.dynamic_update_slice_in_dim(along, piece[None], place, 0)
+        for shift in range(1, ring):
+            arrived = lax.ppermute(piece, "seq", [(i, (i + shift) % ring) for i in range(ring)])
+            along = lax.dynamic_update_slice_in_dim(
+                along, arrived[None], (place + ring - shift) % ring, 0
+            )
+    else:
+        along = lax.all_gather(piece, "seq", axis=0, tiled=False)
     whole = lax.all_gather(along, spread, axis=0, tiled=False)
     whole = whole.transpose(1, 0, 2, 3).reshape(ring, count * size, flat.shape[1])[:, :rows]
     whole = jnp.moveaxis(whole.reshape((ring,) + cells.shape), 0, dim)

time: 225 us -> 195 us (0.87)
  blocking collectives: 65.3 us -> 18 us
  starting transfers between devices: 33.2 us -> 50.9 us
  waiting for transfers between devices: 63 us -> 73.2 us
  local copies, waits for them, and re-layouts: 30.6 us -> 22.6 us
    all_gather x3 -> x0, blocking collectives: 47.7 us -> none  [gather_seq(): along = lax.all_gather(piece, 'seq', axis=0, tiled=False)]
    ppermute x0 -> x9, starting transfers between devices: none -> 15.7 us  [gather_seq(): lax.ppermute(piece, 'seq', [(i, (i + shift) % ring) for i in range(ring)])]
    ppermute x0 -> x9, waiting for transfers between devices: none -> 8.57 us  [gather_seq(): lax.ppermute(piece, 'seq', [(i, (i + shift) % ring) for i in range(ring)])]
    transpose x3 -> x1, local copies, waits for them, and re-layouts: 4.46 us -> 0.6 us  [gather_seq(): whole.transpose(1, 0, 2, 3).reshape(ring, count * size, flat.shape[1])]
    unnamed x59 -> x67, local copies, waits for them, and re-layouts: 2.94 us -> 4.59 us
  transfers between devices with their start and end apart: 15 -> 24, of which waited for: 11 -> 17; matrix products, arithmetic and copies ran while one was open for 9% -> 11% of each run, Pallas kernels for 0% -> 0%
where the time goes in v2:
time: 195 us; the launch traced here: 194 us
  waiting for transfers between devices  73.2 us (38%)
  starting transfers between devices  50.9 us (26%)
  local copies, waits for them, and re-layouts  22.6 us (12%)
  blocking collectives  18 us (9%)
  between operations  15.4 us (8%)
  matrix products  7.02 us (4%)
  other arithmetic  6.41 us (3%)
    all_gather x2, waiting for transfers between devices, gather_seq(): whole = lax.all_gather(along, spread, axis=0, tiled=False)  35.2 us
    ppermute x9, starting transfers between devices, gather_seq(): lax.ppermute(piece, 'seq', [(i, (i + shift) % ring) for i in range(ring)])  15.7 us
    all_gather x1, blocking collectives, gather_seq(): whole = lax.all_gather(along, spread, axis=0, tiled=False)  11.6 us
    ppermute x2, starting transfers between devices, with_halo(): lax.ppermute(tail, axis, [(i, (i + 1) % count) for i in range(ends)])  8.79 us
    ppermute x9, waiting for transfers between devices, gather_seq(): lax.ppermute(piece, 'seq', [(i, (i + shift) % ring) for i in range(ring)])  8.57 us
    all_to_all x1, waiting for transfers between devices, forward(): lax.all_to_all(keyval_send, 'seq', split_axis=0, concat_axis=2, tiled=True)  5.51 us
    all_to_all x1, waiting for transfers between devices, shards(): lax.all_to_all(grad_send, 'seq', split_axis=0, concat_axis=1, tiled=True)  5.49 us
    all_to_all x1, waiting for transfers between devices, shards(): lax.all_to_all(keyval_grad.reshape(devices, rows * 2 * head_size).astype(...  5.16 us
  transfers between devices with their start and end apart: 24, of which 17 were waited for; matrix products, arithmetic and copies ran while one was open for 11% of the time, Pallas kernels for 0%

profile of v2, /device:TPU:0, one launch (start us, length us, event | category | flops | bytes accessed | tf_op | source)
XLA Modules:
  0.0 193.6 jit_solution(10006453348819088747)
XLA Ops:
  7.3 1.0 bitcast_dynamic-update-slice_fusion.7
  8.3 3.1 %collective-permute-start.4 = (bf16[120,384]{1,0:T(8,128)(2,1)S(1)}, bf16[120,384]{1,0:T(8,128)(2,1)S(1)}, u32[]{:S(2)}, u32[]{:S(2)}) collective-permute-start(bf16[120,384]{1,0:T(8,128)(2,1)S(1)} %get-tuple-element.76), channel_id=1, source_target_pairs={{0,4},{4,8},{8,12},{12,0},{1,5},{5,9},{9,13},{13,1},{2,6},{6,10},{... | collective-permute-start | bytes 276488 | tf_op jit(solution)/shard_map/ppermute | solution.py:47
  11.4 2.6 %collective-permute-start.5 = (bf16[120,384]{1,0:T(8,128)(2,1)S(1)}, bf16[120,384]{1,0:T(8,128)(2,1)S(1)}, u32[]{:S(2)}, u32[]{:S(2)}) collective-permute-start(bf16[120,384]{1,0:T(8,128)(2,1)S(1)} %get-tuple-element.76), channel_id=1, source_target_pairs={{0,8},{4,12},{8,0},{12,4},{1,9},{5,13},{9,1},{13,5},{2,10},{6,14},... | collective-permute-start | bytes 276488 | tf_op jit(solution)/shard_map/ppermute | solution.py:47
  14.0 1.3 collective-permute-start.6
  15.3 1.5 collective-permute-done.4
  16.8 3.3 %collective-permute-done.5 = bf16[120,384]{1,0:T(8,128)(2,1)S(1)} collective-permute-done((bf16[120,384]{1,0:T(8,128)(2,1)S(1)}, bf16[120,384]{1,0:T(8,128)(2,1)S(1)}, u32[]{:S(2)}, u32[]{:S(2)}) %collective-permute-start.5) | collective-permute-done | bytes 92192 | tf_op jit(solution)/shard_map/ppermute | solution.py:47
  21.3 0.9 bitcast_dynamic-update-slice_fusion.3
  22.2 2.3 %collective-permute-start = (bf16[144,384]{1,0:T(8,128)(2,1)S(1)}, bf16[144,384]{1,0:T(8,128)(2,1)S(1)}, u32[]{:S(2)}, u32[]{:S(2)}) collective-permute-start(bf16[144,384]{1,0:T(8,128)(2,1)S(1)} %get-tuple-element.78), channel_id=1, source_target_pairs={{0,4},{4,8},{8,12},{12,0},{1,5},{5,9},{9,13},{13,1},{2,6},{6,10},{... | collective-permute-start | bytes 331784 | tf_op jit(solution)/shard_map/ppermute | solution.py:47
  24.5 1.7 collective-permute-start.1
  27.1 1.4 collective-permute-start.8
  28.5 1.2 collective-permute-start.9
  30.1 1.3 collective-permute-start.10
  31.4 3.3 %collective-permute-done.1 = bf16[144,384]{1,0:T(8,128)(2,1)S(1)} collective-permute-done((bf16[144,384]{1,0:T(8,128)(2,1)S(1)}, bf16[144,384]{1,0:T(8,128)(2,1)S(1)}, u32[]{:S(2)}, u32[]{:S(2)}) %collective-permute-start.1) | collective-permute-done | bytes 110624 | tf_op jit(solution)/shard_map/ppermute | solution.py:47
  34.7 4.2 %collective-permute-start.3 = (bf16[2,2,384]{2,1,0:T(2,128)(2,1)S(1)}, bf16[2,2,384]{2,1,0:T(2,128)(2,1)S(1)}, u32[]{:S(2)}, u32[]{:S(2)}) collective-permute-start(bf16[2,2,384]{2,1,0:T(2,128)(2,1)S(1)} %get-tuple-element.106), channel_id=1, source_target_pairs={{0,4},{4,8},{8,12},{1,5},{5,9},{9,13},{2,6},{6,10},{10,14},{3,7},{... | collective-permute-start | bytes 9224 | tf_op jit(solution)/shard_map/ppermute | solution.py:23
  39.0 1.3 collective-permute-start.7
  40.3 0.8 copy-done.13
  41.8 2.6 %collective-permute-done.7 = bf16[2,2,384]{2,1,0:T(2,128)(2,1)S(1)} collective-permute-done((bf16[2,2,384]{2,1,0:T(2,128)(2,1)S(1)}, bf16[2,2,384]{2,1,0:T(2,128)(2,1)S(1)}, u32[]{:S(2)}, u32[]{:S(2)}) %collective-permute-start.7) | collective-permute-done | bytes 3104 | tf_op jit(solution)/shard_map/ppermute | solution.py:25
  44.5 7.9 %all-gather.6.cloned.1.call-done = bf16[4,4,120,384]{3,2,0,1:T(8,128)(2,1)} async-done(((bf16[1,4,120,384]{3,2,0,1:T(8,128)(2,1)}), bf16[4,4,120,384]{3,2,0,1:T(8,128)(2,1)}) %all-gather.6.cloned.1.call-update) | async-done | bytes 1474576 | tf_op jit(solution)/shard_map/all_gather | solution.py:53
  52.4 1.5 fusion.92
  55.1 1.1 fusion.23
  57.4 1.9 all-gather
  59.5 27.3 %all-gather.4.cloned.1.call-done = bf16[4,4,144,384]{3,2,0,1:T(8,128)(2,1)} async-done(((bf16[1,4,144,384]{3,2,0,1:T(8,128)(2,1)}), bf16[4,4,144,384]{3,2,0,1:T(8,128)(2,1)}) %all-gather.4.cloned.1.call-update) | async-done | bytes 1769488 | tf_op jit(solution)/shard_map/all_gather | solution.py:53
  86.8 1.7 copy.135
  89.1 0.9 reshape.307
  90.0 4.6 %all-to-all-start = ((bf16[4,2,6144]{2,1,0:T(2,128)(2,1)}), bf16[4,2,6144]{2,1,0:T(2,128)(2,1)S(1)}, u32[]{:S(2)}, u32[]{:S(2)}) async-start(bf16[4,2,6144]{2,1,0:T(2,128)(2,1)} %reshape.307), calls=%async_computation | async-start | bytes 196608 | tf_op jit(solution)/shard_map/all_to_all | solution.py:206
  95.1 1.0 reshape_reshape.12
  96.1 4.4 %all-to-all-done = bf16[4,2,6144]{2,1,0:T(2,128)(2,1)S(1)} async-done(((bf16[4,2,6144]{2,1,0:T(2,128)(2,1)}), bf16[4,2,6144]{2,1,0:T(2,128)(2,1)S(1)}, u32[]{:S(2)}, u32[]{:S(2)}) %all-to-all-start) | async-done | bytes 98336 | tf_op jit(solution)/shard_map/all_to_all | solution.py:206
  100.5 3.4 %all-to-all-start.1 = ((bf16[4,2,12288]{2,1,0:T(2,128)(2,1)}), bf16[4,2,12288]{2,1,0:T(2,128)(2,1)S(1)}, u32[]{:S(2)}, u32[]{:S(2)}) async-start(bf16[4,2,12288]{2,1,0:T(2,128)(2,1)} %reshape_reshape.12), calls=%async_computation.1 | async-start | bytes 393216 | tf_op jit(solution)/shard_map/all_to_all | solution.py:207
  104.5 5.5 %all-to-all-done.1 = bf16[4,2,12288]{2,1,0:T(2,128)(2,1)S(1)} async-done(((bf16[4,2,12288]{2,1,0:T(2,128)(2,1)}), bf16[4,2,12288]{2,1,0:T(2,128)(2,1)S(1)}, u32[]{:S(2)}, u32[]{:S(2)}) %all-to-all-start.1) | async-done | bytes 196640 | tf_op jit(solution)/shard_map/all_to_all | solution.py:207
  113.1 3.9 %all-to-all-start.2 = ((bf16[4,2,6144]{2,1,0:T(2,128)(2,1)}), bf16[4,2,6144]{2,1,0:T(2,128)(2,1)}, u32[]{:S(2)}, u32[]{:S(2)}) async-start(bf16[4,2,6144]{2,1,0:T(2,128)(2,1)} %copy.146), calls=%async_computation.2 | async-start | bytes 196608 | tf_op jit(solution)/shard_map/all_to_all | solution.py:224
  117.1 11.6 %all_gather.66 = bf16[4,4,96,192]{3,2,1,0:T(8,128)(2,1)S(1)} all-gather(bf16[1,4,96,192]{3,2,1,0:T(8,128)(2,1)S(1)} %bitcast_dynamic-update-slice_fusion.8), channel_id=1, replica_groups=mesh['group'=2,'seq'=4,'batch'=2,'mp'=2] {'group','batch'}, dimensions={0}, use_global_device_ids=true | all-gather | bytes 737280 | tf_op jit(solution)/shard_map/all_gather | solution.py:53
  129.8 1.1 reshape.309
  132.9 1.9 all_gather.67
  135.8 0.9 reduce.9
  137.4 5.1 %all-to-all-start.3 = ((bf16[4,2,3072]{2,1,0:T(2,128)(2,1)}), bf16[4,2,3072]{2,1,0:T(2,128)(2,1)S(1)}, u32[]{:S(2)}, u32[]{:S(2)}) async-start(bf16[4,2,3072]{2,1,0:T(2,128)(2,1)} %reshape.334), calls=%async_computation.3 | async-start | bytes 98304 | tf_op jit(solution)/shard_map/all_to_all | solution.py:297
  142.8 5.5 %all-to-all-done.3 = bf16[4,2,3072]{2,1,0:T(2,128)(2,1)S(1)} async-done(((bf16[4,2,3072]{2,1,0:T(2,128)(2,1)}), bf16[4,2,3072]{2,1,0:T(2,128)(2,1)S(1)}, u32[]{:S(2)}, u32[]{:S(2)}) %all-to-all-start.3) | async-done | bytes 49184 | tf_op jit(solution)/shard_map/all_to_all | solution.py:297
  150.0 0.9 reduce.11
  151.6 3.3 %all-to-all-start.4 = ((bf16[4,2,3072]{2,1,0:T(2,128)(2,1)}), bf16[4,2,3072]{2,1,0:T(2,128)(2,1)S(1)}, u32[]{:S(2)}, u32[]{:S(2)}) async-start(bf16[4,2,3072]{2,1,0:T(2,128)(2,1)} %reshape.338), calls=%async_computation.4 | async-start | bytes 98304 | tf_op jit(solution)/shard_map/all_to_all | solution.py:308
  155.2 1.2 reduce.10
  157.2 3.3 %all-to-all-done.4 = bf16[4,2,3072]{2,1,0:T(2,128)(2,1)S(1)} async-done(((bf16[4,2,3072]{2,1,0:T(2,128)(2,1)}), bf16[4,2,3072]{2,1,0:T(2,128)(2,1)S(1)}, u32[]{:S(2)}, u32[]{:S(2)}) %all-to-all-start.4) | async-done | bytes 49184 | tf_op jit(solution)/shard_map/all_to_all | solution.py:308
  160.5 3.3 %all-to-all-start.5 = ((bf16[4,2,6144]{2,1,0:T(2,128)(2,1)}), bf16[4,2,6144]{2,1,0:T(2,128)(2,1)S(1)}, u32[]{:S(2)}, u32[]{:S(2)}) async-start(bf16[4,2,6144]{2,1,0:T(2,128)(2,1)} %reshape.336), calls=%async_computation.5 | async-start | bytes 196608 | tf_op jit(solution)/shard_map/all_to_all | solution.py:315
  164.5 5.2 %all-to-all-done.5 = bf16[4,2,6144]{2,1,0:T(2,128)(2,1)S(1)} async-done(((bf16[4,2,6144]{2,1,0:T(2,128)(2,1)}), bf16[4,2,6144]{2,1,0:T(2,128)(2,1)S(1)}, u32[]{:S(2)}, u32[]{:S(2)}) %all-to-all-start.5) | async-done | bytes 98336 | tf_op jit(solution)/shard_map/all_to_all | solution.py:315
  172.0 1.0 collective-permute-done.12
  173.2 2.6 %psum.7 = f32[64]{0:T(128)S(1)} all-reduce(f32[64]{0:T(128)S(1)} %fusion.75), channel_id=1, replica_groups=mesh['group'=2,'seq'=4,'batch'=2,'mp'=2] {'mp'}, use_global_device_ids=true, to_apply=%region_7.8 | all-reduce | flops 64 | bytes 512 | tf_op jit(solution)/shard_map/psum | solution.py:346
  176.3 1.3 collective-permute-start.13
  177.9 4.5 %collective-permute-start.14 = (bf16[2,384]{1,0:T(2,128)(2,1)S(1)}, bf16[2,384]{1,0:T(2,128)(2,1)S(1)}, u32[]{:S(2)}, u32[]{:S(2)}) collective-permute-start(bf16[2,384]{1,0:T(2,128)(2,1)S(1)} %get-tuple-element.111), channel_id=1, source_target_pairs={{0,4},{4,8},{8,12},{1,5},{5,9},{9,13},{2,6},{6,10},{10,14},{3,7},{... | collective-permute-start | bytes 4616 | tf_op jit(solution)/shard_map/ppermute | solution.py:23
  183.0 0.8 collective-permute-done.14
  186.0 0.8 fusion.26
  (208 shorter events, 25.0 us)
Async XLA Ops:
  7.2 19.8 %copy-start = (bf16[384,192]{0,1:T(8,128)(2,1)S(1)}, bf16[384,192]{0,1:T(8,128)(2,1)}, u32[]{:S(2)}) copy-start(bf16[384,192]{0,1:T(8,128)(2,1)} %param.13) | copy-start | bytes 442372
  7.2 22.5 %copy-start.15 = (bf16[1,128,384]{2,1,0:T(8,128)(2,1)S(1)}, bf16[1,128,384]{2,1,0:T(8,128)(2,1)}, u32[]{:S(2)}) copy-start(bf16[1,128,384]{2,1,0:T(8,128)(2,1)} %param.7) | copy-start | bytes 294916
  7.2 22.5 %copy-start.19 = (f32[1,128,384]{2,1,0:T(8,128)S(1)}, f32[1,128,384]{2,1,0:T(8,128)}, u32[]{:S(2)}) copy-start(f32[1,128,384]{2,1,0:T(8,128)} %param.8) | copy-start | bytes 589828
  7.2 45.2 %all-gather.6.cloned.1.call-start = ((), (), s32[]{:S(2)}) async-start(), calls=%async_computation.7 | async-start | bytes 1843200 | tf_op jit(solution)/shard_map/all_gather | solution.py:53
  8.3 8.5 %collective-permute-start.4 = (bf16[120,384]{1,0:T(8,128)(2,1)S(1)}, bf16[120,384]{1,0:T(8,128)(2,1)S(1)}, u32[]{:S(2)}, u32[]{:S(2)}) collective-permute-start(bf16[120,384]{1,0:T(8,128)(2,1)S(1)} %get-tuple-element.76), channel_id=1, source_target_pairs={{0,4},{4,8},{8,12},{12,0},{1,5},{5,9},{9,13},{13,1},{2,6},{6,10},{... | collective-permute-start | bytes 276488 | tf_op jit(solution)/shard_map/ppermute | solution.py:47
  11.4 8.8 %collective-permute-start.5 = (bf16[120,384]{1,0:T(8,128)(2,1)S(1)}, bf16[120,384]{1,0:T(8,128)(2,1)S(1)}, u32[]{:S(2)}, u32[]{:S(2)}) collective-permute-start(bf16[120,384]{1,0:T(8,128)(2,1)S(1)} %get-tuple-element.76), channel_id=1, source_target_pairs={{0,8},{4,12},{8,0},{12,4},{1,9},{5,13},{9,1},{13,5},{2,10},{6,14},... | collective-permute-start | bytes 276488 | tf_op jit(solution)/shard_map/ppermute | solution.py:47
  14.0 6.4 %collective-permute-start.6 = (bf16[120,384]{1,0:T(8,128)(2,1)S(1)}, bf16[120,384]{1,0:T(8,128)(2,1)S(1)}, u32[]{:S(2)}, u32[]{:S(2)}) collective-permute-start(bf16[120,384]{1,0:T(8,128)(2,1)S(1)} %get-tuple-element.76), channel_id=1, source_target_pairs={{0,12},{4,0},{8,4},{12,8},{1,13},{5,1},{9,5},{13,9},{2,14},{6,2},{... | collective-permute-start | bytes 276488 | tf_op jit(solution)/shard_map/ppermute | solution.py:47
  20.2 20.9 %copy-start.27 = (f32[768]{0:T(1024)S(1)}, f32[768]{0:T(1024)}, u32[]{:S(2)}) copy-start(f32[768]{0:T(1024)} %param.11) | copy-start | bytes 9220
  21.2 65.6 %all-gather.4.cloned.1.call-start = ((), (), s32[]{:S(2)}) async-start(), calls=%async_computation.6 | async-start | bytes 2211840 | tf_op jit(solution)/shard_map/all_gather | solution.py:53
  22.2 7.9 %collective-permute-start = (bf16[144,384]{1,0:T(8,128)(2,1)S(1)}, bf16[144,384]{1,0:T(8,128)(2,1)S(1)}, u32[]{:S(2)}, u32[]{:S(2)}) collective-permute-start(bf16[144,384]{1,0:T(8,128)(2,1)S(1)} %get-tuple-element.78), channel_id=1, source_target_pairs={{0,4},{4,8},{8,12},{12,0},{1,5},{5,9},{9,13},{13,1},{2,6},{6,10},{... | collective-permute-start | bytes 331784 | tf_op jit(solution)/shard_map/ppermute | solution.py:47
  24.5 10.2 %collective-permute-start.1 = (bf16[144,384]{1,0:T(8,128)(2,1)S(1)}, bf16[144,384]{1,0:T(8,128)(2,1)S(1)}, u32[]{:S(2)}, u32[]{:S(2)}) collective-permute-start(bf16[144,384]{1,0:T(8,128)(2,1)S(1)} %get-tuple-element.78), channel_id=1, source_target_pairs={{0,8},{4,12},{8,0},{12,4},{1,9},{5,13},{9,1},{13,5},{2,10},{6,14},... | collective-permute-start | bytes 331784 | tf_op jit(solution)/shard_map/ppermute | solution.py:47
  26.2 12.7 %collective-permute-start.2 = (bf16[144,384]{1,0:T(8,128)(2,1)S(1)}, bf16[144,384]{1,0:T(8,128)(2,1)S(1)}, u32[]{:S(2)}, u32[]{:S(2)}) collective-permute-start(bf16[144,384]{1,0:T(8,128)(2,1)S(1)} %get-tuple-element.78), channel_id=1, source_target_pairs={{0,12},{4,0},{8,4},{12,8},{1,13},{5,1},{9,5},{13,9},{2,14},{6,2},{... | collective-permute-start | bytes 331784 | tf_op jit(solution)/shard_map/ppermute | solution.py:47
  27.1 67.5 %collective-permute-start.8 = (bf16[96,192]{1,0:T(8,128)(2,1)S(1)}, bf16[96,192]{1,0:T(8,128)(2,1)S(1)}, u32[]{:S(2)}, u32[]{:S(2)}) collective-permute-start(bf16[96,192]{1,0:T(8,128)(2,1)S(1)} %copy.179), channel_id=1, source_target_pairs={{0,4},{4,8},{8,12},{12,0},{1,5},{5,9},{9,13},{13,1},{2,6},{6,10},{... | collective-permute-start | bytes 110600 | tf_op jit(solution)/shard_map/ppermute | solution.py:47
  28.5 75.3 %collective-permute-start.9 = (bf16[96,192]{1,0:T(8,128)(2,1)S(1)}, bf16[96,192]{1,0:T(8,128)(2,1)S(1)}, u32[]{:S(2)}, u32[]{:S(2)}) collective-permute-start(bf16[96,192]{1,0:T(8,128)(2,1)S(1)} %copy.179), channel_id=1, source_target_pairs={{0,8},{4,12},{8,0},{12,4},{1,9},{5,13},{9,1},{13,5},{2,10},{6,14},... | collective-permute-start | bytes 110600 | tf_op jit(solution)/shard_map/ppermute | solution.py:47
  30.1 87.0 %collective-permute-start.10 = (bf16[96,192]{1,0:T(8,128)(2,1)S(1)}, bf16[96,192]{1,0:T(8,128)(2,1)S(1)}, u32[]{:S(2)}, u32[]{:S(2)}) collective-permute-start(bf16[96,192]{1,0:T(8,128)(2,1)S(1)} %copy.179), channel_id=1, source_target_pairs={{0,12},{4,0},{8,4},{12,8},{1,13},{5,1},{9,5},{13,9},{2,14},{6,2},{... | collective-permute-start | bytes 110600 | tf_op jit(solution)/shard_map/ppermute | solution.py:47
  34.7 7.2 %collective-permute-start.3 = (bf16[2,2,384]{2,1,0:T(2,128)(2,1)S(1)}, bf16[2,2,384]{2,1,0:T(2,128)(2,1)S(1)}, u32[]{:S(2)}, u32[]{:S(2)}) collective-permute-start(bf16[2,2,384]{2,1,0:T(2,128)(2,1)S(1)} %get-tuple-element.106), channel_id=1, source_target_pairs={{0,4},{4,8},{8,12},{1,5},{5,9},{9,13},{2,6},{6,10},{10,14},{3,7},{... | collective-permute-start | bytes 9224 | tf_op jit(solution)/shard_map/ppermute | solution.py:23
  39.0 5.5 %collective-permute-start.7 = (bf16[2,2,384]{2,1,0:T(2,128)(2,1)S(1)}, bf16[2,2,384]{2,1,0:T(2,128)(2,1)S(1)}, u32[]{:S(2)}, u32[]{:S(2)}) collective-permute-start(bf16[2,2,384]{2,1,0:T(2,128)(2,1)S(1)} %get-tuple-element.107), channel_id=1, source_target_pairs={{4,0},{8,4},{12,8},{5,1},{9,5},{13,9},{6,2},{10,6},{14,10},{7,3},{... | collective-permute-start | bytes 9224 | tf_op jit(solution)/shard_map/ppermute | solution.py:25
  53.9 1.2 copy-start.3
  53.9 1.2 copy-start.5
  53.9 1.2 copy-start.7
  53.9 1.2 copy-start.9
  59.5 29.0 %copy-start.28 = (f32[2,64]{1,0:T(2,128)}, f32[2,64]{1,0:T(2,128)S(1)}, u32[]{:S(2)}) copy-start(f32[2,64]{1,0:T(2,128)S(1)} %add_rsqrt_fusion) | copy-start | bytes 1540
  90.0 10.4 %all-to-all-start = ((bf16[4,2,6144]{2,1,0:T(2,128)(2,1)}), bf16[4,2,6144]{2,1,0:T(2,128)(2,1)S(1)}, u32[]{:S(2)}, u32[]{:S(2)}) async-start(bf16[4,2,6144]{2,1,0:T(2,128)(2,1)} %reshape.307), calls=%async_computation | async-start | bytes 196608 | tf_op jit(solution)/shard_map/all_to_all | solution.py:206
  100.5 9.6 %all-to-all-start.1 = ((bf16[4,2,12288]{2,1,0:T(2,128)(2,1)}), bf16[4,2,12288]{2,1,0:T(2,128)(2,1)S(1)}, u32[]{:S(2)}, u32[]{:S(2)}) async-start(bf16[4,2,12288]{2,1,0:T(2,128)(2,1)} %reshape_reshape.12), calls=%async_computation.1 | async-start | bytes 393216 | tf_op jit(solution)/shard_map/all_to_all | solution.py:207
  110.0 2.3 %copy-start.11 = (bf16[4,2,12288]{2,1,0:T(2,128)(2,1)}, bf16[4,2,12288]{2,1,0:T(2,128)(2,1)S(1)}, u32[]{:S(2)}) copy-start(bf16[4,2,12288]{2,1,0:T(2,128)(2,1)S(1)} %all-to-all-done.1) | copy-start | bytes 589828
  111.7 5.3 %copy-start.24 = (f32[256]{0:T(256)}, f32[256]{0:T(256)S(1)}, u32[]{:S(2)}) copy-start(f32[256]{0:T(256)S(1)} %log_add_fusion) | copy-start | bytes 3076
  112.0 5.1 %copy-start.21 = (bf16[256,96]{0,1:T(8,128)(2,1)}, bf16[256,96]{0,1:T(8,128)(2,1)S(1)}, u32[]{:S(2)}) copy-start(bf16[256,96]{0,1:T(8,128)(2,1)S(1)} %convolution_convert_fusion.4) | copy-start | bytes 147460
  113.1 16.7 %all-to-all-start.2 = ((bf16[4,2,6144]{2,1,0:T(2,128)(2,1)}), bf16[4,2,6144]{2,1,0:T(2,128)(2,1)}, u32[]{:S(2)}, u32[]{:S(2)}) async-start(bf16[4,2,6144]{2,1,0:T(2,128)(2,1)} %copy.146), calls=%async_computation.2 | async-start | bytes 196608 | tf_op jit(solution)/shard_map/all_to_all | solution.py:224
  129.3 2.3 %copy-start.12 = (bf16[4,2,12288]{2,1,0:T(2,128)(2,1)S(1)}, bf16[4,2,12288]{2,1,0:T(2,128)(2,1)}, u32[]{:S(2)}) copy-start(bf16[4,2,12288]{2,1,0:T(2,128)(2,1)} %copy-done.11) | copy-start | bytes 589828
  129.8 3.1 %copy-start.17 = (bf16[2,64,1,384]{3,1,0,2:T(8,128)(2,1)S(1)}, bf16[2,64,1,384]{3,1,0,2:T(8,128)(2,1)}, u32[]{:S(2)}) copy-start(bf16[2,64,1,384]{3,1,0,2:T(8,128)(2,1)} %copy-done.16) | copy-start | bytes 294916
  131.5 11.1 %copy-start.25 = (f32[256]{0:T(256)S(1)}, f32[256]{0:T(256)}, u32[]{:S(2)}) copy-start(f32[256]{0:T(256)} %copy-done.24) | copy-start | bytes 3076
  131.5 1.4 collective-permute-start.11
  132.2 16.6 %copy-start.22 = (bf16[256,96]{0,1:T(8,128)(2,1)S(1)}, bf16[256,96]{0,1:T(8,128)(2,1)}, u32[]{:S(2)}) copy-start(bf16[256,96]{0,1:T(8,128)(2,1)} %copy-done.21) | copy-start | bytes 147460
  137.4 10.8 %all-to-all-start.3 = ((bf16[4,2,3072]{2,1,0:T(2,128)(2,1)}), bf16[4,2,3072]{2,1,0:T(2,128)(2,1)S(1)}, u32[]{:S(2)}, u32[]{:S(2)}) async-start(bf16[4,2,3072]{2,1,0:T(2,128)(2,1)} %reshape.334), calls=%async_computation.3 | async-start | bytes 98304 | tf_op jit(solution)/shard_map/all_to_all | solution.py:297
  148.8 15.0 %copy-start.29 = (f32[2,64]{1,0:T(2,128)S(1)}, f32[2,64]{1,0:T(2,128)}, u32[]{:S(2)}) copy-start(f32[2,64]{1,0:T(2,128)} %copy-done.28) | copy-start | bytes 1540
  151.6 8.9 %all-to-all-start.4 = ((bf16[4,2,3072]{2,1,0:T(2,128)(2,1)}), bf16[4,2,3072]{2,1,0:T(2,128)(2,1)S(1)}, u32[]{:S(2)}, u32[]{:S(2)}) async-start(bf16[4,2,3072]{2,1,0:T(2,128)(2,1)} %reshape.338), calls=%async_computation.4 | async-start | bytes 98304 | tf_op jit(solution)/shard_map/all_to_all | solution.py:308
  160.5 9.1 %all-to-all-start.5 = ((bf16[4,2,6144]{2,1,0:T(2,128)(2,1)}), bf16[4,2,6144]{2,1,0:T(2,128)(2,1)S(1)}, u32[]{:S(2)}, u32[]{:S(2)}) async-start(bf16[4,2,6144]{2,1,0:T(2,128)(2,1)} %reshape.336), calls=%async_computation.5 | async-start | bytes 196608 | tf_op jit(solution)/shard_map/all_to_all | solution.py:315
  170.8 2.3 %copy-start.23 = (f32[384]{0:T(512)S(1)}, f32[384]{0:T(512)}, u32[]{:S(2)}) copy-start(f32[384]{0:T(512)} %dynamic_slice.46) | copy-start | bytes 4612
  171.8 1.3 collective-permute-start.12
  171.9 10.6 %copy-start.10 = (bf16[1,4,96,384]{3,2,0,1:T(8,128)(2,1)S(1)}, bf16[1,4,96,384]{3,2,0,1:T(8,128)(2,1)}, u32[]{:S(2)}) copy-start(bf16[1,4,96,384]{3,2,0,1:T(8,128)(2,1)} %copy-done.9) | copy-start | bytes 884740
  173.2 9.6 %copy-start.8 = (bf16[1,4,96,384]{3,2,0,1:T(8,128)(2,1)S(1)}, bf16[1,4,96,384]{3,2,0,1:T(8,128)(2,1)}, u32[]{:S(2)}) copy-start(bf16[1,4,96,384]{3,2,0,1:T(8,128)(2,1)} %copy-done.7) | copy-start | bytes 884740
  175.9 7.9 %copy-start.6 = (bf16[1,4,96,384]{3,2,0,1:T(8,128)(2,1)S(1)}, bf16[1,4,96,384]{3,2,0,1:T(8,128)(2,1)}, u32[]{:S(2)}) copy-start(bf16[1,4,96,384]{3,2,0,1:T(8,128)(2,1)} %copy-done.5) | copy-start | bytes 884740
  176.0 8.0 %copy-start.4 = (bf16[1,4,96,384]{3,2,0,1:T(8,128)(2,1)S(1)}, bf16[1,4,96,384]{3,2,0,1:T(8,128)(2,1)}, u32[]{:S(2)}) copy-start(bf16[1,4,96,384]{3,2,0,1:T(8,128)(2,1)} %copy-done.3) | copy-start | bytes 884740
  176.3 6.4 %collective-permute-start.13 = (bf16[2,384]{1,0:T(2,128)(2,1)S(1)}, bf16[2,384]{1,0:T(2,128)(2,1)S(1)}, u32[]{:S(2)}, u32[]{:S(2)}) collective-permute-start(bf16[2,384]{1,0:T(2,128)(2,1)S(1)} %get-tuple-element.110), channel_id=1, source_target_pairs={{4,0},{8,4},{12,8},{5,1},{9,5},{13,9},{6,2},{10,6},{14,10},{7,3},{... | collective-permute-start | bytes 4616 | tf_op jit(solution)/shard_map/ppermute | solution.py:25
  177.6 6.6 %copy-start.2 = (bf16[1,4,96,384]{3,2,0,1:T(8,128)(2,1)S(1)}, bf16[1,4,96,384]{3,2,0,1:T(8,128)(2,1)}, u32[]{:S(2)}) copy-start(bf16[1,4,96,384]{3,2,0,1:T(8,128)(2,1)} %copy-done.1) | copy-start | bytes 884740
  177.9 5.8 %collective-permute-start.14 = (bf16[2,384]{1,0:T(2,128)(2,1)S(1)}, bf16[2,384]{1,0:T(2,128)(2,1)S(1)}, u32[]{:S(2)}, u32[]{:S(2)}) collective-permute-start(bf16[2,384]{1,0:T(2,128)(2,1)S(1)} %get-tuple-element.111), channel_id=1, source_target_pairs={{0,4},{4,8},{8,12},{1,5},{5,9},{9,13},{2,6},{6,10},{10,14},{3,7},{... | collective-permute-start | bytes 4616 | tf_op jit(solution)/shard_map/ppermute | solution.py:23
  182.7 3.3 %copy-start.20 = (f32[1,128,384]{2,1,0:T(8,128)S(1)}, f32[1,128,384]{2,1,0:T(8,128)}, u32[]{:S(2)}) copy-start(f32[1,128,384]{2,1,0:T(8,128)} %param.8) | copy-start | bytes 589828
  184.5 1.4 collective-permute-start.15
  (6 other events, 5.4 us)
Sparse Core Ops, SparseCore 0:
  21.3 31.0 all-gather.5
  54.3 32.4 all-gather.3

commit v3 on v2

--- a/solution.py
+++ b/solution.py
@@ -29,11 +29,13 @@
     return cells
 
 
-def gather_seq(cells, dim):
+def gather_seq(parts):
     spread = ("group", "batch")
     count = lax.axis_size("group") * lax.axis_size("batch")
     ring = lax.axis_size("seq")
-    flat = cells.reshape(-1, cells.shape[-1])
+    width = parts[0][0].shape[-1]
+    flats = [cells.reshape(-1, width) for cells, _ in parts]
+    flat = jnp.concatenate(flats, axis=0) if len(flats) > 1 else flats[0]
     rows = flat.shape[0]
     size = -(-rows // count)
     if size * count != rows:
@@ -51,11 +53,17 @@
     else:
         along = lax.all_gather(piece, "seq", axis=0, tiled=False)
     whole = lax.all_gather(along, spread, axis=0, tiled=False)
-    whole = whole.transpose(1, 0, 2, 3).reshape(ring, count * size, flat.shape[1])[:, :rows]
-    whole = jnp.moveaxis(whole.reshape((ring,) + cells.shape), 0, dim)
-    shape = list(cells.shape)
-    shape[dim] = shape[dim] * ring
-    return whole.reshape(shape)
+    whole = whole.transpose(1, 0, 2, 3).reshape(ring, count * size, width)
+    results = []
+    offset = 0
+    for (cells, dim), part in zip(parts, flats):
+        block = whole[:, offset : offset + part.shape[0]]
+        offset += part.shape[0]
+        block = jnp.moveaxis(block.reshape((ring,) + cells.shape), 0, dim)
+        shape = list(cells.shape)
+        shape[dim] = shape[dim] * ring
+        results.append(block.reshape(shape))
+    return results
 
 
 def swap_mp(cells):
@@ -202,12 +210,16 @@
     keyval_send = jnp.broadcast_to(
         keyval_flat, (head_count, query_groups, pass_count, rows * 2 * head_size)
     ).reshape(devices, pass_count, rows * 2 * head_size)
-    query_in, keyval_in = (
-        lax.all_to_all(query_send, "seq", split_axis=0, concat_axis=2, tiled=True),
-        lax.all_to_all(keyval_send, "seq", split_axis=0, concat_axis=2, tiled=True),
-    )
-    query_heads = query_in.reshape(pass_count, devices * sub_rows, head_size)
-    keyval_heads = keyval_in.reshape(pass_count, devices * rows, 2 * head_size)
+    query_len = query_send.shape[2]
+    both_in = lax.all_to_all(
+        jnp.concatenate([query_send, keyval_send], axis=2),
+        "seq",
+        split_axis=0,
+        concat_axis=2,
+        tiled=True,
+    ).reshape(pass_count, devices, query_len + keyval_send.shape[2])
+    query_heads = both_in[:, :, :query_len].reshape(pass_count, devices * sub_rows, head_size)
+    keyval_heads = both_in[:, :, query_len:].reshape(pass_count, devices * rows, 2 * head_size)
     outputs = []
     masses = []
     for index in range(pass_count):
@@ -250,9 +262,8 @@
 
 
 def shards(features, noise, conv_weight, conv_bias, norm_gain, qkv_weight, out_weight):
-    conv_weight = gather_seq(conv_weight, 1)
-    qkv_weight = gather_seq(qkv_weight, 1)
-    out_weight = gather_seq(out_weight, 1)
+    (conv_weight,) = gather_seq([(conv_weight, 1)])
+    qkv_weight, out_weight = gather_seq([(qkv_weight, 1), (out_weight, 1)])
     clean = features[0]
     moved = (clean.astype(jnp.float32) + noise[0]).astype(jnp.bfloat16)
     joint = forward(
@@ -304,22 +315,22 @@
         log_mass,
         grad_heads,
     )
-    query_back, keyval_back = (
-        lax.all_to_all(
-            query_grad.reshape(devices, sub_rows * head_size).astype(jnp.bfloat16),
-            "seq",
-            split_axis=0,
-            concat_axis=0,
-            tiled=True,
-        ).astype(jnp.float32),
-        lax.all_to_all(
-            keyval_grad.reshape(devices, rows * 2 * head_size).astype(jnp.bfloat16),
-            "seq",
-            split_axis=0,
-            concat_axis=0,
-            tiled=True,
-        ).astype(jnp.float32),
-    )
+    query_len = sub_rows * head_size
+    both_back = lax.all_to_all(
+        jnp.concatenate(
+            [
+                query_grad.reshape(devices, query_len).astype(jnp.bfloat16),
+                keyval_grad.reshape(devices, rows * 2 * head_size).astype(jnp.bfloat16),
+            ],
+            axis=1,
+        ),
+        "seq",
+        split_axis=0,
+        concat_axis=0,
+        tiled=True,
+    ).astype(jnp.float32)
+    query_back = both_back[:, :query_len]
+    keyval_back = both_back[:, query_len:]
     query_rows = (
         query_back.reshape(head_count, query_groups, sub_rows, head_size)
         .transpose(1, 2, 0, 3)

time: 195 us -> 181 us (0.928)
  starting transfers between devices: 50.9 us -> 33.9 us
  waiting for transfers between devices: 73.2 us -> 77.3 us
  blocking collectives: 18 us -> 20.2 us
    all_to_all x0 -> x1, blocking collectives: none -> 13.8 us  [forward(): lax.all_to_all(jnp.concatenate([query_send, keyval_send], axis=2), 'seq',...]
    all_to_all x4 -> x1, waiting for transfers between devices: 18.4 us -> 6.03 us  [shards(): lax.all_to_all(jnp.concatenate([query_grad.reshape(devices, query_len).as...]
    all_gather x1 -> x0, blocking collectives: 11.6 us -> none  [gather_seq(): whole = lax.all_gather(along, spread, axis=0, tiled=False)]
    all_to_all x4 -> x1, starting transfers between devices: 14.5 us -> 3.34 us  [shards(): lax.all_to_all(jnp.concatenate([query_grad.reshape(devices, query_len).as...]
    ppermute x9 -> x6, waiting for transfers between devices: 8.57 us -> 14 us  [gather_seq(): lax.ppermute(piece, 'seq', [(i, (i + shift) % ring) for i in range(ring)])]
    ppermute x2, waiting for transfers between devices: 2.63 us -> 7.84 us  [with_halo(): lax.ppermute(head, axis, [((i + 1) % count, i) for i in range(ends)])]
    ppermute x9 -> x6, starting transfers between devices: 15.7 us -> 11.8 us  [gather_seq(): lax.ppermute(piece, 'seq', [(i, (i + shift) % ring) for i in range(ring)])]
    all_to_all x1, waiting for transfers between devices: 0.01 us -> 3.89 us  [forward(): lax.all_to_all(out_send, 'seq', split_axis=0, concat_axis=0, tiled=True)]
  transfers between devices with their start and end apart: 24 -> 18, of which waited for: 17 -> 15; matrix products, arithmetic and copies ran while one was open for 11% -> 5% of each run, Pallas kernels for 0% -> 0%
where the time goes in v3:
time: 181 us; the launch traced here: 180 us
  waiting for transfers between devices  77.3 us (43%)
  starting transfers between devices  33.9 us (19%)
  local copies, waits for them, and re-layouts  21 us (12%)
  blocking collectives  20.2 us (11%)
  between operations  15.2 us (8%)
  matrix products  7.07 us (4%)
  other arithmetic  5.62 us (3%)
    all_gather x2, waiting for transfers between devices, gather_seq(): whole = lax.all_gather(along, spread, axis=0, tiled=False)  37.5 us
    ppermute x6, waiting for transfers between devices, gather_seq(): lax.ppermute(piece, 'seq', [(i, (i + shift) % ring) for i in range(ring)])  14 us
    all_to_all x1, blocking collectives, forward(): lax.all_to_all(jnp.concatenate([query_send, keyval_send], axis=2), 'seq',...  13.8 us
    ppermute x6, starting transfers between devices, gather_seq(): lax.ppermute(piece, 'seq', [(i, (i + shift) % ring) for i in range(ring)])  11.8 us
    ppermute x2, starting transfers between devices, with_halo(): lax.ppermute(tail, axis, [(i, (i + 1) % count) for i in range(ends)])  8.63 us
    ppermute x2, waiting for transfers between devices, with_halo(): lax.ppermute(head, axis, [((i + 1) % count, i) for i in range(ends)])  7.84 us
    all_to_all x1, waiting for transfers between devices, shards(): lax.all_to_all(jnp.concatenate([query_grad.reshape(devices, query_len).as...  6.03 us
    all_to_all x1, waiting for transfers between devices, shards(): lax.all_to_all(grad_send, 'seq', split_axis=0, concat_axis=1, tiled=True)  5.45 us
  transfers between devices with their start and end apart: 18, of which 15 were waited for; matrix products, arithmetic and copies ran while one was open for 5% of the time, Pallas kernels for 0%

profile of v3, /device:TPU:0, one launch (start us, length us, event | category | flops | bytes accessed | tf_op | source)
XLA Modules:
  0.0 180.3 jit_solution(7411326059482064958)
XLA Ops:
  7.3 1.0 bitcast_dynamic-update-slice_fusion.7
  8.3 3.1 %collective-permute-start.4 = (bf16[120,384]{1,0:T(8,128)(2,1)S(1)}, bf16[120,384]{1,0:T(8,128)(2,1)S(1)}, u32[]{:S(2)}, u32[]{:S(2)}) collective-permute-start(bf16[120,384]{1,0:T(8,128)(2,1)S(1)} %get-tuple-element.76), channel_id=1, source_target_pairs={{0,4},{4,8},{8,12},{12,0},{1,5},{5,9},{9,13},{13,1},{2,6},{6,10},{... | collective-permute-start | bytes 276488 | tf_op jit(solution)/shard_map/ppermute | solution.py:49
  11.4 2.6 %collective-permute-start.5 = (bf16[120,384]{1,0:T(8,128)(2,1)S(1)}, bf16[120,384]{1,0:T(8,128)(2,1)S(1)}, u32[]{:S(2)}, u32[]{:S(2)}) collective-permute-start(bf16[120,384]{1,0:T(8,128)(2,1)S(1)} %get-tuple-element.76), channel_id=1, source_target_pairs={{0,8},{4,12},{8,0},{12,4},{1,9},{5,13},{9,1},{13,5},{2,10},{6,14},... | collective-permute-start | bytes 276488 | tf_op jit(solution)/shard_map/ppermute | solution.py:49
  14.0 1.3 collective-permute-start.6
  15.3 1.5 collective-permute-done.4
  16.8 3.3 %collective-permute-done.5 = bf16[120,384]{1,0:T(8,128)(2,1)S(1)} collective-permute-done((bf16[120,384]{1,0:T(8,128)(2,1)S(1)}, bf16[120,384]{1,0:T(8,128)(2,1)S(1)}, u32[]{:S(2)}, u32[]{:S(2)}) %collective-permute-start.5) | collective-permute-done | bytes 92192 | tf_op jit(solution)/shard_map/ppermute | solution.py:49
  20.4 0.7 copy-done.13
  21.9 2.3 %collective-permute-start = (bf16[192,384]{1,0:T(8,128)(2,1)S(1)}, bf16[192,384]{1,0:T(8,128)(2,1)S(1)}, u32[]{:S(2)}, u32[]{:S(2)}) collective-permute-start(bf16[192,384]{1,0:T(8,128)(2,1)S(1)} %get-tuple-element.78), channel_id=1, source_target_pairs={{0,4},{4,8},{8,12},{12,0},{1,5},{5,9},{9,13},{13,1},{2,6},{6,10},{... | collective-permute-start | bytes 442376 | tf_op jit(solution)/shard_map/ppermute | solution.py:49
  24.1 1.7 collective-permute-start.1
  25.9 0.7 collective-permute-start.2
  26.6 3.9 %collective-permute-done = bf16[192,384]{1,0:T(8,128)(2,1)S(1)} collective-permute-done((bf16[192,384]{1,0:T(8,128)(2,1)S(1)}, bf16[192,384]{1,0:T(8,128)(2,1)S(1)}, u32[]{:S(2)}, u32[]{:S(2)}) %collective-permute-start) | collective-permute-done | bytes 147488 | tf_op jit(solution)/shard_map/ppermute | solution.py:49
  30.5 5.1 %collective-permute-done.1 = bf16[192,384]{1,0:T(8,128)(2,1)S(1)} collective-permute-done((bf16[192,384]{1,0:T(8,128)(2,1)S(1)}, bf16[192,384]{1,0:T(8,128)(2,1)S(1)}, u32[]{:S(2)}, u32[]{:S(2)}) %collective-permute-start.1) | collective-permute-done | bytes 147488 | tf_op jit(solution)/shard_map/ppermute | solution.py:49
  35.7 0.8 copy-done.10
  36.6 5.5 %collective-permute-start.3 = (bf16[2,2,384]{2,1,0:T(2,128)(2,1)S(1)}, bf16[2,2,384]{2,1,0:T(2,128)(2,1)S(1)}, u32[]{:S(2)}, u32[]{:S(2)}) collective-permute-start(bf16[2,2,384]{2,1,0:T(2,128)(2,1)S(1)} %get-tuple-element.106), channel_id=1, source_target_pairs={{0,4},{4,8},{8,12},{1,5},{5,9},{9,13},{2,6},{6,10},{10,14},{3,7},{... | collective-permute-start | bytes 9224 | tf_op jit(solution)/shard_map/ppermute | solution.py:23
  42.1 1.3 collective-permute-start.7
  43.4 4.2 %collective-permute-done.7 = bf16[2,2,384]{2,1,0:T(2,128)(2,1)S(1)} collective-permute-done((bf16[2,2,384]{2,1,0:T(2,128)(2,1)S(1)}, bf16[2,2,384]{2,1,0:T(2,128)(2,1)S(1)}, u32[]{:S(2)}, u32[]{:S(2)}) %collective-permute-start.7) | collective-permute-done | bytes 3104 | tf_op jit(solution)/shard_map/ppermute | solution.py:25
  47.7 4.7 %all-gather.6.cloned.1.call-done = bf16[4,4,120,384]{3,2,0,1:T(8,128)(2,1)} async-done(((bf16[1,4,120,384]{3,2,0,1:T(8,128)(2,1)}), bf16[4,4,120,384]{3,2,0,1:T(8,128)(2,1)}) %all-gather.6.cloned.1.call-update) | async-done | bytes 1474576 | tf_op jit(solution)/shard_map/all_gather | solution.py:55
  52.4 1.5 fusion.94
  55.1 1.1 fusion.23
  56.8 1.9 %all-gather = bf16[2,64,1,768]{3,1,0,2:T(8,128)(2,1)S(1)} all-gather(bf16[2,64,1,384]{3,1,0,2:T(8,128)(2,1)S(1)} %fusion.54), channel_id=2, replica_groups=mesh['group'=2,'seq'=4,'batch'=2,'mp'=2] {'mp'}, dimensions={3}, use_global_device_ids=true | all-gather | bytes 294912 | tf_op jit(solution)/shard_map/all_gather | solution.py:177
  58.9 32.7 %all-gather.4.cloned.1.call-done = bf16[4,4,192,384]{3,2,0,1:T(8,128)(2,1)} async-done(((bf16[1,4,192,384]{3,2,0,1:T(8,128)(2,1)}), bf16[4,4,192,384]{3,2,0,1:T(8,128)(2,1)}) %all-gather.4.cloned.1.call-update) | async-done | bytes 2359312 | tf_op jit(solution)/shard_map/all_gather | solution.py:55
  91.6 1.7 slice.203
  95.9 13.8 %all_to_all.43 = bf16[4,2,18432]{2,1,0:T(2,128)(2,1)S(1)} all-to-all(bf16[4,2,18432]{2,1,0:T(2,128)(2,1)S(1)} %pad_maximum_fusion), channel_id=1, replica_groups=mesh['group'=2,'seq'=4,'batch'=2,'mp'=2] {'seq'}, dimensions={0} | all-to-all | bytes 589824 | tf_op jit(solution)/shard_map/all_to_all | solution.py:214
  112.9 0.7 copy.168
  113.6 3.9 %all-to-all-start.1 = ((bf16[4,2,6144]{2,1,0:T(2,128)(2,1)}), bf16[4,2,6144]{2,1,0:T(2,128)(2,1)}, u32[]{:S(2)}, u32[]{:S(2)}) async-start(bf16[4,2,6144]{2,1,0:T(2,128)(2,1)} %copy.168), calls=%async_computation.1 | async-start | bytes 196608 | tf_op jit(solution)/shard_map/all_to_all | solution.py:236
  117.6 1.1 slice.225
  119.6 3.9 %all-to-all-done.1 = bf16[4,2,6144]{2,1,0:T(2,128)(2,1)} async-done(((bf16[4,2,6144]{2,1,0:T(2,128)(2,1)}), bf16[4,2,6144]{2,1,0:T(2,128)(2,1)}, u32[]{:S(2)}, u32[]{:S(2)}) %all-to-all-start.1) | async-done | bytes 98336 | tf_op jit(solution)/shard_map/all_to_all | solution.py:236
  123.5 1.0 reshape.279
  125.1 0.7 constant_dynamic-slice_fusion.1
  126.5 0.9 collective-permute-done.8
  127.4 0.9 convert_add_fusion
  128.3 1.9 %all_gather.47 = bf16[64,768]{1,0:T(8,128)(2,1)S(1)} all-gather(bf16[64,384]{1,0:T(8,128)(2,1)S(1)} %fusion.85), channel_id=1, replica_groups=mesh['group'=2,'seq'=4,'batch'=2,'mp'=2] {'mp'}, dimensions={1}, use_global_device_ids=true | all-gather | bytes 147456 | tf_op jit(solution)/shard_map/all_gather | solution.py:296
  131.2 0.9 reduce.7
  132.1 0.7 reshape.302
  132.8 3.5 %all-to-all-start.2 = ((bf16[4,2,3072]{2,1,0:T(2,128)(2,1)}), bf16[4,2,3072]{2,1,0:T(2,128)(2,1)S(1)}, u32[]{:S(2)}, u32[]{:S(2)}) async-start(bf16[4,2,3072]{2,1,0:T(2,128)(2,1)} %reshape.302), calls=%async_computation.2 | async-start | bytes 98304 | tf_op jit(solution)/shard_map/all_to_all | solution.py:308
  136.5 5.4 %all-to-all-done.2 = bf16[4,2,3072]{2,1,0:T(2,128)(2,1)S(1)} async-done(((bf16[4,2,3072]{2,1,0:T(2,128)(2,1)}), bf16[4,2,3072]{2,1,0:T(2,128)(2,1)S(1)}, u32[]{:S(2)}, u32[]{:S(2)}) %all-to-all-start.2) | async-done | bytes 49184 | tf_op jit(solution)/shard_map/all_to_all | solution.py:308
  144.0 0.8 reduce.8
  144.9 0.8 reshape.304
  145.6 3.3 %all-to-all-start.3 = ((bf16[4,2,9216]{2,1,0:T(2,128)(2,1)}), bf16[4,2,9216]{2,1,0:T(2,128)(2,1)S(1)}, u32[]{:S(2)}, u32[]{:S(2)}) async-start(bf16[4,2,9216]{2,1,0:T(2,128)(2,1)} %reshape.304), calls=%async_computation.3 | async-start | bytes 294912 | tf_op jit(solution)/shard_map/all_to_all | solution.py:319
  149.0 6.0 %all-to-all-done.3 = bf16[4,2,9216]{2,1,0:T(2,128)(2,1)S(1)} async-done(((bf16[4,2,9216]{2,1,0:T(2,128)(2,1)}), bf16[4,2,9216]{2,1,0:T(2,128)(2,1)S(1)}, u32[]{:S(2)}, u32[]{:S(2)}) %all-to-all-start.3) | async-done | bytes 147488 | tf_op jit(solution)/shard_map/all_to_all | solution.py:319
  156.3 0.6 fusion.10
  157.3 1.0 collective-permute-done.9
  158.4 2.6 %psum.7 = f32[64]{0:T(128)S(1)} all-reduce(f32[64]{0:T(128)S(1)} %fusion.76), channel_id=1, replica_groups=mesh['group'=2,'seq'=4,'batch'=2,'mp'=2] {'mp'}, use_global_device_ids=true, to_apply=%region_7.8 | all-reduce | flops 64 | bytes 512 | tf_op jit(solution)/shard_map/psum | solution.py:357
  161.6 3.1 %collective-permute-start.11 = (bf16[2,384]{1,0:T(2,128)(2,1)S(1)}, bf16[2,384]{1,0:T(2,128)(2,1)S(1)}, u32[]{:S(2)}, u32[]{:S(2)}) collective-permute-start(bf16[2,384]{1,0:T(2,128)(2,1)S(1)} %get-tuple-element.111), channel_id=1, source_target_pairs={{0,4},{4,8},{8,12},{1,5},{5,9},{9,13},{2,6},{6,10},{10,14},{3,7},{... | collective-permute-start | bytes 4616 | tf_op jit(solution)/shard_map/ppermute | solution.py:23
  165.0 1.3 collective-permute-start.10
  166.8 3.7 %collective-permute-done.10 = bf16[2,384]{1,0:T(2,128)(2,1)S(1)} collective-permute-done((bf16[2,384]{1,0:T(2,128)(2,1)S(1)}, bf16[2,384]{1,0:T(2,128)(2,1)S(1)}, u32[]{:S(2)}, u32[]{:S(2)}) %collective-permute-start.10) | collective-permute-done | bytes 1568 | tf_op jit(solution)/shard_map/ppermute | solution.py:25
  171.9 0.7 collective-permute-done.12
  172.7 0.8 fusion.26
  (182 shorter events, 18.2 us)
Async XLA Ops:
  7.2 14.1 %copy-start.21 = (bf16[384,192]{0,1:T(8,128)(2,1)S(1)}, bf16[384,192]{0,1:T(8,128)(2,1)}, u32[]{:S(2)}) copy-start(bf16[384,192]{0,1:T(8,128)(2,1)} %param.13) | copy-start | bytes 442372
  7.2 14.4 %copy-start.18 = (bf16[3,192,384]{2,1,0:T(8,128)(2,1)S(1)}, bf16[3,192,384]{2,1,0:T(8,128)(2,1)}, u32[]{:S(2)}) copy-start(bf16[3,192,384]{2,1,0:T(8,128)(2,1)} %param.12) | copy-start | bytes 1327108
  7.2 45.2 %all-gather.6.cloned.1.call-start = ((), (), s32[]{:S(2)}) async-start(), calls=%async_computation.5 | async-start | bytes 1843200 | tf_op jit(solution)/shard_map/all_gather | solution.py:55
  8.3 8.5 %collective-permute-start.4 = (bf16[120,384]{1,0:T(8,128)(2,1)S(1)}, bf16[120,384]{1,0:T(8,128)(2,1)S(1)}, u32[]{:S(2)}, u32[]{:S(2)}) collective-permute-start(bf16[120,384]{1,0:T(8,128)(2,1)S(1)} %get-tuple-element.76), channel_id=1, source_target_pairs={{0,4},{4,8},{8,12},{12,0},{1,5},{5,9},{9,13},{13,1},{2,6},{6,10},{... | collective-permute-start | bytes 276488 | tf_op jit(solution)/shard_map/ppermute | solution.py:49
  11.4 8.8 %collective-permute-start.5 = (bf16[120,384]{1,0:T(8,128)(2,1)S(1)}, bf16[120,384]{1,0:T(8,128)(2,1)S(1)}, u32[]{:S(2)}, u32[]{:S(2)}) collective-permute-start(bf16[120,384]{1,0:T(8,128)(2,1)S(1)} %get-tuple-element.76), channel_id=1, source_target_pairs={{0,8},{4,12},{8,0},{12,4},{1,9},{5,13},{9,1},{13,5},{2,10},{6,14},... | collective-permute-start | bytes 276488 | tf_op jit(solution)/shard_map/ppermute | solution.py:49
  14.0 6.4 %collective-permute-start.6 = (bf16[120,384]{1,0:T(8,128)(2,1)S(1)}, bf16[120,384]{1,0:T(8,128)(2,1)S(1)}, u32[]{:S(2)}, u32[]{:S(2)}) collective-permute-start(bf16[120,384]{1,0:T(8,128)(2,1)S(1)} %get-tuple-element.76), channel_id=1, source_target_pairs={{0,12},{4,0},{8,4},{12,8},{1,13},{5,1},{9,5},{13,9},{2,14},{6,2},{... | collective-permute-start | bytes 276488 | tf_op jit(solution)/shard_map/ppermute | solution.py:49
  20.4 0.8 copy-start.13
  21.2 70.5 %all-gather.4.cloned.1.call-start = ((), (), s32[]{:S(2)}) async-start(), calls=%async_computation.4 | async-start | bytes 2949120 | tf_op jit(solution)/shard_map/all_gather | solution.py:55
  21.2 15.3 %copy-start.12 = (bf16[1,128,384]{2,1,0:T(8,128)(2,1)S(1)}, bf16[1,128,384]{2,1,0:T(8,128)(2,1)}, u32[]{:S(2)}) copy-start(bf16[1,128,384]{2,1,0:T(8,128)(2,1)} %param.7) | copy-start | bytes 294916
  21.2 15.3 %copy-start.16 = (f32[1,128,384]{2,1,0:T(8,128)S(1)}, f32[1,128,384]{2,1,0:T(8,128)}, u32[]{:S(2)}) copy-start(f32[1,128,384]{2,1,0:T(8,128)} %param.8) | copy-start | bytes 589828
  21.9 8.7 %collective-permute-start = (bf16[192,384]{1,0:T(8,128)(2,1)S(1)}, bf16[192,384]{1,0:T(8,128)(2,1)S(1)}, u32[]{:S(2)}, u32[]{:S(2)}) collective-permute-start(bf16[192,384]{1,0:T(8,128)(2,1)S(1)} %get-tuple-element.78), channel_id=1, source_target_pairs={{0,4},{4,8},{8,12},{12,0},{1,5},{5,9},{9,13},{13,1},{2,6},{6,10},{... | collective-permute-start | bytes 442376 | tf_op jit(solution)/shard_map/ppermute | solution.py:49
  24.1 11.5 %collective-permute-start.1 = (bf16[192,384]{1,0:T(8,128)(2,1)S(1)}, bf16[192,384]{1,0:T(8,128)(2,1)S(1)}, u32[]{:S(2)}, u32[]{:S(2)}) collective-permute-start(bf16[192,384]{1,0:T(8,128)(2,1)S(1)} %get-tuple-element.78), channel_id=1, source_target_pairs={{0,8},{4,12},{8,0},{12,4},{1,9},{5,13},{9,1},{13,5},{2,10},{6,14},... | collective-permute-start | bytes 442376 | tf_op jit(solution)/shard_map/ppermute | solution.py:49
  25.9 9.8 %collective-permute-start.2 = (bf16[192,384]{1,0:T(8,128)(2,1)S(1)}, bf16[192,384]{1,0:T(8,128)(2,1)S(1)}, u32[]{:S(2)}, u32[]{:S(2)}) collective-permute-start(bf16[192,384]{1,0:T(8,128)(2,1)S(1)} %get-tuple-element.78), channel_id=1, source_target_pairs={{0,12},{4,0},{8,4},{12,8},{1,13},{5,1},{9,5},{13,9},{2,14},{6,2},{... | collective-permute-start | bytes 442376 | tf_op jit(solution)/shard_map/ppermute | solution.py:49
  35.7 0.8 copy-start.10
  36.6 6.8 %collective-permute-start.3 = (bf16[2,2,384]{2,1,0:T(2,128)(2,1)S(1)}, bf16[2,2,384]{2,1,0:T(2,128)(2,1)S(1)}, u32[]{:S(2)}, u32[]{:S(2)}) collective-permute-start(bf16[2,2,384]{2,1,0:T(2,128)(2,1)S(1)} %get-tuple-element.106), channel_id=1, source_target_pairs={{0,4},{4,8},{8,12},{1,5},{5,9},{9,13},{2,6},{6,10},{10,14},{3,7},{... | collective-permute-start | bytes 9224 | tf_op jit(solution)/shard_map/ppermute | solution.py:23
  42.1 5.5 %collective-permute-start.7 = (bf16[2,2,384]{2,1,0:T(2,128)(2,1)S(1)}, bf16[2,2,384]{2,1,0:T(2,128)(2,1)S(1)}, u32[]{:S(2)}, u32[]{:S(2)}) collective-permute-start(bf16[2,2,384]{2,1,0:T(2,128)(2,1)S(1)} %get-tuple-element.107), channel_id=1, source_target_pairs={{4,0},{8,4},{12,8},{5,1},{9,5},{13,9},{6,2},{10,6},{14,10},{7,3},{... | collective-permute-start | bytes 9224 | tf_op jit(solution)/shard_map/ppermute | solution.py:25
  53.9 1.2 copy-start
  53.9 1.2 copy-start.2
  53.9 1.2 copy-start.4
  53.9 1.2 copy-start.6
  54.2 0.9 copy-start.22
  93.3 0.7 copy-start.23
  109.7 2.5 %copy-start.8 = (bf16[4,2,18432]{2,1,0:T(2,128)(2,1)}, bf16[4,2,18432]{2,1,0:T(2,128)(2,1)S(1)}, u32[]{:S(2)}) copy-start(bf16[4,2,18432]{2,1,0:T(2,128)(2,1)S(1)} %all_to_all.43) | copy-start | bytes 884740
  110.4 2.4 %copy-start.14 = (bf16[256,96]{1,0:T(8,128)(2,1)}, bf16[256,96]{1,0:T(8,128)(2,1)S(1)}, u32[]{:S(2)}) copy-start(bf16[256,96]{1,0:T(8,128)(2,1)S(1)} %squeeze.83) | copy-start | bytes 147460
  111.5 6.1 %copy-start.19 = (bf16[256,96]{0,1:T(8,128)(2,1)}, bf16[256,96]{0,1:T(8,128)(2,1)S(1)}, u32[]{:S(2)}) copy-start(bf16[256,96]{0,1:T(8,128)(2,1)S(1)} %convolution_convert_fusion.4) | copy-start | bytes 147460
  113.6 9.8 %all-to-all-start.1 = ((bf16[4,2,6144]{2,1,0:T(2,128)(2,1)}), bf16[4,2,6144]{2,1,0:T(2,128)(2,1)}, u32[]{:S(2)}, u32[]{:S(2)}) async-start(bf16[4,2,6144]{2,1,0:T(2,128)(2,1)} %copy.168), calls=%async_computation.1 | async-start | bytes 196608 | tf_op jit(solution)/shard_map/all_to_all | solution.py:236
  119.6 6.2 %copy-start.9 = (bf16[4,2,18432]{2,1,0:T(2,128)(2,1)S(1)}, bf16[4,2,18432]{2,1,0:T(2,128)(2,1)}, u32[]{:S(2)}) copy-start(bf16[4,2,18432]{2,1,0:T(2,128)(2,1)} %copy-done.8) | copy-start | bytes 884740
  125.1 11.2 %copy-start.15 = (bf16[256,96]{1,0:T(8,128)(2,1)S(1)}, bf16[256,96]{1,0:T(8,128)(2,1)}, u32[]{:S(2)}) copy-start(bf16[256,96]{1,0:T(8,128)(2,1)} %copy-done.14) | copy-start | bytes 147460
  125.7 1.6 collective-permute-start.8
  126.5 16.2 %copy-start.20 = (bf16[256,96]{0,1:T(8,128)(2,1)S(1)}, bf16[256,96]{0,1:T(8,128)(2,1)}, u32[]{:S(2)}) copy-start(bf16[256,96]{0,1:T(8,128)(2,1)} %copy-done.19) | copy-start | bytes 147460
  132.8 9.1 %all-to-all-start.2 = ((bf16[4,2,3072]{2,1,0:T(2,128)(2,1)}), bf16[4,2,3072]{2,1,0:T(2,128)(2,1)S(1)}, u32[]{:S(2)}, u32[]{:S(2)}) async-start(bf16[4,2,3072]{2,1,0:T(2,128)(2,1)} %reshape.302), calls=%async_computation.2 | async-start | bytes 98304 | tf_op jit(solution)/shard_map/all_to_all | solution.py:308
  145.6 9.4 %all-to-all-start.3 = ((bf16[4,2,9216]{2,1,0:T(2,128)(2,1)}), bf16[4,2,9216]{2,1,0:T(2,128)(2,1)S(1)}, u32[]{:S(2)}, u32[]{:S(2)}) async-start(bf16[4,2,9216]{2,1,0:T(2,128)(2,1)} %reshape.304), calls=%async_computation.3 | async-start | bytes 294912 | tf_op jit(solution)/shard_map/all_to_all | solution.py:319
  155.7 1.5 copy-start.11
  157.0 1.3 collective-permute-start.9
  157.1 9.2 %copy-start.7 = (bf16[1,4,96,384]{3,2,0,1:T(8,128)(2,1)S(1)}, bf16[1,4,96,384]{3,2,0,1:T(8,128)(2,1)}, u32[]{:S(2)}) copy-start(bf16[1,4,96,384]{3,2,0,1:T(8,128)(2,1)} %copy-done.6) | copy-start | bytes 884740
  158.4 8.2 %copy-start.5 = (bf16[1,4,96,384]{3,2,0,1:T(8,128)(2,1)S(1)}, bf16[1,4,96,384]{3,2,0,1:T(8,128)(2,1)}, u32[]{:S(2)}) copy-start(bf16[1,4,96,384]{3,2,0,1:T(8,128)(2,1)} %copy-done.4) | copy-start | bytes 884740
  161.1 9.4 %copy-start.3 = (bf16[1,4,96,384]{3,2,0,1:T(8,128)(2,1)S(1)}, bf16[1,4,96,384]{3,2,0,1:T(8,128)(2,1)}, u32[]{:S(2)}) copy-start(bf16[1,4,96,384]{3,2,0,1:T(8,128)(2,1)} %copy-done.2) | copy-start | bytes 884740
  161.2 9.5 %copy-start.1 = (bf16[1,4,96,384]{3,2,0,1:T(8,128)(2,1)S(1)}, bf16[1,4,96,384]{3,2,0,1:T(8,128)(2,1)}, u32[]{:S(2)}) copy-start(bf16[1,4,96,384]{3,2,0,1:T(8,128)(2,1)} %copy-done) | copy-start | bytes 884740
  161.6 5.0 %collective-permute-start.11 = (bf16[2,384]{1,0:T(2,128)(2,1)S(1)}, bf16[2,384]{1,0:T(2,128)(2,1)S(1)}, u32[]{:S(2)}, u32[]{:S(2)}) collective-permute-start(bf16[2,384]{1,0:T(2,128)(2,1)S(1)} %get-tuple-element.111), channel_id=1, source_target_pairs={{0,4},{4,8},{8,12},{1,5},{5,9},{9,13},{2,6},{6,10},{10,14},{3,7},{... | collective-permute-start | bytes 4616 | tf_op jit(solution)/shard_map/ppermute | solution.py:23
  165.0 5.5 %collective-permute-start.10 = (bf16[2,384]{1,0:T(2,128)(2,1)S(1)}, bf16[2,384]{1,0:T(2,128)(2,1)S(1)}, u32[]{:S(2)}, u32[]{:S(2)}) collective-permute-start(bf16[2,384]{1,0:T(2,128)(2,1)S(1)} %get-tuple-element.110), channel_id=1, source_target_pairs={{4,0},{8,4},{12,8},{5,1},{9,5},{13,9},{6,2},{10,6},{14,10},{7,3},{... | collective-permute-start | bytes 4616 | tf_op jit(solution)/shard_map/ppermute | solution.py:25
  166.6 6.1 %copy-start.17 = (f32[1,128,384]{2,1,0:T(8,128)S(1)}, f32[1,128,384]{2,1,0:T(8,128)}, u32[]{:S(2)}) copy-start(f32[1,128,384]{2,1,0:T(8,128)} %param.8) | copy-start | bytes 589828
  171.2 1.4 collective-permute-start.12
Sparse Core Ops, SparseCore 0:
  21.3 31.0 all-gather.5
  54.2 37.3 all-gather.3

commit v4 on v3

--- a/solution.py
+++ b/solution.py
@@ -52,7 +52,17 @@
             )
     else:
         along = lax.all_gather(piece, "seq", axis=0, tiled=False)
-    whole = lax.all_gather(along, spread, axis=0, tiled=False)
+    if ring <= 8 and count <= 4:
+        place = lax.axis_index(spread)
+        whole = jnp.zeros((count,) + along.shape, along.dtype)
+        whole = lax.dynamic_update_slice_in_dim(whole, along[None], place, 0)
+        for mask in range(1, count):
+            arrived = lax.ppermute(along, spread, [(i, i ^ mask) for i in range(count)])
+            whole = lax.dynamic_update_slice_in_dim(
+                whole, arrived[None], lax.bitwise_xor(place, mask), 0
+            )
+    else:
+        whole = lax.all_gather(along, spread, axis=0, tiled=False)
     whole = whole.transpose(1, 0, 2, 3).reshape(ring, count * size, width)
     results = []
     offset = 0

time: 181 us -> 206 us (1.14)
  local copies, waits for them, and re-layouts: 21 us -> 67.1 us
  waiting for transfers between devices: 77.3 us -> 45.2 us
  between operations: 15.2 us -> 1.69 us
  starting transfers between devices: 33.9 us -> 45.1 us
  matrix products: 7.07 us -> 12.8 us
  other arithmetic: 5.62 us -> 11.2 us
    all_gather x2 -> x0, waiting for transfers between devices: 37.5 us -> none  [gather_seq(): whole = lax.all_gather(along, spread, axis=0, tiled=False)]
    ppermute x0 -> x6, waiting for transfers between devices: none -> 21.8 us  [gather_seq(): arrived = lax.ppermute(along, spread, [(i, i ^ mask) for i in range(count)])]
    ppermute x6, waiting for transfers between devices: 14 us -> 3.1 us  [gather_seq(): lax.ppermute(piece, 'seq', [(i, (i + shift) % ring) for i in range(ring)])]
    ppermute x0 -> x6, starting transfers between devices: none -> 7.27 us  [gather_seq(): arrived = lax.ppermute(along, spread, [(i, i ^ mask) for i in range(count)])]
    ppermute x6, starting transfers between devices: 11.8 us -> 17.8 us  [gather_seq(): lax.ppermute(piece, 'seq', [(i, (i + shift) % ring) for i in range(ring)])]
    dynamic_update_slice x0 -> x8, local copies, waits for them, and re-layouts: none -> 4.91 us  [the longest x6 3.68 us: gather_seq(): lax.dynamic_update_slice_in_dim(whole, arrived[None], lax.bitwise_xor(pla...]
    convert_element_type x3, local copies, waits for them, and re-layouts: 0.27 us -> 4.62 us  [shards(): query_rows = query_back.reshape(head_count, query_groups, sub_rows, head_...]
    ppermute x2, waiting for transfers between devices: 7.84 us -> 3.68 us  [with_halo(): lax.ppermute(head, axis, [((i + 1) % count, i) for i in range(ends)])]
  transfers between devices with their start and end apart: 18 -> 22, of which waited for: 15 -> 13; matrix products, arithmetic and copies ran while one was open for 5% -> 9% of each run, Pallas kernels for 0% -> 0%
where the time goes in v4:
time: 206 us; the launch traced here: 204 us
  local copies, waits for them, and re-layouts  67.1 us (33%)
  waiting for transfers between devices  45.2 us (22%)
  starting transfers between devices  45.1 us (22%)
  blocking collectives  20.9 us (10%)
  matrix products  12.8 us (6%)
  other arithmetic  11.2 us (5%)
    ppermute x6, waiting for transfers between devices, gather_seq(): arrived = lax.ppermute(along, spread, [(i, i ^ mask) for i in range(count)])  21.8 us
    ppermute x6, starting transfers between devices, gather_seq(): lax.ppermute(piece, 'seq', [(i, (i + shift) % ring) for i in range(ring)])  17.8 us
    all_to_all x1, blocking collectives, forward(): lax.all_to_all(jnp.concatenate([query_send, keyval_send], axis=2), 'seq',...  14.6 us
    ppermute x6, starting transfers between devices, gather_seq(): arrived = lax.ppermute(along, spread, [(i, i ^ mask) for i in range(count)])  7.27 us
    all_to_all x1, waiting for transfers between devices, shards(): lax.all_to_all(jnp.concatenate([query_grad.reshape(devices, query_len).as...  6.12 us
    ppermute x2, starting transfers between devices, with_halo(): lax.ppermute(tail, axis, [(i, (i + 1) % count) for i in range(ends)])  5.71 us
    all_to_all x1, waiting for transfers between devices, shards(): lax.all_to_all(grad_send, 'seq', split_axis=0, concat_axis=1, tiled=True)  5.45 us
    unnamed x48, local copies, waits for them, and re-layouts  5.4 us
  transfers between devices with their start and end apart: 22, of which 13 were waited for; matrix products, arithmetic and copies ran while one was open for 9% of the time, Pallas kernels for 0%

profile of v4, /device:TPU:0, one launch (start us, length us, event | category | flops | bytes accessed | tf_op | source)
XLA Modules:
  0.0 204.0 jit_solution(16825663867720564038)
XLA Ops:
  2.8 1.7 bitcast_dynamic-update-slice_fusion.11
  4.5 3.1 %collective-permute-start = (bf16[192,384]{1,0:T(8,128)(2,1)S(1)}, bf16[192,384]{1,0:T(8,128)(2,1)S(1)}, u32[]{:S(2)}, u32[]{:S(2)}) collective-permute-start(bf16[192,384]{1,0:T(8,128)(2,1)S(1)} %get-tuple-element.78), channel_id=1, source_target_pairs={{0,4},{4,8},{8,12},{12,0},{1,5},{5,9},{9,13},{13,1},{2,6},{6,10},{... | collective-permute-start | bytes 442376 | tf_op jit(solution)/shard_map/ppermute | solution.py:49
  7.5 2.6 %collective-permute-start.1 = (bf16[192,384]{1,0:T(8,128)(2,1)S(1)}, bf16[192,384]{1,0:T(8,128)(2,1)S(1)}, u32[]{:S(2)}, u32[]{:S(2)}) collective-permute-start(bf16[192,384]{1,0:T(8,128)(2,1)S(1)} %get-tuple-element.78), channel_id=1, source_target_pairs={{0,8},{4,12},{8,0},{12,4},{1,9},{5,13},{9,1},{13,5},{2,10},{6,14},... | collective-permute-start | bytes 442376 | tf_op jit(solution)/shard_map/ppermute | solution.py:49
  11.5 2.6 %collective-permute-start.6 = (bf16[2,2,384]{2,1,0:T(2,128)(2,1)S(1)}, bf16[2,2,384]{2,1,0:T(2,128)(2,1)S(1)}, u32[]{:S(2)}, u32[]{:S(2)}) collective-permute-start(bf16[2,2,384]{2,1,0:T(2,128)(2,1)S(1)} %get-tuple-element.106), channel_id=1, source_target_pairs={{0,4},{4,8},{8,12},{1,5},{5,9},{9,13},{2,6},{6,10},{10,14},{3,7},{... | collective-permute-start | bytes 9224 | tf_op jit(solution)/shard_map/ppermute | solution.py:23
  17.1 4.7 %collective-permute-start.7 = (bf16[120,384]{1,0:T(8,128)(2,1)S(1)}, bf16[120,384]{1,0:T(8,128)(2,1)S(1)}, u32[]{:S(2)}, u32[]{:S(2)}) collective-permute-start(bf16[120,384]{1,0:T(8,128)(2,1)S(1)} %get-tuple-element.76), channel_id=1, source_target_pairs={{0,4},{4,8},{8,12},{12,0},{1,5},{5,9},{9,13},{13,1},{2,6},{6,10},{... | collective-permute-start | bytes 276488 | tf_op jit(solution)/shard_map/ppermute | solution.py:49
  21.8 2.7 %collective-permute-start.8 = (bf16[120,384]{1,0:T(8,128)(2,1)S(1)}, bf16[120,384]{1,0:T(8,128)(2,1)S(1)}, u32[]{:S(2)}, u32[]{:S(2)}) collective-permute-start(bf16[120,384]{1,0:T(8,128)(2,1)S(1)} %get-tuple-element.76), channel_id=1, source_target_pairs={{0,8},{4,12},{8,0},{12,4},{1,9},{5,13},{9,1},{13,5},{2,10},{6,14},... | collective-permute-start | bytes 276488 | tf_op jit(solution)/shard_map/ppermute | solution.py:49
  24.5 3.4 %collective-permute-start.9 = (bf16[120,384]{1,0:T(8,128)(2,1)S(1)}, bf16[120,384]{1,0:T(8,128)(2,1)S(1)}, u32[]{:S(2)}, u32[]{:S(2)}) collective-permute-start(bf16[120,384]{1,0:T(8,128)(2,1)S(1)} %get-tuple-element.76), channel_id=1, source_target_pairs={{0,12},{4,0},{8,4},{12,8},{1,13},{5,1},{9,5},{13,9},{2,14},{6,2},{... | collective-permute-start | bytes 276488 | tf_op jit(solution)/shard_map/ppermute | solution.py:49
  28.0 3.1 %collective-permute-done.9 = bf16[120,384]{1,0:T(8,128)(2,1)S(1)} collective-permute-done((bf16[120,384]{1,0:T(8,128)(2,1)S(1)}, bf16[120,384]{1,0:T(8,128)(2,1)S(1)}, u32[]{:S(2)}, u32[]{:S(2)}) %collective-permute-start.9) | collective-permute-done | bytes 92192 | tf_op jit(solution)/shard_map/ppermute | solution.py:49
  31.1 1.6 collective-permute-start.10
  40.6 2.1 %collective-permute-done.10 = bf16[4,120,384]{2,1,0:T(8,128)(2,1)S(1)} collective-permute-done((bf16[4,120,384]{2,1,0:T(8,128)(2,1)S(1)}, bf16[4,120,384]{2,1,0:T(8,128)(2,1)S(1)}, u32[]{:S(2)}, u32[]{:S(2)}) %collective-permute-start.10) | collective-permute-done | bytes 368672 | tf_op jit(solution)/shard_map/ppermute | solution.py:60
  42.6 1.5 collective-permute-start.5
  44.2 7.5 %collective-permute-done.11 = bf16[4,120,384]{2,1,0:T(8,128)(2,1)S(1)} collective-permute-done((bf16[4,120,384]{2,1,0:T(8,128)(2,1)S(1)}, bf16[4,120,384]{2,1,0:T(8,128)(2,1)S(1)}, u32[]{:S(2)}, u32[]{:S(2)}) %collective-permute-start.11) | collective-permute-done | bytes 368672 | tf_op jit(solution)/shard_map/ppermute | solution.py:60
  55.1 2.0 reshape.251
  58.6 1.9 all-gather
  60.7 2.6 %collective-permute-done.3 = bf16[4,192,384]{2,1,0:T(8,128)(2,1)} collective-permute-done((bf16[4,192,384]{2,1,0:T(8,128)(2,1)}, bf16[4,192,384]{2,1,0:T(8,128)(2,1)}, u32[]{:S(2)}, u32[]{:S(2)}) %collective-permute-start.3) | collective-permute-done | bytes 589856 | tf_op jit(solution)/shard_map/ppermute | solution.py:60
  64.5 9.6 %collective-permute-done.4 = bf16[4,192,384]{2,1,0:T(8,128)(2,1)} collective-permute-done((bf16[4,192,384]{2,1,0:T(8,128)(2,1)}, bf16[4,192,384]{2,1,0:T(8,128)(2,1)}, u32[]{:S(2)}, u32[]{:S(2)}) %collective-permute-start.4) | collective-permute-done | bytes 589856 | tf_op jit(solution)/shard_map/ppermute | solution.py:60
  78.5 1.7 reshape_squeeze.11
  80.2 1.6 copy.176
  81.8 1.7 reshape_squeeze.10
  84.4 1.8 maximum_bitcast_fusion
  86.1 2.0 reshape_reshape.8
  88.1 1.7 reshape_squeeze.9
  89.7 1.6 copy.226
  91.3 1.8 reshape.252
  94.4 14.6 %all_to_all.43 = bf16[4,2,18432]{2,1,0:T(2,128)(2,1)S(1)} all-to-all(bf16[4,2,18432]{2,1,0:T(2,128)(2,1)S(1)} %pad_maximum_fusion), channel_id=1, replica_groups=mesh['group'=2,'seq'=4,'batch'=2,'mp'=2] {'seq'}, dimensions={0} | all-to-all | bytes 589824 | tf_op jit(solution)/shard_map/all_to_all | solution.py:224
  110.8 1.5 squeeze.83
  112.4 1.7 copy.177
  114.1 1.9 reshape.254
  117.2 1.8 convolution_convert_fusion.4
  120.6 1.6 stack.21
  122.2 1.5 squeeze.80
  124.9 1.8 convolution_convert_fusion.5
  128.3 1.6 stack.20
  131.5 4.1 %all-to-all-start.1 = ((bf16[4,2,6144]{2,1,0:T(2,128)(2,1)}), bf16[4,2,6144]{2,1,0:T(2,128)(2,1)}, u32[]{:S(2)}, u32[]{:S(2)}) async-start(bf16[4,2,6144]{2,1,0:T(2,128)(2,1)} %copy.180), calls=%async_computation.1 | async-start | bytes 196608 | tf_op jit(solution)/shard_map/all_to_all | solution.py:246
  136.6 1.6 reshape.257
  138.5 2.8 %all-to-all-done.1 = bf16[4,2,6144]{2,1,0:T(2,128)(2,1)} async-done(((bf16[4,2,6144]{2,1,0:T(2,128)(2,1)}), bf16[4,2,6144]{2,1,0:T(2,128)(2,1)}, u32[]{:S(2)}, u32[]{:S(2)}) %all-to-all-start.1) | async-done | bytes 98336 | tf_op jit(solution)/shard_map/all_to_all | solution.py:246
  144.4 1.9 all_gather.7
  148.9 3.3 %all-to-all-start.2 = ((bf16[4,2,3072]{2,1,0:T(2,128)(2,1)}), bf16[4,2,3072]{2,1,0:T(2,128)(2,1)S(1)}, u32[]{:S(2)}, u32[]{:S(2)}) async-start(bf16[4,2,3072]{2,1,0:T(2,128)(2,1)} %reshape.278), calls=%async_computation.2 | async-start | bytes 98304 | tf_op jit(solution)/shard_map/all_to_all | solution.py:318
  152.4 5.5 %all-to-all-done.2 = bf16[4,2,3072]{2,1,0:T(2,128)(2,1)S(1)} async-done(((bf16[4,2,3072]{2,1,0:T(2,128)(2,1)}), bf16[4,2,3072]{2,1,0:T(2,128)(2,1)S(1)}, u32[]{:S(2)}, u32[]{:S(2)}) %all-to-all-start.2) | async-done | bytes 49184 | tf_op jit(solution)/shard_map/all_to_all | solution.py:318
  161.5 4.1 %all-to-all-start.3 = ((bf16[4,2,9216]{2,1,0:T(2,128)(2,1)}), bf16[4,2,9216]{2,1,0:T(2,128)(2,1)}, u32[]{:S(2)}, u32[]{:S(2)}) async-start(bf16[4,2,9216]{2,1,0:T(2,128)(2,1)} %reshape.280), calls=%async_computation.3 | async-start | bytes 294912 | tf_op jit(solution)/shard_map/all_to_all | solution.py:329
  165.6 6.1 %all-to-all-done.3 = bf16[4,2,9216]{2,1,0:T(2,128)(2,1)} async-done(((bf16[4,2,9216]{2,1,0:T(2,128)(2,1)}), bf16[4,2,9216]{2,1,0:T(2,128)(2,1)}, u32[]{:S(2)}, u32[]{:S(2)}) %all-to-all-start.3) | async-done | bytes 147488 | tf_op jit(solution)/shard_map/all_to_all | solution.py:329
  175.3 1.6 convert_element_type.228
  178.4 1.6 convert_element_type.225
  179.9 1.5 convert_element_type.220
  183.0 1.6 convert_element_type.222
  188.3 2.5 %psum.7 = f32[64]{0:T(128)S(1)} all-reduce(f32[64]{0:T(128)S(1)} %fusion.76), channel_id=1, replica_groups=mesh['group'=2,'seq'=4,'batch'=2,'mp'=2] {'mp'}, use_global_device_ids=true, to_apply=%region_7.8 | all-reduce | flops 64 | bytes 512 | tf_op jit(solution)/shard_map/psum | solution.py:367
  192.1 3.1 %collective-permute-start.17 = (bf16[2,384]{1,0:T(2,128)(2,1)S(1)}, bf16[2,384]{1,0:T(2,128)(2,1)S(1)}, u32[]{:S(2)}, u32[]{:S(2)}) collective-permute-start(bf16[2,384]{1,0:T(2,128)(2,1)S(1)} %get-tuple-element.111), channel_id=1, source_target_pairs={{0,4},{4,8},{8,12},{1,5},{5,9},{9,13},{2,6},{6,10},{10,14},{3,7},{... | collective-permute-start | bytes 4616 | tf_op jit(solution)/shard_map/ppermute | solution.py:23
  197.4 3.7 %collective-permute-done.16 = bf16[2,384]{1,0:T(2,128)(2,1)S(1)} collective-permute-done((bf16[2,384]{1,0:T(2,128)(2,1)S(1)}, bf16[2,384]{1,0:T(2,128)(2,1)S(1)}, u32[]{:S(2)}, u32[]{:S(2)}) %collective-permute-start.16) | collective-permute-done | bytes 1568 | tf_op jit(solution)/shard_map/ppermute | solution.py:25
  (192 shorter events, 63.1 us)
Async XLA Ops:
  0.6 10.8 %copy-start.15 = (f32[1,128,384]{2,1,0:T(8,128)S(1)}, f32[1,128,384]{2,1,0:T(8,128)}, u32[]{:S(2)}) copy-start(f32[1,128,384]{2,1,0:T(8,128)} %param.8) | copy-start | bytes 589828
  0.6 10.8 %copy-start.7 = (bf16[1,128,384]{2,1,0:T(8,128)(2,1)S(1)}, bf16[1,128,384]{2,1,0:T(8,128)(2,1)}, u32[]{:S(2)}) copy-start(bf16[1,128,384]{2,1,0:T(8,128)(2,1)} %param.7) | copy-start | bytes 294916
  4.5 29.1 %collective-permute-start = (bf16[192,384]{1,0:T(8,128)(2,1)S(1)}, bf16[192,384]{1,0:T(8,128)(2,1)S(1)}, u32[]{:S(2)}, u32[]{:S(2)}) collective-permute-start(bf16[192,384]{1,0:T(8,128)(2,1)S(1)} %get-tuple-element.78), channel_id=1, source_target_pairs={{0,4},{4,8},{8,12},{12,0},{1,5},{5,9},{9,13},{13,1},{2,6},{6,10},{... | collective-permute-start | bytes 442376 | tf_op jit(solution)/shard_map/ppermute | solution.py:49
  7.5 28.1 %collective-permute-start.1 = (bf16[192,384]{1,0:T(8,128)(2,1)S(1)}, bf16[192,384]{1,0:T(8,128)(2,1)S(1)}, u32[]{:S(2)}, u32[]{:S(2)}) collective-permute-start(bf16[192,384]{1,0:T(8,128)(2,1)S(1)} %get-tuple-element.78), channel_id=1, source_target_pairs={{0,8},{4,12},{8,0},{12,4},{1,9},{5,13},{9,1},{13,5},{2,10},{6,14},... | collective-permute-start | bytes 442376 | tf_op jit(solution)/shard_map/ppermute | solution.py:49
  10.1 26.2 %collective-permute-start.2 = (bf16[192,384]{1,0:T(8,128)(2,1)S(1)}, bf16[192,384]{1,0:T(8,128)(2,1)S(1)}, u32[]{:S(2)}, u32[]{:S(2)}) collective-permute-start(bf16[192,384]{1,0:T(8,128)(2,1)S(1)} %get-tuple-element.78), channel_id=1, source_target_pairs={{0,12},{4,0},{8,4},{12,8},{1,13},{5,1},{9,5},{13,9},{2,14},{6,2},{... | collective-permute-start | bytes 442376 | tf_op jit(solution)/shard_map/ppermute | solution.py:49
  11.5 21.9 %copy-start.9 = (bf16[1,128,384]{2,1,0:T(8,128)(2,1)}, bf16[1,128,384]{2,1,0:T(8,128)(2,1)S(1)}, u32[]{:S(2)}) copy-start(bf16[1,128,384]{2,1,0:T(8,128)(2,1)S(1)} %add_convert_fusion.2) | copy-start | bytes 294916
  11.5 5.5 %collective-permute-start.6 = (bf16[2,2,384]{2,1,0:T(2,128)(2,1)S(1)}, bf16[2,2,384]{2,1,0:T(2,128)(2,1)S(1)}, u32[]{:S(2)}, u32[]{:S(2)}) collective-permute-start(bf16[2,2,384]{2,1,0:T(2,128)(2,1)S(1)} %get-tuple-element.106), channel_id=1, source_target_pairs={{0,4},{4,8},{8,12},{1,5},{5,9},{9,13},{2,6},{6,10},{10,14},{3,7},{... | collective-permute-start | bytes 9224 | tf_op jit(solution)/shard_map/ppermute | solution.py:23
  14.1 7.7 %collective-permute-start.13 = (bf16[2,2,384]{2,1,0:T(2,128)(2,1)S(1)}, bf16[2,2,384]{2,1,0:T(2,128)(2,1)S(1)}, u32[]{:S(2)}, u32[]{:S(2)}) collective-permute-start(bf16[2,2,384]{2,1,0:T(2,128)(2,1)S(1)} %get-tuple-element.107), channel_id=1, source_target_pairs={{4,0},{8,4},{12,8},{5,1},{9,5},{13,9},{6,2},{10,6},{14,10},{7,3},{... | collective-permute-start | bytes 9224 | tf_op jit(solution)/shard_map/ppermute | solution.py:25
  17.1 7.5 %collective-permute-start.7 = (bf16[120,384]{1,0:T(8,128)(2,1)S(1)}, bf16[120,384]{1,0:T(8,128)(2,1)S(1)}, u32[]{:S(2)}, u32[]{:S(2)}) collective-permute-start(bf16[120,384]{1,0:T(8,128)(2,1)S(1)} %get-tuple-element.76), channel_id=1, source_target_pairs={{0,4},{4,8},{8,12},{12,0},{1,5},{5,9},{9,13},{13,1},{2,6},{6,10},{... | collective-permute-start | bytes 276488 | tf_op jit(solution)/shard_map/ppermute | solution.py:49
  21.8 6.2 %collective-permute-start.8 = (bf16[120,384]{1,0:T(8,128)(2,1)S(1)}, bf16[120,384]{1,0:T(8,128)(2,1)S(1)}, u32[]{:S(2)}, u32[]{:S(2)}) collective-permute-start(bf16[120,384]{1,0:T(8,128)(2,1)S(1)} %get-tuple-element.76), channel_id=1, source_target_pairs={{0,8},{4,12},{8,0},{12,4},{1,9},{5,13},{9,1},{13,5},{2,10},{6,14},... | collective-permute-start | bytes 276488 | tf_op jit(solution)/shard_map/ppermute | solution.py:49
  24.5 6.6 %collective-permute-start.9 = (bf16[120,384]{1,0:T(8,128)(2,1)S(1)}, bf16[120,384]{1,0:T(8,128)(2,1)S(1)}, u32[]{:S(2)}, u32[]{:S(2)}) collective-permute-start(bf16[120,384]{1,0:T(8,128)(2,1)S(1)} %get-tuple-element.76), channel_id=1, source_target_pairs={{0,12},{4,0},{8,4},{12,8},{1,13},{5,1},{9,5},{13,9},{2,14},{6,2},{... | collective-permute-start | bytes 276488 | tf_op jit(solution)/shard_map/ppermute | solution.py:49
  31.1 11.5 %collective-permute-start.10 = (bf16[4,120,384]{2,1,0:T(8,128)(2,1)S(1)}, bf16[4,120,384]{2,1,0:T(8,128)(2,1)S(1)}, u32[]{:S(2)}, u32[]{:S(2)}) collective-permute-start(bf16[4,120,384]{2,1,0:T(8,128)(2,1)S(1)} %bitcast_dynamic-update-slice_fusion.12), channel_id=1, source_target_pairs={{0,2},{2,0},{16,18},{18,16},{1,3},{3,1},{17,19},{19,17},{4,6},{6,4... | collective-permute-start | bytes 1105928 | tf_op jit(solution)/shard_map/ppermute | solution.py:60
  32.7 19.0 %collective-permute-start.11 = (bf16[4,120,384]{2,1,0:T(8,128)(2,1)S(1)}, bf16[4,120,384]{2,1,0:T(8,128)(2,1)S(1)}, u32[]{:S(2)}, u32[]{:S(2)}) collective-permute-start(bf16[4,120,384]{2,1,0:T(8,128)(2,1)S(1)} %bitcast_dynamic-update-slice_fusion.12), channel_id=1, source_target_pairs={{0,16},{2,18},{16,0},{18,2},{1,17},{3,19},{17,1},{19,3},{4,20},{6,... | collective-permute-start | bytes 1105928 | tf_op jit(solution)/shard_map/ppermute | solution.py:60
  33.5 18.3 %collective-permute-start.12 = (bf16[4,120,384]{2,1,0:T(8,128)(2,1)S(1)}, bf16[4,120,384]{2,1,0:T(8,128)(2,1)S(1)}, u32[]{:S(2)}, u32[]{:S(2)}) collective-permute-start(bf16[4,120,384]{2,1,0:T(8,128)(2,1)S(1)} %bitcast_dynamic-update-slice_fusion.12), channel_id=1, source_target_pairs={{0,18},{2,16},{16,2},{18,0},{1,19},{3,17},{17,3},{19,1},{4,22},{6,... | collective-permute-start | bytes 1105928 | tf_op jit(solution)/shard_map/ppermute | solution.py:60
  37.0 26.3 %collective-permute-start.3 = (bf16[4,192,384]{2,1,0:T(8,128)(2,1)}, bf16[4,192,384]{2,1,0:T(8,128)(2,1)}, u32[]{:S(2)}, u32[]{:S(2)}) collective-permute-start(bf16[4,192,384]{2,1,0:T(8,128)(2,1)} %bitcast_dynamic-update-slice_fusion.8), channel_id=1, source_target_pairs={{0,2},{2,0},{16,18},{18,16},{1,3},{3,1},{17,19},{19,17},{4,6},{6,4... | collective-permute-start | bytes 1769480 | tf_op jit(solution)/shard_map/ppermute | solution.py:60
  38.5 35.6 %collective-permute-start.4 = (bf16[4,192,384]{2,1,0:T(8,128)(2,1)}, bf16[4,192,384]{2,1,0:T(8,128)(2,1)}, u32[]{:S(2)}, u32[]{:S(2)}) collective-permute-start(bf16[4,192,384]{2,1,0:T(8,128)(2,1)} %bitcast_dynamic-update-slice_fusion.8), channel_id=1, source_target_pairs={{0,16},{2,18},{16,0},{18,2},{1,17},{3,19},{17,1},{19,3},{4,20},{6,... | collective-permute-start | bytes 1769480 | tf_op jit(solution)/shard_map/ppermute | solution.py:60
  42.6 32.6 %collective-permute-start.5 = (bf16[4,192,384]{2,1,0:T(8,128)(2,1)}, bf16[4,192,384]{2,1,0:T(8,128)(2,1)}, u32[]{:S(2)}, u32[]{:S(2)}) collective-permute-start(bf16[4,192,384]{2,1,0:T(8,128)(2,1)} %bitcast_dynamic-update-slice_fusion.8), channel_id=1, source_target_pairs={{0,18},{2,16},{16,2},{18,0},{1,19},{3,17},{17,3},{19,1},{4,22},{6,... | collective-permute-start | bytes 1769480 | tf_op jit(solution)/shard_map/ppermute | solution.py:60
  51.8 0.9 copy-start.8
  51.8 0.9 copy-start.10
  52.0 1.8 copy-start.2
  53.0 0.9 copy-start.19
  58.6 2.1 %copy-start.11 = (bf16[2,64,1,384]{3,1,0,2:T(8,128)(2,1)}, bf16[2,64,1,384]{3,1,0,2:T(8,128)(2,1)S(1)}, u32[]{:S(2)}) copy-start(bf16[2,64,1,384]{3,1,0,2:T(8,128)(2,1)S(1)} %fusion.54) | copy-start | bytes 294916
  76.6 0.7 copy-start.20
  76.8 1.7 copy-start
  109.0 1.1 copy-start.4
  131.5 9.8 %all-to-all-start.1 = ((bf16[4,2,6144]{2,1,0:T(2,128)(2,1)}), bf16[4,2,6144]{2,1,0:T(2,128)(2,1)}, u32[]{:S(2)}, u32[]{:S(2)}) async-start(bf16[4,2,6144]{2,1,0:T(2,128)(2,1)} %copy.180), calls=%async_computation.1 | async-start | bytes 196608 | tf_op jit(solution)/shard_map/all_to_all | solution.py:246
  138.2 4.9 %copy-start.5 = (bf16[4,2,18432]{2,1,0:T(2,128)(2,1)S(1)}, bf16[4,2,18432]{2,1,0:T(2,128)(2,1)}, u32[]{:S(2)}) copy-start(bf16[4,2,18432]{2,1,0:T(2,128)(2,1)} %copy-done.4) | copy-start | bytes 884740
  138.2 6.2 %copy-start.12 = (bf16[2,64,1,384]{3,1,0,2:T(8,128)(2,1)S(1)}, bf16[2,64,1,384]{3,1,0,2:T(8,128)(2,1)}, u32[]{:S(2)}) copy-start(bf16[2,64,1,384]{3,1,0,2:T(8,128)(2,1)} %copy-done.11) | copy-start | bytes 294916
  142.9 9.2 %copy-start.14 = (bf16[256,96]{1,0:T(8,128)(2,1)S(1)}, bf16[256,96]{1,0:T(8,128)(2,1)}, u32[]{:S(2)}) copy-start(bf16[256,96]{1,0:T(8,128)(2,1)} %squeeze.83) | copy-start | bytes 147460
  143.0 1.4 collective-permute-start.14
  143.8 14.7 %copy-start.18 = (bf16[256,96]{0,1:T(8,128)(2,1)S(1)}, bf16[256,96]{0,1:T(8,128)(2,1)}, u32[]{:S(2)}) copy-start(bf16[256,96]{0,1:T(8,128)(2,1)} %convolution_convert_fusion.4) | copy-start | bytes 147460
  148.9 8.9 %all-to-all-start.2 = ((bf16[4,2,3072]{2,1,0:T(2,128)(2,1)}), bf16[4,2,3072]{2,1,0:T(2,128)(2,1)S(1)}, u32[]{:S(2)}, u32[]{:S(2)}) async-start(bf16[4,2,3072]{2,1,0:T(2,128)(2,1)} %reshape.278), calls=%async_computation.2 | async-start | bytes 98304 | tf_op jit(solution)/shard_map/all_to_all | solution.py:318
  161.5 23.0 %copy-start.1 = (bf16[3,4,192,384]{3,2,1,0:T(8,128)(2,1)S(1)}, bf16[3,4,192,384]{3,2,1,0:T(8,128)(2,1)}, u32[]{:S(2)}) copy-start(bf16[3,4,192,384]{3,2,1,0:T(8,128)(2,1)} %copy-done) | copy-start | bytes 5308420
  161.5 10.2 %all-to-all-start.3 = ((bf16[4,2,9216]{2,1,0:T(2,128)(2,1)}), bf16[4,2,9216]{2,1,0:T(2,128)(2,1)}, u32[]{:S(2)}, u32[]{:S(2)}) async-start(bf16[4,2,9216]{2,1,0:T(2,128)(2,1)} %reshape.280), calls=%async_computation.3 | async-start | bytes 294912 | tf_op jit(solution)/shard_map/all_to_all | solution.py:329
  173.9 12.8 %copy-start.6 = (f32[2,128,384]{2,1,0:T(8,128)S(1)}, f32[2,128,384]{2,1,0:T(8,128)}, u32[]{:S(2)}) copy-start(f32[2,128,384]{2,1,0:T(8,128)} %get-tuple-element.113) | copy-start | bytes 1179652
  184.6 1.7 copy-start.13
  186.1 0.6 copy-start.17
  186.1 1.3 collective-permute-start.15
  186.8 10.1 %copy-start.3 = (bf16[1,4,96,384]{3,2,0,1:T(8,128)(2,1)S(1)}, bf16[1,4,96,384]{3,2,0,1:T(8,128)(2,1)}, u32[]{:S(2)}) copy-start(bf16[1,4,96,384]{3,2,0,1:T(8,128)(2,1)} %copy-done.2) | copy-start | bytes 884740
  192.1 5.0 %collective-permute-start.17 = (bf16[2,384]{1,0:T(2,128)(2,1)S(1)}, bf16[2,384]{1,0:T(2,128)(2,1)S(1)}, u32[]{:S(2)}, u32[]{:S(2)}) collective-permute-start(bf16[2,384]{1,0:T(2,128)(2,1)S(1)} %get-tuple-element.111), channel_id=1, source_target_pairs={{0,4},{4,8},{8,12},{1,5},{5,9},{9,13},{2,6},{6,10},{10,14},{3,7},{... | collective-permute-start | bytes 4616 | tf_op jit(solution)/shard_map/ppermute | solution.py:23
  195.6 5.5 %collective-permute-start.16 = (bf16[2,384]{1,0:T(2,128)(2,1)S(1)}, bf16[2,384]{1,0:T(2,128)(2,1)S(1)}, u32[]{:S(2)}, u32[]{:S(2)}) collective-permute-start(bf16[2,384]{1,0:T(2,128)(2,1)S(1)} %get-tuple-element.110), channel_id=1, source_target_pairs={{4,0},{8,4},{12,8},{5,1},{9,5},{13,9},{6,2},{10,6},{14,10},{7,3},{... | collective-permute-start | bytes 4616 | tf_op jit(solution)/shard_map/ppermute | solution.py:25
  197.1 6.1 %copy-start.16 = (f32[1,128,384]{2,1,0:T(8,128)S(1)}, f32[1,128,384]{2,1,0:T(8,128)}, u32[]{:S(2)}) copy-start(f32[1,128,384]{2,1,0:T(8,128)} %param.8) | copy-start | bytes 589828
  201.8 1.4 collective-permute-start.18

commit v5 on v3

--- a/solution.py
+++ b/solution.py
@@ -29,11 +29,10 @@
     return cells
 
 
-def gather_seq(parts):
+def gather_seq(parts, width):
     spread = ("group", "batch")
     count = lax.axis_size("group") * lax.axis_size("batch")
     ring = lax.axis_size("seq")
-    width = parts[0][0].shape[-1]
     flats = [cells.reshape(-1, width) for cells, _ in parts]
     flat = jnp.concatenate(flats, axis=0) if len(flats) > 1 else flats[0]
     rows = flat.shape[0]
@@ -41,19 +40,8 @@
     if size * count != rows:
         flat = jnp.pad(flat, ((0, size * count - rows), (0, 0)))
     piece = lax.dynamic_slice_in_dim(flat, lax.axis_index(spread) * size, size, 0)
-    if ring <= 8:
-        place = lax.axis_index("seq")
-        along = jnp.zeros((ring,) + piece.shape, piece.dtype)
-        along = lax.dynamic_update_slice_in_dim(along, piece[None], place, 0)
-        for shift in range(1, ring):
-            arrived = lax.ppermute(piece, "seq", [(i, (i + shift) % ring) for i in range(ring)])
-            along = lax.dynamic_update_slice_in_dim(
-                along, arrived[None], (place + ring - shift) % ring, 0
-            )
-    else:
-        along = lax.all_gather(piece, "seq", axis=0, tiled=False)
-    whole = lax.all_gather(along, spread, axis=0, tiled=False)
-    whole = whole.transpose(1, 0, 2, 3).reshape(ring, count * size, width)
+    whole = lax.all_gather(piece, ("seq",) + spread, axis=0, tiled=True)
+    whole = whole.reshape(ring, count * size, width)
     results = []
     offset = 0
     for (cells, dim), part in zip(parts, flats):
@@ -262,8 +250,9 @@
 
 
 def shards(features, noise, conv_weight, conv_bias, norm_gain, qkv_weight, out_weight):
-    (conv_weight,) = gather_seq([(conv_weight, 1)])
-    qkv_weight, out_weight = gather_seq([(qkv_weight, 1), (out_weight, 1)])
+    width = conv_weight.shape[-1]
+    (conv_weight,) = gather_seq([(conv_weight, 1)], width)
+    qkv_weight, out_weight = gather_seq([(qkv_weight, 1), (out_weight, 1)], width)
     clean = features[0]
     moved = (clean.astype(jnp.float32) + noise[0]).astype(jnp.bfloat16)
     joint = forward(

time: 181 us -> 225 us (1.24)
  waiting for transfers between devices: 77.3 us -> 131 us
  starting transfers between devices: 33.9 us -> 21.5 us
  other arithmetic: 5.62 us -> 7.89 us
    all_gather x2, waiting for transfers between devices: 37.5 us -> 106 us  [gather_seq(): whole = lax.all_gather(piece, ('seq',) + spread, axis=0, tiled=True)]
    ppermute x6 -> x0, waiting for transfers between devices: 14 us -> none  [gather_seq(): lax.ppermute(piece, 'seq', [(i, (i + shift) % ring) for i in range(ring)])]
    ppermute x6 -> x0, starting transfers between devices: 11.8 us -> none  [gather_seq(): lax.ppermute(piece, 'seq', [(i, (i + shift) % ring) for i in range(ring)])]
  transfers between devices with their start and end apart: 18 -> 12, of which waited for: 15 -> 9; matrix products, arithmetic and copies ran while one was open for 5% -> 6% of each run, Pallas kernels for 0% -> 0%
where the time goes in v5:
time: 225 us; the launch traced here: 224 us
  waiting for transfers between devices  131 us (58%)
  local copies, waits for them, and re-layouts  22.5 us (10%)
  starting transfers between devices  21.5 us (10%)
  blocking collectives  18.4 us (8%)
  between operations  15.2 us (7%)
  other arithmetic  7.89 us (4%)
  matrix products  7.03 us (3%)
    all_gather x2, waiting for transfers between devices, gather_seq(): whole = lax.all_gather(piece, ('seq',) + spread, axis=0, tiled=True)  106 us
    all_to_all x1, blocking collectives, forward(): lax.all_to_all(jnp.concatenate([query_send, keyval_send], axis=2), 'seq',...  11.8 us
    ppermute x2, starting transfers between devices, with_halo(): lax.ppermute(tail, axis, [(i, (i + 1) % count) for i in range(ends)])  8.01 us
    ppermute x2, waiting for transfers between devices, with_halo(): lax.ppermute(head, axis, [((i + 1) % count, i) for i in range(ends)])  7.84 us
    all_to_all x1, waiting for transfers between devices, shards(): lax.all_to_all(jnp.concatenate([query_grad.reshape(devices, query_len).as...  6.13 us
    all_to_all x1, waiting for transfers between devices, shards(): lax.all_to_all(grad_send, 'seq', split_axis=0, concat_axis=1, tiled=True)  5.27 us
  transfers between devices with their start and end apart: 12, of which 9 were waited for; matrix products, arithmetic and copies ran while one was open for 6% of the time, Pallas kernels for 0%

profile of v5, /device:TPU:0, one launch (start us, length us, event | category | flops | bytes accessed | tf_op | source)
XLA Modules:
  0.0 223.8 jit_solution(17035760408753254469)
XLA Ops:
  7.3 0.9 copy-done
  8.2 0.7 constant_dynamic-slice_fusion.2
  8.9 1.0 copy.134
  10.1 1.7 fusion.60
  11.9 5.0 %collective-permute-start = (bf16[2,2,384]{2,1,0:T(2,128)(2,1)S(1)}, bf16[2,2,384]{2,1,0:T(2,128)(2,1)S(1)}, u32[]{:S(2)}, u32[]{:S(2)}) collective-permute-start(bf16[2,2,384]{2,1,0:T(2,128)(2,1)S(1)} %get-tuple-element.93), channel_id=1, source_target_pairs={{0,4},{4,8},{8,12},{1,5},{5,9},{9,13},{2,6},{6,10},{10,14},{3,7},{... | collective-permute-start | bytes 9224 | tf_op jit(solution)/shard_map/ppermute | solution.py:23
  16.8 1.3 collective-permute-start.1
  18.1 4.2 %collective-permute-done.1 = bf16[2,2,384]{2,1,0:T(2,128)(2,1)S(1)} collective-permute-done((bf16[2,2,384]{2,1,0:T(2,128)(2,1)S(1)}, bf16[2,2,384]{2,1,0:T(2,128)(2,1)S(1)}, u32[]{:S(2)}, u32[]{:S(2)}) %collective-permute-start.1) | collective-permute-done | bytes 3104 | tf_op jit(solution)/shard_map/ppermute | solution.py:25
  22.4 48.5 %all-gather.6.cloned.1.call-done = bf16[1920,384]{1,0:T(8,128)(2,1)} async-done(((bf16[120,384]{1,0:T(8,128)(2,1)}), bf16[1920,384]{1,0:T(8,128)(2,1)}) %all-gather.6.cloned.1.call-update) | async-done | bytes 1474576 | tf_op jit(solution)/shard_map/all_gather | solution.py:43
  70.9 1.5 fusion.93
  73.6 1.1 fusion.23
  75.3 1.9 all-gather
  77.4 57.9 %all-gather.4.cloned.1.call-done = bf16[3072,384]{1,0:T(8,128)(2,1)} async-done(((bf16[192,384]{1,0:T(8,128)(2,1)}), bf16[3072,384]{1,0:T(8,128)(2,1)}) %all-gather.4.cloned.1.call-update) | async-done | bytes 2359312 | tf_op jit(solution)/shard_map/all_gather | solution.py:43
  135.3 1.7 slice.203
  137.2 0.5 copy-done.23
  137.7 0.5 fusion.3
  139.6 11.8 %all_to_all.43 = bf16[4,2,18432]{2,1,0:T(2,128)(2,1)S(1)} all-to-all(bf16[4,2,18432]{2,1,0:T(2,128)(2,1)S(1)} %pad_maximum_fusion), channel_id=1, replica_groups=mesh['group'=2,'seq'=4,'batch'=2,'mp'=2] {'seq'}, dimensions={0} | all-to-all | bytes 589824 | tf_op jit(solution)/shard_map/all_to_all | solution.py:202
  151.4 0.4 slice_reduce_fusion.2
  154.8 0.7 copy.144
  155.6 3.9 %all-to-all-start.1 = ((bf16[4,2,6144]{2,1,0:T(2,128)(2,1)}), bf16[4,2,6144]{2,1,0:T(2,128)(2,1)}, u32[]{:S(2)}, u32[]{:S(2)}) async-start(bf16[4,2,6144]{2,1,0:T(2,128)(2,1)} %copy.144), calls=%async_computation.1 | async-start | bytes 196608 | tf_op jit(solution)/shard_map/all_to_all | solution.py:224
  159.6 1.1 slice.225
  160.7 0.5 reshape.257
  161.2 0.3 copy.146
  161.5 3.9 %all-to-all-done.1 = bf16[4,2,6144]{2,1,0:T(2,128)(2,1)} async-done(((bf16[4,2,6144]{2,1,0:T(2,128)(2,1)}), bf16[4,2,6144]{2,1,0:T(2,128)(2,1)}, u32[]{:S(2)}, u32[]{:S(2)}) %all-to-all-start.1) | async-done | bytes 98336 | tf_op jit(solution)/shard_map/all_to_all | solution.py:224
  165.4 1.0 reshape.255
  167.0 0.7 constant_dynamic-slice_fusion.1
  167.7 1.3 slice_reduce_fusion
  168.9 1.1 squeeze.87
  170.0 0.9 convert_add_fusion
  171.0 2.0 all_gather.15
  173.5 0.5 broadcast.223
  174.0 0.9 reduce.7
  174.9 0.7 reshape.278
  175.6 3.5 %all-to-all-start.2 = ((bf16[4,2,3072]{2,1,0:T(2,128)(2,1)}), bf16[4,2,3072]{2,1,0:T(2,128)(2,1)S(1)}, u32[]{:S(2)}, u32[]{:S(2)}) async-start(bf16[4,2,3072]{2,1,0:T(2,128)(2,1)} %reshape.278), calls=%async_computation.2 | async-start | bytes 98304 | tf_op jit(solution)/shard_map/all_to_all | solution.py:297
  179.3 5.3 %all-to-all-done.2 = bf16[4,2,3072]{2,1,0:T(2,128)(2,1)S(1)} async-done(((bf16[4,2,3072]{2,1,0:T(2,128)(2,1)}), bf16[4,2,3072]{2,1,0:T(2,128)(2,1)S(1)}, u32[]{:S(2)}, u32[]{:S(2)}) %all-to-all-start.2) | async-done | bytes 49184 | tf_op jit(solution)/shard_map/all_to_all | solution.py:297
  185.3 0.8 multiply_reduce_fusion
  187.5 0.8 reduce.8
  188.3 0.8 reshape.280
  189.0 3.3 %all-to-all-start.3 = ((bf16[4,2,9216]{2,1,0:T(2,128)(2,1)}), bf16[4,2,9216]{2,1,0:T(2,128)(2,1)S(1)}, u32[]{:S(2)}, u32[]{:S(2)}) async-start(bf16[4,2,9216]{2,1,0:T(2,128)(2,1)} %reshape.280), calls=%async_computation.3 | async-start | bytes 294912 | tf_op jit(solution)/shard_map/all_to_all | solution.py:308
  192.4 6.1 %all-to-all-done.3 = bf16[4,2,9216]{2,1,0:T(2,128)(2,1)S(1)} async-done(((bf16[4,2,9216]{2,1,0:T(2,128)(2,1)}), bf16[4,2,9216]{2,1,0:T(2,128)(2,1)S(1)}, u32[]{:S(2)}, u32[]{:S(2)}) %all-to-all-start.3) | async-done | bytes 147488 | tf_op jit(solution)/shard_map/all_to_all | solution.py:308
  199.9 0.6 fusion.10
  200.8 1.0 collective-permute-done.3
  201.9 2.6 %psum.7 = f32[64]{0:T(128)S(1)} all-reduce(f32[64]{0:T(128)S(1)} %fusion.76), channel_id=1, replica_groups=mesh['group'=2,'seq'=4,'batch'=2,'mp'=2] {'mp'}, use_global_device_ids=true, to_apply=%region_7.8 | all-reduce | flops 64 | bytes 512 | tf_op jit(solution)/shard_map/psum | solution.py:346
  205.1 3.1 %collective-permute-start.5 = (bf16[2,384]{1,0:T(2,128)(2,1)S(1)}, bf16[2,384]{1,0:T(2,128)(2,1)S(1)}, u32[]{:S(2)}, u32[]{:S(2)}) collective-permute-start(bf16[2,384]{1,0:T(2,128)(2,1)S(1)} %get-tuple-element.107), channel_id=1, source_target_pairs={{0,4},{4,8},{8,12},{1,5},{5,9},{9,13},{2,6},{6,10},{10,14},{3,7},{... | collective-permute-start | bytes 4616 | tf_op jit(solution)/shard_map/ppermute | solution.py:23
  208.4 1.3 collective-permute-start.4
  210.2 3.7 %collective-permute-done.4 = bf16[2,384]{1,0:T(2,128)(2,1)S(1)} collective-permute-done((bf16[2,384]{1,0:T(2,128)(2,1)S(1)}, bf16[2,384]{1,0:T(2,128)(2,1)S(1)}, u32[]{:S(2)}, u32[]{:S(2)}) %collective-permute-start.4) | collective-permute-done | bytes 1568 | tf_op jit(solution)/shard_map/ppermute | solution.py:25
  214.7 0.6 slice.306
  215.4 0.7 collective-permute-done.6
  216.1 0.8 fusion.26
  (162 shorter events, 13.6 us)
Async XLA Ops:
  7.2 1.0 copy-start
  7.2 4.6 %copy-start.19 = (f32[1,128,384]{2,1,0:T(8,128)S(1)}, f32[1,128,384]{2,1,0:T(8,128)}, u32[]{:S(2)}) copy-start(f32[1,128,384]{2,1,0:T(8,128)} %param.8) | copy-start | bytes 589828
  7.2 4.6 %copy-start.14 = (bf16[1,128,384]{2,1,0:T(8,128)(2,1)S(1)}, bf16[1,128,384]{2,1,0:T(8,128)(2,1)}, u32[]{:S(2)}) copy-start(bf16[1,128,384]{2,1,0:T(8,128)(2,1)} %param.7) | copy-start | bytes 294916
  7.2 63.7 %all-gather.6.cloned.1.call-start = ((), (), s32[]{:S(2)}) async-start(), calls=%async_computation.5 | async-start | bytes 1566720 | tf_op jit(solution)/shard_map/all_gather | solution.py:43
  8.8 126.5 %all-gather.4.cloned.1.call-start = ((), (), s32[]{:S(2)}) async-start(), calls=%async_computation.4 | async-start | bytes 2506752 | tf_op jit(solution)/shard_map/all_gather | solution.py:43
  11.9 6.3 %collective-permute-start = (bf16[2,2,384]{2,1,0:T(2,128)(2,1)S(1)}, bf16[2,2,384]{2,1,0:T(2,128)(2,1)S(1)}, u32[]{:S(2)}, u32[]{:S(2)}) collective-permute-start(bf16[2,2,384]{2,1,0:T(2,128)(2,1)S(1)} %get-tuple-element.93), channel_id=1, source_target_pairs={{0,4},{4,8},{8,12},{1,5},{5,9},{9,13},{2,6},{6,10},{10,14},{3,7},{... | collective-permute-start | bytes 9224 | tf_op jit(solution)/shard_map/ppermute | solution.py:23
  16.8 5.5 %collective-permute-start.1 = (bf16[2,2,384]{2,1,0:T(2,128)(2,1)S(1)}, bf16[2,2,384]{2,1,0:T(2,128)(2,1)S(1)}, u32[]{:S(2)}, u32[]{:S(2)}) collective-permute-start(bf16[2,2,384]{2,1,0:T(2,128)(2,1)S(1)} %get-tuple-element.94), channel_id=1, source_target_pairs={{4,0},{8,4},{12,8},{5,1},{9,5},{13,9},{6,2},{10,6},{14,10},{7,3},{... | collective-permute-start | bytes 9224 | tf_op jit(solution)/shard_map/ppermute | solution.py:25
  72.4 1.2 copy-start.3
  72.4 1.2 copy-start.5
  72.4 1.2 copy-start.7
  72.4 1.2 copy-start.9
  72.4 1.2 copy-start.1
  72.7 0.9 copy-start.22
  75.3 61.6 %copy-start.15 = (bf16[2,64,1,384]{3,1,0,2:T(8,128)(2,1)}, bf16[2,64,1,384]{3,1,0,2:T(8,128)(2,1)S(1)}, u32[]{:S(2)}) copy-start(bf16[2,64,1,384]{3,1,0,2:T(8,128)(2,1)S(1)} %fusion.54) | copy-start | bytes 294916
  137.0 0.7 copy-start.23
  151.4 0.7 copy-start.11
  152.4 2.4 %copy-start.17 = (bf16[256,96]{1,0:T(8,128)(2,1)}, bf16[256,96]{1,0:T(8,128)(2,1)S(1)}, u32[]{:S(2)}) copy-start(bf16[256,96]{1,0:T(8,128)(2,1)S(1)} %squeeze.83) | copy-start | bytes 147460
  153.4 6.1 %copy-start.21 = (bf16[256,96]{0,1:T(8,128)(2,1)}, bf16[256,96]{0,1:T(8,128)(2,1)S(1)}, u32[]{:S(2)}) copy-start(bf16[256,96]{0,1:T(8,128)(2,1)S(1)} %convolution_convert_fusion.4) | copy-start | bytes 147460
  155.6 9.8 %all-to-all-start.1 = ((bf16[4,2,6144]{2,1,0:T(2,128)(2,1)}), bf16[4,2,6144]{2,1,0:T(2,128)(2,1)}, u32[]{:S(2)}, u32[]{:S(2)}) async-start(bf16[4,2,6144]{2,1,0:T(2,128)(2,1)} %copy.144), calls=%async_computation.1 | async-start | bytes 196608 | tf_op jit(solution)/shard_map/all_to_all | solution.py:224
  161.5 6.2 %copy-start.12 = (bf16[4,2,18432]{2,1,0:T(2,128)(2,1)S(1)}, bf16[4,2,18432]{2,1,0:T(2,128)(2,1)}, u32[]{:S(2)}) copy-start(bf16[4,2,18432]{2,1,0:T(2,128)(2,1)} %copy-done.11) | copy-start | bytes 884740
  161.5 8.5 %copy-start.16 = (bf16[2,64,1,384]{3,1,0,2:T(8,128)(2,1)S(1)}, bf16[2,64,1,384]{3,1,0,2:T(8,128)(2,1)}, u32[]{:S(2)}) copy-start(bf16[2,64,1,384]{3,1,0,2:T(8,128)(2,1)} %copy-done.15) | copy-start | bytes 294916
  167.0 12.1 %copy-start.18 = (bf16[256,96]{1,0:T(8,128)(2,1)S(1)}, bf16[256,96]{1,0:T(8,128)(2,1)}, u32[]{:S(2)}) copy-start(bf16[256,96]{1,0:T(8,128)(2,1)} %copy-done.17) | copy-start | bytes 147460
  167.7 2.3 %collective-permute-start.2 = (bf16[2,64,384]{2,1,0:T(8,128)(2,1)}, bf16[2,64,384]{2,1,0:T(8,128)(2,1)}, u32[]{:S(2)}, u32[]{:S(2)}) collective-permute-start(bf16[2,64,384]{2,1,0:T(8,128)(2,1)} %constant_dynamic-slice_fusion.1), channel_id=1, source_target_pairs={{0,1},{1,0},{2,3},{3,2},{4,5},{5,4},{6,7},{7,6},{8,9},{9,8},{10,11... | collective-permute-start | bytes 294920 | tf_op jit(solution)/shard_map/ppermute | solution.py:58
  175.6 8.9 %all-to-all-start.2 = ((bf16[4,2,3072]{2,1,0:T(2,128)(2,1)}), bf16[4,2,3072]{2,1,0:T(2,128)(2,1)S(1)}, u32[]{:S(2)}, u32[]{:S(2)}) async-start(bf16[4,2,3072]{2,1,0:T(2,128)(2,1)} %reshape.278), calls=%async_computation.2 | async-start | bytes 98304 | tf_op jit(solution)/shard_map/all_to_all | solution.py:297
  189.0 9.5 %all-to-all-start.3 = ((bf16[4,2,9216]{2,1,0:T(2,128)(2,1)}), bf16[4,2,9216]{2,1,0:T(2,128)(2,1)S(1)}, u32[]{:S(2)}, u32[]{:S(2)}) async-start(bf16[4,2,9216]{2,1,0:T(2,128)(2,1)} %reshape.280), calls=%async_computation.3 | async-start | bytes 294912 | tf_op jit(solution)/shard_map/all_to_all | solution.py:308
  199.2 1.4 copy-start.13
  200.5 1.3 collective-permute-start.3
  200.7 9.1 %copy-start.10 = (bf16[1,4,96,384]{3,2,0,1:T(8,128)(2,1)S(1)}, bf16[1,4,96,384]{3,2,0,1:T(8,128)(2,1)}, u32[]{:S(2)}) copy-start(bf16[1,4,96,384]{3,2,0,1:T(8,128)(2,1)} %copy-done.9) | copy-start | bytes 884740
  201.9 8.1 %copy-start.8 = (bf16[1,4,96,384]{3,2,0,1:T(8,128)(2,1)S(1)}, bf16[1,4,96,384]{3,2,0,1:T(8,128)(2,1)}, u32[]{:S(2)}) copy-start(bf16[1,4,96,384]{3,2,0,1:T(8,128)(2,1)} %copy-done.7) | copy-start | bytes 884740
  204.6 9.3 %copy-start.6 = (bf16[1,4,96,384]{3,2,0,1:T(8,128)(2,1)S(1)}, bf16[1,4,96,384]{3,2,0,1:T(8,128)(2,1)}, u32[]{:S(2)}) copy-start(bf16[1,4,96,384]{3,2,0,1:T(8,128)(2,1)} %copy-done.5) | copy-start | bytes 884740
  204.7 9.4 %copy-start.4 = (bf16[1,4,96,384]{3,2,0,1:T(8,128)(2,1)S(1)}, bf16[1,4,96,384]{3,2,0,1:T(8,128)(2,1)}, u32[]{:S(2)}) copy-start(bf16[1,4,96,384]{3,2,0,1:T(8,128)(2,1)} %copy-done.3) | copy-start | bytes 884740
  205.1 4.9 %collective-permute-start.5 = (bf16[2,384]{1,0:T(2,128)(2,1)S(1)}, bf16[2,384]{1,0:T(2,128)(2,1)S(1)}, u32[]{:S(2)}, u32[]{:S(2)}) collective-permute-start(bf16[2,384]{1,0:T(2,128)(2,1)S(1)} %get-tuple-element.107), channel_id=1, source_target_pairs={{0,4},{4,8},{8,12},{1,5},{5,9},{9,13},{2,6},{6,10},{10,14},{3,7},{... | collective-permute-start | bytes 4616 | tf_op jit(solution)/shard_map/ppermute | solution.py:23
  208.1 6.3 %copy-start.2 = (bf16[1,4,96,384]{3,2,0,1:T(8,128)(2,1)S(1)}, bf16[1,4,96,384]{3,2,0,1:T(8,128)(2,1)}, u32[]{:S(2)}) copy-start(bf16[1,4,96,384]{3,2,0,1:T(8,128)(2,1)} %copy-done.1) | copy-start | bytes 884740
  208.4 5.5 %collective-permute-start.4 = (bf16[2,384]{1,0:T(2,128)(2,1)S(1)}, bf16[2,384]{1,0:T(2,128)(2,1)S(1)}, u32[]{:S(2)}, u32[]{:S(2)}) collective-permute-start(bf16[2,384]{1,0:T(2,128)(2,1)S(1)} %get-tuple-element.106), channel_id=1, source_target_pairs={{4,0},{8,4},{12,8},{5,1},{9,5},{13,9},{6,2},{10,6},{14,10},{7,3},{... | collective-permute-start | bytes 4616 | tf_op jit(solution)/shard_map/ppermute | solution.py:25
  210.0 6.2 %copy-start.20 = (f32[1,128,384]{2,1,0:T(8,128)S(1)}, f32[1,128,384]{2,1,0:T(8,128)}, u32[]{:S(2)}) copy-start(f32[1,128,384]{2,1,0:T(8,128)} %param.8) | copy-start | bytes 589828
  214.6 1.4 collective-permute-start.6
Sparse Core Ops, SparseCore 0:
  10.7 60.1 all-gather.5
  74.3 60.9 all-gather.3

commit v6 on v5

--- a/solution.py
+++ b/solution.py
@@ -29,19 +29,40 @@
     return cells
 
 
-def gather_seq(parts, width):
+def ring_gather(piece):
+    ring = lax.axis_size("seq")
+    place = lax.axis_index("seq")
+    along = jnp.zeros((ring,) + piece.shape, piece.dtype)
+    along = lax.dynamic_update_slice_in_dim(along, piece[None], place, 0)
+    for shift in range(1, ring):
+        arrived = lax.ppermute(piece, "seq", [(i, (i + shift) % ring) for i in range(ring)])
+        along = lax.dynamic_update_slice_in_dim(along, arrived[None], (place + ring - shift) % ring, 0)
+    return along
+
+
+def gather_seq(parts, width, direct=0):
     spread = ("group", "batch")
     count = lax.axis_size("group") * lax.axis_size("batch")
     ring = lax.axis_size("seq")
     flats = [cells.reshape(-1, width) for cells, _ in parts]
     flat = jnp.concatenate(flats, axis=0) if len(flats) > 1 else flats[0]
     rows = flat.shape[0]
-    size = -(-rows // count)
-    if size * count != rows:
-        flat = jnp.pad(flat, ((0, size * count - rows), (0, 0)))
-    piece = lax.dynamic_slice_in_dim(flat, lax.axis_index(spread) * size, size, 0)
-    whole = lax.all_gather(piece, ("seq",) + spread, axis=0, tiled=True)
-    whole = whole.reshape(ring, count * size, width)
+    if ring > 8:
+        direct = 0
+    split = rows - direct
+    size = -(-split // count)
+    head = flat[:split]
+    if size * count != split:
+        head = jnp.pad(head, ((0, size * count - split), (0, 0)))
+    piece = lax.dynamic_slice_in_dim(head, lax.axis_index(spread) * size, size, 0)
+    if ring <= 8:
+        along = ring_gather(piece)
+    else:
+        along = lax.all_gather(piece, "seq", axis=0, tiled=False)
+    whole = lax.all_gather(along, spread, axis=0, tiled=False)
+    whole = whole.transpose(1, 0, 2, 3).reshape(ring, count * size, width)[:, :split]
+    if direct:
+        whole = jnp.concatenate([whole, ring_gather(flat[split:])], axis=1)
     results = []
     offset = 0
     for (cells, dim), part in zip(parts, flats):
@@ -251,7 +272,8 @@
 
 def shards(features, noise, conv_weight, conv_bias, norm_gain, qkv_weight, out_weight):
     width = conv_weight.shape[-1]
-    (conv_weight,) = gather_seq([(conv_weight, 1)], width)
+    conv_rows = conv_weight.size // width
+    (conv_weight,) = gather_seq([(conv_weight, 1)], width, conv_rows // 2 // 16 * 16)
     qkv_weight, out_weight = gather_seq([(qkv_weight, 1), (out_weight, 1)], width)
     clean = features[0]
     moved = (clean.astype(jnp.float32) + noise[0]).astype(jnp.bfloat16)

time: 225 us -> 184 us (0.82)
  waiting for transfers between devices: 131 us -> 34.6 us
  local copies, waits for them, and re-layouts: 22.5 us -> 45.7 us
  blocking collectives: 18.4 us -> 35 us
  starting transfers between devices: 21.5 us -> 37.7 us
    all_gather x2 -> x1, waiting for transfers between devices: 106 us -> 0.02 us  [gather_seq(): whole = lax.all_gather(along, spread, axis=0, tiled=False)]
    dynamic_update_slice x0 -> x11, local copies, waits for them, and re-layouts: none -> 25.1 us  [the longest x9 18.8 us: ring_gather(): lax.dynamic_update_slice_in_dim(along, arrived[None], (place + ring - shi...]
    ppermute x0 -> x9, starting transfers between devices: none -> 17.6 us  [ring_gather(): lax.ppermute(piece, 'seq', [(i, (i + shift) % ring) for i in range(ring)])]
    all_gather x0 -> x1, blocking collectives: none -> 13.9 us  [gather_seq(): whole = lax.all_gather(along, spread, axis=0, tiled=False)]
    ppermute x0 -> x9, waiting for transfers between devices: none -> 13 us  [ring_gather(): lax.ppermute(piece, 'seq', [(i, (i + shift) % ring) for i in range(ring)])]
    ppermute x2, waiting for transfers between devices: 7.84 us -> 3.67 us  [with_halo(): lax.ppermute(head, axis, [((i + 1) % count, i) for i in range(ends)])]
    all_to_all x1, blocking collectives: 11.8 us -> 14.5 us  [forward(): lax.all_to_all(jnp.concatenate([query_send, keyval_send], axis=2), 'seq',...]
  transfers between devices with their start and end apart: 12 -> 20, of which waited for: 9 -> 10; matrix products, arithmetic and copies ran while one was open for 6% -> 19% of each run, Pallas kernels for 0% -> 0%
where the time goes in v6:
time: 184 us; the launch traced here: 183 us
  local copies, waits for them, and re-layouts  45.7 us (25%)
  starting transfers between devices  37.7 us (20%)
  blocking collectives  35 us (19%)
  waiting for transfers between devices  34.6 us (19%)
  between operations  15.4 us (8%)
  other arithmetic  7.42 us (4%)
  matrix products  7.04 us (4%)
    dynamic_update_slice x9, local copies, waits for them, and re-layouts, ring_gather(): lax.dynamic_update_slice_in_dim(along, arrived[None], (place + ring - shi...  18.8 us
    ppermute x9, starting transfers between devices, ring_gather(): lax.ppermute(piece, 'seq', [(i, (i + shift) % ring) for i in range(ring)])  17.6 us
    all_to_all x1, blocking collectives, forward(): lax.all_to_all(jnp.concatenate([query_send, keyval_send], axis=2), 'seq',...  14.5 us
    all_gather x1, blocking collectives, gather_seq(): whole = lax.all_gather(along, spread, axis=0, tiled=False)  13.9 us
    ppermute x9, waiting for transfers between devices, ring_gather(): lax.ppermute(piece, 'seq', [(i, (i + shift) % ring) for i in range(ring)])  13 us
    ppermute x2, starting transfers between devices, with_halo(): lax.ppermute(tail, axis, [(i, (i + 1) % count) for i in range(ends)])  6.79 us
    dynamic_update_slice x2, local copies, waits for them, and re-layouts, ring_gather(): along = lax.dynamic_update_slice_in_dim(along, piece[None], place, 0)  6.25 us
    all_to_all x1, waiting for transfers between devices, shards(): lax.all_to_all(jnp.concatenate([query_grad.reshape(devices, query_len).as...  6.03 us
  transfers between devices with their start and end apart: 20, of which 10 were waited for; matrix products, arithmetic and copies ran while one was open for 19% of the time, Pallas kernels for 0%

profile of v6, /device:TPU:0, one launch (start us, length us, event | category | flops | bytes accessed | tf_op | source)
XLA Modules:
  0.0 182.8 jit_solution(12854686887337304423)
XLA Ops:
  7.2 1.0 copy.189
  8.5 1.1 bitcast_dynamic-update-slice_fusion.3
  9.6 3.1 %collective-permute-start = (bf16[192,384]{1,0:T(8,128)(2,1)S(1)}, bf16[192,384]{1,0:T(8,128)(2,1)S(1)}, u32[]{:S(2)}, u32[]{:S(2)}) collective-permute-start(bf16[192,384]{1,0:T(8,128)(2,1)S(1)} %get-tuple-element.76), channel_id=1, source_target_pairs={{0,4},{4,8},{8,12},{12,0},{1,5},{5,9},{9,13},{13,1},{2,6},{6,10},{... | collective-permute-start | bytes 442376 | tf_op jit(solution)/shard_map/ppermute | solution.py:38
  12.7 2.6 %collective-permute-start.1 = (bf16[192,384]{1,0:T(8,128)(2,1)S(1)}, bf16[192,384]{1,0:T(8,128)(2,1)S(1)}, u32[]{:S(2)}, u32[]{:S(2)}) collective-permute-start(bf16[192,384]{1,0:T(8,128)(2,1)S(1)} %get-tuple-element.76), channel_id=1, source_target_pairs={{0,8},{4,12},{8,0},{12,4},{1,9},{5,13},{9,1},{13,5},{2,10},{6,14},... | collective-permute-start | bytes 442376 | tf_op jit(solution)/shard_map/ppermute | solution.py:38
  15.3 1.3 collective-permute-start.2
  16.6 2.9 %collective-permute-done = bf16[192,384]{1,0:T(8,128)(2,1)S(1)} collective-permute-done((bf16[192,384]{1,0:T(8,128)(2,1)S(1)}, bf16[192,384]{1,0:T(8,128)(2,1)S(1)}, u32[]{:S(2)}, u32[]{:S(2)}) %collective-permute-start) | collective-permute-done | bytes 147488 | tf_op jit(solution)/shard_map/ppermute | solution.py:38
  19.6 5.4 %collective-permute-done.1 = bf16[192,384]{1,0:T(8,128)(2,1)S(1)} collective-permute-done((bf16[192,384]{1,0:T(8,128)(2,1)S(1)}, bf16[192,384]{1,0:T(8,128)(2,1)S(1)}, u32[]{:S(2)}, u32[]{:S(2)}) %collective-permute-start.1) | collective-permute-done | bytes 147488 | tf_op jit(solution)/shard_map/ppermute | solution.py:38
  25.1 0.8 copy-done.10
  26.0 3.6 %collective-permute-start.7 = (bf16[240,384]{1,0:T(8,128)(2,1)S(1)}, bf16[240,384]{1,0:T(8,128)(2,1)S(1)}, u32[]{:S(2)}, u32[]{:S(2)}) collective-permute-start(bf16[240,384]{1,0:T(8,128)(2,1)S(1)} %get-tuple-element.92), channel_id=1, source_target_pairs={{0,4},{4,8},{8,12},{12,0},{1,5},{5,9},{9,13},{13,1},{2,6},{6,10},{... | collective-permute-start | bytes 552968 | tf_op jit(solution)/shard_map/ppermute | solution.py:38
  29.6 1.7 collective-permute-start.8
  31.5 3.6 %collective-permute-start.3 = (bf16[2,2,384]{2,1,0:T(2,128)(2,1)S(1)}, bf16[2,2,384]{2,1,0:T(2,128)(2,1)S(1)}, u32[]{:S(2)}, u32[]{:S(2)}) collective-permute-start(bf16[2,2,384]{2,1,0:T(2,128)(2,1)S(1)} %get-tuple-element.107), channel_id=1, source_target_pairs={{0,4},{4,8},{8,12},{1,5},{5,9},{9,13},{2,6},{6,10},{10,14},{3,7},{... | collective-permute-start | bytes 9224 | tf_op jit(solution)/shard_map/ppermute | solution.py:23
  35.1 1.3 collective-permute-start.10
  37.1 4.8 %dynamic_update_slice.55 = bf16[4,240,384]{2,0,1:T(4,128)(2,1)S(1)} dynamic-update-slice(bf16[4,240,384]{2,0,1:T(4,128)(2,1)S(1)} %broadcast_in_dim.27, bf16[1,240,384]{2,0,1:T(2,128)(2,1)S(1)} %copy.197, s32[]{:T(128)S(6)} %select_n.63, s32[]{:T(128)} %constant.148.clone.1, s32[]{:T(128)} %constant.148.clone.1) | dynamic-update-slice | bytes 368644 | tf_op jit(solution)/shard_map/dynamic_update_slice | solution.py:36
  41.9 1.5 dynamic_update_slice.51
  43.4 4.7 %collective-permute-start.9 = (bf16[240,384]{1,0:T(8,128)(2,1)S(1)}, bf16[240,384]{1,0:T(8,128)(2,1)S(1)}, u32[]{:S(2)}, u32[]{:S(2)}) collective-permute-start(bf16[240,384]{1,0:T(8,128)(2,1)S(1)} %get-tuple-element.92), channel_id=1, source_target_pairs={{0,12},{4,0},{8,4},{12,8},{1,13},{5,1},{9,5},{13,9},{2,14},{6,2},{... | collective-permute-start | bytes 552968 | tf_op jit(solution)/shard_map/ppermute | solution.py:38
  48.7 4.6 %collective-permute-done.5 = bf16[60,384]{1,0:T(8,128)(2,1)S(1)} collective-permute-done((bf16[60,384]{1,0:T(8,128)(2,1)S(1)}, bf16[60,384]{1,0:T(8,128)(2,1)S(1)}, u32[]{:S(2)}, u32[]{:S(2)}) %collective-permute-start.5) | collective-permute-done | bytes 46112 | tf_op jit(solution)/shard_map/ppermute | solution.py:38
  53.5 1.5 dynamic_update_slice.52
  54.9 1.5 dynamic_update_slice.53
  56.4 1.5 dynamic_update_slice.54
  57.9 13.9 %all_gather.45 = bf16[4,4,60,384]{3,1,2,0:T(4,128)(2,1)S(1)} all-gather(bf16[1,4,60,384]{3,1,2,0:T(4,128)(2,1)S(1)} %dynamic_update_slice.54), channel_id=1, replica_groups=mesh['group'=2,'seq'=4,'batch'=2,'mp'=2] {'group','batch'}, dimensions={0}, use_global_device_ids=true | all-gather | bytes 921600 | tf_op jit(solution)/shard_map/all_gather | solution.py:62
  72.7 4.8 %dynamic_update_slice.56 = bf16[4,240,384]{2,0,1:T(4,128)(2,1)S(1)} dynamic-update-slice(bf16[4,240,384]{2,0,1:T(4,128)(2,1)S(1)} %dynamic_update_slice.55, bf16[1,240,384]{2,0,1:T(2,128)(2,1)S(1)} %copy.198, s32[]{:T(128)S(6)} %select_n.65, s32[]{:T(128)} %constant.148.clone.1, s32[]{:T(128)} %constant.148.clone.1) | dynamic-update-slice | bytes 368644 | tf_op jit(solution)/shard_map/dynamic_update_slice | solution.py:39
  77.5 4.8 %dynamic_update_slice.57 = bf16[4,240,384]{2,0,1:T(4,128)(2,1)S(1)} dynamic-update-slice(bf16[4,240,384]{2,0,1:T(4,128)(2,1)S(1)} %dynamic_update_slice.56, bf16[1,240,384]{2,0,1:T(2,128)(2,1)S(1)} %copy.199, s32[]{:T(128)S(6)} %select_n.67, s32[]{:T(128)} %constant.148.clone.1, s32[]{:T(128)} %constant.148.clone.1) | dynamic-update-slice | bytes 368644 | tf_op jit(solution)/shard_map/dynamic_update_slice | solution.py:39
  82.3 4.8 %dynamic_update_slice.58 = bf16[4,240,384]{2,0,1:T(4,128)(2,1)S(1)} dynamic-update-slice(bf16[4,240,384]{2,0,1:T(4,128)(2,1)S(1)} %dynamic_update_slice.57, bf16[1,240,384]{2,0,1:T(2,128)(2,1)S(1)} %copy.200, s32[]{:T(128)S(6)} %select_n.69, s32[]{:T(128)} %constant.148.clone.1, s32[]{:T(128)} %constant.148.clone.1) | dynamic-update-slice | bytes 368644 | tf_op jit(solution)/shard_map/dynamic_update_slice | solution.py:39
  87.1 1.0 pad_maximum_fusion
  89.7 1.1 fusion.23
  91.4 2.1 %all-gather = bf16[2,64,1,768]{3,1,0,2:T(8,128)(2,1)S(1)} all-gather(bf16[2,64,1,384]{3,1,0,2:T(8,128)(2,1)S(1)} %fusion.54), channel_id=2, replica_groups=mesh['group'=2,'seq'=4,'batch'=2,'mp'=2] {'mp'}, dimensions={3}, use_global_device_ids=true | all-gather | bytes 294912 | tf_op jit(solution)/shard_map/all_gather | solution.py:186
  93.6 1.7 slice.211
  98.0 14.5 %all_to_all.43 = bf16[4,2,18432]{2,1,0:T(2,128)(2,1)S(1)} all-to-all(bf16[4,2,18432]{2,1,0:T(2,128)(2,1)S(1)} %pad_maximum_fusion.1), channel_id=1, replica_groups=mesh['group'=2,'seq'=4,'batch'=2,'mp'=2] {'seq'}, dimensions={0} | all-to-all | bytes 589824 | tf_op jit(solution)/shard_map/all_to_all | solution.py:223
  116.3 3.9 %all-to-all-start.1 = ((bf16[4,2,6144]{2,1,0:T(2,128)(2,1)}), bf16[4,2,6144]{2,1,0:T(2,128)(2,1)}, u32[]{:S(2)}, u32[]{:S(2)}) async-start(bf16[4,2,6144]{2,1,0:T(2,128)(2,1)} %copy.210), calls=%async_computation.1 | async-start | bytes 196608 | tf_op jit(solution)/shard_map/all_to_all | solution.py:245
  120.3 1.1 slice.235
  122.2 3.9 %all-to-all-done.1 = bf16[4,2,6144]{2,1,0:T(2,128)(2,1)} async-done(((bf16[4,2,6144]{2,1,0:T(2,128)(2,1)}), bf16[4,2,6144]{2,1,0:T(2,128)(2,1)}, u32[]{:S(2)}, u32[]{:S(2)}) %all-to-all-start.1) | async-done | bytes 98336 | tf_op jit(solution)/shard_map/all_to_all | solution.py:245
  126.1 1.0 reshape.287
  129.2 0.9 collective-permute-done.11
  130.1 0.9 convert_add_fusion
  131.0 1.9 %all_gather.47 = bf16[64,768]{1,0:T(8,128)(2,1)S(1)} all-gather(bf16[64,384]{1,0:T(8,128)(2,1)S(1)} %fusion.85), channel_id=1, replica_groups=mesh['group'=2,'seq'=4,'batch'=2,'mp'=2] {'mp'}, dimensions={1}, use_global_device_ids=true | all-gather | bytes 147456 | tf_op jit(solution)/shard_map/all_gather | solution.py:307
  133.9 0.9 reduce.7
  135.5 3.3 %all-to-all-start.2 = ((bf16[4,2,3072]{2,1,0:T(2,128)(2,1)}), bf16[4,2,3072]{2,1,0:T(2,128)(2,1)S(1)}, u32[]{:S(2)}, u32[]{:S(2)}) async-start(bf16[4,2,3072]{2,1,0:T(2,128)(2,1)} %reshape.310), calls=%async_computation.2 | async-start | bytes 98304 | tf_op jit(solution)/shard_map/all_to_all | solution.py:319
  139.0 5.5 %all-to-all-done.2 = bf16[4,2,3072]{2,1,0:T(2,128)(2,1)S(1)} async-done(((bf16[4,2,3072]{2,1,0:T(2,128)(2,1)}), bf16[4,2,3072]{2,1,0:T(2,128)(2,1)S(1)}, u32[]{:S(2)}, u32[]{:S(2)}) %all-to-all-start.2) | async-done | bytes 49184 | tf_op jit(solution)/shard_map/all_to_all | solution.py:319
  146.6 0.8 reduce.8
  147.4 0.8 reshape.312
  148.1 3.3 %all-to-all-start.3 = ((bf16[4,2,9216]{2,1,0:T(2,128)(2,1)}), bf16[4,2,9216]{2,1,0:T(2,128)(2,1)S(1)}, u32[]{:S(2)}, u32[]{:S(2)}) async-start(bf16[4,2,9216]{2,1,0:T(2,128)(2,1)} %reshape.312), calls=%async_computation.3 | async-start | bytes 294912 | tf_op jit(solution)/shard_map/all_to_all | solution.py:330
  151.5 6.0 %all-to-all-done.3 = bf16[4,2,9216]{2,1,0:T(2,128)(2,1)S(1)} async-done(((bf16[4,2,9216]{2,1,0:T(2,128)(2,1)}), bf16[4,2,9216]{2,1,0:T(2,128)(2,1)S(1)}, u32[]{:S(2)}, u32[]{:S(2)}) %all-to-all-start.3) | async-done | bytes 147488 | tf_op jit(solution)/shard_map/all_to_all | solution.py:330
  159.8 1.0 collective-permute-done.12
  160.9 2.6 %psum.7 = f32[64]{0:T(128)S(1)} all-reduce(f32[64]{0:T(128)S(1)} %fusion.76), channel_id=1, replica_groups=mesh['group'=2,'seq'=4,'batch'=2,'mp'=2] {'mp'}, use_global_device_ids=true, to_apply=%region_7.8 | all-reduce | flops 64 | bytes 512 | tf_op jit(solution)/shard_map/psum | solution.py:368
  164.1 3.1 %collective-permute-start.14 = (bf16[2,384]{1,0:T(2,128)(2,1)S(1)}, bf16[2,384]{1,0:T(2,128)(2,1)S(1)}, u32[]{:S(2)}, u32[]{:S(2)}) collective-permute-start(bf16[2,384]{1,0:T(2,128)(2,1)S(1)} %get-tuple-element.112), channel_id=1, source_target_pairs={{0,4},{4,8},{8,12},{1,5},{5,9},{9,13},{2,6},{6,10},{10,14},{3,7},{... | collective-permute-start | bytes 4616 | tf_op jit(solution)/shard_map/ppermute | solution.py:23
  167.5 1.3 collective-permute-start.13
  169.3 3.7 %collective-permute-done.13 = bf16[2,384]{1,0:T(2,128)(2,1)S(1)} collective-permute-done((bf16[2,384]{1,0:T(2,128)(2,1)S(1)}, bf16[2,384]{1,0:T(2,128)(2,1)S(1)}, u32[]{:S(2)}, u32[]{:S(2)}) %collective-permute-start.13) | collective-permute-done | bytes 1568 | tf_op jit(solution)/shard_map/ppermute | solution.py:25
  175.2 0.8 fusion.26
  (200 shorter events, 23.6 us)
Async XLA Ops:
  7.2 86.5 %all-gather.3.cloned.1.call-start = ((), (), s32[]{:S(2)}) async-start(), calls=%async_computation.4 | async-start | bytes 2949120 | tf_op jit(solution)/shard_map/all_gather | solution.py:62
  8.3 17.7 %copy-start.19 = (bf16[5,96,384]{2,1,0:T(8,128)(2,1)S(1)}, bf16[5,96,384]{2,1,0:T(8,128)(2,1)}, u32[]{:S(2)}) copy-start(bf16[5,96,384]{2,1,0:T(8,128)(2,1)} %param.9) | copy-start | bytes 1105924
  8.5 23.0 %copy-start.12 = (bf16[1,128,384]{2,1,0:T(8,128)(2,1)S(1)}, bf16[1,128,384]{2,1,0:T(8,128)(2,1)}, u32[]{:S(2)}) copy-start(bf16[1,128,384]{2,1,0:T(8,128)(2,1)} %param.7) | copy-start | bytes 294916
  8.5 22.9 %copy-start.15 = (f32[1,128,384]{2,1,0:T(8,128)S(1)}, f32[1,128,384]{2,1,0:T(8,128)}, u32[]{:S(2)}) copy-start(f32[1,128,384]{2,1,0:T(8,128)} %param.8) | copy-start | bytes 589828
  9.6 9.9 %collective-permute-start = (bf16[192,384]{1,0:T(8,128)(2,1)S(1)}, bf16[192,384]{1,0:T(8,128)(2,1)S(1)}, u32[]{:S(2)}, u32[]{:S(2)}) collective-permute-start(bf16[192,384]{1,0:T(8,128)(2,1)S(1)} %get-tuple-element.76), channel_id=1, source_target_pairs={{0,4},{4,8},{8,12},{12,0},{1,5},{5,9},{9,13},{13,1},{2,6},{6,10},{... | collective-permute-start | bytes 442376 | tf_op jit(solution)/shard_map/ppermute | solution.py:38
  12.7 12.3 %collective-permute-start.1 = (bf16[192,384]{1,0:T(8,128)(2,1)S(1)}, bf16[192,384]{1,0:T(8,128)(2,1)S(1)}, u32[]{:S(2)}, u32[]{:S(2)}) collective-permute-start(bf16[192,384]{1,0:T(8,128)(2,1)S(1)} %get-tuple-element.76), channel_id=1, source_target_pairs={{0,8},{4,12},{8,0},{12,4},{1,9},{5,13},{9,1},{13,5},{2,10},{6,14},... | collective-permute-start | bytes 442376 | tf_op jit(solution)/shard_map/ppermute | solution.py:38
  15.3 9.7 %collective-permute-start.2 = (bf16[192,384]{1,0:T(8,128)(2,1)S(1)}, bf16[192,384]{1,0:T(8,128)(2,1)S(1)}, u32[]{:S(2)}, u32[]{:S(2)}) collective-permute-start(bf16[192,384]{1,0:T(8,128)(2,1)S(1)} %get-tuple-element.76), channel_id=1, source_target_pairs={{0,12},{4,0},{8,4},{12,8},{1,13},{5,1},{9,5},{13,9},{2,14},{6,2},{... | collective-permute-start | bytes 442376 | tf_op jit(solution)/shard_map/ppermute | solution.py:38
  25.1 0.8 copy-start.10
  26.0 45.9 %collective-permute-start.7 = (bf16[240,384]{1,0:T(8,128)(2,1)S(1)}, bf16[240,384]{1,0:T(8,128)(2,1)S(1)}, u32[]{:S(2)}, u32[]{:S(2)}) collective-permute-start(bf16[240,384]{1,0:T(8,128)(2,1)S(1)} %get-tuple-element.92), channel_id=1, source_target_pairs={{0,4},{4,8},{8,12},{12,0},{1,5},{5,9},{9,13},{13,1},{2,6},{6,10},{... | collective-permute-start | bytes 552968 | tf_op jit(solution)/shard_map/ppermute | solution.py:38
  29.6 42.5 %collective-permute-start.8 = (bf16[240,384]{1,0:T(8,128)(2,1)S(1)}, bf16[240,384]{1,0:T(8,128)(2,1)S(1)}, u32[]{:S(2)}, u32[]{:S(2)}) collective-permute-start(bf16[240,384]{1,0:T(8,128)(2,1)S(1)} %get-tuple-element.92), channel_id=1, source_target_pairs={{0,8},{4,12},{8,0},{12,4},{1,9},{5,13},{9,1},{13,5},{2,10},{6,14},... | collective-permute-start | bytes 552968 | tf_op jit(solution)/shard_map/ppermute | solution.py:38
  31.3 16.8 %collective-permute-start.4 = (bf16[60,384]{1,0:T(8,128)(2,1)S(1)}, bf16[60,384]{1,0:T(8,128)(2,1)S(1)}, u32[]{:S(2)}, u32[]{:S(2)}) collective-permute-start(bf16[60,384]{1,0:T(8,128)(2,1)S(1)} %constant_dynamic-slice_fusion.2), channel_id=1, source_target_pairs={{0,4},{4,8},{8,12},{12,0},{1,5},{5,9},{9,13},{13,1},{2,6},{6,10},{... | collective-permute-start | bytes 138248 | tf_op jit(solution)/shard_map/ppermute | solution.py:38
  31.5 11.9 %collective-permute-start.3 = (bf16[2,2,384]{2,1,0:T(2,128)(2,1)S(1)}, bf16[2,2,384]{2,1,0:T(2,128)(2,1)S(1)}, u32[]{:S(2)}, u32[]{:S(2)}) collective-permute-start(bf16[2,2,384]{2,1,0:T(2,128)(2,1)S(1)} %get-tuple-element.107), channel_id=1, source_target_pairs={{0,4},{4,8},{8,12},{1,5},{5,9},{9,13},{2,6},{6,10},{10,14},{3,7},{... | collective-permute-start | bytes 9224 | tf_op jit(solution)/shard_map/ppermute | solution.py:23
  35.1 12.9 %collective-permute-start.10 = (bf16[2,2,384]{2,1,0:T(2,128)(2,1)S(1)}, bf16[2,2,384]{2,1,0:T(2,128)(2,1)S(1)}, u32[]{:S(2)}, u32[]{:S(2)}) collective-permute-start(bf16[2,2,384]{2,1,0:T(2,128)(2,1)S(1)} %get-tuple-element.108), channel_id=1, source_target_pairs={{4,0},{8,4},{12,8},{5,1},{9,5},{13,9},{6,2},{10,6},{14,10},{7,3},{... | collective-permute-start | bytes 9224 | tf_op jit(solution)/shard_map/ppermute | solution.py:25
  43.4 29.1 %collective-permute-start.9 = (bf16[240,384]{1,0:T(8,128)(2,1)S(1)}, bf16[240,384]{1,0:T(8,128)(2,1)S(1)}, u32[]{:S(2)}, u32[]{:S(2)}) collective-permute-start(bf16[240,384]{1,0:T(8,128)(2,1)S(1)} %get-tuple-element.92), channel_id=1, source_target_pairs={{0,12},{4,0},{8,4},{12,8},{1,13},{5,1},{9,5},{13,9},{2,14},{6,2},{... | collective-permute-start | bytes 552968 | tf_op jit(solution)/shard_map/ppermute | solution.py:38
  48.1 5.2 %collective-permute-start.5 = (bf16[60,384]{1,0:T(8,128)(2,1)S(1)}, bf16[60,384]{1,0:T(8,128)(2,1)S(1)}, u32[]{:S(2)}, u32[]{:S(2)}) collective-permute-start(bf16[60,384]{1,0:T(8,128)(2,1)S(1)} %constant_dynamic-slice_fusion.2), channel_id=1, source_target_pairs={{0,8},{4,12},{8,0},{12,4},{1,9},{5,13},{9,1},{13,5},{2,10},{6,14},... | collective-permute-start | bytes 138248 | tf_op jit(solution)/shard_map/ppermute | solution.py:38
  48.1 5.3 %collective-permute-start.6 = (bf16[60,384]{1,0:T(8,128)(2,1)S(1)}, bf16[60,384]{1,0:T(8,128)(2,1)S(1)}, u32[]{:S(2)}, u32[]{:S(2)}) collective-permute-start(bf16[60,384]{1,0:T(8,128)(2,1)S(1)} %constant_dynamic-slice_fusion.2), channel_id=1, source_target_pairs={{0,12},{4,0},{8,4},{12,8},{1,13},{5,1},{9,5},{13,9},{2,14},{6,2},{... | collective-permute-start | bytes 138248 | tf_op jit(solution)/shard_map/ppermute | solution.py:38
  88.4 1.2 copy-start
  88.5 1.2 copy-start.2
  88.5 1.2 copy-start.4
  88.5 1.2 copy-start.6
  88.8 0.9 copy-start.20
  95.3 0.7 copy-start.21
  112.4 2.5 %copy-start.8 = (bf16[4,2,18432]{2,1,0:T(2,128)(2,1)}, bf16[4,2,18432]{2,1,0:T(2,128)(2,1)S(1)}, u32[]{:S(2)}) copy-start(bf16[4,2,18432]{2,1,0:T(2,128)(2,1)S(1)} %all_to_all.43) | copy-start | bytes 884740
  113.1 2.4 %copy-start.13 = (bf16[256,96]{1,0:T(8,128)(2,1)}, bf16[256,96]{1,0:T(8,128)(2,1)S(1)}, u32[]{:S(2)}) copy-start(bf16[256,96]{1,0:T(8,128)(2,1)S(1)} %squeeze.83) | copy-start | bytes 147460
  114.2 6.1 %copy-start.17 = (bf16[256,96]{0,1:T(8,128)(2,1)}, bf16[256,96]{0,1:T(8,128)(2,1)S(1)}, u32[]{:S(2)}) copy-start(bf16[256,96]{0,1:T(8,128)(2,1)S(1)} %convolution_convert_fusion.4) | copy-start | bytes 147460
  116.3 9.8 %all-to-all-start.1 = ((bf16[4,2,6144]{2,1,0:T(2,128)(2,1)}), bf16[4,2,6144]{2,1,0:T(2,128)(2,1)}, u32[]{:S(2)}, u32[]{:S(2)}) async-start(bf16[4,2,6144]{2,1,0:T(2,128)(2,1)} %copy.210), calls=%async_computation.1 | async-start | bytes 196608 | tf_op jit(solution)/shard_map/all_to_all | solution.py:245
  122.2 6.2 %copy-start.9 = (bf16[4,2,18432]{2,1,0:T(2,128)(2,1)S(1)}, bf16[4,2,18432]{2,1,0:T(2,128)(2,1)}, u32[]{:S(2)}) copy-start(bf16[4,2,18432]{2,1,0:T(2,128)(2,1)} %copy-done.8) | copy-start | bytes 884740
  127.8 11.0 %copy-start.14 = (bf16[256,96]{1,0:T(8,128)(2,1)S(1)}, bf16[256,96]{1,0:T(8,128)(2,1)}, u32[]{:S(2)}) copy-start(bf16[256,96]{1,0:T(8,128)(2,1)} %copy-done.13) | copy-start | bytes 147460
  128.4 1.6 collective-permute-start.11
  129.2 16.0 %copy-start.18 = (bf16[256,96]{0,1:T(8,128)(2,1)S(1)}, bf16[256,96]{0,1:T(8,128)(2,1)}, u32[]{:S(2)}) copy-start(bf16[256,96]{0,1:T(8,128)(2,1)} %copy-done.17) | copy-start | bytes 147460
  135.5 8.9 %all-to-all-start.2 = ((bf16[4,2,3072]{2,1,0:T(2,128)(2,1)}), bf16[4,2,3072]{2,1,0:T(2,128)(2,1)S(1)}, u32[]{:S(2)}, u32[]{:S(2)}) async-start(bf16[4,2,3072]{2,1,0:T(2,128)(2,1)} %reshape.310), calls=%async_computation.2 | async-start | bytes 98304 | tf_op jit(solution)/shard_map/all_to_all | solution.py:319
  148.1 9.4 %all-to-all-start.3 = ((bf16[4,2,9216]{2,1,0:T(2,128)(2,1)}), bf16[4,2,9216]{2,1,0:T(2,128)(2,1)S(1)}, u32[]{:S(2)}, u32[]{:S(2)}) async-start(bf16[4,2,9216]{2,1,0:T(2,128)(2,1)} %reshape.312), calls=%async_computation.3 | async-start | bytes 294912 | tf_op jit(solution)/shard_map/all_to_all | solution.py:330
  158.2 1.5 copy-start.11
  159.5 1.3 collective-permute-start.12
  159.6 9.2 %copy-start.7 = (bf16[1,4,96,384]{3,2,0,1:T(8,128)(2,1)S(1)}, bf16[1,4,96,384]{3,2,0,1:T(8,128)(2,1)}, u32[]{:S(2)}) copy-start(bf16[1,4,96,384]{3,2,0,1:T(8,128)(2,1)} %copy-done.6) | copy-start | bytes 884740
  160.9 8.2 %copy-start.5 = (bf16[1,4,96,384]{3,2,0,1:T(8,128)(2,1)S(1)}, bf16[1,4,96,384]{3,2,0,1:T(8,128)(2,1)}, u32[]{:S(2)}) copy-start(bf16[1,4,96,384]{3,2,0,1:T(8,128)(2,1)} %copy-done.4) | copy-start | bytes 884740
  163.6 9.4 %copy-start.3 = (bf16[1,4,96,384]{3,2,0,1:T(8,128)(2,1)S(1)}, bf16[1,4,96,384]{3,2,0,1:T(8,128)(2,1)}, u32[]{:S(2)}) copy-start(bf16[1,4,96,384]{3,2,0,1:T(8,128)(2,1)} %copy-done.2) | copy-start | bytes 884740
  163.7 9.5 %copy-start.1 = (bf16[1,4,96,384]{3,2,0,1:T(8,128)(2,1)S(1)}, bf16[1,4,96,384]{3,2,0,1:T(8,128)(2,1)}, u32[]{:S(2)}) copy-start(bf16[1,4,96,384]{3,2,0,1:T(8,128)(2,1)} %copy-done) | copy-start | bytes 884740
  164.1 5.0 %collective-permute-start.14 = (bf16[2,384]{1,0:T(2,128)(2,1)S(1)}, bf16[2,384]{1,0:T(2,128)(2,1)S(1)}, u32[]{:S(2)}, u32[]{:S(2)}) collective-permute-start(bf16[2,384]{1,0:T(2,128)(2,1)S(1)} %get-tuple-element.112), channel_id=1, source_target_pairs={{0,4},{4,8},{8,12},{1,5},{5,9},{9,13},{2,6},{6,10},{10,14},{3,7},{... | collective-permute-start | bytes 4616 | tf_op jit(solution)/shard_map/ppermute | solution.py:23
  167.5 5.5 %collective-permute-start.13 = (bf16[2,384]{1,0:T(2,128)(2,1)S(1)}, bf16[2,384]{1,0:T(2,128)(2,1)S(1)}, u32[]{:S(2)}, u32[]{:S(2)}) collective-permute-start(bf16[2,384]{1,0:T(2,128)(2,1)S(1)} %get-tuple-element.111), channel_id=1, source_target_pairs={{4,0},{8,4},{12,8},{5,1},{9,5},{13,9},{6,2},{10,6},{14,10},{7,3},{... | collective-permute-start | bytes 4616 | tf_op jit(solution)/shard_map/ppermute | solution.py:25
  169.1 6.1 %copy-start.16 = (f32[1,128,384]{2,1,0:T(8,128)S(1)}, f32[1,128,384]{2,1,0:T(8,128)}, u32[]{:S(2)}) copy-start(f32[1,128,384]{2,1,0:T(8,128)} %param.8) | copy-start | bytes 589828
  173.7 1.4 collective-permute-start.15
Sparse Core Ops, SparseCore 0:
  26.0 41.7 all-gather.2

commit v7 on v6

--- a/solution.py
+++ b/solution.py
@@ -40,16 +40,16 @@
     return along
 
 
-def gather_seq(parts, width, direct=0):
+def gather_seq(parts, width):
     spread = ("group", "batch")
     count = lax.axis_size("group") * lax.axis_size("batch")
     ring = lax.axis_size("seq")
     flats = [cells.reshape(-1, width) for cells, _ in parts]
     flat = jnp.concatenate(flats, axis=0) if len(flats) > 1 else flats[0]
     rows = flat.shape[0]
-    if ring > 8:
-        direct = 0
-    split = rows - direct
+    paired = lax.axis_size("group") == 2 and lax.axis_size("batch") == 2 and ring <= 8
+    halves = rows // 2 // (4 * count) * (4 * count) if paired else 0
+    split = rows - halves
     size = -(-split // count)
     head = flat[:split]
     if size * count != split:
@@ -61,8 +61,25 @@
         along = lax.all_gather(piece, "seq", axis=0, tiled=False)
     whole = lax.all_gather(along, spread, axis=0, tiled=False)
     whole = whole.transpose(1, 0, 2, 3).reshape(ring, count * size, width)[:, :split]
-    if direct:
-        whole = jnp.concatenate([whole, ring_gather(flat[split:])], axis=1)
+    if halves:
+        tail = flat[split:]
+        half = halves // 2
+        parity = (lax.axis_index("group") + lax.axis_index("batch")) % 2
+        mine = ring_gather(lax.dynamic_slice_in_dim(tail, parity * half, half, 0))
+        swap = [(0, 1), (1, 0)]
+        other = jnp.concatenate(
+            [
+                lax.ppermute(mine[:, : half // 2], "batch", swap),
+                lax.ppermute(mine[:, half // 2 :], "group", swap),
+            ],
+            axis=1,
+        )
+        both = jnp.where(
+            parity == 0,
+            jnp.concatenate([mine, other], axis=1),
+            jnp.concatenate([other, mine], axis=1),
+        )
+        whole = jnp.concatenate([whole, both], axis=1)
     results = []
     offset = 0
     for (cells, dim), part in zip(parts, flats):
@@ -272,8 +289,7 @@
 
 def shards(features, noise, conv_weight, conv_bias, norm_gain, qkv_weight, out_weight):
     width = conv_weight.shape[-1]
-    conv_rows = conv_weight.size // width
-    (conv_weight,) = gather_seq([(conv_weight, 1)], width, conv_rows // 2 // 16 * 16)
+    (conv_weight,) = gather_seq([(conv_weight, 1)], width)
     qkv_weight, out_weight = gather_seq([(qkv_weight, 1), (out_weight, 1)], width)
     clean = features[0]
     moved = (clean.astype(jnp.float32) + noise[0]).astype(jnp.bfloat16)

time: 184 us -> 201 us (1.092)
  local copies, waits for them, and re-layouts: 45.7 us -> 55.1 us
  waiting for transfers between devices: 34.6 us -> 25.5 us
  other arithmetic: 7.42 us -> 15.2 us
  starting transfers between devices: 37.7 us -> 45 us
  matrix products: 7.04 us -> 11.2 us
  blocking collectives: 35 us -> 32.3 us
    ppermute x9 -> x12, waiting for transfers between devices: 13 us -> 2.01 us  [ring_gather(): lax.ppermute(piece, 'seq', [(i, (i + shift) % ring) for i in range(ring)])]
    dynamic_update_slice x9 -> x12, local copies, waits for them, and re-layouts: 18.8 us -> 13.1 us  [ring_gather(): lax.dynamic_update_slice_in_dim(along, arrived[None], (place + ring - shi...]
    ppermute x0 -> x4, starting transfers between devices: none -> 4.12 us  [the longest x2 2.39 us: gather_seq(): lax.ppermute(mine[:, half // 2:], 'group', swap)]
    ppermute x9 -> x12, starting transfers between devices: 17.6 us -> 21.7 us  [ring_gather(): lax.ppermute(piece, 'seq', [(i, (i + shift) % ring) for i in range(ring)])]
    another operation x2, local copies, waits for them, and re-layouts: 0.14 us -> 3.24 us  [forward(): query_send = projected[0].reshape(pass_count, query_groups, sub_rows, hea...]
    ppermute x0 -> x4, waiting for transfers between devices: none -> 2.74 us  [the longest x2 1.46 us: gather_seq(): lax.ppermute(mine[:, :half // 2], 'batch', swap)]
    all_gather x1, blocking collectives: 13.9 us -> 11.4 us  [gather_seq(): whole = lax.all_gather(along, spread, axis=0, tiled=False)]
    dot_general x2, matrix products: 0.56 us -> 3 us  [collect(): jnp.dot(soft_weights, value_block, preferred_element_type=jnp.float32)]
  transfers between devices with their start and end apart: 20 -> 27, of which waited for: 10 -> 14; matrix products, arithmetic and copies ran while one was open for 19% -> 16% of each run, Pallas kernels for 0% -> 0%
where the time goes in v7:
time: 201 us; the launch traced here: 200 us
  local copies, waits for them, and re-layouts  55.1 us (27%)
  starting transfers between devices  45 us (22%)
  blocking collectives  32.3 us (16%)
  waiting for transfers between devices  25.5 us (13%)
  between operations  15.5 us (8%)
  other arithmetic  15.2 us (8%)
  matrix products  11.2 us (6%)
    ppermute x12, starting transfers between devices, ring_gather(): lax.ppermute(piece, 'seq', [(i, (i + shift) % ring) for i in range(ring)])  21.7 us
    all_to_all x1, blocking collectives, forward(): lax.all_to_all(jnp.concatenate([query_send, keyval_send], axis=2), 'seq',...  14.2 us
    dynamic_update_slice x12, local copies, waits for them, and re-layouts, ring_gather(): lax.dynamic_update_slice_in_dim(along, arrived[None], (place + ring - shi...  13.1 us
    all_gather x1, blocking collectives, gather_seq(): whole = lax.all_gather(along, spread, axis=0, tiled=False)  11.4 us
    all_to_all x1, waiting for transfers between devices, shards(): lax.all_to_all(jnp.concatenate([query_grad.reshape(devices, query_len).as...  6.03 us
    ppermute x2, starting transfers between devices, with_halo(): lax.ppermute(tail, axis, [(i, (i + 1) % count) for i in range(ends)])  5.92 us
    all_to_all x1, waiting for transfers between devices, shards(): lax.all_to_all(grad_send, 'seq', split_axis=0, concat_axis=1, tiled=True)  5.45 us
    unnamed x54, local copies, waits for them, and re-layouts  4.82 us
  transfers between devices with their start and end apart: 27, of which 14 were waited for; matrix products, arithmetic and copies ran while one was open for 16% of the time, Pallas kernels for 0%

profile of v7, /device:TPU:0, one launch (start us, length us, event | category | flops | bytes accessed | tf_op | source)
XLA Modules:
  0.0 199.8 jit_solution(5549281593756225807)
XLA Ops:
  8.6 1.7 bitcast_dynamic-update-slice_fusion.3
  10.3 3.1 %collective-permute-start.3 = (bf16[192,384]{1,0:T(8,128)(2,1)}, bf16[192,384]{1,0:T(8,128)(2,1)S(1)}, u32[]{:S(2)}, u32[]{:S(2)}) collective-permute-start(bf16[192,384]{1,0:T(8,128)(2,1)} %get-tuple-element.78), channel_id=1, source_target_pairs={{0,4},{4,8},{8,12},{12,0},{1,5},{5,9},{9,13},{13,1},{2,6},{6,10},{... | collective-permute-start | bytes 442376 | tf_op jit(solution)/shard_map/ppermute | solution.py:38
  13.4 2.6 %collective-permute-start.4 = (bf16[192,384]{1,0:T(8,128)(2,1)}, bf16[192,384]{1,0:T(8,128)(2,1)S(1)}, u32[]{:S(2)}, u32[]{:S(2)}) collective-permute-start(bf16[192,384]{1,0:T(8,128)(2,1)} %get-tuple-element.78), channel_id=1, source_target_pairs={{0,8},{4,12},{8,0},{12,4},{1,9},{5,13},{9,1},{13,5},{2,10},{6,14},... | collective-permute-start | bytes 442376 | tf_op jit(solution)/shard_map/ppermute | solution.py:38
  16.2 2.8 %collective-permute-start.8 = (bf16[2,2,384]{2,1,0:T(2,128)(2,1)S(1)}, bf16[2,2,384]{2,1,0:T(2,128)(2,1)S(1)}, u32[]{:S(2)}, u32[]{:S(2)}) collective-permute-start(bf16[2,2,384]{2,1,0:T(2,128)(2,1)S(1)} %get-tuple-element.112), channel_id=1, source_target_pairs={{0,4},{4,8},{8,12},{1,5},{5,9},{9,13},{2,6},{6,10},{10,14},{3,7},{... | collective-permute-start | bytes 9224 | tf_op jit(solution)/shard_map/ppermute | solution.py:23
  19.0 1.3 collective-permute-start.17
  20.9 2.6 %dynamic_update_slice.71 = bf16[4,120,384]{2,0,1:T(4,128)(2,1)S(1)} dynamic-update-slice(bf16[4,120,384]{2,0,1:T(4,128)(2,1)S(1)} %broadcast_in_dim.44, bf16[1,120,384]{2,0,1:T(2,128)(2,1)S(1)} %copy.198, s32[]{:T(128)S(6)} %select_n.101, s32[]{:T(128)} %constant.166.clone.1, s32[]{:T(128)} %constant.166.clone.1) | dynamic-update-slice | bytes 184324 | tf_op jit(solution)/shard_map/dynamic_update_slice | solution.py:36
  23.5 1.5 dynamic_update_slice.67
  25.0 4.2 %collective-permute-start.10 = (bf16[60,384]{1,0:T(8,128)(2,1)S(1)}, bf16[60,384]{1,0:T(8,128)(2,1)S(1)}, u32[]{:S(2)}, u32[]{:S(2)}) collective-permute-start(bf16[60,384]{1,0:T(8,128)(2,1)S(1)} %constant_dynamic-slice_fusion.3), channel_id=1, source_target_pairs={{0,8},{4,12},{8,0},{12,4},{1,9},{5,13},{9,1},{13,5},{2,10},{6,14},... | collective-permute-start | bytes 138248 | tf_op jit(solution)/shard_map/ppermute | solution.py:38
  29.2 1.5 collective-permute-start.11
  31.4 3.1 %collective-permute-start.1 = (bf16[96,384]{1,0:T(8,128)(2,1)S(1)}, bf16[96,384]{1,0:T(8,128)(2,1)}, u32[]{:S(2)}, u32[]{:S(2)}) collective-permute-start(bf16[96,384]{1,0:T(8,128)(2,1)S(1)} %get-tuple-element.76), channel_id=1, source_target_pairs={{0,8},{4,12},{8,0},{12,4},{1,9},{5,13},{9,1},{13,5},{2,10},{6,14},... | collective-permute-start | bytes 221192 | tf_op jit(solution)/shard_map/ppermute | solution.py:38
  34.9 2.2 %collective-permute-start.2 = (bf16[96,384]{1,0:T(8,128)(2,1)S(1)}, bf16[96,384]{1,0:T(8,128)(2,1)S(1)}, u32[]{:S(2)}, u32[]{:S(2)}) collective-permute-start(bf16[96,384]{1,0:T(8,128)(2,1)S(1)} %get-tuple-element.76), channel_id=1, source_target_pairs={{0,12},{4,0},{8,4},{12,8},{1,13},{5,1},{9,5},{13,9},{2,14},{6,2},{... | collective-permute-start | bytes 221192 | tf_op jit(solution)/shard_map/ppermute | solution.py:38
  37.1 1.5 dynamic_update_slice.68
  38.6 1.5 dynamic_update_slice.69
  40.1 1.5 dynamic_update_slice.70
  41.6 11.4 %all_gather.45 = bf16[4,4,60,384]{3,1,2,0:T(4,128)(2,1)S(1)} all-gather(bf16[1,4,60,384]{3,1,2,0:T(4,128)(2,1)S(1)} %dynamic_update_slice.70), channel_id=1, replica_groups=mesh['group'=2,'seq'=4,'batch'=2,'mp'=2] {'group','batch'}, dimensions={0}, use_global_device_ids=true | all-gather | bytes 921600 | tf_op jit(solution)/shard_map/all_gather | solution.py:62
  53.0 1.2 collective-permute-start.13
  55.1 3.0 %collective-permute-start.14 = (bf16[120,384]{1,0:T(8,128)(2,1)S(1)}, bf16[120,384]{1,0:T(8,128)(2,1)}, u32[]{:S(2)}, u32[]{:S(2)}) collective-permute-start(bf16[120,384]{1,0:T(8,128)(2,1)S(1)} %constant_dynamic-slice_fusion.2), channel_id=1, source_target_pairs={{0,12},{4,0},{8,4},{12,8},{1,13},{5,1},{9,5},{13,9},{2,14},{6,2},{... | collective-permute-start | bytes 276488 | tf_op jit(solution)/shard_map/ppermute | solution.py:38
  62.2 2.6 %dynamic_update_slice.72 = bf16[4,120,384]{2,0,1:T(4,128)(2,1)S(1)} dynamic-update-slice(bf16[4,120,384]{2,0,1:T(4,128)(2,1)S(1)} %dynamic_update_slice.71, bf16[1,120,384]{2,0,1:T(2,128)(2,1)S(1)} %copy.199, s32[]{:T(128)S(6)} %select_n.103, s32[]{:T(128)} %constant.166.clone.1, s32[]{:T(128)} %constant.166.clone.1) | dynamic-update-slice | bytes 184324 | tf_op jit(solution)/shard_map/dynamic_update_slice | solution.py:39
  64.8 2.6 %dynamic_update_slice.73 = bf16[4,120,384]{2,0,1:T(4,128)(2,1)S(1)} dynamic-update-slice(bf16[4,120,384]{2,0,1:T(4,128)(2,1)S(1)} %dynamic_update_slice.72, bf16[1,120,384]{2,0,1:T(2,128)(2,1)S(1)} %copy.200, s32[]{:T(128)S(6)} %select_n.105, s32[]{:T(128)} %constant.166.clone.1, s32[]{:T(128)} %constant.166.clone.1) | dynamic-update-slice | bytes 184324 | tf_op jit(solution)/shard_map/dynamic_update_slice | solution.py:39
  67.3 2.6 %dynamic_update_slice.74 = bf16[4,120,384]{2,0,1:T(4,128)(2,1)S(1)} dynamic-update-slice(bf16[4,120,384]{2,0,1:T(4,128)(2,1)S(1)} %dynamic_update_slice.73, bf16[1,120,384]{2,0,1:T(2,128)(2,1)S(1)} %copy.201, s32[]{:T(128)S(6)} %select_n.107, s32[]{:T(128)} %constant.166.clone.1, s32[]{:T(128)} %constant.166.clone.1) | dynamic-update-slice | bytes 184324 | tf_op jit(solution)/shard_map/dynamic_update_slice | solution.py:39
  73.0 1.2 collective-permute-start.7
  75.1 1.3 collective-permute-done.16
  76.3 1.5 collective-permute-done.15
  82.9 2.1 %all-gather = bf16[2,64,1,768]{3,1,0,2:T(8,128)(2,1)S(1)} all-gather(bf16[2,64,1,384]{3,1,0,2:T(8,128)(2,1)S(1)} %fusion.54), channel_id=2, replica_groups=mesh['group'=2,'seq'=4,'batch'=2,'mp'=2] {'mp'}, dimensions={3}, use_global_device_ids=true | all-gather | bytes 294912 | tf_op jit(solution)/shard_map/all_gather | solution.py:203
  85.9 1.6 maximum_select_fusion
  87.6 1.4 pad_maximum_fusion
  93.6 1.8 maximum_bitcast_fusion
  95.4 1.3 reshape_reshape.4
  96.6 1.7 reshape_squeeze.9
  98.3 1.6 copy.257
  99.9 1.8 reshape.285
  102.8 14.2 %all_to_all.43 = bf16[4,2,18432]{2,1,0:T(2,128)(2,1)S(1)} all-to-all(bf16[4,2,18432]{2,1,0:T(2,128)(2,1)S(1)} %pad_maximum_fusion.2), channel_id=1, replica_groups=mesh['group'=2,'seq'=4,'batch'=2,'mp'=2] {'seq'}, dimensions={0} | all-to-all | bytes 589824 | tf_op jit(solution)/shard_map/all_to_all | solution.py:240
  119.1 1.8 copy.208
  120.8 1.9 reshape.287
  123.9 1.2 convolution_convert_fusion.4
  128.1 1.8 convolution_convert_fusion.5
  133.3 3.9 %all-to-all-start.1 = ((bf16[4,2,6144]{2,1,0:T(2,128)(2,1)}), bf16[4,2,6144]{2,1,0:T(2,128)(2,1)}, u32[]{:S(2)}, u32[]{:S(2)}) async-start(bf16[4,2,6144]{2,1,0:T(2,128)(2,1)} %copy.211), calls=%async_computation.1 | async-start | bytes 196608 | tf_op jit(solution)/shard_map/all_to_all | solution.py:262
  138.2 1.6 reshape.290
  140.1 3.0 %all-to-all-done.1 = bf16[4,2,6144]{2,1,0:T(2,128)(2,1)} async-done(((bf16[4,2,6144]{2,1,0:T(2,128)(2,1)}), bf16[4,2,6144]{2,1,0:T(2,128)(2,1)}, u32[]{:S(2)}, u32[]{:S(2)}) %all-to-all-start.1) | async-done | bytes 98336 | tf_op jit(solution)/shard_map/all_to_all | solution.py:262
  148.0 1.9 all_gather.47
  152.4 3.3 %all-to-all-start.2 = ((bf16[4,2,3072]{2,1,0:T(2,128)(2,1)}), bf16[4,2,3072]{2,1,0:T(2,128)(2,1)S(1)}, u32[]{:S(2)}, u32[]{:S(2)}) async-start(bf16[4,2,3072]{2,1,0:T(2,128)(2,1)} %reshape.311), calls=%async_computation.2 | async-start | bytes 98304 | tf_op jit(solution)/shard_map/all_to_all | solution.py:335
  155.9 5.5 %all-to-all-done.2 = bf16[4,2,3072]{2,1,0:T(2,128)(2,1)S(1)} async-done(((bf16[4,2,3072]{2,1,0:T(2,128)(2,1)}), bf16[4,2,3072]{2,1,0:T(2,128)(2,1)S(1)}, u32[]{:S(2)}, u32[]{:S(2)}) %all-to-all-start.2) | async-done | bytes 49184 | tf_op jit(solution)/shard_map/all_to_all | solution.py:335
  165.1 3.3 %all-to-all-start.3 = ((bf16[4,2,9216]{2,1,0:T(2,128)(2,1)}), bf16[4,2,9216]{2,1,0:T(2,128)(2,1)S(1)}, u32[]{:S(2)}, u32[]{:S(2)}) async-start(bf16[4,2,9216]{2,1,0:T(2,128)(2,1)} %reshape.313), calls=%async_computation.3 | async-start | bytes 294912 | tf_op jit(solution)/shard_map/all_to_all | solution.py:346
  168.4 6.0 %all-to-all-done.3 = bf16[4,2,9216]{2,1,0:T(2,128)(2,1)S(1)} async-done(((bf16[4,2,9216]{2,1,0:T(2,128)(2,1)}), bf16[4,2,9216]{2,1,0:T(2,128)(2,1)S(1)}, u32[]{:S(2)}, u32[]{:S(2)}) %all-to-all-start.3) | async-done | bytes 147488 | tf_op jit(solution)/shard_map/all_to_all | solution.py:346
  177.9 2.6 %psum.7 = f32[64]{0:T(128)S(1)} all-reduce(f32[64]{0:T(128)S(1)} %fusion.76), channel_id=1, replica_groups=mesh['group'=2,'seq'=4,'batch'=2,'mp'=2] {'mp'}, use_global_device_ids=true, to_apply=%region_7.8 | all-reduce | flops 64 | bytes 512 | tf_op jit(solution)/shard_map/psum | solution.py:384
  181.0 3.1 %collective-permute-start.21 = (bf16[2,384]{1,0:T(2,128)(2,1)S(1)}, bf16[2,384]{1,0:T(2,128)(2,1)S(1)}, u32[]{:S(2)}, u32[]{:S(2)}) collective-permute-start(bf16[2,384]{1,0:T(2,128)(2,1)S(1)} %get-tuple-element.126), channel_id=1, source_target_pairs={{0,4},{4,8},{8,12},{1,5},{5,9},{9,13},{2,6},{6,10},{10,14},{3,7},{... | collective-permute-start | bytes 4616 | tf_op jit(solution)/shard_map/ppermute | solution.py:23
  184.5 1.3 collective-permute-start.20
  186.3 3.7 %collective-permute-done.20 = bf16[2,384]{1,0:T(2,128)(2,1)S(1)} collective-permute-done((bf16[2,384]{1,0:T(2,128)(2,1)S(1)}, bf16[2,384]{1,0:T(2,128)(2,1)S(1)}, u32[]{:S(2)}, u32[]{:S(2)}) %collective-permute-start.20) | collective-permute-done | bytes 1568 | tf_op jit(solution)/shard_map/ppermute | solution.py:25
  (230 shorter events, 53.0 us)
Async XLA Ops:
  7.2 8.8 %copy-start.20 = (bf16[5,96,384]{2,1,0:T(8,128)(2,1)S(1)}, bf16[5,96,384]{2,1,0:T(8,128)(2,1)}, u32[]{:S(2)}) copy-start(bf16[5,96,384]{2,1,0:T(8,128)(2,1)} %param.9) | copy-start | bytes 1105924
  7.2 8.9 %copy-start.16 = (f32[1,128,384]{2,1,0:T(8,128)S(1)}, f32[1,128,384]{2,1,0:T(8,128)}, u32[]{:S(2)}) copy-start(f32[1,128,384]{2,1,0:T(8,128)} %param.8) | copy-start | bytes 589828
  7.2 8.9 %copy-start.11 = (bf16[1,128,384]{2,1,0:T(8,128)(2,1)S(1)}, bf16[1,128,384]{2,1,0:T(8,128)(2,1)}, u32[]{:S(2)}) copy-start(bf16[1,128,384]{2,1,0:T(8,128)(2,1)} %param.7) | copy-start | bytes 294916
  7.2 80.4 %all-gather.3.cloned.1.call-start = ((), (), s32[]{:S(2)}) async-start(), calls=%async_computation.4 | async-start | bytes 1474560 | tf_op jit(solution)/shard_map/all_gather | solution.py:62
  7.3 13.0 %copy-start.12 = (bf16[3,192,384]{2,1,0:T(8,128)(2,1)S(1)}, bf16[3,192,384]{2,1,0:T(8,128)(2,1)}, u32[]{:S(2)}) copy-start(bf16[3,192,384]{2,1,0:T(8,128)(2,1)} %param.12) | copy-start | bytes 1327108
  10.3 61.8 %collective-permute-start.3 = (bf16[192,384]{1,0:T(8,128)(2,1)}, bf16[192,384]{1,0:T(8,128)(2,1)S(1)}, u32[]{:S(2)}, u32[]{:S(2)}) collective-permute-start(bf16[192,384]{1,0:T(8,128)(2,1)} %get-tuple-element.78), channel_id=1, source_target_pairs={{0,4},{4,8},{8,12},{12,0},{1,5},{5,9},{9,13},{13,1},{2,6},{6,10},{... | collective-permute-start | bytes 442376 | tf_op jit(solution)/shard_map/ppermute | solution.py:38
  13.4 58.7 %collective-permute-start.4 = (bf16[192,384]{1,0:T(8,128)(2,1)}, bf16[192,384]{1,0:T(8,128)(2,1)S(1)}, u32[]{:S(2)}, u32[]{:S(2)}) collective-permute-start(bf16[192,384]{1,0:T(8,128)(2,1)} %get-tuple-element.78), channel_id=1, source_target_pairs={{0,8},{4,12},{8,0},{12,4},{1,9},{5,13},{9,1},{13,5},{2,10},{6,14},... | collective-permute-start | bytes 442376 | tf_op jit(solution)/shard_map/ppermute | solution.py:38
  16.1 14.7 %collective-permute-start.9 = (bf16[60,384]{1,0:T(8,128)(2,1)S(1)}, bf16[60,384]{1,0:T(8,128)(2,1)S(1)}, u32[]{:S(2)}, u32[]{:S(2)}) collective-permute-start(bf16[60,384]{1,0:T(8,128)(2,1)S(1)} %constant_dynamic-slice_fusion.3), channel_id=1, source_target_pairs={{0,4},{4,8},{8,12},{12,0},{1,5},{5,9},{9,13},{13,1},{2,6},{6,10},{... | collective-permute-start | bytes 138248 | tf_op jit(solution)/shard_map/ppermute | solution.py:38
  16.2 8.8 %collective-permute-start.8 = (bf16[2,2,384]{2,1,0:T(2,128)(2,1)S(1)}, bf16[2,2,384]{2,1,0:T(2,128)(2,1)S(1)}, u32[]{:S(2)}, u32[]{:S(2)}) collective-permute-start(bf16[2,2,384]{2,1,0:T(2,128)(2,1)S(1)} %get-tuple-element.112), channel_id=1, source_target_pairs={{0,4},{4,8},{8,12},{1,5},{5,9},{9,13},{2,6},{6,10},{10,14},{3,7},{... | collective-permute-start | bytes 9224 | tf_op jit(solution)/shard_map/ppermute | solution.py:23
  19.0 10.2 %collective-permute-start.17 = (bf16[2,2,384]{2,1,0:T(2,128)(2,1)S(1)}, bf16[2,2,384]{2,1,0:T(2,128)(2,1)S(1)}, u32[]{:S(2)}, u32[]{:S(2)}) collective-permute-start(bf16[2,2,384]{2,1,0:T(2,128)(2,1)S(1)} %get-tuple-element.113), channel_id=1, source_target_pairs={{4,0},{8,4},{12,8},{5,1},{9,5},{13,9},{6,2},{10,6},{14,10},{7,3},{... | collective-permute-start | bytes 9224 | tf_op jit(solution)/shard_map/ppermute | solution.py:25
  25.0 6.4 %collective-permute-start.10 = (bf16[60,384]{1,0:T(8,128)(2,1)S(1)}, bf16[60,384]{1,0:T(8,128)(2,1)S(1)}, u32[]{:S(2)}, u32[]{:S(2)}) collective-permute-start(bf16[60,384]{1,0:T(8,128)(2,1)S(1)} %constant_dynamic-slice_fusion.3), channel_id=1, source_target_pairs={{0,8},{4,12},{8,0},{12,4},{1,9},{5,13},{9,1},{13,5},{2,10},{6,14},... | collective-permute-start | bytes 138248 | tf_op jit(solution)/shard_map/ppermute | solution.py:38
  29.2 5.7 %collective-permute-start.11 = (bf16[60,384]{1,0:T(8,128)(2,1)S(1)}, bf16[60,384]{1,0:T(8,128)(2,1)S(1)}, u32[]{:S(2)}, u32[]{:S(2)}) collective-permute-start(bf16[60,384]{1,0:T(8,128)(2,1)S(1)} %constant_dynamic-slice_fusion.3), channel_id=1, source_target_pairs={{0,12},{4,0},{8,4},{12,8},{1,13},{5,1},{9,5},{13,9},{2,14},{6,2},{... | collective-permute-start | bytes 138248 | tf_op jit(solution)/shard_map/ppermute | solution.py:38
  30.8 22.2 %collective-permute-start = (bf16[96,384]{1,0:T(8,128)(2,1)S(1)}, bf16[96,384]{1,0:T(8,128)(2,1)S(1)}, u32[]{:S(2)}, u32[]{:S(2)}) collective-permute-start(bf16[96,384]{1,0:T(8,128)(2,1)S(1)} %get-tuple-element.76), channel_id=1, source_target_pairs={{0,4},{4,8},{8,12},{12,0},{1,5},{5,9},{9,13},{13,1},{2,6},{6,10},{... | collective-permute-start | bytes 221192 | tf_op jit(solution)/shard_map/ppermute | solution.py:38
  31.4 21.6 %collective-permute-start.1 = (bf16[96,384]{1,0:T(8,128)(2,1)S(1)}, bf16[96,384]{1,0:T(8,128)(2,1)}, u32[]{:S(2)}, u32[]{:S(2)}) collective-permute-start(bf16[96,384]{1,0:T(8,128)(2,1)S(1)} %get-tuple-element.76), channel_id=1, source_target_pairs={{0,8},{4,12},{8,0},{12,4},{1,9},{5,13},{9,1},{13,5},{2,10},{6,14},... | collective-permute-start | bytes 221192 | tf_op jit(solution)/shard_map/ppermute | solution.py:38
  34.9 20.2 %collective-permute-start.2 = (bf16[96,384]{1,0:T(8,128)(2,1)S(1)}, bf16[96,384]{1,0:T(8,128)(2,1)S(1)}, u32[]{:S(2)}, u32[]{:S(2)}) collective-permute-start(bf16[96,384]{1,0:T(8,128)(2,1)S(1)} %get-tuple-element.76), channel_id=1, source_target_pairs={{0,12},{4,0},{8,4},{12,8},{1,13},{5,1},{9,5},{13,9},{2,14},{6,2},{... | collective-permute-start | bytes 221192 | tf_op jit(solution)/shard_map/ppermute | solution.py:38
  53.0 6.5 %collective-permute-start.12 = (bf16[120,384]{1,0:T(8,128)(2,1)S(1)}, bf16[120,384]{1,0:T(8,128)(2,1)S(1)}, u32[]{:S(2)}, u32[]{:S(2)}) collective-permute-start(bf16[120,384]{1,0:T(8,128)(2,1)S(1)} %constant_dynamic-slice_fusion.2), channel_id=1, source_target_pairs={{0,4},{4,8},{8,12},{12,0},{1,5},{5,9},{9,13},{13,1},{2,6},{6,10},{... | collective-permute-start | bytes 276488 | tf_op jit(solution)/shard_map/ppermute | solution.py:38
  53.0 7.6 %collective-permute-start.13 = (bf16[120,384]{1,0:T(8,128)(2,1)S(1)}, bf16[120,384]{1,0:T(8,128)(2,1)S(1)}, u32[]{:S(2)}, u32[]{:S(2)}) collective-permute-start(bf16[120,384]{1,0:T(8,128)(2,1)S(1)} %constant_dynamic-slice_fusion.2), channel_id=1, source_target_pairs={{0,8},{4,12},{8,0},{12,4},{1,9},{5,13},{9,1},{13,5},{2,10},{6,14},... | collective-permute-start | bytes 276488 | tf_op jit(solution)/shard_map/ppermute | solution.py:38
  55.1 6.0 %collective-permute-start.14 = (bf16[120,384]{1,0:T(8,128)(2,1)S(1)}, bf16[120,384]{1,0:T(8,128)(2,1)}, u32[]{:S(2)}, u32[]{:S(2)}) collective-permute-start(bf16[120,384]{1,0:T(8,128)(2,1)S(1)} %constant_dynamic-slice_fusion.2), channel_id=1, source_target_pairs={{0,12},{4,0},{8,4},{12,8},{1,13},{5,1},{9,5},{13,9},{2,14},{6,2},{... | collective-permute-start | bytes 276488 | tf_op jit(solution)/shard_map/ppermute | solution.py:38
  59.4 12.7 %collective-permute-start.5 = (bf16[192,384]{1,0:T(8,128)(2,1)}, bf16[192,384]{1,0:T(8,128)(2,1)S(1)}, u32[]{:S(2)}, u32[]{:S(2)}) collective-permute-start(bf16[192,384]{1,0:T(8,128)(2,1)} %get-tuple-element.78), channel_id=1, source_target_pairs={{0,12},{4,0},{8,4},{12,8},{1,13},{5,1},{9,5},{13,9},{2,14},{6,2},{... | collective-permute-start | bytes 442376 | tf_op jit(solution)/shard_map/ppermute | solution.py:38
  70.0 6.3 %collective-permute-start.16 = (bf16[4,60,384]{2,0,1:T(4,128)(2,1)S(1)}, bf16[4,60,384]{2,0,1:T(4,128)(2,1)S(1)}, u32[]{:S(2)}, u32[]{:S(2)}) collective-permute-start(bf16[4,60,384]{2,0,1:T(4,128)(2,1)S(1)} %get-tuple-element.106), channel_id=1, source_target_pairs={{0,16},{16,0},{1,17},{17,1},{2,18},{18,2},{3,19},{19,3},{4,20},{20... | collective-permute-start | bytes 552968 | tf_op jit(solution)/shard_map/ppermute | solution.py:73
  71.2 6.6 %collective-permute-start.15 = (bf16[4,60,384]{2,0,1:T(4,128)(2,1)S(1)}, bf16[4,60,384]{2,0,1:T(4,128)(2,1)S(1)}, u32[]{:S(2)}, u32[]{:S(2)}) collective-permute-start(bf16[4,60,384]{2,0,1:T(4,128)(2,1)S(1)} %get-tuple-element.96), channel_id=1, source_target_pairs={{0,2},{2,0},{1,3},{3,1},{4,6},{6,4},{5,7},{7,5},{8,10},{10,8},{9,1... | collective-permute-start | bytes 552968 | tf_op jit(solution)/shard_map/ppermute | solution.py:72
  73.0 12.2 %collective-permute-start.7 = (bf16[4,96,384]{2,1,0:T(8,128)(2,1)}, bf16[4,96,384]{2,1,0:T(8,128)(2,1)S(1)}, u32[]{:S(2)}, u32[]{:S(2)}) collective-permute-start(bf16[4,96,384]{2,1,0:T(8,128)(2,1)} %get-tuple-element.91), channel_id=1, source_target_pairs={{0,16},{16,0},{1,17},{17,1},{2,18},{18,2},{3,19},{19,3},{4,20},{20... | collective-permute-start | bytes 884744 | tf_op jit(solution)/shard_map/ppermute | solution.py:73
  74.2 11.7 %collective-permute-start.6 = (bf16[4,96,384]{2,1,0:T(8,128)(2,1)S(1)}, bf16[4,96,384]{2,1,0:T(8,128)(2,1)}, u32[]{:S(2)}, u32[]{:S(2)}) collective-permute-start(bf16[4,96,384]{2,1,0:T(8,128)(2,1)S(1)} %get-tuple-element.90), channel_id=1, source_target_pairs={{0,2},{2,0},{1,3},{3,1},{4,6},{6,4},{5,7},{7,5},{8,10},{10,8},{9,1... | collective-permute-start | bytes 884744 | tf_op jit(solution)/shard_map/ppermute | solution.py:72
  80.0 1.2 copy-start
  80.0 1.2 copy-start.2
  80.0 1.2 copy-start.4
  80.0 1.2 copy-start.6
  80.3 0.9 copy-start.22
  117.1 1.1 copy-start.8
  119.0 13.5 %copy-start.14 = (bf16[256,96]{1,0:T(8,128)(2,1)}, bf16[256,96]{1,0:T(8,128)(2,1)S(1)}, u32[]{:S(2)}) copy-start(bf16[256,96]{1,0:T(8,128)(2,1)S(1)} %squeeze.83) | copy-start | bytes 147460
  125.1 12.2 %copy-start.18 = (bf16[256,96]{0,1:T(8,128)(2,1)}, bf16[256,96]{0,1:T(8,128)(2,1)S(1)}, u32[]{:S(2)}) copy-start(bf16[256,96]{0,1:T(8,128)(2,1)S(1)} %convolution_convert_fusion.4) | copy-start | bytes 147460
  133.3 9.8 %all-to-all-start.1 = ((bf16[4,2,6144]{2,1,0:T(2,128)(2,1)}), bf16[4,2,6144]{2,1,0:T(2,128)(2,1)}, u32[]{:S(2)}, u32[]{:S(2)}) async-start(bf16[4,2,6144]{2,1,0:T(2,128)(2,1)} %copy.211), calls=%async_computation.1 | async-start | bytes 196608 | tf_op jit(solution)/shard_map/all_to_all | solution.py:262
  140.1 5.3 %copy-start.9 = (bf16[4,2,18432]{2,1,0:T(2,128)(2,1)S(1)}, bf16[4,2,18432]{2,1,0:T(2,128)(2,1)}, u32[]{:S(2)}) copy-start(bf16[4,2,18432]{2,1,0:T(2,128)(2,1)} %copy-done.8) | copy-start | bytes 884740
  144.7 11.0 %copy-start.15 = (bf16[256,96]{1,0:T(8,128)(2,1)S(1)}, bf16[256,96]{1,0:T(8,128)(2,1)}, u32[]{:S(2)}) copy-start(bf16[256,96]{1,0:T(8,128)(2,1)} %copy-done.14) | copy-start | bytes 147460
  145.4 1.6 collective-permute-start.18
  146.2 16.0 %copy-start.19 = (bf16[256,96]{0,1:T(8,128)(2,1)S(1)}, bf16[256,96]{0,1:T(8,128)(2,1)}, u32[]{:S(2)}) copy-start(bf16[256,96]{0,1:T(8,128)(2,1)} %copy-done.18) | copy-start | bytes 147460
  152.4 8.9 %all-to-all-start.2 = ((bf16[4,2,3072]{2,1,0:T(2,128)(2,1)}), bf16[4,2,3072]{2,1,0:T(2,128)(2,1)S(1)}, u32[]{:S(2)}, u32[]{:S(2)}) async-start(bf16[4,2,3072]{2,1,0:T(2,128)(2,1)} %reshape.311), calls=%async_computation.2 | async-start | bytes 98304 | tf_op jit(solution)/shard_map/all_to_all | solution.py:335
  165.1 9.4 %all-to-all-start.3 = ((bf16[4,2,9216]{2,1,0:T(2,128)(2,1)}), bf16[4,2,9216]{2,1,0:T(2,128)(2,1)S(1)}, u32[]{:S(2)}, u32[]{:S(2)}) async-start(bf16[4,2,9216]{2,1,0:T(2,128)(2,1)} %reshape.313), calls=%async_computation.3 | async-start | bytes 294912 | tf_op jit(solution)/shard_map/all_to_all | solution.py:346
  175.1 1.5 copy-start.10
  176.5 1.3 collective-permute-start.19
  176.6 9.2 %copy-start.7 = (bf16[1,4,96,384]{3,2,0,1:T(8,128)(2,1)S(1)}, bf16[1,4,96,384]{3,2,0,1:T(8,128)(2,1)}, u32[]{:S(2)}) copy-start(bf16[1,4,96,384]{3,2,0,1:T(8,128)(2,1)} %copy-done.6) | copy-start | bytes 884740
  177.9 8.2 %copy-start.5 = (bf16[1,4,96,384]{3,2,0,1:T(8,128)(2,1)S(1)}, bf16[1,4,96,384]{3,2,0,1:T(8,128)(2,1)}, u32[]{:S(2)}) copy-start(bf16[1,4,96,384]{3,2,0,1:T(8,128)(2,1)} %copy-done.4) | copy-start | bytes 884740
  180.6 9.4 %copy-start.3 = (bf16[1,4,96,384]{3,2,0,1:T(8,128)(2,1)S(1)}, bf16[1,4,96,384]{3,2,0,1:T(8,128)(2,1)}, u32[]{:S(2)}) copy-start(bf16[1,4,96,384]{3,2,0,1:T(8,128)(2,1)} %copy-done.2) | copy-start | bytes 884740
  180.7 9.5 %copy-start.1 = (bf16[1,4,96,384]{3,2,0,1:T(8,128)(2,1)S(1)}, bf16[1,4,96,384]{3,2,0,1:T(8,128)(2,1)}, u32[]{:S(2)}) copy-start(bf16[1,4,96,384]{3,2,0,1:T(8,128)(2,1)} %copy-done) | copy-start | bytes 884740
  181.0 5.0 %collective-permute-start.21 = (bf16[2,384]{1,0:T(2,128)(2,1)S(1)}, bf16[2,384]{1,0:T(2,128)(2,1)S(1)}, u32[]{:S(2)}, u32[]{:S(2)}) collective-permute-start(bf16[2,384]{1,0:T(2,128)(2,1)S(1)} %get-tuple-element.126), channel_id=1, source_target_pairs={{0,4},{4,8},{8,12},{1,5},{5,9},{9,13},{2,6},{6,10},{10,14},{3,7},{... | collective-permute-start | bytes 4616 | tf_op jit(solution)/shard_map/ppermute | solution.py:23
  184.5 5.5 %collective-permute-start.20 = (bf16[2,384]{1,0:T(2,128)(2,1)S(1)}, bf16[2,384]{1,0:T(2,128)(2,1)S(1)}, u32[]{:S(2)}, u32[]{:S(2)}) collective-permute-start(bf16[2,384]{1,0:T(2,128)(2,1)S(1)} %get-tuple-element.125), channel_id=1, source_target_pairs={{4,0},{8,4},{12,8},{5,1},{9,5},{13,9},{6,2},{10,6},{14,10},{7,3},{... | collective-permute-start | bytes 4616 | tf_op jit(solution)/shard_map/ppermute | solution.py:25
  186.0 6.1 %copy-start.17 = (f32[1,128,384]{2,1,0:T(8,128)S(1)}, f32[1,128,384]{2,1,0:T(8,128)}, u32[]{:S(2)}) copy-start(f32[1,128,384]{2,1,0:T(8,128)} %param.8) | copy-start | bytes 589828
  190.7 1.4 collective-permute-start.22
  (3 other events, 2.1 us)
Sparse Core Ops, SparseCore 0:
  59.0 28.5 all-gather.2

commit v8 on v4

--- a/solution.py
+++ b/solution.py
@@ -29,11 +29,10 @@
     return cells
 
 
-def gather_seq(parts):
+def gather_seq(parts, width):
     spread = ("group", "batch")
     count = lax.axis_size("group") * lax.axis_size("batch")
     ring = lax.axis_size("seq")
-    width = parts[0][0].shape[-1]
     flats = [cells.reshape(-1, width) for cells, _ in parts]
     flat = jnp.concatenate(flats, axis=0) if len(flats) > 1 else flats[0]
     rows = flat.shape[0]
@@ -272,8 +271,10 @@
 
 
 def shards(features, noise, conv_weight, conv_bias, norm_gain, qkv_weight, out_weight):
-    (conv_weight,) = gather_seq([(conv_weight, 1)])
-    qkv_weight, out_weight = gather_seq([(qkv_weight, 1), (out_weight, 1)])
+    width = conv_weight.shape[-1]
+    (conv_weight,) = gather_seq([(conv_weight, 1)], width)
+    (qkv_weight,) = gather_seq([(qkv_weight, 1)], width)
+    (out_weight,) = gather_seq([(out_weight, 1)], width)
     clean = features[0]
     moved = (clean.astype(jnp.float32) + noise[0]).astype(jnp.bfloat16)
     joint = forward(

time: 206 us -> 163 us (0.79)
  local copies, waits for them, and re-layouts: 67.1 us -> 26.8 us
  waiting for transfers between devices: 45.2 us -> 60.9 us
  blocking collectives: 20.9 us -> 6.43 us
  starting transfers between devices: 45.1 us -> 51.1 us
  matrix products: 12.8 us -> 7.18 us
  other arithmetic: 11.2 us -> 7.8 us
    all_to_all x1 -> x0, blocking collectives: 14.6 us -> none  [forward(): lax.all_to_all(jnp.concatenate([query_send, keyval_send], axis=2), 'seq',...]
    all_to_all x0 -> x1, waiting for transfers between devices: none -> 7.13 us  [forward(): lax.all_to_all(jnp.concatenate([query_send, keyval_send], axis=2), 'seq',...]
    ppermute x6 -> x9, starting transfers between devices: 7.27 us -> 13.3 us  [gather_seq(): arrived = lax.ppermute(along, spread, [(i, i ^ mask) for i in range(count)])]
    convert_element_type x3, local copies, waits for them, and re-layouts: 4.62 us -> 0.27 us  [shards(): query_rows = query_back.reshape(head_count, query_groups, sub_rows, head_...]
    ppermute x6 -> x9, waiting for transfers between devices: 3.1 us -> 6.97 us  [gather_seq(): lax.ppermute(piece, 'seq', [(i, (i + shift) % ring) for i in range(ring)])]
    all_to_all x0 -> x1, starting transfers between devices: none -> 3.81 us  [forward(): lax.all_to_all(jnp.concatenate([query_send, keyval_send], axis=2), 'seq',...]
    ppermute x6 -> x9, waiting for transfers between devices: 21.8 us -> 25.4 us  [gather_seq(): arrived = lax.ppermute(along, spread, [(i, i ^ mask) for i in range(count)])]
    another operation x2, local copies, waits for them, and re-layouts: 3.26 us -> 0.14 us  [forward(): projected[2].reshape(pass_count, rows, head_count, head_size)]
  transfers between devices with their start and end apart: 22 -> 29, of which waited for: 13 -> 16; matrix products, arithmetic and copies ran while one was open for 9% -> 17% of each run, Pallas kernels for 0% -> 0%
where the time goes in v8:
time: 163 us; the launch traced here: 162 us
  waiting for transfers between devices  60.9 us (37%)
  starting transfers between devices  51.1 us (31%)
  local copies, waits for them, and re-layouts  26.8 us (16%)
  other arithmetic  7.8 us (5%)
  matrix products  7.18 us (4%)
  blocking collectives  6.43 us (4%)
  between operations  1.97 us (1%)
    ppermute x9, waiting for transfers between devices, gather_seq(): arrived = lax.ppermute(along, spread, [(i, i ^ mask) for i in range(count)])  25.4 us
    ppermute x9, starting transfers between devices, gather_seq(): lax.ppermute(piece, 'seq', [(i, (i + shift) % ring) for i in range(ring)])  14.7 us
    ppermute x9, starting transfers between devices, gather_seq(): arrived = lax.ppermute(along, spread, [(i, i ^ mask) for i in range(count)])  13.3 us
    all_to_all x1, waiting for transfers between devices, forward(): lax.all_to_all(jnp.concatenate([query_send, keyval_send], axis=2), 'seq',...  7.13 us
    ppermute x9, waiting for transfers between devices, gather_seq(): lax.ppermute(piece, 'seq', [(i, (i + shift) % ring) for i in range(ring)])  6.97 us
    all_to_all x1, waiting for transfers between devices, shards(): lax.all_to_all(jnp.concatenate([query_grad.reshape(devices, query_len).as...  6.03 us
    ppermute x2, starting transfers between devices, with_halo(): lax.ppermute(tail, axis, [(i, (i + 1) % count) for i in range(ends)])  5.72 us
    all_to_all x1, waiting for transfers between devices, shards(): lax.all_to_all(grad_send, 'seq', split_axis=0, concat_axis=1, tiled=True)  5.45 us
  transfers between devices with their start and end apart: 29, of which 16 were waited for; matrix products, arithmetic and copies ran while one was open for 17% of the time, Pallas kernels for 0%

profile of v8, /device:TPU:0, one launch (start us, length us, event | category | flops | bytes accessed | tf_op | source)
XLA Modules:
  0.0 162.1 jit_solution(14027952196058738281)
XLA Ops:
  1.6 3.1 %collective-permute-start = (bf16[144,384]{1,0:T(8,128)(2,1)S(1)}, bf16[144,384]{1,0:T(8,128)(2,1)S(1)}, u32[]{:S(2)}, u32[]{:S(2)}) collective-permute-start(bf16[144,384]{1,0:T(8,128)(2,1)S(1)} %get-tuple-element.80), channel_id=1, source_target_pairs={{0,4},{4,8},{8,12},{12,0},{1,5},{5,9},{9,13},{13,1},{2,6},{6,10},{... | collective-permute-start | bytes 331784 | tf_op jit(solution)/shard_map/ppermute | solution.py:48
  4.7 2.6 %collective-permute-start.1 = (bf16[144,384]{1,0:T(8,128)(2,1)S(1)}, bf16[144,384]{1,0:T(8,128)(2,1)S(1)}, u32[]{:S(2)}, u32[]{:S(2)}) collective-permute-start(bf16[144,384]{1,0:T(8,128)(2,1)S(1)} %get-tuple-element.80), channel_id=1, source_target_pairs={{0,8},{4,12},{8,0},{12,4},{1,9},{5,13},{9,1},{13,5},{2,10},{6,14},... | collective-permute-start | bytes 331784 | tf_op jit(solution)/shard_map/ppermute | solution.py:48
  7.3 1.3 collective-permute-start.2
  8.7 1.0 add_convert_fusion.2
  10.4 2.6 %collective-permute-start.6 = (bf16[2,2,384]{2,1,0:T(2,128)(2,1)S(1)}, bf16[2,2,384]{2,1,0:T(2,128)(2,1)S(1)}, u32[]{:S(2)}, u32[]{:S(2)}) collective-permute-start(bf16[2,2,384]{2,1,0:T(2,128)(2,1)S(1)} %get-tuple-element.108), channel_id=1, source_target_pairs={{0,4},{4,8},{8,12},{1,5},{5,9},{9,13},{2,6},{6,10},{10,14},{3,7},{... | collective-permute-start | bytes 9224 | tf_op jit(solution)/shard_map/ppermute | solution.py:23
  13.0 1.3 collective-permute-start.13
  14.3 1.0 copy.195
  17.9 2.6 %collective-permute-start.14 = (bf16[48,384]{1,0:T(8,128)(2,1)S(1)}, bf16[48,384]{1,0:T(8,128)(2,1)S(1)}, u32[]{:S(2)}, u32[]{:S(2)}) collective-permute-start(bf16[48,384]{1,0:T(8,128)(2,1)S(1)} %get-tuple-element.76), channel_id=1, source_target_pairs={{0,4},{4,8},{8,12},{12,0},{1,5},{5,9},{9,13},{13,1},{2,6},{6,10},{... | collective-permute-start | bytes 110600 | tf_op jit(solution)/shard_map/ppermute | solution.py:48
  20.9 2.7 %collective-permute-done.14 = bf16[48,384]{1,0:T(8,128)(2,1)S(1)} collective-permute-done((bf16[48,384]{1,0:T(8,128)(2,1)S(1)}, bf16[48,384]{1,0:T(8,128)(2,1)S(1)}, u32[]{:S(2)}, u32[]{:S(2)}) %collective-permute-start.14) | collective-permute-done | bytes 36896 | tf_op jit(solution)/shard_map/ppermute | solution.py:48
  25.4 0.9 collective-permute-start.7
  26.9 1.7 %collective-permute-done.16 = bf16[48,384]{1,0:T(8,128)(2,1)S(1)} collective-permute-done((bf16[48,384]{1,0:T(8,128)(2,1)S(1)}, bf16[48,384]{1,0:T(8,128)(2,1)S(1)}, u32[]{:S(2)}, u32[]{:S(2)}) %collective-permute-start.16) | collective-permute-done | bytes 36896 | tf_op jit(solution)/shard_map/ppermute | solution.py:48
  30.2 0.9 bitcast_dynamic-update-slice_fusion.10
  31.2 1.3 collective-permute-done.7
  32.5 2.3 %collective-permute-start.9 = (bf16[120,384]{1,0:T(8,128)(2,1)S(1)}, bf16[120,384]{1,0:T(8,128)(2,1)S(1)}, u32[]{:S(2)}, u32[]{:S(2)}) collective-permute-start(bf16[120,384]{1,0:T(8,128)(2,1)S(1)} %get-tuple-element.78), channel_id=1, source_target_pairs={{0,12},{4,0},{8,4},{12,8},{1,13},{5,1},{9,5},{13,9},{2,14},{6,2},{... | collective-permute-start | bytes 276488 | tf_op jit(solution)/shard_map/ppermute | solution.py:48
  34.8 1.5 collective-permute-start.17
  37.0 1.5 collective-permute-start.18
  38.8 1.5 collective-permute-start.19
  40.9 1.6 collective-permute-start.11
  42.8 7.1 %collective-permute-done.10 = bf16[4,120,384]{2,1,0:T(8,128)(2,1)S(1)} collective-permute-done((bf16[4,120,384]{2,1,0:T(8,128)(2,1)S(1)}, bf16[4,120,384]{2,1,0:T(8,128)(2,1)S(1)}, u32[]{:S(2)}, u32[]{:S(2)}) %collective-permute-start.10) | collective-permute-done | bytes 368672 | tf_op jit(solution)/shard_map/ppermute | solution.py:59
  49.9 3.3 %collective-permute-start.12 = (bf16[4,120,384]{2,1,0:T(8,128)(2,1)S(1)}, bf16[4,120,384]{2,1,0:T(8,128)(2,1)S(1)}, u32[]{:S(2)}, u32[]{:S(2)}) collective-permute-start(bf16[4,120,384]{2,1,0:T(8,128)(2,1)S(1)} %bitcast_dynamic-update-slice_fusion.16), channel_id=1, source_target_pairs={{0,18},{2,16},{16,2},{18,0},{1,19},{3,17},{17,3},{19,1},{4,22},{6,... | collective-permute-start | bytes 1105928 | tf_op jit(solution)/shard_map/ppermute | solution.py:59
  54.0 8.7 %collective-permute-done.12 = bf16[4,120,384]{2,1,0:T(8,128)(2,1)S(1)} collective-permute-done((bf16[4,120,384]{2,1,0:T(8,128)(2,1)S(1)}, bf16[4,120,384]{2,1,0:T(8,128)(2,1)S(1)}, u32[]{:S(2)}, u32[]{:S(2)}) %collective-permute-start.12) | collective-permute-done | bytes 368672 | tf_op jit(solution)/shard_map/ppermute | solution.py:59
  62.6 1.2 collective-permute-start.4
  65.4 1.2 fusion.23
  66.6 1.2 reshape.239
  68.2 1.9 %all-gather = bf16[2,64,1,768]{3,1,0,2:T(8,128)(2,1)S(1)} all-gather(bf16[2,64,1,384]{3,1,0,2:T(8,128)(2,1)S(1)} %fusion.54), channel_id=2, replica_groups=mesh['group'=2,'seq'=4,'batch'=2,'mp'=2] {'mp'}, dimensions={3}, use_global_device_ids=true | all-gather | bytes 294912 | tf_op jit(solution)/shard_map/all_gather | solution.py:186
  70.3 1.5 collective-permute-start.5
  71.7 1.1 bitcast_dynamic-update-slice_fusion.1
  72.8 1.1 bitcast_dynamic-update-slice_fusion
  73.9 9.5 %collective-permute-done.5 = bf16[4,144,384]{2,1,0:T(8,128)(2,1)S(1)} collective-permute-done((bf16[4,144,384]{2,1,0:T(8,128)(2,1)S(1)}, bf16[4,144,384]{2,1,0:T(8,128)(2,1)S(1)}, u32[]{:S(2)}, u32[]{:S(2)}) %collective-permute-start.5) | collective-permute-done | bytes 442400 | tf_op jit(solution)/shard_map/ppermute | solution.py:59
  85.5 1.0 pad_maximum_fusion
  86.4 3.8 %all-to-all-start = ((bf16[4,2,18432]{2,1,0:T(2,128)(2,1)}), bf16[4,2,18432]{2,1,0:T(2,128)(2,1)S(1)}, u32[]{:S(2)}, u32[]{:S(2)}) async-start(bf16[4,2,18432]{2,1,0:T(2,128)(2,1)} %pad_maximum_fusion), calls=%async_computation | async-start | bytes 589824 | tf_op jit(solution)/shard_map/all_to_all | solution.py:223
  90.2 0.9 bitcast_dynamic-update-slice_fusion.9
  91.2 0.9 bitcast_dynamic-update-slice_fusion.8
  92.1 7.1 %all-to-all-done = bf16[4,2,18432]{2,1,0:T(2,128)(2,1)S(1)} async-done(((bf16[4,2,18432]{2,1,0:T(2,128)(2,1)}), bf16[4,2,18432]{2,1,0:T(2,128)(2,1)S(1)}, u32[]{:S(2)}, u32[]{:S(2)}) %all-to-all-start) | async-done | bytes 294944 | tf_op jit(solution)/shard_map/all_to_all | solution.py:223
  103.2 4.1 %all-to-all-start.1 = ((bf16[4,2,6144]{2,1,0:T(2,128)(2,1)}), bf16[4,2,6144]{2,1,0:T(2,128)(2,1)}, u32[]{:S(2)}, u32[]{:S(2)}) async-start(bf16[4,2,6144]{2,1,0:T(2,128)(2,1)} %copy.193), calls=%async_computation.1 | async-start | bytes 196608 | tf_op jit(solution)/shard_map/all_to_all | solution.py:245
  107.3 0.9 bitcast_dynamic-update-slice_fusion.11
  109.0 4.0 %all-to-all-done.1 = bf16[4,2,6144]{2,1,0:T(2,128)(2,1)} async-done(((bf16[4,2,6144]{2,1,0:T(2,128)(2,1)}), bf16[4,2,6144]{2,1,0:T(2,128)(2,1)}, u32[]{:S(2)}, u32[]{:S(2)}) %all-to-all-start.1) | async-done | bytes 98336 | tf_op jit(solution)/shard_map/all_to_all | solution.py:245
  113.0 1.0 reshape.243
  117.1 1.9 %all_gather.7 = bf16[64,768]{1,0:T(8,128)(2,1)S(1)} all-gather(bf16[64,384]{1,0:T(8,128)(2,1)S(1)} %fusion.84), channel_id=1, replica_groups=mesh['group'=2,'seq'=4,'batch'=2,'mp'=2] {'mp'}, dimensions={1}, use_global_device_ids=true | all-gather | bytes 147456 | tf_op jit(solution)/shard_map/all_gather | solution.py:307
  121.6 3.3 %all-to-all-start.2 = ((bf16[4,2,3072]{2,1,0:T(2,128)(2,1)}), bf16[4,2,3072]{2,1,0:T(2,128)(2,1)S(1)}, u32[]{:S(2)}, u32[]{:S(2)}) async-start(bf16[4,2,3072]{2,1,0:T(2,128)(2,1)} %reshape.266), calls=%async_computation.2 | async-start | bytes 98304 | tf_op jit(solution)/shard_map/all_to_all | solution.py:319
  125.1 5.4 %all-to-all-done.2 = bf16[4,2,3072]{2,1,0:T(2,128)(2,1)S(1)} async-done(((bf16[4,2,3072]{2,1,0:T(2,128)(2,1)}), bf16[4,2,3072]{2,1,0:T(2,128)(2,1)S(1)}, u32[]{:S(2)}, u32[]{:S(2)}) %all-to-all-start.2) | async-done | bytes 49184 | tf_op jit(solution)/shard_map/all_to_all | solution.py:319
  134.2 3.3 %all-to-all-start.3 = ((bf16[4,2,9216]{2,1,0:T(2,128)(2,1)}), bf16[4,2,9216]{2,1,0:T(2,128)(2,1)S(1)}, u32[]{:S(2)}, u32[]{:S(2)}) async-start(bf16[4,2,9216]{2,1,0:T(2,128)(2,1)} %reshape.268), calls=%async_computation.3 | async-start | bytes 294912 | tf_op jit(solution)/shard_map/all_to_all | solution.py:330
  137.6 6.0 %all-to-all-done.3 = bf16[4,2,9216]{2,1,0:T(2,128)(2,1)S(1)} async-done(((bf16[4,2,9216]{2,1,0:T(2,128)(2,1)}), bf16[4,2,9216]{2,1,0:T(2,128)(2,1)S(1)}, u32[]{:S(2)}, u32[]{:S(2)}) %all-to-all-start.3) | async-done | bytes 147488 | tf_op jit(solution)/shard_map/all_to_all | solution.py:330
  145.8 1.0 collective-permute-done.21
  147.0 2.6 %psum.7 = f32[64]{0:T(128)S(1)} all-reduce(f32[64]{0:T(128)S(1)} %fusion.75), channel_id=1, replica_groups=mesh['group'=2,'seq'=4,'batch'=2,'mp'=2] {'mp'}, use_global_device_ids=true, to_apply=%region_7.8 | all-reduce | flops 64 | bytes 512 | tf_op jit(solution)/shard_map/psum | solution.py:368
  150.1 3.1 %collective-permute-start.23 = (bf16[2,384]{1,0:T(2,128)(2,1)S(1)}, bf16[2,384]{1,0:T(2,128)(2,1)S(1)}, u32[]{:S(2)}, u32[]{:S(2)}) collective-permute-start(bf16[2,384]{1,0:T(2,128)(2,1)S(1)} %get-tuple-element.113), channel_id=1, source_target_pairs={{0,4},{4,8},{8,12},{1,5},{5,9},{9,13},{2,6},{6,10},{10,14},{3,7},{... | collective-permute-start | bytes 4616 | tf_op jit(solution)/shard_map/ppermute | solution.py:23
  153.6 1.3 collective-permute-start.22
  155.4 3.7 %collective-permute-done.22 = bf16[2,384]{1,0:T(2,128)(2,1)S(1)} collective-permute-done((bf16[2,384]{1,0:T(2,128)(2,1)S(1)}, bf16[2,384]{1,0:T(2,128)(2,1)S(1)}, u32[]{:S(2)}, u32[]{:S(2)}) %collective-permute-start.22) | collective-permute-done | bytes 1568 | tf_op jit(solution)/shard_map/ppermute | solution.py:25
  (217 shorter events, 35.1 us)
Async XLA Ops:
  0.6 20.2 %copy-start.13 = (bf16[1,128,384]{2,1,0:T(8,128)(2,1)S(1)}, bf16[1,128,384]{2,1,0:T(8,128)(2,1)}, u32[]{:S(2)}) copy-start(bf16[1,128,384]{2,1,0:T(8,128)(2,1)} %param.7) | copy-start | bytes 294916
  0.6 17.2 %copy-start.22 = (f32[768]{0:T(1024)S(1)}, f32[768]{0:T(1024)}, u32[]{:S(2)}) copy-start(f32[768]{0:T(1024)} %param.11) | copy-start | bytes 9220
  1.6 37.1 %collective-permute-start = (bf16[144,384]{1,0:T(8,128)(2,1)S(1)}, bf16[144,384]{1,0:T(8,128)(2,1)S(1)}, u32[]{:S(2)}, u32[]{:S(2)}) collective-permute-start(bf16[144,384]{1,0:T(8,128)(2,1)S(1)} %get-tuple-element.80), channel_id=1, source_target_pairs={{0,4},{4,8},{8,12},{12,0},{1,5},{5,9},{9,13},{13,1},{2,6},{6,10},{... | collective-permute-start | bytes 331784 | tf_op jit(solution)/shard_map/ppermute | solution.py:48
  4.7 35.5 %collective-permute-start.1 = (bf16[144,384]{1,0:T(8,128)(2,1)S(1)}, bf16[144,384]{1,0:T(8,128)(2,1)S(1)}, u32[]{:S(2)}, u32[]{:S(2)}) collective-permute-start(bf16[144,384]{1,0:T(8,128)(2,1)S(1)} %get-tuple-element.80), channel_id=1, source_target_pairs={{0,8},{4,12},{8,0},{12,4},{1,9},{5,13},{9,1},{13,5},{2,10},{6,14},... | collective-permute-start | bytes 331784 | tf_op jit(solution)/shard_map/ppermute | solution.py:48
  7.3 33.6 %collective-permute-start.2 = (bf16[144,384]{1,0:T(8,128)(2,1)S(1)}, bf16[144,384]{1,0:T(8,128)(2,1)S(1)}, u32[]{:S(2)}, u32[]{:S(2)}) collective-permute-start(bf16[144,384]{1,0:T(8,128)(2,1)S(1)} %get-tuple-element.80), channel_id=1, source_target_pairs={{0,12},{4,0},{8,4},{12,8},{1,13},{5,1},{9,5},{13,9},{2,14},{6,2},{... | collective-permute-start | bytes 331784 | tf_op jit(solution)/shard_map/ppermute | solution.py:48
  10.4 7.5 %collective-permute-start.6 = (bf16[2,2,384]{2,1,0:T(2,128)(2,1)S(1)}, bf16[2,2,384]{2,1,0:T(2,128)(2,1)S(1)}, u32[]{:S(2)}, u32[]{:S(2)}) collective-permute-start(bf16[2,2,384]{2,1,0:T(2,128)(2,1)S(1)} %get-tuple-element.108), channel_id=1, source_target_pairs={{0,4},{4,8},{8,12},{1,5},{5,9},{9,13},{2,6},{6,10},{10,14},{3,7},{... | collective-permute-start | bytes 9224 | tf_op jit(solution)/shard_map/ppermute | solution.py:23
  13.0 7.5 %collective-permute-start.13 = (bf16[2,2,384]{2,1,0:T(2,128)(2,1)S(1)}, bf16[2,2,384]{2,1,0:T(2,128)(2,1)S(1)}, u32[]{:S(2)}, u32[]{:S(2)}) collective-permute-start(bf16[2,2,384]{2,1,0:T(2,128)(2,1)S(1)} %get-tuple-element.109), channel_id=1, source_target_pairs={{4,0},{8,4},{12,8},{5,1},{9,5},{13,9},{6,2},{10,6},{14,10},{7,3},{... | collective-permute-start | bytes 9224 | tf_op jit(solution)/shard_map/ppermute | solution.py:25
  17.9 5.8 %collective-permute-start.14 = (bf16[48,384]{1,0:T(8,128)(2,1)S(1)}, bf16[48,384]{1,0:T(8,128)(2,1)S(1)}, u32[]{:S(2)}, u32[]{:S(2)}) collective-permute-start(bf16[48,384]{1,0:T(8,128)(2,1)S(1)} %get-tuple-element.76), channel_id=1, source_target_pairs={{0,4},{4,8},{8,12},{12,0},{1,5},{5,9},{9,13},{13,1},{2,6},{6,10},{... | collective-permute-start | bytes 110600 | tf_op jit(solution)/shard_map/ppermute | solution.py:48
  20.5 4.9 %collective-permute-start.15 = (bf16[48,384]{1,0:T(8,128)(2,1)S(1)}, bf16[48,384]{1,0:T(8,128)(2,1)S(1)}, u32[]{:S(2)}, u32[]{:S(2)}) collective-permute-start(bf16[48,384]{1,0:T(8,128)(2,1)S(1)} %get-tuple-element.76), channel_id=1, source_target_pairs={{0,8},{4,12},{8,0},{12,4},{1,9},{5,13},{9,1},{13,5},{2,10},{6,14},... | collective-permute-start | bytes 110600 | tf_op jit(solution)/shard_map/ppermute | solution.py:48
  23.7 5.0 %collective-permute-start.16 = (bf16[48,384]{1,0:T(8,128)(2,1)S(1)}, bf16[48,384]{1,0:T(8,128)(2,1)S(1)}, u32[]{:S(2)}, u32[]{:S(2)}) collective-permute-start(bf16[48,384]{1,0:T(8,128)(2,1)S(1)} %get-tuple-element.76), channel_id=1, source_target_pairs={{0,12},{4,0},{8,4},{12,8},{1,13},{5,1},{9,5},{13,9},{2,14},{6,2},{... | collective-permute-start | bytes 110600 | tf_op jit(solution)/shard_map/ppermute | solution.py:48
  25.4 7.1 %collective-permute-start.7 = (bf16[120,384]{1,0:T(8,128)(2,1)S(1)}, bf16[120,384]{1,0:T(8,128)(2,1)S(1)}, u32[]{:S(2)}, u32[]{:S(2)}) collective-permute-start(bf16[120,384]{1,0:T(8,128)(2,1)S(1)} %get-tuple-element.78), channel_id=1, source_target_pairs={{0,4},{4,8},{8,12},{12,0},{1,5},{5,9},{9,13},{13,1},{2,6},{6,10},{... | collective-permute-start | bytes 276488 | tf_op jit(solution)/shard_map/ppermute | solution.py:48
  28.7 6.1 %collective-permute-start.8 = (bf16[120,384]{1,0:T(8,128)(2,1)S(1)}, bf16[120,384]{1,0:T(8,128)(2,1)S(1)}, u32[]{:S(2)}, u32[]{:S(2)}) collective-permute-start(bf16[120,384]{1,0:T(8,128)(2,1)S(1)} %get-tuple-element.78), channel_id=1, source_target_pairs={{0,8},{4,12},{8,0},{12,4},{1,9},{5,13},{9,1},{13,5},{2,10},{6,14},... | collective-permute-start | bytes 276488 | tf_op jit(solution)/shard_map/ppermute | solution.py:48
  31.2 7.3 %copy-start.10 = (bf16[4,4,48,384]{3,2,0,1:T(8,128)(2,1)}, bf16[4,4,48,384]{3,2,0,1:T(8,128)(2,1)S(1)}, u32[]{:S(2)}) copy-start(bf16[4,4,48,384]{3,2,0,1:T(8,128)(2,1)S(1)} %bitcast_dynamic-update-slice_fusion.10) | copy-start | bytes 1769476
  32.5 4.6 %collective-permute-start.9 = (bf16[120,384]{1,0:T(8,128)(2,1)S(1)}, bf16[120,384]{1,0:T(8,128)(2,1)S(1)}, u32[]{:S(2)}, u32[]{:S(2)}) collective-permute-start(bf16[120,384]{1,0:T(8,128)(2,1)S(1)} %get-tuple-element.78), channel_id=1, source_target_pairs={{0,12},{4,0},{8,4},{12,8},{1,13},{5,1},{9,5},{13,9},{2,14},{6,2},{... | collective-permute-start | bytes 276488 | tf_op jit(solution)/shard_map/ppermute | solution.py:48
  34.8 55.4 %collective-permute-start.17 = (bf16[4,48,384]{2,1,0:T(8,128)(2,1)}, bf16[4,48,384]{2,1,0:T(8,128)(2,1)}, u32[]{:S(2)}, u32[]{:S(2)}) collective-permute-start(bf16[4,48,384]{2,1,0:T(8,128)(2,1)} %bitcast_dynamic-update-slice_fusion.20), channel_id=1, source_target_pairs={{0,2},{2,0},{16,18},{18,16},{1,3},{3,1},{17,19},{19,17},{4,6},{6,4... | collective-permute-start | bytes 442376 | tf_op jit(solution)/shard_map/ppermute | solution.py:59
  37.0 54.2 %collective-permute-start.18 = (bf16[4,48,384]{2,1,0:T(8,128)(2,1)}, bf16[4,48,384]{2,1,0:T(8,128)(2,1)}, u32[]{:S(2)}, u32[]{:S(2)}) collective-permute-start(bf16[4,48,384]{2,1,0:T(8,128)(2,1)} %bitcast_dynamic-update-slice_fusion.20), channel_id=1, source_target_pairs={{0,16},{2,18},{16,0},{18,2},{1,17},{3,19},{17,1},{19,3},{4,20},{6,... | collective-permute-start | bytes 442376 | tf_op jit(solution)/shard_map/ppermute | solution.py:59
  38.8 68.5 %collective-permute-start.19 = (bf16[4,48,384]{2,1,0:T(8,128)(2,1)}, bf16[4,48,384]{2,1,0:T(8,128)(2,1)}, u32[]{:S(2)}, u32[]{:S(2)}) collective-permute-start(bf16[4,48,384]{2,1,0:T(8,128)(2,1)} %bitcast_dynamic-update-slice_fusion.20), channel_id=1, source_target_pairs={{0,18},{2,16},{16,2},{18,0},{1,19},{3,17},{17,3},{19,1},{4,22},{6,... | collective-permute-start | bytes 442376 | tf_op jit(solution)/shard_map/ppermute | solution.py:59
  40.3 9.6 %collective-permute-start.10 = (bf16[4,120,384]{2,1,0:T(8,128)(2,1)S(1)}, bf16[4,120,384]{2,1,0:T(8,128)(2,1)S(1)}, u32[]{:S(2)}, u32[]{:S(2)}) collective-permute-start(bf16[4,120,384]{2,1,0:T(8,128)(2,1)S(1)} %bitcast_dynamic-update-slice_fusion.16), channel_id=1, source_target_pairs={{0,2},{2,0},{16,18},{18,16},{1,3},{3,1},{17,19},{19,17},{4,6},{6,4... | collective-permute-start | bytes 1105928 | tf_op jit(solution)/shard_map/ppermute | solution.py:59
  40.9 12.3 %collective-permute-start.11 = (bf16[4,120,384]{2,1,0:T(8,128)(2,1)S(1)}, bf16[4,120,384]{2,1,0:T(8,128)(2,1)S(1)}, u32[]{:S(2)}, u32[]{:S(2)}) collective-permute-start(bf16[4,120,384]{2,1,0:T(8,128)(2,1)S(1)} %bitcast_dynamic-update-slice_fusion.16), channel_id=1, source_target_pairs={{0,16},{2,18},{16,0},{18,2},{1,17},{3,19},{17,1},{19,3},{4,20},{6,... | collective-permute-start | bytes 1105928 | tf_op jit(solution)/shard_map/ppermute | solution.py:59
  49.9 12.7 %collective-permute-start.12 = (bf16[4,120,384]{2,1,0:T(8,128)(2,1)S(1)}, bf16[4,120,384]{2,1,0:T(8,128)(2,1)S(1)}, u32[]{:S(2)}, u32[]{:S(2)}) collective-permute-start(bf16[4,120,384]{2,1,0:T(8,128)(2,1)S(1)} %bitcast_dynamic-update-slice_fusion.16), channel_id=1, source_target_pairs={{0,18},{2,16},{16,2},{18,0},{1,19},{3,17},{17,3},{19,1},{4,22},{6,... | collective-permute-start | bytes 1105928 | tf_op jit(solution)/shard_map/ppermute | solution.py:59
  53.3 17.0 %collective-permute-start.3 = (bf16[4,144,384]{2,1,0:T(8,128)(2,1)S(1)}, bf16[4,144,384]{2,1,0:T(8,128)(2,1)}, u32[]{:S(2)}, u32[]{:S(2)}) collective-permute-start(bf16[4,144,384]{2,1,0:T(8,128)(2,1)S(1)} %bitcast_dynamic-update-slice_fusion.12), channel_id=1, source_target_pairs={{0,2},{2,0},{16,18},{18,16},{1,3},{3,1},{17,19},{19,17},{4,6},{6,4... | collective-permute-start | bytes 1327112 | tf_op jit(solution)/shard_map/ppermute | solution.py:59
  62.6 10.2 %collective-permute-start.4 = (bf16[4,144,384]{2,1,0:T(8,128)(2,1)S(1)}, bf16[4,144,384]{2,1,0:T(8,128)(2,1)}, u32[]{:S(2)}, u32[]{:S(2)}) collective-permute-start(bf16[4,144,384]{2,1,0:T(8,128)(2,1)S(1)} %bitcast_dynamic-update-slice_fusion.12), channel_id=1, source_target_pairs={{0,16},{2,18},{16,0},{18,2},{1,17},{3,19},{17,1},{19,3},{4,20},{6,... | collective-permute-start | bytes 1327112 | tf_op jit(solution)/shard_map/ppermute | solution.py:59
  64.1 1.2 copy-start.2
  64.1 1.2 copy-start.4
  68.2 15.4 %copy-start.14 = (bf16[2,64,1,384]{3,1,0,2:T(8,128)(2,1)}, bf16[2,64,1,384]{3,1,0,2:T(8,128)(2,1)S(1)}, u32[]{:S(2)}) copy-start(bf16[2,64,1,384]{3,1,0,2:T(8,128)(2,1)S(1)} %fusion.54) | copy-start | bytes 294916
  70.3 13.2 %collective-permute-start.5 = (bf16[4,144,384]{2,1,0:T(8,128)(2,1)S(1)}, bf16[4,144,384]{2,1,0:T(8,128)(2,1)S(1)}, u32[]{:S(2)}, u32[]{:S(2)}) collective-permute-start(bf16[4,144,384]{2,1,0:T(8,128)(2,1)S(1)} %bitcast_dynamic-update-slice_fusion.12), channel_id=1, source_target_pairs={{0,18},{2,16},{16,2},{18,0},{1,19},{3,17},{17,3},{19,1},{4,22},{6,... | collective-permute-start | bytes 1327112 | tf_op jit(solution)/shard_map/ppermute | solution.py:59
  84.4 5.9 %copy-start.11 = (bf16[4,4,48,384]{3,2,0,1:T(8,128)(2,1)S(1)}, bf16[4,4,48,384]{3,2,0,1:T(8,128)(2,1)}, u32[]{:S(2)}) copy-start(bf16[4,4,48,384]{3,2,0,1:T(8,128)(2,1)} %copy-done.10) | copy-start | bytes 1769476
  86.4 12.8 %all-to-all-start = ((bf16[4,2,18432]{2,1,0:T(2,128)(2,1)}), bf16[4,2,18432]{2,1,0:T(2,128)(2,1)S(1)}, u32[]{:S(2)}, u32[]{:S(2)}) async-start(bf16[4,2,18432]{2,1,0:T(2,128)(2,1)} %pad_maximum_fusion), calls=%async_computation | async-start | bytes 589824 | tf_op jit(solution)/shard_map/all_to_all | solution.py:223
  100.0 2.4 %copy-start.16 = (bf16[256,96]{1,0:T(8,128)(2,1)}, bf16[256,96]{1,0:T(8,128)(2,1)S(1)}, u32[]{:S(2)}) copy-start(bf16[256,96]{1,0:T(8,128)(2,1)S(1)} %squeeze.83) | copy-start | bytes 147460
  101.0 7.2 %copy-start.19 = (bf16[256,96]{0,1:T(8,128)(2,1)}, bf16[256,96]{0,1:T(8,128)(2,1)S(1)}, u32[]{:S(2)}) copy-start(bf16[256,96]{0,1:T(8,128)(2,1)S(1)} %convolution_convert_fusion.4) | copy-start | bytes 147460
  103.2 9.8 %all-to-all-start.1 = ((bf16[4,2,6144]{2,1,0:T(2,128)(2,1)}), bf16[4,2,6144]{2,1,0:T(2,128)(2,1)}, u32[]{:S(2)}, u32[]{:S(2)}) async-start(bf16[4,2,6144]{2,1,0:T(2,128)(2,1)} %copy.193), calls=%async_computation.1 | async-start | bytes 196608 | tf_op jit(solution)/shard_map/all_to_all | solution.py:245
  108.7 7.5 %copy-start.15 = (bf16[2,64,1,384]{3,1,0,2:T(8,128)(2,1)S(1)}, bf16[2,64,1,384]{3,1,0,2:T(8,128)(2,1)}, u32[]{:S(2)}) copy-start(bf16[2,64,1,384]{3,1,0,2:T(8,128)(2,1)} %copy-done.14) | copy-start | bytes 294916
  114.6 10.2 %copy-start.17 = (bf16[256,96]{1,0:T(8,128)(2,1)S(1)}, bf16[256,96]{1,0:T(8,128)(2,1)}, u32[]{:S(2)}) copy-start(bf16[256,96]{1,0:T(8,128)(2,1)} %copy-done.16) | copy-start | bytes 147460
  114.6 1.5 collective-permute-start.20
  115.5 15.8 %copy-start.20 = (bf16[256,96]{0,1:T(8,128)(2,1)S(1)}, bf16[256,96]{0,1:T(8,128)(2,1)}, u32[]{:S(2)}) copy-start(bf16[256,96]{0,1:T(8,128)(2,1)} %copy-done.19) | copy-start | bytes 147460
  121.6 8.9 %all-to-all-start.2 = ((bf16[4,2,3072]{2,1,0:T(2,128)(2,1)}), bf16[4,2,3072]{2,1,0:T(2,128)(2,1)S(1)}, u32[]{:S(2)}, u32[]{:S(2)}) async-start(bf16[4,2,3072]{2,1,0:T(2,128)(2,1)} %reshape.266), calls=%async_computation.2 | async-start | bytes 98304 | tf_op jit(solution)/shard_map/all_to_all | solution.py:319
  134.2 9.4 %all-to-all-start.3 = ((bf16[4,2,9216]{2,1,0:T(2,128)(2,1)}), bf16[4,2,9216]{2,1,0:T(2,128)(2,1)S(1)}, u32[]{:S(2)}, u32[]{:S(2)}) async-start(bf16[4,2,9216]{2,1,0:T(2,128)(2,1)} %reshape.268), calls=%async_computation.3 | async-start | bytes 294912 | tf_op jit(solution)/shard_map/all_to_all | solution.py:330
  144.2 1.4 copy-start.12
  145.6 1.3 collective-permute-start.21
  145.7 9.2 %copy-start.9 = (bf16[1,4,96,384]{3,2,0,1:T(8,128)(2,1)S(1)}, bf16[1,4,96,384]{3,2,0,1:T(8,128)(2,1)}, u32[]{:S(2)}) copy-start(bf16[1,4,96,384]{3,2,0,1:T(8,128)(2,1)} %copy-done.8) | copy-start | bytes 884740
  147.0 8.2 %copy-start.7 = (bf16[1,4,96,384]{3,2,0,1:T(8,128)(2,1)S(1)}, bf16[1,4,96,384]{3,2,0,1:T(8,128)(2,1)}, u32[]{:S(2)}) copy-start(bf16[1,4,96,384]{3,2,0,1:T(8,128)(2,1)} %copy-done.6) | copy-start | bytes 884740
  149.7 9.4 %copy-start.5 = (bf16[1,4,96,384]{3,2,0,1:T(8,128)(2,1)S(1)}, bf16[1,4,96,384]{3,2,0,1:T(8,128)(2,1)}, u32[]{:S(2)}) copy-start(bf16[1,4,96,384]{3,2,0,1:T(8,128)(2,1)} %copy-done.4) | copy-start | bytes 884740
  149.8 9.5 %copy-start.3 = (bf16[1,4,96,384]{3,2,0,1:T(8,128)(2,1)S(1)}, bf16[1,4,96,384]{3,2,0,1:T(8,128)(2,1)}, u32[]{:S(2)}) copy-start(bf16[1,4,96,384]{3,2,0,1:T(8,128)(2,1)} %copy-done.2) | copy-start | bytes 884740
  150.1 5.0 %collective-permute-start.23 = (bf16[2,384]{1,0:T(2,128)(2,1)S(1)}, bf16[2,384]{1,0:T(2,128)(2,1)S(1)}, u32[]{:S(2)}, u32[]{:S(2)}) collective-permute-start(bf16[2,384]{1,0:T(2,128)(2,1)S(1)} %get-tuple-element.113), channel_id=1, source_target_pairs={{0,4},{4,8},{8,12},{1,5},{5,9},{9,13},{2,6},{6,10},{10,14},{3,7},{... | collective-permute-start | bytes 4616 | tf_op jit(solution)/shard_map/ppermute | solution.py:23
  153.3 6.3 %copy-start.1 = (bf16[1,4,96,384]{3,2,0,1:T(8,128)(2,1)S(1)}, bf16[1,4,96,384]{3,2,0,1:T(8,128)(2,1)}, u32[]{:S(2)}) copy-start(bf16[1,4,96,384]{3,2,0,1:T(8,128)(2,1)} %copy-done) | copy-start | bytes 884740
  153.6 5.5 %collective-permute-start.22 = (bf16[2,384]{1,0:T(2,128)(2,1)S(1)}, bf16[2,384]{1,0:T(2,128)(2,1)S(1)}, u32[]{:S(2)}, u32[]{:S(2)}) collective-permute-start(bf16[2,384]{1,0:T(2,128)(2,1)S(1)} %get-tuple-element.112), channel_id=1, source_target_pairs={{4,0},{8,4},{12,8},{5,1},{9,5},{13,9},{6,2},{10,6},{14,10},{7,3},{... | collective-permute-start | bytes 4616 | tf_op jit(solution)/shard_map/ppermute | solution.py:25
  155.1 6.2 %copy-start.18 = (f32[1,128,384]{2,1,0:T(8,128)S(1)}, f32[1,128,384]{2,1,0:T(8,128)}, u32[]{:S(2)}) copy-start(f32[1,128,384]{2,1,0:T(8,128)} %param.8) | copy-start | bytes 589828
  159.8 1.4 collective-permute-start.24
  (4 other events, 4.4 us)

commit v9 on v8

--- a/solution.py
+++ b/solution.py
@@ -29,7 +29,7 @@
     return cells
 
 
-def gather_seq(parts, width):
+def gather_seq(parts, width, after=(None, None)):
     spread = ("group", "batch")
     count = lax.axis_size("group") * lax.axis_size("batch")
     ring = lax.axis_size("seq")
@@ -40,6 +40,8 @@
     if size * count != rows:
         flat = jnp.pad(flat, ((0, size * count - rows), (0, 0)))
     piece = lax.dynamic_slice_in_dim(flat, lax.axis_index(spread) * size, size, 0)
+    if after[0] is not None:
+        piece = lax.optimization_barrier((piece, after[0]))[0]
     if ring <= 8:
         place = lax.axis_index("seq")
         along = jnp.zeros((ring,) + piece.shape, piece.dtype)
@@ -51,6 +53,8 @@
             )
     else:
         along = lax.all_gather(piece, "seq", axis=0, tiled=False)
+    if after[1] is not None:
+        along = lax.optimization_barrier((along, after[1]))[0]
     if ring <= 8 and count <= 4:
         place = lax.axis_index(spread)
         whole = jnp.zeros((count,) + along.shape, along.dtype)
@@ -64,6 +68,7 @@
         whole = lax.all_gather(along, spread, axis=0, tiled=False)
     whole = whole.transpose(1, 0, 2, 3).reshape(ring, count * size, width)
     results = []
+    stages = (along, whole)
     offset = 0
     for (cells, dim), part in zip(parts, flats):
         block = whole[:, offset : offset + part.shape[0]]
@@ -72,7 +77,7 @@
         shape = list(cells.shape)
         shape[dim] = shape[dim] * ring
         results.append(block.reshape(shape))
-    return results
+    return results, stages
 
 
 def swap_mp(cells):
@@ -272,9 +277,9 @@
 
 def shards(features, noise, conv_weight, conv_bias, norm_gain, qkv_weight, out_weight):
     width = conv_weight.shape[-1]
-    (conv_weight,) = gather_seq([(conv_weight, 1)], width)
-    (qkv_weight,) = gather_seq([(qkv_weight, 1)], width)
-    (out_weight,) = gather_seq([(out_weight, 1)], width)
+    (conv_weight,), conv_stages = gather_seq([(conv_weight, 1)], width)
+    (qkv_weight,), qkv_stages = gather_seq([(qkv_weight, 1)], width, conv_stages)
+    (out_weight,), _ = gather_seq([(out_weight, 1)], width, (qkv_stages[1], qkv_stages[1]))
     clean = features[0]
     moved = (clean.astype(jnp.float32) + noise[0]).astype(jnp.bfloat16)
     joint = forward(

time: 163 us -> 180 us (1.10); the launches traced: 162 us -> 177 us
  waiting for transfers between devices: 60.9 us -> 26.9 us
  local copies, waits for them, and re-layouts: 26.8 us -> 58.5 us
  starting transfers between devices: 51.1 us -> 58.8 us
  other arithmetic: 7.8 us -> 12.9 us
  matrix products: 7.18 us -> 11.6 us
    ppermute x9, waiting for transfers between devices: 25.4 us -> 14.6 us  [gather_seq(): arrived = lax.ppermute(along, spread, [(i, i ^ mask) for i in range(count)])]
    all_to_all x1, waiting for transfers between devices: 7.13 us -> 0.01 us  [forward(): lax.all_to_all(jnp.concatenate([query_send, keyval_send], axis=2), 'seq',...]
    ppermute x9, waiting for transfers between devices: 6.97 us -> 0.36 us  [gather_seq(): lax.ppermute(piece, 'seq', [(i, (i + shift) % ring) for i in range(ring)])]
    ppermute x2, waiting for transfers between devices: 3.66 us -> 0.01 us  [with_halo(): lax.ppermute(head, axis, [((i + 1) % count, i) for i in range(ends)])]
    all_to_all x1, waiting for transfers between devices: 3.96 us -> 0.55 us  [forward(): lax.all_to_all(out_send, 'seq', split_axis=0, concat_axis=0, tiled=True)]
    ppermute x2, starting transfers between devices: 5.72 us -> 9.09 us  [with_halo(): lax.ppermute(tail, axis, [(i, (i + 1) % count) for i in range(ends)])]
    transpose x2, local copies, waits for them, and re-layouts: 0.52 us -> 3.13 us  [gather_seq(): block = jnp.moveaxis(block.reshape((ring,) + cells.shape), 0, dim)]
    dynamic_update_slice x9, local copies, waits for them, and re-layouts: 1.97 us -> 4.29 us  [gather_seq(): lax.dynamic_update_slice_in_dim(along, arrived[None], (place + ring - shi...]
  transfers between devices with their start and end apart: 29 -> 29, of which waited for: 16 -> 12; matrix products, arithmetic and copies ran while one was open for 17% -> 29% of each run, Pallas kernels for 0% -> 0%
where the time goes in v9:
time: 180 us; the launch traced here: 177 us
  starting transfers between devices  58.8 us (33%)
  local copies, waits for them, and re-layouts  58.5 us (32%)
  waiting for transfers between devices  26.9 us (15%)
  other arithmetic  12.9 us (7%)
  matrix products  11.6 us (6%)
  blocking collectives  6.58 us (4%)
  between operations  1.83 us (1%)
    ppermute x9, starting transfers between devices, gather_seq(): lax.ppermute(piece, 'seq', [(i, (i + shift) % ring) for i in range(ring)])  16.4 us
    ppermute x9, waiting for transfers between devices, gather_seq(): arrived = lax.ppermute(along, spread, [(i, i ^ mask) for i in range(count)])  14.6 us
    ppermute x9, starting transfers between devices, gather_seq(): arrived = lax.ppermute(along, spread, [(i, i ^ mask) for i in range(count)])  14.2 us
    ppermute x2, starting transfers between devices, with_halo(): lax.ppermute(tail, axis, [(i, (i + 1) % count) for i in range(ends)])  9.09 us
    dynamic_update_slice x9, local copies, waits for them, and re-layouts, gather_seq(): lax.dynamic_update_slice_in_dim(whole, arrived[None], lax.bitwise_xor(pla...  6.43 us
    all_to_all x1, starting transfers between devices, forward(): lax.all_to_all(out_send, 'seq', split_axis=0, concat_axis=0, tiled=True)  5.05 us
    all_to_all x1, waiting for transfers between devices, shards(): lax.all_to_all(jnp.concatenate([query_grad.reshape(devices, query_len).as...  4.76 us
    all_to_all x1, waiting for transfers between devices, shards(): lax.all_to_all(grad_send, 'seq', split_axis=0, concat_axis=1, tiled=True)  4.65 us
  transfers between devices with their start and end apart: 29, of which 12 were waited for; matrix products, arithmetic and copies ran while one was open for 29% of the time, Pallas kernels for 0%

profile of v9, /device:TPU:0, one launch (start us, length us, event | category | flops | bytes accessed | tf_op | source)
XLA Modules:
  0.0 177.1 jit_solution(4943780490904530117)
XLA Ops:
  1.7 3.1 %collective-permute-start = (bf16[120,384]{1,0:T(8,128)(2,1)S(1)}, bf16[120,384]{1,0:T(8,128)(2,1)S(1)}, u32[]{:S(2)}, u32[]{:S(2)}) collective-permute-start(bf16[120,384]{1,0:T(8,128)(2,1)S(1)} %get-tuple-element.88), channel_id=1, source_target_pairs={{0,4},{4,8},{8,12},{12,0},{1,5},{5,9},{9,13},{13,1},{2,6},{6,10},{... | collective-permute-start | bytes 276488 | tf_op jit(solution)/shard_map/ppermute | solution.py:50
  4.8 2.6 %collective-permute-start.1 = (bf16[120,384]{1,0:T(8,128)(2,1)S(1)}, bf16[120,384]{1,0:T(8,128)(2,1)S(1)}, u32[]{:S(2)}, u32[]{:S(2)}) collective-permute-start(bf16[120,384]{1,0:T(8,128)(2,1)S(1)} %get-tuple-element.88), channel_id=1, source_target_pairs={{0,8},{4,12},{8,0},{12,4},{1,9},{5,13},{9,1},{13,5},{2,10},{6,14},... | collective-permute-start | bytes 276488 | tf_op jit(solution)/shard_map/ppermute | solution.py:50
  7.4 1.3 collective-permute-start.2
  10.5 1.3 collective-permute-start.13
  11.8 4.5 %collective-permute-start.9 = (bf16[2,2,384]{2,1,0:T(2,128)(2,1)S(1)}, bf16[2,2,384]{2,1,0:T(2,128)(2,1)S(1)}, u32[]{:S(2)}, u32[]{:S(2)}) collective-permute-start(bf16[2,2,384]{2,1,0:T(2,128)(2,1)S(1)} %get-tuple-element.110), channel_id=1, source_target_pairs={{0,4},{4,8},{8,12},{1,5},{5,9},{9,13},{2,6},{6,10},{10,14},{3,7},{... | collective-permute-start | bytes 9224 | tf_op jit(solution)/shard_map/ppermute | solution.py:23
  18.6 1.6 collective-permute-start.3
  20.3 2.8 %collective-permute-start.5 = (bf16[144,384]{1,0:T(8,128)(2,1)S(1)}, bf16[144,384]{1,0:T(8,128)(2,1)S(1)}, u32[]{:S(2)}, u32[]{:S(2)}) collective-permute-start(bf16[144,384]{1,0:T(8,128)(2,1)S(1)} %constant_dynamic-slice_fusion.4), channel_id=1, source_target_pairs={{0,12},{4,0},{8,4},{12,8},{1,13},{5,1},{9,5},{13,9},{2,14},{6,2},{... | collective-permute-start | bytes 331784 | tf_op jit(solution)/shard_map/ppermute | solution.py:50
  23.2 1.5 collective-permute-start.10
  24.7 1.5 collective-permute-start.11
  26.5 2.2 %collective-permute-start.12 = (bf16[4,120,384]{2,1,0:T(8,128)(2,1)S(1)}, bf16[4,120,384]{2,1,0:T(8,128)(2,1)S(1)}, u32[]{:S(2)}, u32[]{:S(2)}) collective-permute-start(bf16[4,120,384]{2,1,0:T(8,128)(2,1)S(1)} %bitcast_dynamic-update-slice_fusion.16), channel_id=1, source_target_pairs={{0,18},{2,16},{16,2},{18,0},{1,19},{3,17},{17,3},{19,1},{4,22},{6,... | collective-permute-start | bytes 1105928 | tf_op jit(solution)/shard_map/ppermute | solution.py:63
  29.1 1.6 collective-permute-start.6
  30.6 1.5 collective-permute-start.7
  32.4 2.2 %collective-permute-done.10 = bf16[4,120,384]{2,1,0:T(8,128)(2,1)S(1)} collective-permute-done((bf16[4,120,384]{2,1,0:T(8,128)(2,1)S(1)}, bf16[4,120,384]{2,1,0:T(8,128)(2,1)S(1)}, u32[]{:S(2)}, u32[]{:S(2)}) %collective-permute-start.10) | collective-permute-done | bytes 368672 | tf_op jit(solution)/shard_map/ppermute | solution.py:63
  34.6 2.4 %collective-permute-start.8 = (bf16[4,144,384]{2,1,0:T(8,128)(2,1)S(1)}, bf16[4,144,384]{2,1,0:T(8,128)(2,1)}, u32[]{:S(2)}, u32[]{:S(2)}) collective-permute-start(bf16[4,144,384]{2,1,0:T(8,128)(2,1)S(1)} %bitcast_dynamic-update-slice_fusion.12), channel_id=1, source_target_pairs={{0,18},{2,16},{16,2},{18,0},{1,19},{3,17},{17,3},{19,1},{4,22},{6,... | collective-permute-start | bytes 1327112 | tf_op jit(solution)/shard_map/ppermute | solution.py:63
  37.2 5.9 %collective-permute-done.11 = bf16[4,120,384]{2,1,0:T(8,128)(2,1)S(1)} collective-permute-done((bf16[4,120,384]{2,1,0:T(8,128)(2,1)S(1)}, bf16[4,120,384]{2,1,0:T(8,128)(2,1)S(1)}, u32[]{:S(2)}, u32[]{:S(2)}) %collective-permute-start.11) | collective-permute-done | bytes 368672 | tf_op jit(solution)/shard_map/ppermute | solution.py:63
  44.9 1.3 fusion.23
  46.2 2.0 %reshape.243 = f32[2,64,2,384]{3,2,1,0:T(2,128)} reshape(f32[2,128,384]{2,1,0:T(8,128)} %get-tuple-element.125) | data formatting | bytes 786432 | tf_op jit(solution)/shard_map/reshape | solution.py:188
  48.1 1.6 fusion.93
  49.7 1.9 %all-gather = bf16[2,64,1,768]{3,1,0,2:T(8,128)(2,1)S(1)} all-gather(bf16[2,64,1,384]{3,1,0,2:T(8,128)(2,1)S(1)} %fusion.54), channel_id=2, replica_groups=mesh['group'=2,'seq'=4,'batch'=2,'mp'=2] {'mp'}, dimensions={3}, use_global_device_ids=true | all-gather | bytes 294912 | tf_op jit(solution)/shard_map/all_gather | solution.py:191
  53.2 5.8 %collective-permute-done.7 = bf16[4,144,384]{2,1,0:T(8,128)(2,1)} collective-permute-done((bf16[4,144,384]{2,1,0:T(8,128)(2,1)S(1)}, bf16[4,144,384]{2,1,0:T(8,128)(2,1)}, u32[]{:S(2)}, u32[]{:S(2)}) %collective-permute-start.7) | collective-permute-done | bytes 442400 | tf_op jit(solution)/shard_map/ppermute | solution.py:63
  61.8 1.3 collective-permute-start.15
  63.1 2.8 %collective-permute-start.16 = (bf16[48,384]{1,0:T(8,128)(2,1)S(1)}, bf16[48,384]{1,0:T(8,128)(2,1)}, u32[]{:S(2)}, u32[]{:S(2)}) collective-permute-start(bf16[48,384]{1,0:T(8,128)(2,1)S(1)} %constant_dynamic-slice_fusion.2), channel_id=1, source_target_pairs={{0,12},{4,0},{8,4},{12,8},{1,13},{5,1},{9,5},{13,9},{2,14},{6,2},{... | collective-permute-start | bytes 110600 | tf_op jit(solution)/shard_map/ppermute | solution.py:50
  65.9 1.7 copy.181
  73.1 3.5 %all-to-all-start = ((bf16[4,2,18432]{2,1,0:T(2,128)(2,1)}), bf16[4,2,18432]{2,1,0:T(2,128)(2,1)S(1)}, u32[]{:S(2)}, u32[]{:S(2)}) async-start(bf16[4,2,18432]{2,1,0:T(2,128)(2,1)} %pad_maximum_fusion), calls=%async_computation | async-start | bytes 589824 | tf_op jit(solution)/shard_map/all_to_all | solution.py:228
  76.6 1.4 bitcast_dynamic-update-slice_fusion.22
  77.9 1.4 bitcast_dynamic-update-slice_fusion.21
  79.3 1.4 bitcast_dynamic-update-slice_fusion.20
  80.9 1.9 %collective-permute-start.18 = (bf16[4,48,384]{2,1,0:T(8,128)(2,1)}, bf16[4,48,384]{2,1,0:T(8,128)(2,1)S(1)}, u32[]{:S(2)}, u32[]{:S(2)}) collective-permute-start(bf16[4,48,384]{2,1,0:T(8,128)(2,1)} %bitcast_dynamic-update-slice_fusion.20), channel_id=1, source_target_pairs={{0,16},{2,18},{16,0},{18,2},{1,17},{3,19},{17,1},{19,3},{4,20},{6,... | collective-permute-start | bytes 442376 | tf_op jit(solution)/shard_map/ppermute | solution.py:63
  82.8 1.4 collective-permute-start.19
  85.1 1.6 bitcast_dynamic-update-slice_fusion.10
  98.6 5.1 %all-to-all-start.1 = ((bf16[4,2,6144]{2,1,0:T(2,128)(2,1)}), bf16[4,2,6144]{2,1,0:T(2,128)(2,1)}, u32[]{:S(2)}, u32[]{:S(2)}) async-start(bf16[4,2,6144]{2,1,0:T(2,128)(2,1)} %copy.193), calls=%async_computation.1 | async-start | bytes 196608 | tf_op jit(solution)/shard_map/all_to_all | solution.py:250
  103.7 1.6 bitcast_dynamic-update-slice_fusion.11
  105.3 2.3 %reshape_reshape.16 = bf16[4,384,192]{2,1,0:T(8,128)(2,1)} reshape(bf16[4,4,48,384]{3,2,1,0:T(8,128)(2,1)} %bitcast.74) | data formatting | bytes 1179648 | tf_op jit(solution)/shard_map/reshape;reshape | solution.py:76
  107.6 1.5 copy.199
  109.6 1.7 reshape.247
  111.3 1.6 copy.194
  113.0 1.7 reshape.248
  117.2 2.2 %slice_reduce_fusion = bf16[4,12288]{1,0:T(4,128)(2,1)} fusion(bf16[2,4,18432]{2,0,1:T(2,128)(2,1)} %bitcast.267), kind=kLoop, calls=%fused_computation.84 | loop fusion | bytes 196608 | tf_op jit(solution)/shard_map/slice | solution.py:289
  119.4 1.7 squeeze.87
  122.8 2.0 %all_gather.7 = bf16[64,768]{1,0:T(8,128)(2,1)S(1)} all-gather(bf16[64,384]{1,0:T(8,128)(2,1)S(1)} %fusion.84), channel_id=1, replica_groups=mesh['group'=2,'seq'=4,'batch'=2,'mp'=2] {'mp'}, dimensions={1}, use_global_device_ids=true | all-gather | bytes 147456 | tf_op jit(solution)/shard_map/all_gather | solution.py:312
  128.9 4.6 %all-to-all-start.2 = ((bf16[4,2,3072]{2,1,0:T(2,128)(2,1)}), bf16[4,2,3072]{2,1,0:T(2,128)(2,1)S(1)}, u32[]{:S(2)}, u32[]{:S(2)}) async-start(bf16[4,2,3072]{2,1,0:T(2,128)(2,1)} %reshape.271), calls=%async_computation.2 | async-start | bytes 98304 | tf_op jit(solution)/shard_map/all_to_all | solution.py:324
  134.5 4.7 %all-to-all-done.2 = bf16[4,2,3072]{2,1,0:T(2,128)(2,1)S(1)} async-done(((bf16[4,2,3072]{2,1,0:T(2,128)(2,1)}), bf16[4,2,3072]{2,1,0:T(2,128)(2,1)S(1)}, u32[]{:S(2)}, u32[]{:S(2)}) %all-to-all-start.2) | async-done | bytes 49184 | tf_op jit(solution)/shard_map/all_to_all | solution.py:324
  146.5 3.3 %all-to-all-start.3 = ((bf16[4,2,9216]{2,1,0:T(2,128)(2,1)}), bf16[4,2,9216]{2,1,0:T(2,128)(2,1)S(1)}, u32[]{:S(2)}, u32[]{:S(2)}) async-start(bf16[4,2,9216]{2,1,0:T(2,128)(2,1)} %reshape.273), calls=%async_computation.3 | async-start | bytes 294912 | tf_op jit(solution)/shard_map/all_to_all | solution.py:335
  151.1 4.8 %all-to-all-done.3 = bf16[4,2,9216]{2,1,0:T(2,128)(2,1)S(1)} async-done(((bf16[4,2,9216]{2,1,0:T(2,128)(2,1)}), bf16[4,2,9216]{2,1,0:T(2,128)(2,1)S(1)}, u32[]{:S(2)}, u32[]{:S(2)}) %all-to-all-start.3) | async-done | bytes 147488 | tf_op jit(solution)/shard_map/all_to_all | solution.py:335
  159.0 1.5 fusion.10
  162.8 2.6 %psum.7 = f32[64]{0:T(128)S(1)} all-reduce(f32[64]{0:T(128)S(1)} %fusion.75), channel_id=1, replica_groups=mesh['group'=2,'seq'=4,'batch'=2,'mp'=2] {'mp'}, use_global_device_ids=true, to_apply=%region_7.8 | all-reduce | flops 64 | bytes 512 | tf_op jit(solution)/shard_map/psum | solution.py:373
  166.7 1.3 collective-permute-start.22
  168.3 4.5 %collective-permute-start.23 = (bf16[2,384]{1,0:T(2,128)(2,1)S(1)}, bf16[2,384]{1,0:T(2,128)(2,1)S(1)}, u32[]{:S(2)}, u32[]{:S(2)}) collective-permute-start(bf16[2,384]{1,0:T(2,128)(2,1)S(1)} %get-tuple-element.124), channel_id=1, source_target_pairs={{0,4},{4,8},{8,12},{1,5},{5,9},{9,13},{2,6},{6,10},{10,14},{3,7},{... | collective-permute-start | bytes 4616 | tf_op jit(solution)/shard_map/ppermute | solution.py:23
  (223 shorter events, 59.8 us)
Async XLA Ops:
  0.6 16.9 %copy-start = (bf16[3,192,384]{2,1,0:T(8,128)(2,1)S(1)}, bf16[3,192,384]{2,1,0:T(8,128)(2,1)}, u32[]{:S(2)}) copy-start(bf16[3,192,384]{2,1,0:T(8,128)(2,1)} %param.12) | copy-start | bytes 1327108
  0.6 17.7 %copy-start.12 = (bf16[1,128,384]{2,1,0:T(8,128)(2,1)S(1)}, bf16[1,128,384]{2,1,0:T(8,128)(2,1)}, u32[]{:S(2)}) copy-start(bf16[1,128,384]{2,1,0:T(8,128)(2,1)} %param.7) | copy-start | bytes 294916
  0.7 17.0 %copy-start.21 = (f32[768]{0:T(1024)S(1)}, f32[768]{0:T(1024)}, u32[]{:S(2)}) copy-start(f32[768]{0:T(1024)} %param.11) | copy-start | bytes 9220
  1.7 16.7 %collective-permute-start = (bf16[120,384]{1,0:T(8,128)(2,1)S(1)}, bf16[120,384]{1,0:T(8,128)(2,1)S(1)}, u32[]{:S(2)}, u32[]{:S(2)}) collective-permute-start(bf16[120,384]{1,0:T(8,128)(2,1)S(1)} %get-tuple-element.88), channel_id=1, source_target_pairs={{0,4},{4,8},{8,12},{12,0},{1,5},{5,9},{9,13},{13,1},{2,6},{6,10},{... | collective-permute-start | bytes 276488 | tf_op jit(solution)/shard_map/ppermute | solution.py:50
  4.8 13.7 %collective-permute-start.1 = (bf16[120,384]{1,0:T(8,128)(2,1)S(1)}, bf16[120,384]{1,0:T(8,128)(2,1)S(1)}, u32[]{:S(2)}, u32[]{:S(2)}) collective-permute-start(bf16[120,384]{1,0:T(8,128)(2,1)S(1)} %get-tuple-element.88), channel_id=1, source_target_pairs={{0,8},{4,12},{8,0},{12,4},{1,9},{5,13},{9,1},{13,5},{2,10},{6,14},... | collective-permute-start | bytes 276488 | tf_op jit(solution)/shard_map/ppermute | solution.py:50
  7.4 11.1 %collective-permute-start.2 = (bf16[120,384]{1,0:T(8,128)(2,1)S(1)}, bf16[120,384]{1,0:T(8,128)(2,1)S(1)}, u32[]{:S(2)}, u32[]{:S(2)}) collective-permute-start(bf16[120,384]{1,0:T(8,128)(2,1)S(1)} %get-tuple-element.88), channel_id=1, source_target_pairs={{0,12},{4,0},{8,4},{12,8},{1,13},{5,1},{9,5},{13,9},{2,14},{6,2},{... | collective-permute-start | bytes 276488 | tf_op jit(solution)/shard_map/ppermute | solution.py:50
  10.5 7.9 %collective-permute-start.13 = (bf16[2,2,384]{2,1,0:T(2,128)(2,1)S(1)}, bf16[2,2,384]{2,1,0:T(2,128)(2,1)S(1)}, u32[]{:S(2)}, u32[]{:S(2)}) collective-permute-start(bf16[2,2,384]{2,1,0:T(2,128)(2,1)S(1)} %get-tuple-element.111), channel_id=1, source_target_pairs={{4,0},{8,4},{12,8},{5,1},{9,5},{13,9},{6,2},{10,6},{14,10},{7,3},{... | collective-permute-start | bytes 9224 | tf_op jit(solution)/shard_map/ppermute | solution.py:25
  11.8 6.6 %collective-permute-start.9 = (bf16[2,2,384]{2,1,0:T(2,128)(2,1)S(1)}, bf16[2,2,384]{2,1,0:T(2,128)(2,1)S(1)}, u32[]{:S(2)}, u32[]{:S(2)}) collective-permute-start(bf16[2,2,384]{2,1,0:T(2,128)(2,1)S(1)} %get-tuple-element.110), channel_id=1, source_target_pairs={{0,4},{4,8},{8,12},{1,5},{5,9},{9,13},{2,6},{6,10},{10,14},{3,7},{... | collective-permute-start | bytes 9224 | tf_op jit(solution)/shard_map/ppermute | solution.py:23
  18.6 7.9 %collective-permute-start.3 = (bf16[144,384]{1,0:T(8,128)(2,1)S(1)}, bf16[144,384]{1,0:T(8,128)(2,1)S(1)}, u32[]{:S(2)}, u32[]{:S(2)}) collective-permute-start(bf16[144,384]{1,0:T(8,128)(2,1)S(1)} %constant_dynamic-slice_fusion.4), channel_id=1, source_target_pairs={{0,4},{4,8},{8,12},{12,0},{1,5},{5,9},{9,13},{13,1},{2,6},{6,10},{... | collective-permute-start | bytes 331784 | tf_op jit(solution)/shard_map/ppermute | solution.py:50
  20.1 8.9 %collective-permute-start.4 = (bf16[144,384]{1,0:T(8,128)(2,1)S(1)}, bf16[144,384]{1,0:T(8,128)(2,1)S(1)}, u32[]{:S(2)}, u32[]{:S(2)}) collective-permute-start(bf16[144,384]{1,0:T(8,128)(2,1)S(1)} %constant_dynamic-slice_fusion.4), channel_id=1, source_target_pairs={{0,8},{4,12},{8,0},{12,4},{1,9},{5,13},{9,1},{13,5},{2,10},{6,14},... | collective-permute-start | bytes 331784 | tf_op jit(solution)/shard_map/ppermute | solution.py:50
  20.3 8.7 %collective-permute-start.5 = (bf16[144,384]{1,0:T(8,128)(2,1)S(1)}, bf16[144,384]{1,0:T(8,128)(2,1)S(1)}, u32[]{:S(2)}, u32[]{:S(2)}) collective-permute-start(bf16[144,384]{1,0:T(8,128)(2,1)S(1)} %constant_dynamic-slice_fusion.4), channel_id=1, source_target_pairs={{0,12},{4,0},{8,4},{12,8},{1,13},{5,1},{9,5},{13,9},{2,14},{6,2},{... | collective-permute-start | bytes 331784 | tf_op jit(solution)/shard_map/ppermute | solution.py:50
  23.2 11.5 %collective-permute-start.10 = (bf16[4,120,384]{2,1,0:T(8,128)(2,1)S(1)}, bf16[4,120,384]{2,1,0:T(8,128)(2,1)S(1)}, u32[]{:S(2)}, u32[]{:S(2)}) collective-permute-start(bf16[4,120,384]{2,1,0:T(8,128)(2,1)S(1)} %bitcast_dynamic-update-slice_fusion.16), channel_id=1, source_target_pairs={{0,2},{2,0},{16,18},{18,16},{1,3},{3,1},{17,19},{19,17},{4,6},{6,4... | collective-permute-start | bytes 1105928 | tf_op jit(solution)/shard_map/ppermute | solution.py:63
  24.7 18.3 %collective-permute-start.11 = (bf16[4,120,384]{2,1,0:T(8,128)(2,1)S(1)}, bf16[4,120,384]{2,1,0:T(8,128)(2,1)S(1)}, u32[]{:S(2)}, u32[]{:S(2)}) collective-permute-start(bf16[4,120,384]{2,1,0:T(8,128)(2,1)S(1)} %bitcast_dynamic-update-slice_fusion.16), channel_id=1, source_target_pairs={{0,16},{2,18},{16,0},{18,2},{1,17},{3,19},{17,1},{19,3},{4,20},{6,... | collective-permute-start | bytes 1105928 | tf_op jit(solution)/shard_map/ppermute | solution.py:63
  26.5 17.0 %collective-permute-start.12 = (bf16[4,120,384]{2,1,0:T(8,128)(2,1)S(1)}, bf16[4,120,384]{2,1,0:T(8,128)(2,1)S(1)}, u32[]{:S(2)}, u32[]{:S(2)}) collective-permute-start(bf16[4,120,384]{2,1,0:T(8,128)(2,1)S(1)} %bitcast_dynamic-update-slice_fusion.16), channel_id=1, source_target_pairs={{0,18},{2,16},{16,2},{18,0},{1,19},{3,17},{17,3},{19,1},{4,22},{6,... | collective-permute-start | bytes 1105928 | tf_op jit(solution)/shard_map/ppermute | solution.py:63
  29.1 23.0 %collective-permute-start.6 = (bf16[4,144,384]{2,1,0:T(8,128)(2,1)S(1)}, bf16[4,144,384]{2,1,0:T(8,128)(2,1)}, u32[]{:S(2)}, u32[]{:S(2)}) collective-permute-start(bf16[4,144,384]{2,1,0:T(8,128)(2,1)S(1)} %bitcast_dynamic-update-slice_fusion.12), channel_id=1, source_target_pairs={{0,2},{2,0},{16,18},{18,16},{1,3},{3,1},{17,19},{19,17},{4,6},{6,4... | collective-permute-start | bytes 1327112 | tf_op jit(solution)/shard_map/ppermute | solution.py:63
  30.6 28.3 %collective-permute-start.7 = (bf16[4,144,384]{2,1,0:T(8,128)(2,1)S(1)}, bf16[4,144,384]{2,1,0:T(8,128)(2,1)}, u32[]{:S(2)}, u32[]{:S(2)}) collective-permute-start(bf16[4,144,384]{2,1,0:T(8,128)(2,1)S(1)} %bitcast_dynamic-update-slice_fusion.12), channel_id=1, source_target_pairs={{0,16},{2,18},{16,0},{18,2},{1,17},{3,19},{17,1},{19,3},{4,20},{6,... | collective-permute-start | bytes 1327112 | tf_op jit(solution)/shard_map/ppermute | solution.py:63
  34.6 25.4 %collective-permute-start.8 = (bf16[4,144,384]{2,1,0:T(8,128)(2,1)S(1)}, bf16[4,144,384]{2,1,0:T(8,128)(2,1)}, u32[]{:S(2)}, u32[]{:S(2)}) collective-permute-start(bf16[4,144,384]{2,1,0:T(8,128)(2,1)S(1)} %bitcast_dynamic-update-slice_fusion.12), channel_id=1, source_target_pairs={{0,18},{2,16},{16,2},{18,0},{1,19},{3,17},{17,3},{19,1},{4,22},{6,... | collective-permute-start | bytes 1327112 | tf_op jit(solution)/shard_map/ppermute | solution.py:63
  43.7 1.2 copy-start.2
  51.8 15.8 %copy-start.22 = (f32[2,64]{1,0:T(2,128)}, f32[2,64]{1,0:T(2,128)S(1)}, u32[]{:S(2)}) copy-start(f32[2,64]{1,0:T(2,128)S(1)} %add_rsqrt_fusion) | copy-start | bytes 1540
  61.2 4.7 %copy-start.1 = (bf16[4,4,144,384]{3,2,0,1:T(8,128)(2,1)}, bf16[4,4,144,384]{3,2,0,1:T(8,128)(2,1)S(1)}, u32[]{:S(2)}) copy-start(bf16[4,4,144,384]{3,2,0,1:T(8,128)(2,1)S(1)} %bitcast_dynamic-update-slice_fusion.3) | copy-start | bytes 5308420
  61.2 15.3 %collective-permute-start.14 = (bf16[48,384]{1,0:T(8,128)(2,1)S(1)}, bf16[48,384]{1,0:T(8,128)(2,1)}, u32[]{:S(2)}, u32[]{:S(2)}) collective-permute-start(bf16[48,384]{1,0:T(8,128)(2,1)S(1)} %constant_dynamic-slice_fusion.2), channel_id=1, source_target_pairs={{0,4},{4,8},{8,12},{12,0},{1,5},{5,9},{9,13},{13,1},{2,6},{6,10},{... | collective-permute-start | bytes 110600 | tf_op jit(solution)/shard_map/ppermute | solution.py:50
  61.8 16.1 %collective-permute-start.15 = (bf16[48,384]{1,0:T(8,128)(2,1)S(1)}, bf16[48,384]{1,0:T(8,128)(2,1)}, u32[]{:S(2)}, u32[]{:S(2)}) collective-permute-start(bf16[48,384]{1,0:T(8,128)(2,1)S(1)} %constant_dynamic-slice_fusion.2), channel_id=1, source_target_pairs={{0,8},{4,12},{8,0},{12,4},{1,9},{5,13},{9,1},{13,5},{2,10},{6,14},... | collective-permute-start | bytes 110600 | tf_op jit(solution)/shard_map/ppermute | solution.py:50
  63.1 16.3 %collective-permute-start.16 = (bf16[48,384]{1,0:T(8,128)(2,1)S(1)}, bf16[48,384]{1,0:T(8,128)(2,1)}, u32[]{:S(2)}, u32[]{:S(2)}) collective-permute-start(bf16[48,384]{1,0:T(8,128)(2,1)S(1)} %constant_dynamic-slice_fusion.2), channel_id=1, source_target_pairs={{0,12},{4,0},{8,4},{12,8},{1,13},{5,1},{9,5},{13,9},{2,14},{6,2},{... | collective-permute-start | bytes 110600 | tf_op jit(solution)/shard_map/ppermute | solution.py:50
  73.1 15.0 %all-to-all-start = ((bf16[4,2,18432]{2,1,0:T(2,128)(2,1)}), bf16[4,2,18432]{2,1,0:T(2,128)(2,1)S(1)}, u32[]{:S(2)}, u32[]{:S(2)}) async-start(bf16[4,2,18432]{2,1,0:T(2,128)(2,1)} %pad_maximum_fusion), calls=%async_computation | async-start | bytes 589824 | tf_op jit(solution)/shard_map/all_to_all | solution.py:228
  80.7 6.0 %collective-permute-start.17 = (bf16[4,48,384]{2,1,0:T(8,128)(2,1)}, bf16[4,48,384]{2,1,0:T(8,128)(2,1)S(1)}, u32[]{:S(2)}, u32[]{:S(2)}) collective-permute-start(bf16[4,48,384]{2,1,0:T(8,128)(2,1)} %bitcast_dynamic-update-slice_fusion.20), channel_id=1, source_target_pairs={{0,2},{2,0},{16,18},{18,16},{1,3},{3,1},{17,19},{19,17},{4,6},{6,4... | collective-permute-start | bytes 442376 | tf_op jit(solution)/shard_map/ppermute | solution.py:63
  80.9 6.5 %collective-permute-start.18 = (bf16[4,48,384]{2,1,0:T(8,128)(2,1)}, bf16[4,48,384]{2,1,0:T(8,128)(2,1)S(1)}, u32[]{:S(2)}, u32[]{:S(2)}) collective-permute-start(bf16[4,48,384]{2,1,0:T(8,128)(2,1)} %bitcast_dynamic-update-slice_fusion.20), channel_id=1, source_target_pairs={{0,16},{2,18},{16,0},{18,2},{1,17},{3,19},{17,1},{19,3},{4,20},{6,... | collective-permute-start | bytes 442376 | tf_op jit(solution)/shard_map/ppermute | solution.py:63
  82.8 20.9 %collective-permute-start.19 = (bf16[4,48,384]{2,1,0:T(8,128)(2,1)}, bf16[4,48,384]{2,1,0:T(8,128)(2,1)}, u32[]{:S(2)}, u32[]{:S(2)}) collective-permute-start(bf16[4,48,384]{2,1,0:T(8,128)(2,1)} %bitcast_dynamic-update-slice_fusion.20), channel_id=1, source_target_pairs={{0,18},{2,16},{16,2},{18,0},{1,19},{3,17},{17,3},{19,1},{4,22},{6,... | collective-permute-start | bytes 442376 | tf_op jit(solution)/shard_map/ppermute | solution.py:63
  88.1 8.3 %copy-start.8 = (bf16[4,2,18432]{2,1,0:T(2,128)(2,1)}, bf16[4,2,18432]{2,1,0:T(2,128)(2,1)S(1)}, u32[]{:S(2)}) copy-start(bf16[4,2,18432]{2,1,0:T(2,128)(2,1)S(1)} %all-to-all-done) | copy-start | bytes 884740
  96.4 11.2 %copy-start.19 = (f32[256]{0:T(256)}, f32[256]{0:T(256)S(1)}, u32[]{:S(2)}) copy-start(f32[256]{0:T(256)S(1)} %log_add_fusion) | copy-start | bytes 3076
  96.7 10.9 %copy-start.17 = (bf16[256,96]{0,1:T(8,128)(2,1)}, bf16[256,96]{0,1:T(8,128)(2,1)S(1)}, u32[]{:S(2)}) copy-start(bf16[256,96]{0,1:T(8,128)(2,1)S(1)} %convolution_convert_fusion.4) | copy-start | bytes 147460
  98.6 11.0 %all-to-all-start.1 = ((bf16[4,2,6144]{2,1,0:T(2,128)(2,1)}), bf16[4,2,6144]{2,1,0:T(2,128)(2,1)}, u32[]{:S(2)}, u32[]{:S(2)}) async-start(bf16[4,2,6144]{2,1,0:T(2,128)(2,1)} %copy.193), calls=%async_computation.1 | async-start | bytes 196608 | tf_op jit(solution)/shard_map/all_to_all | solution.py:250
  117.2 3.9 %collective-permute-start.20 = (bf16[2,64,384]{2,1,0:T(8,128)(2,1)}, bf16[2,64,384]{2,1,0:T(8,128)(2,1)}, u32[]{:S(2)}, u32[]{:S(2)}) collective-permute-start(bf16[2,64,384]{2,1,0:T(8,128)(2,1)} %constant_dynamic-slice_fusion.1), channel_id=1, source_target_pairs={{0,1},{1,0},{2,3},{3,2},{4,5},{5,4},{6,7},{7,6},{8,9},{9,8},{10,11... | collective-permute-start | bytes 294920 | tf_op jit(solution)/shard_map/ppermute | solution.py:84
  125.7 16.3 %copy-start.13 = (bf16[256,192]{1,0:T(8,128)(2,1)S(1)}, bf16[256,192]{1,0:T(8,128)(2,1)}, u32[]{:S(2)}) copy-start(bf16[256,192]{1,0:T(8,128)(2,1)} %squeeze.87) | copy-start | bytes 294916
  128.9 10.3 %all-to-all-start.2 = ((bf16[4,2,3072]{2,1,0:T(2,128)(2,1)}), bf16[4,2,3072]{2,1,0:T(2,128)(2,1)S(1)}, u32[]{:S(2)}, u32[]{:S(2)}) async-start(bf16[4,2,3072]{2,1,0:T(2,128)(2,1)} %reshape.271), calls=%async_computation.2 | async-start | bytes 98304 | tf_op jit(solution)/shard_map/all_to_all | solution.py:324
  146.5 9.3 %all-to-all-start.3 = ((bf16[4,2,9216]{2,1,0:T(2,128)(2,1)}), bf16[4,2,9216]{2,1,0:T(2,128)(2,1)S(1)}, u32[]{:S(2)}, u32[]{:S(2)}) async-start(bf16[4,2,9216]{2,1,0:T(2,128)(2,1)} %reshape.273), calls=%async_computation.3 | async-start | bytes 294912 | tf_op jit(solution)/shard_map/all_to_all | solution.py:335
  156.5 4.7 %copy-start.11 = (f32[2,128,384]{2,1,0:T(8,128)S(1)}, f32[2,128,384]{2,1,0:T(8,128)}, u32[]{:S(2)}) copy-start(f32[2,128,384]{2,1,0:T(8,128)} %get-tuple-element.126) | copy-start | bytes 1179652
  158.3 7.1 %copy-start.10 = (f32[2,64,384]{2,1,0:T(8,128)S(1)}, f32[2,64,384]{2,1,0:T(8,128)}, u32[]{:S(2)}) copy-start(f32[2,64,384]{2,1,0:T(8,128)} %copy-done.9) | copy-start | bytes 589828
  159.0 1.6 copy-start.23
  159.0 2.8 %copy-start.18 = (f32[384]{0:T(512)S(1)}, f32[384]{0:T(512)}, u32[]{:S(2)}) copy-start(f32[384]{0:T(512)} %dynamic_slice.46) | copy-start | bytes 4612
  159.0 6.4 %copy-start.24 = (f32[64]{0:T(128)S(1)}, f32[64]{0:T(128)}, u32[]{:S(2)}) copy-start(f32[64]{0:T(128)} %multiply_multiply_fusion.5) | copy-start | bytes 772
  160.5 1.3 collective-permute-start.21
  161.2 11.7 %copy-start.7 = (bf16[1,4,96,384]{3,2,0,1:T(8,128)(2,1)S(1)}, bf16[1,4,96,384]{3,2,0,1:T(8,128)(2,1)}, u32[]{:S(2)}) copy-start(bf16[1,4,96,384]{3,2,0,1:T(8,128)(2,1)} %copy-done.6) | copy-start | bytes 884740
  162.8 10.4 %copy-start.5 = (bf16[1,4,96,384]{3,2,0,1:T(8,128)(2,1)S(1)}, bf16[1,4,96,384]{3,2,0,1:T(8,128)(2,1)}, u32[]{:S(2)}) copy-start(bf16[1,4,96,384]{3,2,0,1:T(8,128)(2,1)} %copy-done.4) | copy-start | bytes 884740
  166.3 7.9 %copy-start.3 = (bf16[1,4,96,384]{3,2,0,1:T(8,128)(2,1)S(1)}, bf16[1,4,96,384]{3,2,0,1:T(8,128)(2,1)}, u32[]{:S(2)}) copy-start(bf16[1,4,96,384]{3,2,0,1:T(8,128)(2,1)} %copy-done.2) | copy-start | bytes 884740
  166.7 6.4 %collective-permute-start.22 = (bf16[2,384]{1,0:T(2,128)(2,1)S(1)}, bf16[2,384]{1,0:T(2,128)(2,1)S(1)}, u32[]{:S(2)}, u32[]{:S(2)}) collective-permute-start(bf16[2,384]{1,0:T(2,128)(2,1)S(1)} %get-tuple-element.114), channel_id=1, source_target_pairs={{4,0},{8,4},{12,8},{5,1},{9,5},{13,9},{6,2},{10,6},{14,10},{7,3},{... | collective-permute-start | bytes 4616 | tf_op jit(solution)/shard_map/ppermute | solution.py:25
  168.3 5.8 %collective-permute-start.23 = (bf16[2,384]{1,0:T(2,128)(2,1)S(1)}, bf16[2,384]{1,0:T(2,128)(2,1)S(1)}, u32[]{:S(2)}, u32[]{:S(2)}) collective-permute-start(bf16[2,384]{1,0:T(2,128)(2,1)S(1)} %get-tuple-element.124), channel_id=1, source_target_pairs={{0,4},{4,8},{8,12},{1,5},{5,9},{9,13},{2,6},{6,10},{10,14},{3,7},{... | collective-permute-start | bytes 4616 | tf_op jit(solution)/shard_map/ppermute | solution.py:23
  173.1 3.3 %copy-start.15 = (f32[1,128,384]{2,1,0:T(8,128)S(1)}, f32[1,128,384]{2,1,0:T(8,128)}, u32[]{:S(2)}) copy-start(f32[1,128,384]{2,1,0:T(8,128)} %param.8) | copy-start | bytes 589828
  174.9 1.4 collective-permute-start.24
  (6 other events, 5.2 us)

commit v10 on v9

--- a/solution.py
+++ b/solution.py
@@ -27,6 +27,45 @@
             axis=dim,
         )
     return cells
+
+
+def gather_blocks(cells, dim, after=(None, None)):
+    spread = ("group", "batch")
+    count = lax.axis_size("group") * lax.axis_size("batch")
+    ring = lax.axis_size("seq")
+    last = dim == cells.ndim - 1
+    split = 0 if last else dim
+    size = cells.shape[split] // count
+    piece = lax.dynamic_slice_in_dim(cells, lax.axis_index(spread) * size, size, split)
+    if after[0] is not None:
+        piece = lax.optimization_barrier((piece, after[0]))[0]
+    slot = cells.ndim - 1 if last else dim
+    piece = jnp.expand_dims(piece, slot)
+    along = jnp.zeros(piece.shape[:slot] + (ring,) + piece.shape[slot + 1 :], cells.dtype)
+
+    def place(block, target, axis, index):
+        start = [0] * target.ndim
+        start[axis] = index
+        return lax.dynamic_update_slice(target, block, start)
+
+    seq_at = lax.axis_index("seq")
+    along = place(piece, along, slot, seq_at)
+    for shift in range(1, ring):
+        arrived = lax.ppermute(piece, "seq", [(i, (i + shift) % ring) for i in range(ring)])
+        along = place(arrived, along, slot, (seq_at + ring - shift) % ring)
+    if after[1] is not None:
+        along = lax.optimization_barrier((along, after[1]))[0]
+    lane = 0 if last else dim + 1
+    along = jnp.expand_dims(along, lane)
+    whole = jnp.zeros(along.shape[:lane] + (count,) + along.shape[lane + 1 :], cells.dtype)
+    gb_at = lax.axis_index(spread)
+    whole = place(along, whole, lane, gb_at)
+    for mask in range(1, count):
+        arrived = lax.ppermute(along, spread, [(i, i ^ mask) for i in range(count)])
+        whole = place(arrived, whole, lane, lax.bitwise_xor(gb_at, mask))
+    shape = list(cells.shape)
+    shape[dim] = shape[dim] * ring
+    return whole.reshape(shape), (along, whole)
 
 
 def gather_seq(parts, width, after=(None, None)):
@@ -277,9 +316,21 @@
 
 def shards(features, noise, conv_weight, conv_bias, norm_gain, qkv_weight, out_weight):
     width = conv_weight.shape[-1]
-    (conv_weight,), conv_stages = gather_seq([(conv_weight, 1)], width)
-    (qkv_weight,), qkv_stages = gather_seq([(qkv_weight, 1)], width, conv_stages)
-    (out_weight,), _ = gather_seq([(out_weight, 1)], width, (qkv_stages[1], qkv_stages[1]))
+    direct = (
+        lax.axis_size("seq") <= 8
+        and lax.axis_size("group") * lax.axis_size("batch") <= 4
+        and conv_weight.shape[1] % (4 * lax.axis_size("group") * lax.axis_size("batch")) == 0
+        and qkv_weight.shape[1] % (4 * lax.axis_size("group") * lax.axis_size("batch")) == 0
+        and out_weight.shape[0] % (4 * lax.axis_size("group") * lax.axis_size("batch")) == 0
+    )
+    if direct:
+        conv_weight, _ = gather_blocks(conv_weight, 1)
+        qkv_weight, _ = gather_blocks(qkv_weight, 1)
+        out_weight, _ = gather_blocks(out_weight, 1)
+    else:
+        (conv_weight,), _ = gather_seq([(conv_weight, 1)], width)
+        (qkv_weight,), _ = gather_seq([(qkv_weight, 1)], width)
+        (out_weight,), _ = gather_seq([(out_weight, 1)], width)
     clean = features[0]
     moved = (clean.astype(jnp.float32) + noise[0]).astype(jnp.bfloat16)
     joint = forward(

time: 180 us -> 187 us (1.039)
  waiting for transfers between devices: 26.9 us -> 41.5 us
  starting transfers between devices: 58.8 us -> 54.1 us
  other arithmetic: 12.9 us -> 8.65 us
    ppermute x18, waiting for transfers between devices: 15 us -> 25.3 us  [the longest x9 18.6 us: gather_blocks(): arrived = lax.ppermute(along, spread, [(i, i ^ mask) for i in range(count)])]
    dynamic_update_slice x24, local copies, waits for them, and re-layouts: 14.1 us -> 22.2 us  [place(): return lax.dynamic_update_slice(target, block, start)]
    ppermute x2, waiting for transfers between devices: 0.01 us -> 3.42 us  [with_halo(): lax.ppermute(head, axis, [((i + 1) % count, i) for i in range(ends)])]
    ppermute x2, starting transfers between devices: 9.09 us -> 5.8 us  [with_halo(): lax.ppermute(tail, axis, [(i, (i + 1) % count) for i in range(ends)])]
    transpose x2 -> x0, local copies, waits for them, and re-layouts: 3.13 us -> none  [gather_seq(): block = jnp.moveaxis(block.reshape((ring,) + cells.shape), 0, dim)]
    reshape x1 -> x2, local copies, waits for them, and re-layouts: 0.15 us -> 3.08 us  [gather_blocks(): return (whole.reshape(shape), (along, whole))]
    slice x2, local copies, waits for them, and re-layouts: 0.97 us -> 3.5 us  [forward(): both_in[:, :, query_len:].reshape(pass_count, devices * rows, 2 * head_size)]
    another operation x1 -> x0, local copies, waits for them, and re-layouts: 2.29 us -> none  [gather_seq(): block = jnp.moveaxis(block.reshape((ring,) + cells.shape), 0, dim)]
  transfers between devices with their start and end apart: 29 -> 29, of which waited for: 12 -> 14; matrix products, arithmetic and copies ran while one was open for 29% -> 32% of each run, Pallas kernels for 0% -> 0%
where the time goes in v10:
time: 187 us; the launch traced here: 185 us
  local copies, waits for them, and re-layouts  59.8 us (32%)
  starting transfers between devices  54.1 us (29%)
  waiting for transfers between devices  41.5 us (22%)
  matrix products  12.6 us (7%)
  other arithmetic  8.65 us (5%)
  blocking collectives  6.58 us (4%)
  between operations  1.9 us (1%)
    dynamic_update_slice x24, local copies, waits for them, and re-layouts, place(): return lax.dynamic_update_slice(target, block, start)  22.2 us
    ppermute x9, waiting for transfers between devices, gather_blocks(): arrived = lax.ppermute(along, spread, [(i, i ^ mask) for i in range(count)])  18.6 us
    ppermute x9, starting transfers between devices, gather_blocks(): lax.ppermute(piece, 'seq', [(i, (i + shift) % ring) for i in range(ring)])  17.1 us
    ppermute x9, starting transfers between devices, gather_blocks(): arrived = lax.ppermute(along, spread, [(i, i ^ mask) for i in range(count)])  12.6 us
    ppermute x9, waiting for transfers between devices, gather_blocks(): lax.ppermute(piece, 'seq', [(i, (i + shift) % ring) for i in range(ring)])  6.71 us
    ppermute x2, starting transfers between devices, with_halo(): lax.ppermute(tail, axis, [(i, (i + 1) % count) for i in range(ends)])  5.8 us
    all_to_all x1, waiting for transfers between devices, shards(): lax.all_to_all(jnp.concatenate([query_grad.reshape(devices, query_len).as...  5.72 us
    all_to_all x1, waiting for transfers between devices, shards(): lax.all_to_all(grad_send, 'seq', split_axis=0, concat_axis=1, tiled=True)  4.65 us
  transfers between devices with their start and end apart: 29, of which 14 were waited for; matrix products, arithmetic and copies ran while one was open for 32% of the time, Pallas kernels for 0%

profile of v10, /device:TPU:0, one launch (start us, length us, event | category | flops | bytes accessed | tf_op | source)
XLA Modules:
  0.0 185.2 jit_solution(10537389086985586629)
XLA Ops:
  1.6 3.1 %collective-permute-start = (bf16[3,1,48,384]{3,2,0,1:T(8,128)(2,1)S(1)}, bf16[3,1,48,384]{3,2,0,1:T(8,128)(2,1)S(1)}, u32[]{:S(2)}, u32[]{:S(2)}) collective-permute-start(bf16[3,1,48,384]{3,2,0,1:T(8,128)(2,1)S(1)} %dynamic-slice_bitcast_fusion), channel_id=1, source_target_pairs={{0,4},{4,8},{8,12},{12,0},{1,5},{5,9},{9,13},{13,1},{2,6},{6,10},{... | collective-permute-start | bytes 331784 | tf_op jit(solution)/shard_map/ppermute | solution.py:54
  4.7 2.6 %collective-permute-start.1 = (bf16[3,1,48,384]{3,2,0,1:T(8,128)(2,1)S(1)}, bf16[3,1,48,384]{3,2,0,1:T(8,128)(2,1)S(1)}, u32[]{:S(2)}, u32[]{:S(2)}) collective-permute-start(bf16[3,1,48,384]{3,2,0,1:T(8,128)(2,1)S(1)} %dynamic-slice_bitcast_fusion), channel_id=1, source_target_pairs={{0,8},{4,12},{8,0},{12,4},{1,9},{5,13},{9,1},{13,5},{2,10},{6,14},... | collective-permute-start | bytes 331784 | tf_op jit(solution)/shard_map/ppermute | solution.py:54
  7.3 1.3 collective-permute-start.2
  10.4 2.6 %collective-permute-start.6 = (bf16[2,2,384]{2,1,0:T(2,128)(2,1)S(1)}, bf16[2,2,384]{2,1,0:T(2,128)(2,1)S(1)}, u32[]{:S(2)}, u32[]{:S(2)}) collective-permute-start(bf16[2,2,384]{2,1,0:T(2,128)(2,1)S(1)} %get-tuple-element.93), channel_id=1, source_target_pairs={{0,4},{4,8},{8,12},{1,5},{5,9},{9,13},{2,6},{6,10},{10,14},{3,7},{... | collective-permute-start | bytes 9224 | tf_op jit(solution)/shard_map/ppermute | solution.py:23
  13.0 1.3 collective-permute-start.13
  17.2 2.7 %collective-permute-start.7 = (bf16[5,1,24,384]{3,2,0,1:T(8,128)(2,1)S(1)}, bf16[5,1,24,384]{3,2,0,1:T(8,128)(2,1)S(1)}, u32[]{:S(2)}, u32[]{:S(2)}) collective-permute-start(bf16[5,1,24,384]{3,2,0,1:T(8,128)(2,1)S(1)} %dynamic-slice_bitcast_fusion.1), channel_id=1, source_target_pairs={{0,4},{4,8},{8,12},{12,0},{1,5},{5,9},{9,13},{13,1},{2,6},{6,10},{... | collective-permute-start | bytes 276488 | tf_op jit(solution)/shard_map/ppermute | solution.py:54
  20.3 3.3 %collective-permute-done.7 = bf16[5,1,24,384]{3,2,0,1:T(8,128)(2,1)S(1)} collective-permute-done((bf16[5,1,24,384]{3,2,0,1:T(8,128)(2,1)S(1)}, bf16[5,1,24,384]{3,2,0,1:T(8,128)(2,1)S(1)}, u32[]{:S(2)}, u32[]{:S(2)}) %collective-permute-start.7) | collective-permute-done | bytes 92192 | tf_op jit(solution)/shard_map/ppermute | solution.py:54
  24.9 2.3 %collective-permute-done.8 = bf16[5,1,24,384]{3,2,0,1:T(8,128)(2,1)S(1)} collective-permute-done((bf16[5,1,24,384]{3,2,0,1:T(8,128)(2,1)S(1)}, bf16[5,1,24,384]{3,2,0,1:T(8,128)(2,1)S(1)}, u32[]{:S(2)}, u32[]{:S(2)}) %collective-permute-start.8) | collective-permute-done | bytes 92192 | tf_op jit(solution)/shard_map/ppermute | solution.py:54
  28.2 1.6 collective-permute-start.10
  29.8 1.5 collective-permute-start.11
  32.2 1.6 collective-permute-start.3
  33.8 1.5 collective-permute-start.4
  35.6 4.2 %collective-permute-done.10 = bf16[5,4,1,24,384]{4,3,2,1,0:T(8,128)(2,1)S(1)} collective-permute-done((bf16[5,4,1,24,384]{4,3,2,1,0:T(8,128)(2,1)S(1)}, bf16[5,4,1,24,384]{4,3,2,1,0:T(8,128)(2,1)S(1)}, u32[]{:S(2)}, u32[]{:S(2)}) %collective-permute-start.10) | collective-permute-done | bytes 368672 | tf_op jit(solution)/shard_map/ppermute | solution.py:64
  39.8 2.4 %collective-permute-start.5 = (bf16[3,4,1,48,384]{4,3,2,1,0:T(8,128)(2,1)S(1)}, bf16[3,4,1,48,384]{4,3,2,1,0:T(8,128)(2,1)}, u32[]{:S(2)}, u32[]{:S(2)}) collective-permute-start(bf16[3,4,1,48,384]{4,3,2,1,0:T(8,128)(2,1)S(1)} %bitcast_dynamic-update-slice_fusion), channel_id=1, source_target_pairs={{0,18},{2,16},{16,2},{18,0},{1,19},{3,17},{17,3},{19,1},{4,22},{6,... | collective-permute-start | bytes 1327112 | tf_op jit(solution)/shard_map/ppermute | solution.py:64
  42.3 6.9 %collective-permute-done.11 = bf16[5,4,1,24,384]{4,3,2,1,0:T(8,128)(2,1)S(1)} collective-permute-done((bf16[5,4,1,24,384]{4,3,2,1,0:T(8,128)(2,1)S(1)}, bf16[5,4,1,24,384]{4,3,2,1,0:T(8,128)(2,1)S(1)}, u32[]{:S(2)}, u32[]{:S(2)}) %collective-permute-start.11) | collective-permute-done | bytes 368672 | tf_op jit(solution)/shard_map/ppermute | solution.py:64
  52.8 1.5 fusion.97
  54.3 1.9 %all-gather = bf16[2,64,1,768]{3,1,0,2:T(8,128)(2,1)S(1)} all-gather(bf16[2,64,1,384]{3,1,0,2:T(8,128)(2,1)S(1)} %fusion.57), channel_id=2, replica_groups=mesh['group'=2,'seq'=4,'batch'=2,'mp'=2] {'mp'}, dimensions={3}, use_global_device_ids=true | all-gather | bytes 294912 | tf_op jit(solution)/shard_map/all_gather | solution.py:230
  58.4 6.0 %collective-permute-done.4 = bf16[3,4,1,48,384]{4,3,2,1,0:T(8,128)(2,1)} collective-permute-done((bf16[3,4,1,48,384]{4,3,2,1,0:T(8,128)(2,1)S(1)}, bf16[3,4,1,48,384]{4,3,2,1,0:T(8,128)(2,1)}, u32[]{:S(2)}, u32[]{:S(2)}) %collective-permute-start.4) | collective-permute-done | bytes 442400 | tf_op jit(solution)/shard_map/ppermute | solution.py:64
  69.3 4.1 %all-to-all-start = ((bf16[4,2,18432]{2,1,0:T(2,128)(2,1)}), bf16[4,2,18432]{2,1,0:T(2,128)(2,1)}, u32[]{:S(2)}, u32[]{:S(2)}) async-start(bf16[4,2,18432]{2,1,0:T(2,128)(2,1)} %pad_maximum_fusion), calls=%async_computation | async-start | bytes 589824 | tf_op jit(solution)/shard_map/all_to_all | solution.py:267
  73.6 2.1 %collective-permute-start.14 = (bf16[96,1,192]{2,0,1:T(8,128)(2,1)S(1)}, bf16[96,1,192]{2,0,1:T(8,128)(2,1)S(1)}, u32[]{:S(2)}, u32[]{:S(2)}) collective-permute-start(bf16[96,1,192]{2,0,1:T(8,128)(2,1)S(1)} %bitcast.209), channel_id=1, source_target_pairs={{0,4},{4,8},{8,12},{12,0},{1,5},{5,9},{9,13},{13,1},{2,6},{6,10},{... | collective-permute-start | bytes 110600 | tf_op jit(solution)/shard_map/ppermute | solution.py:54
  75.7 2.3 %collective-permute-start.15 = (bf16[96,1,192]{2,0,1:T(8,128)(2,1)S(1)}, bf16[96,1,192]{2,0,1:T(8,128)(2,1)S(1)}, u32[]{:S(2)}, u32[]{:S(2)}) collective-permute-start(bf16[96,1,192]{2,0,1:T(8,128)(2,1)S(1)} %bitcast.210), channel_id=1, source_target_pairs={{0,8},{4,12},{8,0},{12,4},{1,9},{5,13},{9,1},{13,5},{2,10},{6,14},... | collective-permute-start | bytes 110600 | tf_op jit(solution)/shard_map/ppermute | solution.py:54
  78.0 1.5 collective-permute-start.16
  80.3 3.1 %dynamic_update_slice.103 = bf16[1,96,4,192]{3,2,1,0:T(4,128)(2,1)} dynamic-update-slice(bf16[1,96,4,192]{3,2,1,0:T(4,128)(2,1)} %broadcast_in_dim.102, bf16[1,96,1,192]{3,2,1,0:T(2,128)(2,1)S(1)} %copy.164, s32[]{:T(128)} %constant.152.clone.1, s32[]{:T(128)} %constant.152.clone.1, s32[]{:T(128)S(6)} %select_n.86, s32[]{:T(128)} %constant.152.clone.1) | dynamic-update-slice | bytes 73732 | tf_op jit(solution)/shard_map/dynamic_update_slice | solution.py:49
  83.7 3.1 %dynamic_update_slice.104 = bf16[1,96,4,192]{3,2,1,0:T(4,128)(2,1)} dynamic-update-slice(bf16[1,96,4,192]{3,2,1,0:T(4,128)(2,1)} %dynamic_update_slice.103, bf16[1,96,1,192]{3,2,1,0:T(2,128)(2,1)S(1)} %copy.165, s32[]{:T(128)} %constant.152.clone.1, s32[]{:T(128)} %constant.152.clone.1, s32[]{:T(128)S(6)} %select_n.88, s32[]{:T(128)} %constant.152.clone.1) | dynamic-update-slice | bytes 73732 | tf_op jit(solution)/shard_map/dynamic_update_slice | solution.py:49
  86.8 3.1 %dynamic_update_slice.105 = bf16[1,96,4,192]{3,2,1,0:T(4,128)(2,1)} dynamic-update-slice(bf16[1,96,4,192]{3,2,1,0:T(4,128)(2,1)} %dynamic_update_slice.104, bf16[1,96,1,192]{3,2,1,0:T(2,128)(2,1)S(1)} %copy.166, s32[]{:T(128)} %constant.152.clone.1, s32[]{:T(128)} %constant.152.clone.1, s32[]{:T(128)S(6)} %select_n.90, s32[]{:T(128)} %constant.152.clone.1) | dynamic-update-slice | bytes 73732 | tf_op jit(solution)/shard_map/dynamic_update_slice | solution.py:49
  90.0 3.1 %dynamic_update_slice.106 = bf16[1,96,4,192]{3,2,1,0:T(4,128)(2,1)} dynamic-update-slice(bf16[1,96,4,192]{3,2,1,0:T(4,128)(2,1)} %dynamic_update_slice.105, bf16[1,96,1,192]{3,2,1,0:T(2,128)(2,1)S(1)} %copy.167, s32[]{:T(128)} %constant.152.clone.1, s32[]{:T(128)} %constant.152.clone.1, s32[]{:T(128)S(6)} %select_n.92, s32[]{:T(128)} %constant.152.clone.1) | dynamic-update-slice | bytes 73732 | tf_op jit(solution)/shard_map/dynamic_update_slice | solution.py:49
  94.1 1.7 collective-permute-start.18
  95.8 1.4 collective-permute-start.19
  100.1 1.4 slice_reduce_fusion.2
  101.5 1.7 slice.210
  103.4 1.8 copy.158
  105.2 1.9 %reshape.258 = bf16[2,256,192]{2,1,0:T(8,128)(2,1)} reshape(bf16[2,4,12288]{2,1,0:T(4,128)(2,1)} %copy.158) | data formatting | bytes 393216 | tf_op jit(solution)/shard_map/reshape | solution.py:275
  110.7 1.6 stack.21
  118.8 3.9 %all-to-all-start.1 = ((bf16[4,2,6144]{2,1,0:T(2,128)(2,1)}), bf16[4,2,6144]{2,1,0:T(2,128)(2,1)}, u32[]{:S(2)}, u32[]{:S(2)}) async-start(bf16[4,2,6144]{2,1,0:T(2,128)(2,1)} %copy.161), calls=%async_computation.1 | async-start | bytes 196608 | tf_op jit(solution)/shard_map/all_to_all | solution.py:289
  124.7 1.6 reshape.275
  126.3 1.5 reshape.261
  130.4 1.7 reshape.260
  132.1 1.4 convolution_convert_fusion.1
  134.2 2.2 %slice_reduce_fusion = bf16[4,12288]{1,0:T(4,128)(2,1)} fusion(bf16[2,4,18432]{2,0,1:T(2,128)(2,1)} %bitcast.33), kind=kLoop, calls=%fused_computation.76 | loop fusion | bytes 196608 | tf_op jit(solution)/shard_map/slice | solution.py:340
  136.4 1.7 squeeze.87
  139.1 2.0 %all_gather.7 = bf16[64,768]{1,0:T(8,128)(2,1)S(1)} all-gather(bf16[64,384]{1,0:T(8,128)(2,1)S(1)} %fusion.88), channel_id=1, replica_groups=mesh['group'=2,'seq'=4,'batch'=2,'mp'=2] {'mp'}, dimensions={1}, use_global_device_ids=true | all-gather | bytes 147456 | tf_op jit(solution)/shard_map/all_gather | solution.py:363
  143.8 4.4 %all-to-all-start.2 = ((bf16[4,2,3072]{2,1,0:T(2,128)(2,1)}), bf16[4,2,3072]{2,1,0:T(2,128)(2,1)S(1)}, u32[]{:S(2)}, u32[]{:S(2)}) async-start(bf16[4,2,3072]{2,1,0:T(2,128)(2,1)} %reshape.282), calls=%async_computation.2 | async-start | bytes 98304 | tf_op jit(solution)/shard_map/all_to_all | solution.py:375
  149.2 4.7 %all-to-all-done.2 = bf16[4,2,3072]{2,1,0:T(2,128)(2,1)S(1)} async-done(((bf16[4,2,3072]{2,1,0:T(2,128)(2,1)}), bf16[4,2,3072]{2,1,0:T(2,128)(2,1)S(1)}, u32[]{:S(2)}, u32[]{:S(2)}) %all-to-all-start.2) | async-done | bytes 49184 | tf_op jit(solution)/shard_map/all_to_all | solution.py:375
  157.6 3.6 %all-to-all-start.3 = ((bf16[4,2,9216]{2,1,0:T(2,128)(2,1)}), bf16[4,2,9216]{2,1,0:T(2,128)(2,1)S(1)}, u32[]{:S(2)}, u32[]{:S(2)}) async-start(bf16[4,2,9216]{2,1,0:T(2,128)(2,1)} %reshape.284), calls=%async_computation.3 | async-start | bytes 294912 | tf_op jit(solution)/shard_map/all_to_all | solution.py:386
  161.2 5.7 %all-to-all-done.3 = bf16[4,2,9216]{2,1,0:T(2,128)(2,1)S(1)} async-done(((bf16[4,2,9216]{2,1,0:T(2,128)(2,1)}), bf16[4,2,9216]{2,1,0:T(2,128)(2,1)S(1)}, u32[]{:S(2)}, u32[]{:S(2)}) %all-to-all-start.3) | async-done | bytes 147488 | tf_op jit(solution)/shard_map/all_to_all | solution.py:386
  170.3 2.6 %psum.7 = f32[64]{0:T(128)S(1)} all-reduce(f32[64]{0:T(128)S(1)} %fusion.79), channel_id=1, replica_groups=mesh['group'=2,'seq'=4,'batch'=2,'mp'=2] {'mp'}, use_global_device_ids=true, to_apply=%region_7.8 | all-reduce | flops 64 | bytes 512 | tf_op jit(solution)/shard_map/psum | solution.py:424
  173.4 3.2 %collective-permute-start.23 = (bf16[2,384]{1,0:T(2,128)(2,1)S(1)}, bf16[2,384]{1,0:T(2,128)(2,1)S(1)}, u32[]{:S(2)}, u32[]{:S(2)}) collective-permute-start(bf16[2,384]{1,0:T(2,128)(2,1)S(1)} %get-tuple-element.107), channel_id=1, source_target_pairs={{0,4},{4,8},{8,12},{1,5},{5,9},{9,13},{2,6},{6,10},{10,14},{3,7},{... | collective-permute-start | bytes 4616 | tf_op jit(solution)/shard_map/ppermute | solution.py:23
  179.0 3.4 %collective-permute-done.22 = bf16[2,384]{1,0:T(2,128)(2,1)S(1)} collective-permute-done((bf16[2,384]{1,0:T(2,128)(2,1)S(1)}, bf16[2,384]{1,0:T(2,128)(2,1)S(1)}, u32[]{:S(2)}, u32[]{:S(2)}) %collective-permute-start.22) | collective-permute-done | bytes 1568 | tf_op jit(solution)/shard_map/ppermute | solution.py:25
  (214 shorter events, 57.3 us)
Async XLA Ops:
  0.6 72.8 %copy-start = (bf16[384,192]{0,1:T(8,128)(2,1)S(1)}, bf16[384,192]{0,1:T(8,128)(2,1)}, u32[]{:S(2)}) copy-start(bf16[384,192]{0,1:T(8,128)(2,1)} %param.13) | copy-start | bytes 442372
  0.6 19.6 %copy-start.9 = (bf16[1,128,384]{2,1,0:T(8,128)(2,1)S(1)}, bf16[1,128,384]{2,1,0:T(8,128)(2,1)}, u32[]{:S(2)}) copy-start(bf16[1,128,384]{2,1,0:T(8,128)(2,1)} %param.7) | copy-start | bytes 294916
  1.6 29.9 %collective-permute-start = (bf16[3,1,48,384]{3,2,0,1:T(8,128)(2,1)S(1)}, bf16[3,1,48,384]{3,2,0,1:T(8,128)(2,1)S(1)}, u32[]{:S(2)}, u32[]{:S(2)}) collective-permute-start(bf16[3,1,48,384]{3,2,0,1:T(8,128)(2,1)S(1)} %dynamic-slice_bitcast_fusion), channel_id=1, source_target_pairs={{0,4},{4,8},{8,12},{12,0},{1,5},{5,9},{9,13},{13,1},{2,6},{6,10},{... | collective-permute-start | bytes 331784 | tf_op jit(solution)/shard_map/ppermute | solution.py:54
  4.7 27.4 %collective-permute-start.1 = (bf16[3,1,48,384]{3,2,0,1:T(8,128)(2,1)S(1)}, bf16[3,1,48,384]{3,2,0,1:T(8,128)(2,1)S(1)}, u32[]{:S(2)}, u32[]{:S(2)}) collective-permute-start(bf16[3,1,48,384]{3,2,0,1:T(8,128)(2,1)S(1)} %dynamic-slice_bitcast_fusion), channel_id=1, source_target_pairs={{0,8},{4,12},{8,0},{12,4},{1,9},{5,13},{9,1},{13,5},{2,10},{6,14},... | collective-permute-start | bytes 331784 | tf_op jit(solution)/shard_map/ppermute | solution.py:54
  7.3 24.8 %collective-permute-start.2 = (bf16[3,1,48,384]{3,2,0,1:T(8,128)(2,1)S(1)}, bf16[3,1,48,384]{3,2,0,1:T(8,128)(2,1)S(1)}, u32[]{:S(2)}, u32[]{:S(2)}) collective-permute-start(bf16[3,1,48,384]{3,2,0,1:T(8,128)(2,1)S(1)} %dynamic-slice_bitcast_fusion), channel_id=1, source_target_pairs={{0,12},{4,0},{8,4},{12,8},{1,13},{5,1},{9,5},{13,9},{2,14},{6,2},{... | collective-permute-start | bytes 331784 | tf_op jit(solution)/shard_map/ppermute | solution.py:54
  10.4 6.8 %collective-permute-start.6 = (bf16[2,2,384]{2,1,0:T(2,128)(2,1)S(1)}, bf16[2,2,384]{2,1,0:T(2,128)(2,1)S(1)}, u32[]{:S(2)}, u32[]{:S(2)}) collective-permute-start(bf16[2,2,384]{2,1,0:T(2,128)(2,1)S(1)} %get-tuple-element.93), channel_id=1, source_target_pairs={{0,4},{4,8},{8,12},{1,5},{5,9},{9,13},{2,6},{6,10},{10,14},{3,7},{... | collective-permute-start | bytes 9224 | tf_op jit(solution)/shard_map/ppermute | solution.py:23
  13.0 6.9 %collective-permute-start.13 = (bf16[2,2,384]{2,1,0:T(2,128)(2,1)S(1)}, bf16[2,2,384]{2,1,0:T(2,128)(2,1)S(1)}, u32[]{:S(2)}, u32[]{:S(2)}) collective-permute-start(bf16[2,2,384]{2,1,0:T(2,128)(2,1)S(1)} %get-tuple-element.94), channel_id=1, source_target_pairs={{4,0},{8,4},{12,8},{5,1},{9,5},{13,9},{6,2},{10,6},{14,10},{7,3},{... | collective-permute-start | bytes 9224 | tf_op jit(solution)/shard_map/ppermute | solution.py:25
  17.2 6.4 %collective-permute-start.7 = (bf16[5,1,24,384]{3,2,0,1:T(8,128)(2,1)S(1)}, bf16[5,1,24,384]{3,2,0,1:T(8,128)(2,1)S(1)}, u32[]{:S(2)}, u32[]{:S(2)}) collective-permute-start(bf16[5,1,24,384]{3,2,0,1:T(8,128)(2,1)S(1)} %dynamic-slice_bitcast_fusion.1), channel_id=1, source_target_pairs={{0,4},{4,8},{8,12},{12,0},{1,5},{5,9},{9,13},{13,1},{2,6},{6,10},{... | collective-permute-start | bytes 276488 | tf_op jit(solution)/shard_map/ppermute | solution.py:54
  19.9 7.2 %collective-permute-start.8 = (bf16[5,1,24,384]{3,2,0,1:T(8,128)(2,1)S(1)}, bf16[5,1,24,384]{3,2,0,1:T(8,128)(2,1)S(1)}, u32[]{:S(2)}, u32[]{:S(2)}) collective-permute-start(bf16[5,1,24,384]{3,2,0,1:T(8,128)(2,1)S(1)} %dynamic-slice_bitcast_fusion.1), channel_id=1, source_target_pairs={{0,8},{4,12},{8,0},{12,4},{1,9},{5,13},{9,1},{13,5},{2,10},{6,14},... | collective-permute-start | bytes 276488 | tf_op jit(solution)/shard_map/ppermute | solution.py:54
  23.7 4.6 %collective-permute-start.9 = (bf16[5,1,24,384]{3,2,0,1:T(8,128)(2,1)S(1)}, bf16[5,1,24,384]{3,2,0,1:T(8,128)(2,1)S(1)}, u32[]{:S(2)}, u32[]{:S(2)}) collective-permute-start(bf16[5,1,24,384]{3,2,0,1:T(8,128)(2,1)S(1)} %dynamic-slice_bitcast_fusion.1), channel_id=1, source_target_pairs={{0,12},{4,0},{8,4},{12,8},{1,13},{5,1},{9,5},{13,9},{2,14},{6,2},{... | collective-permute-start | bytes 276488 | tf_op jit(solution)/shard_map/ppermute | solution.py:54
  28.2 11.5 %collective-permute-start.10 = (bf16[5,4,1,24,384]{4,3,2,1,0:T(8,128)(2,1)S(1)}, bf16[5,4,1,24,384]{4,3,2,1,0:T(8,128)(2,1)S(1)}, u32[]{:S(2)}, u32[]{:S(2)}) collective-permute-start(bf16[5,4,1,24,384]{4,3,2,1,0:T(8,128)(2,1)S(1)} %bitcast_dynamic-update-slice_fusion.6), channel_id=1, source_target_pairs={{0,2},{2,0},{16,18},{18,16},{1,3},{3,1},{17,19},{19,17},{4,6},{6,4... | collective-permute-start | bytes 1105928 | tf_op jit(solution)/shard_map/ppermute | solution.py:64
  29.8 19.4 %collective-permute-start.11 = (bf16[5,4,1,24,384]{4,3,2,1,0:T(8,128)(2,1)S(1)}, bf16[5,4,1,24,384]{4,3,2,1,0:T(8,128)(2,1)S(1)}, u32[]{:S(2)}, u32[]{:S(2)}) collective-permute-start(bf16[5,4,1,24,384]{4,3,2,1,0:T(8,128)(2,1)S(1)} %bitcast_dynamic-update-slice_fusion.6), channel_id=1, source_target_pairs={{0,16},{2,18},{16,0},{18,2},{1,17},{3,19},{17,1},{19,3},{4,20},{6,... | collective-permute-start | bytes 1105928 | tf_op jit(solution)/shard_map/ppermute | solution.py:64
  31.6 17.7 %collective-permute-start.12 = (bf16[5,4,1,24,384]{4,3,2,1,0:T(8,128)(2,1)S(1)}, bf16[5,4,1,24,384]{4,3,2,1,0:T(8,128)(2,1)S(1)}, u32[]{:S(2)}, u32[]{:S(2)}) collective-permute-start(bf16[5,4,1,24,384]{4,3,2,1,0:T(8,128)(2,1)S(1)} %bitcast_dynamic-update-slice_fusion.6), channel_id=1, source_target_pairs={{0,18},{2,16},{16,2},{18,0},{1,19},{3,17},{17,3},{19,1},{4,22},{6,... | collective-permute-start | bytes 1105928 | tf_op jit(solution)/shard_map/ppermute | solution.py:64
  32.2 25.0 %collective-permute-start.3 = (bf16[3,4,1,48,384]{4,3,2,1,0:T(8,128)(2,1)S(1)}, bf16[3,4,1,48,384]{4,3,2,1,0:T(8,128)(2,1)}, u32[]{:S(2)}, u32[]{:S(2)}) collective-permute-start(bf16[3,4,1,48,384]{4,3,2,1,0:T(8,128)(2,1)S(1)} %bitcast_dynamic-update-slice_fusion), channel_id=1, source_target_pairs={{0,2},{2,0},{16,18},{18,16},{1,3},{3,1},{17,19},{19,17},{4,6},{6,4... | collective-permute-start | bytes 1327112 | tf_op jit(solution)/shard_map/ppermute | solution.py:64
  33.8 30.6 %collective-permute-start.4 = (bf16[3,4,1,48,384]{4,3,2,1,0:T(8,128)(2,1)S(1)}, bf16[3,4,1,48,384]{4,3,2,1,0:T(8,128)(2,1)}, u32[]{:S(2)}, u32[]{:S(2)}) collective-permute-start(bf16[3,4,1,48,384]{4,3,2,1,0:T(8,128)(2,1)S(1)} %bitcast_dynamic-update-slice_fusion), channel_id=1, source_target_pairs={{0,16},{2,18},{16,0},{18,2},{1,17},{3,19},{17,1},{19,3},{4,20},{6,... | collective-permute-start | bytes 1327112 | tf_op jit(solution)/shard_map/ppermute | solution.py:64
  39.8 25.7 %collective-permute-start.5 = (bf16[3,4,1,48,384]{4,3,2,1,0:T(8,128)(2,1)S(1)}, bf16[3,4,1,48,384]{4,3,2,1,0:T(8,128)(2,1)}, u32[]{:S(2)}, u32[]{:S(2)}) collective-permute-start(bf16[3,4,1,48,384]{4,3,2,1,0:T(8,128)(2,1)S(1)} %bitcast_dynamic-update-slice_fusion), channel_id=1, source_target_pairs={{0,18},{2,16},{16,2},{18,0},{1,19},{3,17},{17,3},{19,1},{4,22},{6,... | collective-permute-start | bytes 1327112 | tf_op jit(solution)/shard_map/ppermute | solution.py:64
  49.5 1.2 copy-start.1
  49.5 1.2 copy-start.3
  49.5 1.2 copy-start.5
  49.5 1.2 copy-start.15
  54.3 12.3 %copy-start.16 = (f32[768]{0:T(1024)S(1)}, f32[768]{0:T(1024)}, u32[]{:S(2)}) copy-start(f32[768]{0:T(1024)} %param.11) | copy-start | bytes 9220
  56.4 10.7 %copy-start.17 = (f32[2,64]{1,0:T(2,128)}, f32[2,64]{1,0:T(2,128)S(1)}, u32[]{:S(2)}) copy-start(f32[2,64]{1,0:T(2,128)S(1)} %add_rsqrt_fusion) | copy-start | bytes 1540
  69.3 30.8 %all-to-all-start = ((bf16[4,2,18432]{2,1,0:T(2,128)(2,1)}), bf16[4,2,18432]{2,1,0:T(2,128)(2,1)}, u32[]{:S(2)}, u32[]{:S(2)}) async-start(bf16[4,2,18432]{2,1,0:T(2,128)(2,1)} %pad_maximum_fusion), calls=%async_computation | async-start | bytes 589824 | tf_op jit(solution)/shard_map/all_to_all | solution.py:267
  73.6 9.8 %collective-permute-start.14 = (bf16[96,1,192]{2,0,1:T(8,128)(2,1)S(1)}, bf16[96,1,192]{2,0,1:T(8,128)(2,1)S(1)}, u32[]{:S(2)}, u32[]{:S(2)}) collective-permute-start(bf16[96,1,192]{2,0,1:T(8,128)(2,1)S(1)} %bitcast.209), channel_id=1, source_target_pairs={{0,4},{4,8},{8,12},{12,0},{1,5},{5,9},{9,13},{13,1},{2,6},{6,10},{... | collective-permute-start | bytes 110600 | tf_op jit(solution)/shard_map/ppermute | solution.py:54
  75.7 7.8 %collective-permute-start.15 = (bf16[96,1,192]{2,0,1:T(8,128)(2,1)S(1)}, bf16[96,1,192]{2,0,1:T(8,128)(2,1)S(1)}, u32[]{:S(2)}, u32[]{:S(2)}) collective-permute-start(bf16[96,1,192]{2,0,1:T(8,128)(2,1)S(1)} %bitcast.210), channel_id=1, source_target_pairs={{0,8},{4,12},{8,0},{12,4},{1,9},{5,13},{9,1},{13,5},{2,10},{6,14},... | collective-permute-start | bytes 110600 | tf_op jit(solution)/shard_map/ppermute | solution.py:54
  78.0 5.6 %collective-permute-start.16 = (bf16[96,1,192]{2,0,1:T(8,128)(2,1)S(1)}, bf16[96,1,192]{2,0,1:T(8,128)(2,1)S(1)}, u32[]{:S(2)}, u32[]{:S(2)}) collective-permute-start(bf16[96,1,192]{2,0,1:T(8,128)(2,1)S(1)} %bitcast.211), channel_id=1, source_target_pairs={{0,12},{4,0},{8,4},{12,8},{1,13},{5,1},{9,5},{13,9},{2,14},{6,2},{... | collective-permute-start | bytes 110600 | tf_op jit(solution)/shard_map/ppermute | solution.py:54
  93.1 6.0 %collective-permute-start.17 = (bf16[1,96,4,192]{3,2,1,0:T(4,128)(2,1)}, bf16[1,96,4,192]{3,2,1,0:T(4,128)(2,1)}, u32[]{:S(2)}, u32[]{:S(2)}) collective-permute-start(bf16[1,96,4,192]{3,2,1,0:T(4,128)(2,1)} %dynamic_update_slice.106), channel_id=1, source_target_pairs={{0,2},{2,0},{16,18},{18,16},{1,3},{3,1},{17,19},{19,17},{4,6},{6,4... | collective-permute-start | bytes 442376 | tf_op jit(solution)/shard_map/ppermute | solution.py:64
  94.1 28.6 %collective-permute-start.18 = (bf16[1,96,4,192]{3,2,1,0:T(4,128)(2,1)}, bf16[1,96,4,192]{3,2,1,0:T(4,128)(2,1)}, u32[]{:S(2)}, u32[]{:S(2)}) collective-permute-start(bf16[1,96,4,192]{3,2,1,0:T(4,128)(2,1)} %dynamic_update_slice.106), channel_id=1, source_target_pairs={{0,16},{2,18},{16,0},{18,2},{1,17},{3,19},{17,1},{19,3},{4,20},{6,... | collective-permute-start | bytes 442376 | tf_op jit(solution)/shard_map/ppermute | solution.py:64
  95.8 27.9 %collective-permute-start.19 = (bf16[1,96,4,192]{3,2,1,0:T(4,128)(2,1)}, bf16[1,96,4,192]{3,2,1,0:T(4,128)(2,1)}, u32[]{:S(2)}, u32[]{:S(2)}) collective-permute-start(bf16[1,96,4,192]{3,2,1,0:T(4,128)(2,1)} %dynamic_update_slice.106), channel_id=1, source_target_pairs={{0,18},{2,16},{16,2},{18,0},{1,19},{3,17},{17,3},{19,1},{4,22},{6,... | collective-permute-start | bytes 442376 | tf_op jit(solution)/shard_map/ppermute | solution.py:64
  108.2 0.5 copy-start.14
  118.8 9.8 %all-to-all-start.1 = ((bf16[4,2,6144]{2,1,0:T(2,128)(2,1)}), bf16[4,2,6144]{2,1,0:T(2,128)(2,1)}, u32[]{:S(2)}, u32[]{:S(2)}) async-start(bf16[4,2,6144]{2,1,0:T(2,128)(2,1)} %copy.161), calls=%async_computation.1 | async-start | bytes 196608 | tf_op jit(solution)/shard_map/all_to_all | solution.py:289
  127.8 13.3 %copy-start.7 = (bf16[384,768]{1,0:T(8,128)(2,1)S(1)}, bf16[384,768]{1,0:T(8,128)(2,1)}, u32[]{:S(2)}) copy-start(bf16[384,768]{1,0:T(8,128)(2,1)} %reshape.261) | copy-start | bytes 1769476
  133.4 4.6 %copy-start.11 = (bf16[2,64,768]{2,1,0:T(8,128)(2,1)}, bf16[2,64,768]{2,1,0:T(8,128)(2,1)S(1)}, u32[]{:S(2)}) copy-start(bf16[2,64,768]{2,1,0:T(8,128)(2,1)S(1)} %convolution_convert_fusion.1) | copy-start | bytes 589828
  134.2 3.9 %collective-permute-start.20 = (bf16[2,64,384]{2,1,0:T(8,128)(2,1)}, bf16[2,64,384]{2,1,0:T(8,128)(2,1)}, u32[]{:S(2)}, u32[]{:S(2)}) collective-permute-start(bf16[2,64,384]{2,1,0:T(8,128)(2,1)} %constant_dynamic-slice_fusion.1), channel_id=1, source_target_pairs={{0,1},{1,0},{2,3},{3,2},{4,5},{5,4},{6,7},{7,6},{8,9},{9,8},{10,11... | collective-permute-start | bytes 294920 | tf_op jit(solution)/shard_map/ppermute | solution.py:123
  141.4 13.2 %copy-start.10 = (bf16[256,192]{1,0:T(8,128)(2,1)S(1)}, bf16[256,192]{1,0:T(8,128)(2,1)}, u32[]{:S(2)}) copy-start(bf16[256,192]{1,0:T(8,128)(2,1)} %squeeze.87) | copy-start | bytes 294916
  143.8 10.1 %all-to-all-start.2 = ((bf16[4,2,3072]{2,1,0:T(2,128)(2,1)}), bf16[4,2,3072]{2,1,0:T(2,128)(2,1)S(1)}, u32[]{:S(2)}, u32[]{:S(2)}) async-start(bf16[4,2,3072]{2,1,0:T(2,128)(2,1)} %reshape.282), calls=%async_computation.2 | async-start | bytes 98304 | tf_op jit(solution)/shard_map/all_to_all | solution.py:375
  154.4 6.7 %copy-start.18 = (f32[2,64]{1,0:T(2,128)S(1)}, f32[2,64]{1,0:T(2,128)}, u32[]{:S(2)}) copy-start(f32[2,64]{1,0:T(2,128)} %copy-done.17) | copy-start | bytes 1540
  157.6 9.3 %all-to-all-start.3 = ((bf16[4,2,9216]{2,1,0:T(2,128)(2,1)}), bf16[4,2,9216]{2,1,0:T(2,128)(2,1)S(1)}, u32[]{:S(2)}, u32[]{:S(2)}) async-start(bf16[4,2,9216]{2,1,0:T(2,128)(2,1)} %reshape.284), calls=%async_computation.3 | async-start | bytes 294912 | tf_op jit(solution)/shard_map/all_to_all | solution.py:386
  167.5 1.5 copy-start.8
  167.9 2.3 %copy-start.13 = (f32[384]{0:T(512)S(1)}, f32[384]{0:T(512)}, u32[]{:S(2)}) copy-start(f32[384]{0:T(512)} %dynamic_slice.46) | copy-start | bytes 4612
  168.9 1.3 collective-permute-start.21
  169.0 9.2 %copy-start.6 = (bf16[1,4,4,24,384]{4,3,2,1,0:T(8,128)(2,1)S(1)}, bf16[1,4,4,24,384]{4,3,2,1,0:T(8,128)(2,1)}, u32[]{:S(2)}) copy-start(bf16[1,4,4,24,384]{4,3,2,1,0:T(8,128)(2,1)} %copy-done.5) | copy-start | bytes 884740
  170.3 8.2 %copy-start.4 = (bf16[1,4,4,24,384]{4,3,2,1,0:T(8,128)(2,1)S(1)}, bf16[1,4,4,24,384]{4,3,2,1,0:T(8,128)(2,1)}, u32[]{:S(2)}) copy-start(bf16[1,4,4,24,384]{4,3,2,1,0:T(8,128)(2,1)} %copy-done.3) | copy-start | bytes 884740
  173.0 5.8 %copy-start.2 = (bf16[1,4,4,24,384]{4,3,2,1,0:T(8,128)(2,1)S(1)}, bf16[1,4,4,24,384]{4,3,2,1,0:T(8,128)(2,1)}, u32[]{:S(2)}) copy-start(bf16[1,4,4,24,384]{4,3,2,1,0:T(8,128)(2,1)} %copy-done.1) | copy-start | bytes 884740
  173.4 5.1 %collective-permute-start.23 = (bf16[2,384]{1,0:T(2,128)(2,1)S(1)}, bf16[2,384]{1,0:T(2,128)(2,1)S(1)}, u32[]{:S(2)}, u32[]{:S(2)}) collective-permute-start(bf16[2,384]{1,0:T(2,128)(2,1)S(1)} %get-tuple-element.107), channel_id=1, source_target_pairs={{0,4},{4,8},{8,12},{1,5},{5,9},{9,13},{2,6},{6,10},{10,14},{3,7},{... | collective-permute-start | bytes 4616 | tf_op jit(solution)/shard_map/ppermute | solution.py:23
  177.0 5.5 %collective-permute-start.22 = (bf16[2,384]{1,0:T(2,128)(2,1)S(1)}, bf16[2,384]{1,0:T(2,128)(2,1)S(1)}, u32[]{:S(2)}, u32[]{:S(2)}) collective-permute-start(bf16[2,384]{1,0:T(2,128)(2,1)S(1)} %get-tuple-element.106), channel_id=1, source_target_pairs={{4,0},{8,4},{12,8},{5,1},{9,5},{13,9},{6,2},{10,6},{14,10},{7,3},{... | collective-permute-start | bytes 4616 | tf_op jit(solution)/shard_map/ppermute | solution.py:25
  178.5 5.9 %copy-start.12 = (f32[1,128,384]{2,1,0:T(8,128)S(1)}, f32[1,128,384]{2,1,0:T(8,128)}, u32[]{:S(2)}) copy-start(f32[1,128,384]{2,1,0:T(8,128)} %param.8) | copy-start | bytes 589828
  182.9 1.4 collective-permute-start.24

commit v11 on v10

--- a/solution.py
+++ b/solution.py
@@ -39,7 +39,7 @@
     piece = lax.dynamic_slice_in_dim(cells, lax.axis_index(spread) * size, size, split)
     if after[0] is not None:
         piece = lax.optimization_barrier((piece, after[0]))[0]
-    slot = cells.ndim - 1 if last else dim
+    slot = 0 if last else dim
     piece = jnp.expand_dims(piece, slot)
     along = jnp.zeros(piece.shape[:slot] + (ring,) + piece.shape[slot + 1 :], cells.dtype)
 
@@ -63,6 +63,8 @@
     for mask in range(1, count):
         arrived = lax.ppermute(along, spread, [(i, i ^ mask) for i in range(count)])
         whole = place(arrived, whole, lane, lax.bitwise_xor(gb_at, mask))
+    if last:
+        whole = jnp.moveaxis(whole, 1, -2)
     shape = list(cells.shape)
     shape[dim] = shape[dim] * ring
     return whole.reshape(shape), (along, whole)
@@ -327,6 +329,7 @@
         conv_weight, _ = gather_blocks(conv_weight, 1)
         qkv_weight, _ = gather_blocks(qkv_weight, 1)
         out_weight, _ = gather_blocks(out_weight, 1)
+        qkv_weight, out_weight = lax.optimization_barrier((qkv_weight, out_weight))
     else:
         (conv_weight,), _ = gather_seq([(conv_weight, 1)], width)
         (qkv_weight,), _ = gather_seq([(qkv_weight, 1)], width)

time: 187 us -> 185 us (0.989)
  blocking collectives: 6.58 us -> 19.7 us
  waiting for transfers between devices: 41.5 us -> 30.7 us
  matrix products: 12.6 us -> 9.07 us
  starting transfers between devices: 54.1 us -> 51.9 us
    all_to_all x0 -> x1, blocking collectives: none -> 13.2 us  [forward(): lax.all_to_all(jnp.concatenate([query_send, keyval_send], axis=2), 'seq',...]
    ppermute x9, waiting for transfers between devices: 18.6 us -> 7.78 us  [gather_blocks(): arrived = lax.ppermute(along, spread, [(i, i ^ mask) for i in range(count)])]
    dynamic_update_slice x24, local copies, waits for them, and re-layouts: 22.2 us -> 31.2 us  [place(): return lax.dynamic_update_slice(target, block, start)]
    ppermute x9, waiting for transfers between devices: 6.71 us -> 1.77 us  [gather_blocks(): lax.ppermute(piece, 'seq', [(i, (i + shift) % ring) for i in range(ring)])]
    all_to_all x1 -> x0, starting transfers between devices: 4.09 us -> none  [forward(): lax.all_to_all(jnp.concatenate([query_send, keyval_send], axis=2), 'seq',...]
    all_to_all x1, waiting for transfers between devices: 0.74 us -> 4.45 us  [forward(): lax.all_to_all(out_send, 'seq', split_axis=0, concat_axis=0, tiled=True)]
    slice x2, local copies, waits for them, and re-layouts: 3.5 us -> 0.29 us  [forward(): both_in[:, :, query_len:].reshape(pass_count, devices * rows, 2 * head_size)]
    ppermute x9, starting transfers between devices: 17.1 us -> 20.3 us  [gather_blocks(): lax.ppermute(piece, 'seq', [(i, (i + shift) % ring) for i in range(ring)])]
  transfers between devices with their start and end apart: 29 -> 28, of which waited for: 14 -> 12; matrix products, arithmetic and copies ran while one was open for 32% -> 26% of each run, Pallas kernels for 0% -> 0%
where the time goes in v11:
time: 185 us; the launch traced here: 183 us
  local copies, waits for them, and re-layouts  61.4 us (33%)
  starting transfers between devices  51.9 us (28%)
  waiting for transfers between devices  30.7 us (17%)
  blocking collectives  19.7 us (11%)
  matrix products  9.07 us (5%)
  other arithmetic  8.75 us (5%)
  between operations  1.97 us (1%)
    dynamic_update_slice x24, local copies, waits for them, and re-layouts, place(): return lax.dynamic_update_slice(target, block, start)  31.2 us
    ppermute x9, starting transfers between devices, gather_blocks(): lax.ppermute(piece, 'seq', [(i, (i + shift) % ring) for i in range(ring)])  20.3 us
    ppermute x9, starting transfers between devices, gather_blocks(): arrived = lax.ppermute(along, spread, [(i, i ^ mask) for i in range(count)])  13.2 us
    all_to_all x1, blocking collectives, forward(): lax.all_to_all(jnp.concatenate([query_send, keyval_send], axis=2), 'seq',...  13.2 us
    ppermute x9, waiting for transfers between devices, gather_blocks(): arrived = lax.ppermute(along, spread, [(i, i ^ mask) for i in range(count)])  7.78 us
    all_to_all x1, waiting for transfers between devices, shards(): lax.all_to_all(jnp.concatenate([query_grad.reshape(devices, query_len).as...  6.11 us
    ppermute x2, starting transfers between devices, with_halo(): lax.ppermute(tail, axis, [(i, (i + 1) % count) for i in range(ends)])  5.76 us
    all_to_all x1, waiting for transfers between devices, shards(): lax.all_to_all(grad_send, 'seq', split_axis=0, concat_axis=1, tiled=True)  5.44 us
  transfers between devices with their start and end apart: 28, of which 12 were waited for; matrix products, arithmetic and copies ran while one was open for 26% of the time, Pallas kernels for 0%

profile of v11, /device:TPU:0, one launch (start us, length us, event | category | flops | bytes accessed | tf_op | source)
XLA Modules:
  0.0 183.5 jit_solution(7866837045259653200)
XLA Ops:
  1.7 3.1 %collective-permute-start = (bf16[3,1,48,384]{3,2,0,1:T(8,128)(2,1)S(1)}, bf16[3,1,48,384]{3,2,0,1:T(8,128)(2,1)S(1)}, u32[]{:S(2)}, u32[]{:S(2)}) collective-permute-start(bf16[3,1,48,384]{3,2,0,1:T(8,128)(2,1)S(1)} %dynamic-slice_bitcast_fusion), channel_id=1, source_target_pairs={{0,4},{4,8},{8,12},{12,0},{1,5},{5,9},{9,13},{13,1},{2,6},{6,10},{... | collective-permute-start | bytes 331784 | tf_op jit(solution)/shard_map/ppermute | solution.py:54
  4.8 2.6 %collective-permute-start.1 = (bf16[3,1,48,384]{3,2,0,1:T(8,128)(2,1)S(1)}, bf16[3,1,48,384]{3,2,0,1:T(8,128)(2,1)S(1)}, u32[]{:S(2)}, u32[]{:S(2)}) collective-permute-start(bf16[3,1,48,384]{3,2,0,1:T(8,128)(2,1)S(1)} %dynamic-slice_bitcast_fusion), channel_id=1, source_target_pairs={{0,8},{4,12},{8,0},{12,4},{1,9},{5,13},{9,1},{13,5},{2,10},{6,14},... | collective-permute-start | bytes 331784 | tf_op jit(solution)/shard_map/ppermute | solution.py:54
  9.5 2.7 %collective-permute-start.12 = (bf16[2,2,384]{2,1,0:T(2,128)(2,1)S(1)}, bf16[2,2,384]{2,1,0:T(2,128)(2,1)S(1)}, u32[]{:S(2)}, u32[]{:S(2)}) collective-permute-start(bf16[2,2,384]{2,1,0:T(2,128)(2,1)S(1)} %get-tuple-element.106), channel_id=1, source_target_pairs={{0,4},{4,8},{8,12},{1,5},{5,9},{9,13},{2,6},{6,10},{10,14},{3,7},{... | collective-permute-start | bytes 9224 | tf_op jit(solution)/shard_map/ppermute | solution.py:23
  12.2 1.3 collective-permute-start.19
  14.3 1.6 bitcast_dynamic-update-slice_fusion.3
  18.2 3.1 %dynamic_update_slice.95 = bf16[1,4,96,192]{3,1,2,0:T(4,128)(2,1)} dynamic-update-slice(bf16[1,4,96,192]{3,1,2,0:T(4,128)(2,1)} %broadcast_in_dim.95, bf16[1,1,96,192]{3,1,2,0:T(2,128)(2,1)S(1)} %copy.152, s32[]{:T(128)} %constant.152.clone.1, s32[]{:T(128)S(6)} %select_n.86, s32[]{:T(128)} %constant.152.clone.1, s32[]{:T(128)} %constant.152.clone.1) | dynamic-update-slice | bytes 73732 | tf_op jit(solution)/shard_map/dynamic_update_slice | solution.py:49
  21.3 4.1 %collective-permute-start.7 = (bf16[1,96,192]{2,1,0:T(8,128)(2,1)S(1)}, bf16[1,96,192]{2,1,0:T(8,128)(2,1)S(1)}, u32[]{:S(2)}, u32[]{:S(2)}) collective-permute-start(bf16[1,96,192]{2,1,0:T(8,128)(2,1)S(1)} %bitcast.221), channel_id=1, source_target_pairs={{0,8},{4,12},{8,0},{12,4},{1,9},{5,13},{9,1},{13,5},{2,10},{6,14},... | collective-permute-start | bytes 110600 | tf_op jit(solution)/shard_map/ppermute | solution.py:54
  25.4 1.5 collective-permute-start.8
  27.9 3.3 %collective-permute-start.13 = (bf16[5,1,24,384]{3,2,0,1:T(8,128)(2,1)S(1)}, bf16[5,1,24,384]{3,2,0,1:T(8,128)(2,1)S(1)}, u32[]{:S(2)}, u32[]{:S(2)}) collective-permute-start(bf16[5,1,24,384]{3,2,0,1:T(8,128)(2,1)S(1)} %dynamic-slice_bitcast_fusion.1), channel_id=1, source_target_pairs={{0,4},{4,8},{8,12},{12,0},{1,5},{5,9},{9,13},{13,1},{2,6},{6,10},{... | collective-permute-start | bytes 276488 | tf_op jit(solution)/shard_map/ppermute | solution.py:54
  31.2 5.6 %collective-permute-start.14 = (bf16[5,1,24,384]{3,2,0,1:T(8,128)(2,1)S(1)}, bf16[5,1,24,384]{3,2,0,1:T(8,128)(2,1)S(1)}, u32[]{:S(2)}, u32[]{:S(2)}) collective-permute-start(bf16[5,1,24,384]{3,2,0,1:T(8,128)(2,1)S(1)} %dynamic-slice_bitcast_fusion.1), channel_id=1, source_target_pairs={{0,8},{4,12},{8,0},{12,4},{1,9},{5,13},{9,1},{13,5},{2,10},{6,14},... | collective-permute-start | bytes 276488 | tf_op jit(solution)/shard_map/ppermute | solution.py:54
  36.8 3.1 %dynamic_update_slice.96 = bf16[1,4,96,192]{3,1,2,0:T(4,128)(2,1)} dynamic-update-slice(bf16[1,4,96,192]{3,1,2,0:T(4,128)(2,1)} %dynamic_update_slice.95, bf16[1,1,96,192]{3,1,2,0:T(2,128)(2,1)S(1)} %copy.153, s32[]{:T(128)} %constant.152.clone.1, s32[]{:T(128)S(6)} %select_n.88, s32[]{:T(128)} %constant.152.clone.1, s32[]{:T(128)} %constant.152.clone.1) | dynamic-update-slice | bytes 73732 | tf_op jit(solution)/shard_map/dynamic_update_slice | solution.py:49
  40.0 3.1 %dynamic_update_slice.97 = bf16[1,4,96,192]{3,1,2,0:T(4,128)(2,1)} dynamic-update-slice(bf16[1,4,96,192]{3,1,2,0:T(4,128)(2,1)} %dynamic_update_slice.96, bf16[1,1,96,192]{3,1,2,0:T(2,128)(2,1)S(1)} %copy.154, s32[]{:T(128)} %constant.152.clone.1, s32[]{:T(128)S(6)} %select_n.90, s32[]{:T(128)} %constant.152.clone.1, s32[]{:T(128)} %constant.152.clone.1) | dynamic-update-slice | bytes 73732 | tf_op jit(solution)/shard_map/dynamic_update_slice | solution.py:49
  43.1 3.1 %dynamic_update_slice.98 = bf16[1,4,96,192]{3,1,2,0:T(4,128)(2,1)} dynamic-update-slice(bf16[1,4,96,192]{3,1,2,0:T(4,128)(2,1)} %dynamic_update_slice.97, bf16[1,1,96,192]{3,1,2,0:T(2,128)(2,1)S(1)} %copy.155, s32[]{:T(128)} %constant.152.clone.1, s32[]{:T(128)S(6)} %select_n.92, s32[]{:T(128)} %constant.152.clone.1, s32[]{:T(128)} %constant.152.clone.1) | dynamic-update-slice | bytes 73732 | tf_op jit(solution)/shard_map/dynamic_update_slice | solution.py:49
  46.3 1.1 broadcast_in_dim.94
  47.3 1.7 constant_dynamic-update-slice_fusion.7
  49.7 1.5 collective-permute-start.9
  51.8 1.8 collective-permute-done.15
  53.6 1.5 collective-permute-start.10
  57.0 1.5 collective-permute-start.11
  60.3 1.5 collective-permute-start.17
  62.7 1.1 constant_dynamic-update-slice_fusion.11
  63.8 1.5 collective-permute-start.18
  66.1 1.5 collective-permute-start.3
  68.4 2.1 %collective-permute-start.4 = (bf16[3,4,1,48,384]{4,3,2,1,0:T(8,128)(2,1)}, bf16[3,4,1,48,384]{4,3,2,1,0:T(8,128)(2,1)}, u32[]{:S(2)}, u32[]{:S(2)}) collective-permute-start(bf16[3,4,1,48,384]{4,3,2,1,0:T(8,128)(2,1)} %bitcast_dynamic-update-slice_fusion), channel_id=1, source_target_pairs={{0,16},{2,18},{16,0},{18,2},{1,17},{3,19},{17,1},{19,3},{4,20},{6,... | collective-permute-start | bytes 1327112 | tf_op jit(solution)/shard_map/ppermute | solution.py:64
  71.2 2.6 %reshape.255 = bf16[384,768]{1,0:T(8,128)(2,1)} reshape(bf16[4,96,4,192]{3,2,1,0:T(4,128)(2,1)} %bitcast.11) | data formatting | bytes 1179648 | tf_op jit(solution)/shard_map/reshape | solution.py:70
  73.9 1.5 collective-permute-start.5
  76.5 3.9 %collective-permute-done.17 = bf16[5,4,1,24,384]{4,3,2,1,0:T(8,128)(2,1)} collective-permute-done((bf16[5,4,1,24,384]{4,3,2,1,0:T(8,128)(2,1)}, bf16[5,4,1,24,384]{4,3,2,1,0:T(8,128)(2,1)}, u32[]{:S(2)}, u32[]{:S(2)}) %collective-permute-start.17) | collective-permute-done | bytes 368672 | tf_op jit(solution)/shard_map/ppermute | solution.py:64
  85.8 1.9 %all-gather = bf16[2,64,1,768]{3,1,0,2:T(8,128)(2,1)S(1)} all-gather(bf16[2,64,1,384]{3,1,0,2:T(8,128)(2,1)S(1)} %fusion.65), channel_id=2, replica_groups=mesh['group'=2,'seq'=4,'batch'=2,'mp'=2] {'mp'}, dimensions={3}, use_global_device_ids=true | all-gather | bytes 294912 | tf_op jit(solution)/shard_map/all_gather | solution.py:232
  87.8 1.1 constant_dynamic-update-slice_fusion.10
  88.9 3.1 %collective-permute-done.4 = bf16[3,4,1,48,384]{4,3,2,1,0:T(8,128)(2,1)} collective-permute-done((bf16[3,4,1,48,384]{4,3,2,1,0:T(8,128)(2,1)}, bf16[3,4,1,48,384]{4,3,2,1,0:T(8,128)(2,1)}, u32[]{:S(2)}, u32[]{:S(2)}) %collective-permute-start.4) | collective-permute-done | bytes 442400 | tf_op jit(solution)/shard_map/ppermute | solution.py:64
  93.4 1.1 constant_dynamic-update-slice_fusion.8
  96.4 13.2 %all_to_all.43 = bf16[4,2,18432]{2,1,0:T(2,128)(2,1)S(1)} all-to-all(bf16[4,2,18432]{2,1,0:T(2,128)(2,1)S(1)} %pad_maximum_fusion), channel_id=1, replica_groups=mesh['group'=2,'seq'=4,'batch'=2,'mp'=2] {'seq'}, dimensions={0} | all-to-all | bytes 589824 | tf_op jit(solution)/shard_map/all_to_all | solution.py:269
  113.2 1.5 copy.165
  114.7 1.6 stack.21
  116.3 1.5 squeeze.80
  122.6 3.3 %all-to-all-start.1 = ((bf16[4,2,6144]{2,1,0:T(2,128)(2,1)}), bf16[4,2,6144]{2,1,0:T(2,128)(2,1)S(1)}, u32[]{:S(2)}, u32[]{:S(2)}) async-start(bf16[4,2,6144]{2,1,0:T(2,128)(2,1)} %copy.166), calls=%async_computation.1 | async-start | bytes 196608 | tf_op jit(solution)/shard_map/all_to_all | solution.py:291
  125.9 1.3 dynamic_slice.46
  127.3 4.5 %all-to-all-done.1 = bf16[4,2,6144]{2,1,0:T(2,128)(2,1)S(1)} async-done(((bf16[4,2,6144]{2,1,0:T(2,128)(2,1)}), bf16[4,2,6144]{2,1,0:T(2,128)(2,1)S(1)}, u32[]{:S(2)}, u32[]{:S(2)}) %all-to-all-start.1) | async-done | bytes 98336 | tf_op jit(solution)/shard_map/all_to_all | solution.py:291
  133.7 1.2 slice_reduce_fusion
  137.1 2.0 %all_gather.7 = bf16[64,768]{1,0:T(8,128)(2,1)S(1)} all-gather(bf16[64,384]{1,0:T(8,128)(2,1)S(1)} %fusion.96), channel_id=1, replica_groups=mesh['group'=2,'seq'=4,'batch'=2,'mp'=2] {'mp'}, dimensions={1}, use_global_device_ids=true | all-gather | bytes 147456 | tf_op jit(solution)/shard_map/all_gather | solution.py:366
  143.2 3.3 %all-to-all-start.2 = ((bf16[4,2,3072]{2,1,0:T(2,128)(2,1)}), bf16[4,2,3072]{2,1,0:T(2,128)(2,1)S(1)}, u32[]{:S(2)}, u32[]{:S(2)}) async-start(bf16[4,2,3072]{2,1,0:T(2,128)(2,1)} %reshape.281), calls=%async_computation.2 | async-start | bytes 98304 | tf_op jit(solution)/shard_map/all_to_all | solution.py:378
  146.7 5.4 %all-to-all-done.2 = bf16[4,2,3072]{2,1,0:T(2,128)(2,1)S(1)} async-done(((bf16[4,2,3072]{2,1,0:T(2,128)(2,1)}), bf16[4,2,3072]{2,1,0:T(2,128)(2,1)S(1)}, u32[]{:S(2)}, u32[]{:S(2)}) %all-to-all-start.2) | async-done | bytes 49184 | tf_op jit(solution)/shard_map/all_to_all | solution.py:378
  155.9 3.3 %all-to-all-start.3 = ((bf16[4,2,9216]{2,1,0:T(2,128)(2,1)}), bf16[4,2,9216]{2,1,0:T(2,128)(2,1)S(1)}, u32[]{:S(2)}, u32[]{:S(2)}) async-start(bf16[4,2,9216]{2,1,0:T(2,128)(2,1)} %reshape.283), calls=%async_computation.3 | async-start | bytes 294912 | tf_op jit(solution)/shard_map/all_to_all | solution.py:389
  159.2 6.1 %all-to-all-done.3 = bf16[4,2,9216]{2,1,0:T(2,128)(2,1)S(1)} async-done(((bf16[4,2,9216]{2,1,0:T(2,128)(2,1)}), bf16[4,2,9216]{2,1,0:T(2,128)(2,1)S(1)}, u32[]{:S(2)}, u32[]{:S(2)}) %all-to-all-start.3) | async-done | bytes 147488 | tf_op jit(solution)/shard_map/all_to_all | solution.py:389
  168.8 2.6 %psum.7 = f32[64]{0:T(128)S(1)} all-reduce(f32[64]{0:T(128)S(1)} %fusion.87), channel_id=1, replica_groups=mesh['group'=2,'seq'=4,'batch'=2,'mp'=2] {'mp'}, use_global_device_ids=true, to_apply=%region_7.8 | all-reduce | flops 64 | bytes 512 | tf_op jit(solution)/shard_map/psum | solution.py:427
  171.9 3.0 %collective-permute-start.23 = (bf16[2,384]{1,0:T(2,128)(2,1)S(1)}, bf16[2,384]{1,0:T(2,128)(2,1)S(1)}, u32[]{:S(2)}, u32[]{:S(2)}) collective-permute-start(bf16[2,384]{1,0:T(2,128)(2,1)S(1)} %get-tuple-element.111), channel_id=1, source_target_pairs={{0,4},{4,8},{8,12},{1,5},{5,9},{9,13},{2,6},{6,10},{10,14},{3,7},{... | collective-permute-start | bytes 4616 | tf_op jit(solution)/shard_map/ppermute | solution.py:23
  175.2 1.3 collective-permute-start.22
  177.3 3.4 %collective-permute-done.22 = bf16[2,384]{1,0:T(2,128)(2,1)S(1)} collective-permute-done((bf16[2,384]{1,0:T(2,128)(2,1)S(1)}, bf16[2,384]{1,0:T(2,128)(2,1)S(1)}, u32[]{:S(2)}, u32[]{:S(2)}) %collective-permute-start.22) | collective-permute-done | bytes 1568 | tf_op jit(solution)/shard_map/ppermute | solution.py:25
  (234 shorter events, 52.5 us)
Async XLA Ops:
  0.6 6.7 %copy-start = (bf16[384,192]{0,1:T(8,128)(2,1)S(1)}, bf16[384,192]{0,1:T(8,128)(2,1)}, u32[]{:S(2)}) copy-start(bf16[384,192]{0,1:T(8,128)(2,1)} %param.13) | copy-start | bytes 442372
  0.6 26.3 %copy-start.14 = (bf16[1,128,384]{2,1,0:T(8,128)(2,1)S(1)}, bf16[1,128,384]{2,1,0:T(8,128)(2,1)}, u32[]{:S(2)}) copy-start(bf16[1,128,384]{2,1,0:T(8,128)(2,1)} %param.7) | copy-start | bytes 294916
  0.7 15.2 %copy-start.22 = (bf16[5,96,384]{2,1,0:T(8,128)(2,1)S(1)}, bf16[5,96,384]{2,1,0:T(8,128)(2,1)}, u32[]{:S(2)}) copy-start(bf16[5,96,384]{2,1,0:T(8,128)(2,1)} %param.9) | copy-start | bytes 1105924
  1.7 55.3 %collective-permute-start = (bf16[3,1,48,384]{3,2,0,1:T(8,128)(2,1)S(1)}, bf16[3,1,48,384]{3,2,0,1:T(8,128)(2,1)S(1)}, u32[]{:S(2)}, u32[]{:S(2)}) collective-permute-start(bf16[3,1,48,384]{3,2,0,1:T(8,128)(2,1)S(1)} %dynamic-slice_bitcast_fusion), channel_id=1, source_target_pairs={{0,4},{4,8},{8,12},{12,0},{1,5},{5,9},{9,13},{13,1},{2,6},{6,10},{... | collective-permute-start | bytes 331784 | tf_op jit(solution)/shard_map/ppermute | solution.py:54
  4.8 54.4 %collective-permute-start.1 = (bf16[3,1,48,384]{3,2,0,1:T(8,128)(2,1)S(1)}, bf16[3,1,48,384]{3,2,0,1:T(8,128)(2,1)S(1)}, u32[]{:S(2)}, u32[]{:S(2)}) collective-permute-start(bf16[3,1,48,384]{3,2,0,1:T(8,128)(2,1)S(1)} %dynamic-slice_bitcast_fusion), channel_id=1, source_target_pairs={{0,8},{4,12},{8,0},{12,4},{1,9},{5,13},{9,1},{13,5},{2,10},{6,14},... | collective-permute-start | bytes 331784 | tf_op jit(solution)/shard_map/ppermute | solution.py:54
  7.6 20.2 %collective-permute-start.6 = (bf16[1,96,192]{2,1,0:T(8,128)(2,1)S(1)}, bf16[1,96,192]{2,1,0:T(8,128)(2,1)S(1)}, u32[]{:S(2)}, u32[]{:S(2)}) collective-permute-start(bf16[1,96,192]{2,1,0:T(8,128)(2,1)S(1)} %bitcast.219), channel_id=1, source_target_pairs={{0,4},{4,8},{8,12},{12,0},{1,5},{5,9},{9,13},{13,1},{2,6},{6,10},{... | collective-permute-start | bytes 110600 | tf_op jit(solution)/shard_map/ppermute | solution.py:54
  8.7 31.3 %copy-start.15 = (bf16[1,128,384]{2,1,0:T(8,128)(2,1)}, bf16[1,128,384]{2,1,0:T(8,128)(2,1)S(1)}, u32[]{:S(2)}) copy-start(bf16[1,128,384]{2,1,0:T(8,128)(2,1)S(1)} %add_convert_fusion.2) | copy-start | bytes 294916
  9.5 11.8 %collective-permute-start.12 = (bf16[2,2,384]{2,1,0:T(2,128)(2,1)S(1)}, bf16[2,2,384]{2,1,0:T(2,128)(2,1)S(1)}, u32[]{:S(2)}, u32[]{:S(2)}) collective-permute-start(bf16[2,2,384]{2,1,0:T(2,128)(2,1)S(1)} %get-tuple-element.106), channel_id=1, source_target_pairs={{0,4},{4,8},{8,12},{1,5},{5,9},{9,13},{2,6},{6,10},{10,14},{3,7},{... | collective-permute-start | bytes 9224 | tf_op jit(solution)/shard_map/ppermute | solution.py:23
  12.2 13.2 %collective-permute-start.19 = (bf16[2,2,384]{2,1,0:T(2,128)(2,1)S(1)}, bf16[2,2,384]{2,1,0:T(2,128)(2,1)S(1)}, u32[]{:S(2)}, u32[]{:S(2)}) collective-permute-start(bf16[2,2,384]{2,1,0:T(2,128)(2,1)S(1)} %get-tuple-element.107), channel_id=1, source_target_pairs={{4,0},{8,4},{12,8},{5,1},{9,5},{13,9},{6,2},{10,6},{14,10},{7,3},{... | collective-permute-start | bytes 9224 | tf_op jit(solution)/shard_map/ppermute | solution.py:25
  21.3 6.5 %collective-permute-start.7 = (bf16[1,96,192]{2,1,0:T(8,128)(2,1)S(1)}, bf16[1,96,192]{2,1,0:T(8,128)(2,1)S(1)}, u32[]{:S(2)}, u32[]{:S(2)}) collective-permute-start(bf16[1,96,192]{2,1,0:T(8,128)(2,1)S(1)} %bitcast.221), channel_id=1, source_target_pairs={{0,8},{4,12},{8,0},{12,4},{1,9},{5,13},{9,1},{13,5},{2,10},{6,14},... | collective-permute-start | bytes 110600 | tf_op jit(solution)/shard_map/ppermute | solution.py:54
  25.4 5.8 %collective-permute-start.8 = (bf16[1,96,192]{2,1,0:T(8,128)(2,1)S(1)}, bf16[1,96,192]{2,1,0:T(8,128)(2,1)S(1)}, u32[]{:S(2)}, u32[]{:S(2)}) collective-permute-start(bf16[1,96,192]{2,1,0:T(8,128)(2,1)S(1)} %bitcast.222), channel_id=1, source_target_pairs={{0,12},{4,0},{8,4},{12,8},{1,13},{5,1},{9,5},{13,9},{2,14},{6,2},{... | collective-permute-start | bytes 110600 | tf_op jit(solution)/shard_map/ppermute | solution.py:54
  27.7 32.6 %collective-permute-start.2 = (bf16[3,1,48,384]{3,2,0,1:T(8,128)(2,1)S(1)}, bf16[3,1,48,384]{3,2,0,1:T(8,128)(2,1)S(1)}, u32[]{:S(2)}, u32[]{:S(2)}) collective-permute-start(bf16[3,1,48,384]{3,2,0,1:T(8,128)(2,1)S(1)} %dynamic-slice_bitcast_fusion), channel_id=1, source_target_pairs={{0,12},{4,0},{8,4},{12,8},{1,13},{5,1},{9,5},{13,9},{2,14},{6,2},{... | collective-permute-start | bytes 331784 | tf_op jit(solution)/shard_map/ppermute | solution.py:54
  27.9 21.2 %collective-permute-start.13 = (bf16[5,1,24,384]{3,2,0,1:T(8,128)(2,1)S(1)}, bf16[5,1,24,384]{3,2,0,1:T(8,128)(2,1)S(1)}, u32[]{:S(2)}, u32[]{:S(2)}) collective-permute-start(bf16[5,1,24,384]{3,2,0,1:T(8,128)(2,1)S(1)} %dynamic-slice_bitcast_fusion.1), channel_id=1, source_target_pairs={{0,4},{4,8},{8,12},{12,0},{1,5},{5,9},{9,13},{13,1},{2,6},{6,10},{... | collective-permute-start | bytes 276488 | tf_op jit(solution)/shard_map/ppermute | solution.py:54
  31.2 18.5 %collective-permute-start.14 = (bf16[5,1,24,384]{3,2,0,1:T(8,128)(2,1)S(1)}, bf16[5,1,24,384]{3,2,0,1:T(8,128)(2,1)S(1)}, u32[]{:S(2)}, u32[]{:S(2)}) collective-permute-start(bf16[5,1,24,384]{3,2,0,1:T(8,128)(2,1)S(1)} %dynamic-slice_bitcast_fusion.1), channel_id=1, source_target_pairs={{0,8},{4,12},{8,0},{12,4},{1,9},{5,13},{9,1},{13,5},{2,10},{6,14},... | collective-permute-start | bytes 276488 | tf_op jit(solution)/shard_map/ppermute | solution.py:54
  49.0 4.6 %collective-permute-start.15 = (bf16[5,1,24,384]{3,2,0,1:T(8,128)(2,1)S(1)}, bf16[5,1,24,384]{3,2,0,1:T(8,128)(2,1)S(1)}, u32[]{:S(2)}, u32[]{:S(2)}) collective-permute-start(bf16[5,1,24,384]{3,2,0,1:T(8,128)(2,1)S(1)} %dynamic-slice_bitcast_fusion.1), channel_id=1, source_target_pairs={{0,12},{4,0},{8,4},{12,8},{1,13},{5,1},{9,5},{13,9},{2,14},{6,2},{... | collective-permute-start | bytes 276488 | tf_op jit(solution)/shard_map/ppermute | solution.py:54
  49.7 14.1 %collective-permute-start.9 = (bf16[1,4,96,192]{3,1,2,0:T(4,128)(2,1)}, bf16[1,4,96,192]{3,1,2,0:T(4,128)(2,1)S(1)}, u32[]{:S(2)}, u32[]{:S(2)}) collective-permute-start(bf16[1,4,96,192]{3,1,2,0:T(4,128)(2,1)} %dynamic_update_slice.98), channel_id=1, source_target_pairs={{0,2},{2,0},{16,18},{18,16},{1,3},{3,1},{17,19},{19,17},{4,6},{6,4... | collective-permute-start | bytes 442376 | tf_op jit(solution)/shard_map/ppermute | solution.py:64
  53.6 12.5 %collective-permute-start.10 = (bf16[1,4,96,192]{3,1,2,0:T(4,128)(2,1)}, bf16[1,4,96,192]{3,1,2,0:T(4,128)(2,1)S(1)}, u32[]{:S(2)}, u32[]{:S(2)}) collective-permute-start(bf16[1,4,96,192]{3,1,2,0:T(4,128)(2,1)} %dynamic_update_slice.98), channel_id=1, source_target_pairs={{0,16},{2,18},{16,0},{18,2},{1,17},{3,19},{17,1},{19,3},{4,20},{6,... | collective-permute-start | bytes 442376 | tf_op jit(solution)/shard_map/ppermute | solution.py:64
  57.0 11.4 %collective-permute-start.11 = (bf16[1,4,96,192]{3,1,2,0:T(4,128)(2,1)}, bf16[1,4,96,192]{3,1,2,0:T(4,128)(2,1)S(1)}, u32[]{:S(2)}, u32[]{:S(2)}) collective-permute-start(bf16[1,4,96,192]{3,1,2,0:T(4,128)(2,1)} %dynamic_update_slice.98), channel_id=1, source_target_pairs={{0,18},{2,16},{16,2},{18,0},{1,19},{3,17},{17,3},{19,1},{4,22},{6,... | collective-permute-start | bytes 442376 | tf_op jit(solution)/shard_map/ppermute | solution.py:64
  59.1 14.8 %collective-permute-start.16 = (bf16[5,4,1,24,384]{4,3,2,1,0:T(8,128)(2,1)}, bf16[5,4,1,24,384]{4,3,2,1,0:T(8,128)(2,1)}, u32[]{:S(2)}, u32[]{:S(2)}) collective-permute-start(bf16[5,4,1,24,384]{4,3,2,1,0:T(8,128)(2,1)} %bitcast_dynamic-update-slice_fusion.6), channel_id=1, source_target_pairs={{0,2},{2,0},{16,18},{18,16},{1,3},{3,1},{17,19},{19,17},{4,6},{6,4... | collective-permute-start | bytes 1105928 | tf_op jit(solution)/shard_map/ppermute | solution.py:64
  60.3 20.1 %collective-permute-start.17 = (bf16[5,4,1,24,384]{4,3,2,1,0:T(8,128)(2,1)}, bf16[5,4,1,24,384]{4,3,2,1,0:T(8,128)(2,1)}, u32[]{:S(2)}, u32[]{:S(2)}) collective-permute-start(bf16[5,4,1,24,384]{4,3,2,1,0:T(8,128)(2,1)} %bitcast_dynamic-update-slice_fusion.6), channel_id=1, source_target_pairs={{0,16},{2,18},{16,0},{18,2},{1,17},{3,19},{17,1},{19,3},{4,20},{6,... | collective-permute-start | bytes 1105928 | tf_op jit(solution)/shard_map/ppermute | solution.py:64
  63.8 18.1 %collective-permute-start.18 = (bf16[5,4,1,24,384]{4,3,2,1,0:T(8,128)(2,1)}, bf16[5,4,1,24,384]{4,3,2,1,0:T(8,128)(2,1)}, u32[]{:S(2)}, u32[]{:S(2)}) collective-permute-start(bf16[5,4,1,24,384]{4,3,2,1,0:T(8,128)(2,1)} %bitcast_dynamic-update-slice_fusion.6), channel_id=1, source_target_pairs={{0,18},{2,16},{16,2},{18,0},{1,19},{3,17},{17,3},{19,1},{4,22},{6,... | collective-permute-start | bytes 1105928 | tf_op jit(solution)/shard_map/ppermute | solution.py:64
  66.1 21.7 %collective-permute-start.3 = (bf16[3,4,1,48,384]{4,3,2,1,0:T(8,128)(2,1)}, bf16[3,4,1,48,384]{4,3,2,1,0:T(8,128)(2,1)}, u32[]{:S(2)}, u32[]{:S(2)}) collective-permute-start(bf16[3,4,1,48,384]{4,3,2,1,0:T(8,128)(2,1)} %bitcast_dynamic-update-slice_fusion), channel_id=1, source_target_pairs={{0,2},{2,0},{16,18},{18,16},{1,3},{3,1},{17,19},{19,17},{4,6},{6,4... | collective-permute-start | bytes 1327112 | tf_op jit(solution)/shard_map/ppermute | solution.py:64
  68.4 23.7 %collective-permute-start.4 = (bf16[3,4,1,48,384]{4,3,2,1,0:T(8,128)(2,1)}, bf16[3,4,1,48,384]{4,3,2,1,0:T(8,128)(2,1)}, u32[]{:S(2)}, u32[]{:S(2)}) collective-permute-start(bf16[3,4,1,48,384]{4,3,2,1,0:T(8,128)(2,1)} %bitcast_dynamic-update-slice_fusion), channel_id=1, source_target_pairs={{0,16},{2,18},{16,0},{18,2},{1,17},{3,19},{17,1},{19,3},{4,20},{6,... | collective-permute-start | bytes 1327112 | tf_op jit(solution)/shard_map/ppermute | solution.py:64
  73.9 19.5 %collective-permute-start.5 = (bf16[3,4,1,48,384]{4,3,2,1,0:T(8,128)(2,1)}, bf16[3,4,1,48,384]{4,3,2,1,0:T(8,128)(2,1)}, u32[]{:S(2)}, u32[]{:S(2)}) collective-permute-start(bf16[3,4,1,48,384]{4,3,2,1,0:T(8,128)(2,1)} %bitcast_dynamic-update-slice_fusion), channel_id=1, source_target_pairs={{0,18},{2,16},{16,2},{18,0},{1,19},{3,17},{17,3},{19,1},{4,22},{6,... | collective-permute-start | bytes 1327112 | tf_op jit(solution)/shard_map/ppermute | solution.py:64
  81.5 1.8 copy-start.13
  83.2 1.5 copy-start.4
  85.7 8.8 %copy-start.27 = (f32[768]{0:T(1024)S(1)}, f32[768]{0:T(1024)}, u32[]{:S(2)}) copy-start(f32[768]{0:T(1024)} %param.11) | copy-start | bytes 9220
  87.8 7.1 %copy-start.28 = (f32[2,64]{1,0:T(2,128)}, f32[2,64]{1,0:T(2,128)S(1)}, u32[]{:S(2)}) copy-start(f32[2,64]{1,0:T(2,128)S(1)} %add_rsqrt_fusion) | copy-start | bytes 1540
  111.6 20.5 %copy-start.1 = (bf16[384,768]{1,0:T(8,128)(2,1)S(1)}, bf16[384,768]{1,0:T(8,128)(2,1)}, u32[]{:S(2)}) copy-start(bf16[384,768]{1,0:T(8,128)(2,1)} %reshape.255) | copy-start | bytes 1769476
  122.6 9.1 %all-to-all-start.1 = ((bf16[4,2,6144]{2,1,0:T(2,128)(2,1)}), bf16[4,2,6144]{2,1,0:T(2,128)(2,1)S(1)}, u32[]{:S(2)}, u32[]{:S(2)}) async-start(bf16[4,2,6144]{2,1,0:T(2,128)(2,1)} %copy.166), calls=%async_computation.1 | async-start | bytes 196608 | tf_op jit(solution)/shard_map/all_to_all | solution.py:291
  133.1 13.4 %copy-start.18 = (bf16[256,96]{1,0:T(8,128)(2,1)S(1)}, bf16[256,96]{1,0:T(8,128)(2,1)}, u32[]{:S(2)}) copy-start(bf16[256,96]{1,0:T(8,128)(2,1)} %copy-done.17) | copy-start | bytes 147460
  133.1 13.4 %copy-start.25 = (f32[256]{0:T(256)S(1)}, f32[256]{0:T(256)}, u32[]{:S(2)}) copy-start(f32[256]{0:T(256)} %copy-done.24) | copy-start | bytes 3076
  133.7 2.3 %collective-permute-start.20 = (bf16[2,64,384]{2,1,0:T(8,128)(2,1)}, bf16[2,64,384]{2,1,0:T(8,128)(2,1)}, u32[]{:S(2)}, u32[]{:S(2)}) collective-permute-start(bf16[2,64,384]{2,1,0:T(8,128)(2,1)} %constant_dynamic-slice_fusion.1), channel_id=1, source_target_pairs={{0,1},{1,0},{2,3},{3,2},{4,5},{5,4},{6,7},{7,6},{8,9},{9,8},{10,11... | collective-permute-start | bytes 294920 | tf_op jit(solution)/shard_map/ppermute | solution.py:125
  136.0 16.9 %copy-start.21 = (bf16[256,96]{0,1:T(8,128)(2,1)S(1)}, bf16[256,96]{0,1:T(8,128)(2,1)}, u32[]{:S(2)}) copy-start(bf16[256,96]{0,1:T(8,128)(2,1)} %convolution_convert_fusion.3) | copy-start | bytes 147460
  143.2 8.9 %all-to-all-start.2 = ((bf16[4,2,3072]{2,1,0:T(2,128)(2,1)}), bf16[4,2,3072]{2,1,0:T(2,128)(2,1)S(1)}, u32[]{:S(2)}, u32[]{:S(2)}) async-start(bf16[4,2,3072]{2,1,0:T(2,128)(2,1)} %reshape.281), calls=%async_computation.2 | async-start | bytes 98304 | tf_op jit(solution)/shard_map/all_to_all | solution.py:378
  152.7 6.5 %copy-start.29 = (f32[2,64]{1,0:T(2,128)S(1)}, f32[2,64]{1,0:T(2,128)}, u32[]{:S(2)}) copy-start(f32[2,64]{1,0:T(2,128)} %copy-done.28) | copy-start | bytes 1540
  155.9 9.5 %all-to-all-start.3 = ((bf16[4,2,9216]{2,1,0:T(2,128)(2,1)}), bf16[4,2,9216]{2,1,0:T(2,128)(2,1)S(1)}, u32[]{:S(2)}, u32[]{:S(2)}) async-start(bf16[4,2,9216]{2,1,0:T(2,128)(2,1)} %reshape.283), calls=%async_computation.3 | async-start | bytes 294912 | tf_op jit(solution)/shard_map/all_to_all | solution.py:389
  166.4 2.3 %copy-start.23 = (f32[384]{0:T(512)S(1)}, f32[384]{0:T(512)}, u32[]{:S(2)}) copy-start(f32[384]{0:T(512)} %dynamic_slice.46) | copy-start | bytes 4612
  167.3 1.3 collective-permute-start.21
  167.5 9.1 %copy-start.11 = (bf16[1,4,4,24,384]{4,3,2,1,0:T(8,128)(2,1)S(1)}, bf16[1,4,4,24,384]{4,3,2,1,0:T(8,128)(2,1)}, u32[]{:S(2)}) copy-start(bf16[1,4,4,24,384]{4,3,2,1,0:T(8,128)(2,1)} %copy-done.10) | copy-start | bytes 884740
  168.7 8.1 %copy-start.9 = (bf16[1,4,4,24,384]{4,3,2,1,0:T(8,128)(2,1)S(1)}, bf16[1,4,4,24,384]{4,3,2,1,0:T(8,128)(2,1)}, u32[]{:S(2)}) copy-start(bf16[1,4,4,24,384]{4,3,2,1,0:T(8,128)(2,1)} %copy-done.8) | copy-start | bytes 884740
  171.5 5.6 %copy-start.7 = (bf16[1,4,4,24,384]{4,3,2,1,0:T(8,128)(2,1)S(1)}, bf16[1,4,4,24,384]{4,3,2,1,0:T(8,128)(2,1)}, u32[]{:S(2)}) copy-start(bf16[1,4,4,24,384]{4,3,2,1,0:T(8,128)(2,1)} %copy-done.6) | copy-start | bytes 884740
  171.6 9.2 %copy-start.5 = (bf16[1,4,4,24,384]{4,3,2,1,0:T(8,128)(2,1)S(1)}, bf16[1,4,4,24,384]{4,3,2,1,0:T(8,128)(2,1)}, u32[]{:S(2)}) copy-start(bf16[1,4,4,24,384]{4,3,2,1,0:T(8,128)(2,1)} %copy-done.4) | copy-start | bytes 884740
  171.7 9.2 %copy-start.3 = (bf16[1,4,4,24,384]{4,3,2,1,0:T(8,128)(2,1)S(1)}, bf16[1,4,4,24,384]{4,3,2,1,0:T(8,128)(2,1)}, u32[]{:S(2)}) copy-start(bf16[1,4,4,24,384]{4,3,2,1,0:T(8,128)(2,1)} %copy-done.2) | copy-start | bytes 884740
  171.9 4.9 %collective-permute-start.23 = (bf16[2,384]{1,0:T(2,128)(2,1)S(1)}, bf16[2,384]{1,0:T(2,128)(2,1)S(1)}, u32[]{:S(2)}, u32[]{:S(2)}) collective-permute-start(bf16[2,384]{1,0:T(2,128)(2,1)S(1)} %get-tuple-element.111), channel_id=1, source_target_pairs={{0,4},{4,8},{8,12},{1,5},{5,9},{9,13},{2,6},{6,10},{10,14},{3,7},{... | collective-permute-start | bytes 4616 | tf_op jit(solution)/shard_map/ppermute | solution.py:23
  175.2 5.5 %collective-permute-start.22 = (bf16[2,384]{1,0:T(2,128)(2,1)S(1)}, bf16[2,384]{1,0:T(2,128)(2,1)S(1)}, u32[]{:S(2)}, u32[]{:S(2)}) collective-permute-start(bf16[2,384]{1,0:T(2,128)(2,1)S(1)} %get-tuple-element.110), channel_id=1, source_target_pairs={{4,0},{8,4},{12,8},{5,1},{9,5},{13,9},{6,2},{10,6},{14,10},{7,3},{... | collective-permute-start | bytes 4616 | tf_op jit(solution)/shard_map/ppermute | solution.py:25
  176.8 5.9 %copy-start.20 = (f32[1,128,384]{2,1,0:T(8,128)S(1)}, f32[1,128,384]{2,1,0:T(8,128)}, u32[]{:S(2)}) copy-start(f32[1,128,384]{2,1,0:T(8,128)} %param.8) | copy-start | bytes 589828
  181.2 1.4 collective-permute-start.24
  (10 other events, 11.6 us)

commit v12 on v8

--- a/solution.py
+++ b/solution.py
@@ -79,6 +79,14 @@
     return lax.ppermute(cells, "mp", [(0, 1), (1, 0)])
 
 
+def join_mp(cells, dim):
+    other = swap_mp(cells)
+    first = lax.axis_index("mp") == 0
+    return jnp.where(
+        first, jnp.concatenate([cells, other], axis=dim), jnp.concatenate([other, cells], axis=dim)
+    )
+
+
 def add_halves(cells, dim):
     half = cells.shape[dim] // 2
     index = lax.axis_index("mp")
@@ -183,7 +191,7 @@
     paired = jax.nn.gelu(pre_act).reshape(pass_count, positions // 2, 2, half_width)
     pooled = (0.5 * (paired[:, :, 0] + paired[:, :, 1])).astype(jnp.bfloat16)
     pooled_wide = lax.optimization_barrier(pooled).astype(jnp.float32)
-    whole = lax.all_gather(pooled, "mp", axis=2, tiled=True)
+    whole = join_mp(pooled, 2)
     whole_wide = whole.astype(jnp.float32)
     row_scale = lax.rsqrt(jnp.mean(whole_wide * whole_wide, axis=2, keepdims=True) + epsilon)
     normed = (whole_wide * row_scale * norm_gain).astype(jnp.bfloat16)
@@ -304,7 +312,7 @@
     sub_rows = rows // query_groups
     difference = mixed - clean_mixed
     difference_half = difference.astype(jnp.bfloat16)
-    difference_whole = lax.all_gather(difference_half, "mp", axis=1, tiled=True)
+    difference_whole = join_mp(difference_half, 1)
     out_grad = jnp.einsum(
         "rf,hf->rh",
         difference_whole,
@@ -365,7 +373,8 @@
     offset_mp = lax.axis_index("mp") * half_width
     gain_own = lax.dynamic_slice_in_dim(norm_gain, offset_mp, half_width, 0)
     normed_grad = add_halves(normed_terms.astype(jnp.bfloat16), 1)
-    weighted = lax.psum(jnp.sum(normed_grad * gain_own * pooled_wide, axis=1, keepdims=True), "mp")
+    weighted_own = jnp.sum(normed_grad * gain_own * pooled_wide, axis=1, keepdims=True)
+    weighted = weighted_own + swap_mp(weighted_own)
     pooled_grad = (
         difference + row_scale * gain_own * normed_grad - pooled_wide * row_scale**3 * weighted / F
     )

time: 163 us -> 164 us (level)
  blocking collectives: 6.43 us -> 0 us
  starting transfers between devices: 51.1 us -> 54.2 us
  matrix products: 7.18 us -> 8.97 us
    all_gather x2 -> x0, blocking collectives: 3.82 us -> none  [the longest x1 1.95 us: forward(): whole = lax.all_gather(pooled, 'mp', axis=2, tiled=True)]
    psum x1 -> x0, blocking collectives: 2.6 us -> none  [shards(): lax.psum(jnp.sum(normed_grad * gain_own * pooled_wide, axis=1, keepdims=T...]
    ppermute x9, starting transfers between devices: 13.3 us -> 15.7 us  [gather_seq(): arrived = lax.ppermute(along, spread, [(i, i ^ mask) for i in range(count)])]
    ppermute x9, waiting for transfers between devices: 25.4 us -> 23.1 us  [gather_seq(): arrived = lax.ppermute(along, spread, [(i, i ^ mask) for i in range(count)])]
    ppermute x3 -> x6, waiting for transfers between devices: 2.32 us -> 4.43 us  [swap_mp(): return lax.ppermute(cells, 'mp', [(0, 1), (1, 0)])]
    unnamed x52 -> x54, local copies, waits for them, and re-layouts: 2.83 us -> 4.08 us
  transfers between devices with their start and end apart: 29 -> 32, of which waited for: 16 -> 18; matrix products, arithmetic and copies ran while one was open for 17% -> 17% of each run, Pallas kernels for 0% -> 0%
where the time goes in v12:
time: 164 us; the launch traced here: 163 us
  waiting for transfers between devices  62.1 us (38%)
  starting transfers between devices  54.2 us (33%)
  local copies, waits for them, and re-layouts  28.1 us (17%)
  matrix products  8.97 us (5%)
  other arithmetic  7.86 us (5%)
  between operations  1.99 us (1%)
    ppermute x9, waiting for transfers between devices, gather_seq(): arrived = lax.ppermute(along, spread, [(i, i ^ mask) for i in range(count)])  23.1 us
    ppermute x9, starting transfers between devices, gather_seq(): arrived = lax.ppermute(along, spread, [(i, i ^ mask) for i in range(count)])  15.7 us
    ppermute x9, starting transfers between devices, gather_seq(): lax.ppermute(piece, 'seq', [(i, (i + shift) % ring) for i in range(ring)])  14.7 us
    all_to_all x1, waiting for transfers between devices, forward(): lax.all_to_all(jnp.concatenate([query_send, keyval_send], axis=2), 'seq',...  8.57 us
    ppermute x9, waiting for transfers between devices, gather_seq(): lax.ppermute(piece, 'seq', [(i, (i + shift) % ring) for i in range(ring)])  6.97 us
    all_to_all x1, waiting for transfers between devices, shards(): lax.all_to_all(jnp.concatenate([query_grad.reshape(devices, query_len).as...  5.89 us
    ppermute x2, starting transfers between devices, with_halo(): lax.ppermute(tail, axis, [(i, (i + 1) % count) for i in range(ends)])  5.71 us
    all_to_all x1, waiting for transfers between devices, shards(): lax.all_to_all(grad_send, 'seq', split_axis=0, concat_axis=1, tiled=True)  5.45 us
  transfers between devices with their start and end apart: 32, of which 18 were waited for; matrix products, arithmetic and copies ran while one was open for 17% of the time, Pallas kernels for 0%

profile of v12, /device:TPU:0, one launch (start us, length us, event | category | flops | bytes accessed | tf_op | source)
XLA Modules:
  0.0 163.2 jit_solution(12566444222469938902)
XLA Ops:
  1.6 3.1 %collective-permute-start = (bf16[144,384]{1,0:T(8,128)(2,1)S(1)}, bf16[144,384]{1,0:T(8,128)(2,1)S(1)}, u32[]{:S(2)}, u32[]{:S(2)}) collective-permute-start(bf16[144,384]{1,0:T(8,128)(2,1)S(1)} %get-tuple-element.80), channel_id=1, source_target_pairs={{0,4},{4,8},{8,12},{12,0},{1,5},{5,9},{9,13},{13,1},{2,6},{6,10},{... | collective-permute-start | bytes 331784 | tf_op jit(solution)/shard_map/ppermute | solution.py:48
  4.7 2.6 %collective-permute-start.1 = (bf16[144,384]{1,0:T(8,128)(2,1)S(1)}, bf16[144,384]{1,0:T(8,128)(2,1)S(1)}, u32[]{:S(2)}, u32[]{:S(2)}) collective-permute-start(bf16[144,384]{1,0:T(8,128)(2,1)S(1)} %get-tuple-element.80), channel_id=1, source_target_pairs={{0,8},{4,12},{8,0},{12,4},{1,9},{5,13},{9,1},{13,5},{2,10},{6,14},... | collective-permute-start | bytes 331784 | tf_op jit(solution)/shard_map/ppermute | solution.py:48
  7.3 1.3 collective-permute-start.2
  8.7 1.0 add_convert_fusion.2
  10.4 2.6 %collective-permute-start.6 = (bf16[2,2,384]{2,1,0:T(2,128)(2,1)S(1)}, bf16[2,2,384]{2,1,0:T(2,128)(2,1)S(1)}, u32[]{:S(2)}, u32[]{:S(2)}) collective-permute-start(bf16[2,2,384]{2,1,0:T(2,128)(2,1)S(1)} %get-tuple-element.108), channel_id=1, source_target_pairs={{0,4},{4,8},{8,12},{1,5},{5,9},{9,13},{2,6},{6,10},{10,14},{3,7},{... | collective-permute-start | bytes 9224 | tf_op jit(solution)/shard_map/ppermute | solution.py:23
  13.0 1.3 collective-permute-start.13
  14.3 1.0 copy.195
  17.8 2.6 %collective-permute-start.15 = (bf16[48,384]{1,0:T(8,128)(2,1)S(1)}, bf16[48,384]{1,0:T(8,128)(2,1)S(1)}, u32[]{:S(2)}, u32[]{:S(2)}) collective-permute-start(bf16[48,384]{1,0:T(8,128)(2,1)S(1)} %get-tuple-element.76), channel_id=1, source_target_pairs={{0,4},{4,8},{8,12},{12,0},{1,5},{5,9},{9,13},{13,1},{2,6},{6,10},{... | collective-permute-start | bytes 110600 | tf_op jit(solution)/shard_map/ppermute | solution.py:48
  20.8 2.7 %collective-permute-done.15 = bf16[48,384]{1,0:T(8,128)(2,1)S(1)} collective-permute-done((bf16[48,384]{1,0:T(8,128)(2,1)S(1)}, bf16[48,384]{1,0:T(8,128)(2,1)S(1)}, u32[]{:S(2)}, u32[]{:S(2)}) %collective-permute-start.15) | collective-permute-done | bytes 36896 | tf_op jit(solution)/shard_map/ppermute | solution.py:48
  25.3 0.9 collective-permute-start.7
  26.8 1.7 %collective-permute-done.17 = bf16[48,384]{1,0:T(8,128)(2,1)S(1)} collective-permute-done((bf16[48,384]{1,0:T(8,128)(2,1)S(1)}, bf16[48,384]{1,0:T(8,128)(2,1)S(1)}, u32[]{:S(2)}, u32[]{:S(2)}) %collective-permute-start.17) | collective-permute-done | bytes 36896 | tf_op jit(solution)/shard_map/ppermute | solution.py:48
  30.1 0.9 bitcast_dynamic-update-slice_fusion.10
  31.1 1.3 collective-permute-done.7
  32.4 2.3 %collective-permute-start.9 = (bf16[120,384]{1,0:T(8,128)(2,1)S(1)}, bf16[120,384]{1,0:T(8,128)(2,1)S(1)}, u32[]{:S(2)}, u32[]{:S(2)}) collective-permute-start(bf16[120,384]{1,0:T(8,128)(2,1)S(1)} %get-tuple-element.78), channel_id=1, source_target_pairs={{0,12},{4,0},{8,4},{12,8},{1,13},{5,1},{9,5},{13,9},{2,14},{6,2},{... | collective-permute-start | bytes 276488 | tf_op jit(solution)/shard_map/ppermute | solution.py:48
  34.7 1.5 collective-permute-start.18
  36.9 1.5 collective-permute-start.19
  38.7 1.5 collective-permute-start.20
  40.8 1.6 collective-permute-start.11
  42.7 7.1 %collective-permute-done.10 = bf16[4,120,384]{2,1,0:T(8,128)(2,1)S(1)} collective-permute-done((bf16[4,120,384]{2,1,0:T(8,128)(2,1)S(1)}, bf16[4,120,384]{2,1,0:T(8,128)(2,1)S(1)}, u32[]{:S(2)}, u32[]{:S(2)}) %collective-permute-start.10) | collective-permute-done | bytes 368672 | tf_op jit(solution)/shard_map/ppermute | solution.py:59
  49.8 3.3 %collective-permute-start.12 = (bf16[4,120,384]{2,1,0:T(8,128)(2,1)S(1)}, bf16[4,120,384]{2,1,0:T(8,128)(2,1)S(1)}, u32[]{:S(2)}, u32[]{:S(2)}) collective-permute-start(bf16[4,120,384]{2,1,0:T(8,128)(2,1)S(1)} %bitcast_dynamic-update-slice_fusion.16), channel_id=1, source_target_pairs={{0,18},{2,16},{16,2},{18,0},{1,19},{3,17},{17,3},{19,1},{4,22},{6,... | collective-permute-start | bytes 1105928 | tf_op jit(solution)/shard_map/ppermute | solution.py:59
  53.9 8.7 %collective-permute-done.12 = bf16[4,120,384]{2,1,0:T(8,128)(2,1)S(1)} collective-permute-done((bf16[4,120,384]{2,1,0:T(8,128)(2,1)S(1)}, bf16[4,120,384]{2,1,0:T(8,128)(2,1)S(1)}, u32[]{:S(2)}, u32[]{:S(2)}) %collective-permute-start.12) | collective-permute-done | bytes 368672 | tf_op jit(solution)/shard_map/ppermute | solution.py:59
  62.5 1.2 collective-permute-start.4
  65.3 1.3 fusion.23
  66.5 1.2 reshape.239
  68.1 3.9 %collective-permute-start.5 = (bf16[4,144,384]{2,1,0:T(8,128)(2,1)S(1)}, bf16[4,144,384]{2,1,0:T(8,128)(2,1)S(1)}, u32[]{:S(2)}, u32[]{:S(2)}) collective-permute-start(bf16[4,144,384]{2,1,0:T(8,128)(2,1)S(1)} %bitcast_dynamic-update-slice_fusion.12), channel_id=1, source_target_pairs={{0,18},{2,16},{16,2},{18,0},{1,19},{3,17},{17,3},{19,1},{4,22},{6,... | collective-permute-start | bytes 1327112 | tf_op jit(solution)/shard_map/ppermute | solution.py:59
  72.0 1.1 bitcast_dynamic-update-slice_fusion.1
  73.1 7.3 %collective-permute-done.4 = bf16[4,144,384]{2,1,0:T(8,128)(2,1)} collective-permute-done((bf16[4,144,384]{2,1,0:T(8,128)(2,1)S(1)}, bf16[4,144,384]{2,1,0:T(8,128)(2,1)}, u32[]{:S(2)}, u32[]{:S(2)}) %collective-permute-start.4) | collective-permute-done | bytes 442400 | tf_op jit(solution)/shard_map/ppermute | solution.py:59
  80.4 1.1 bitcast_dynamic-update-slice_fusion
  84.0 1.0 pad_maximum_fusion
  85.0 3.5 %all-to-all-start = ((bf16[4,2,18432]{2,1,0:T(2,128)(2,1)}), bf16[4,2,18432]{2,1,0:T(2,128)(2,1)S(1)}, u32[]{:S(2)}, u32[]{:S(2)}) async-start(bf16[4,2,18432]{2,1,0:T(2,128)(2,1)} %pad_maximum_fusion), calls=%async_computation | async-start | bytes 589824 | tf_op jit(solution)/shard_map/all_to_all | solution.py:231
  90.4 8.6 %all-to-all-done = bf16[4,2,18432]{2,1,0:T(2,128)(2,1)S(1)} async-done(((bf16[4,2,18432]{2,1,0:T(2,128)(2,1)}), bf16[4,2,18432]{2,1,0:T(2,128)(2,1)S(1)}, u32[]{:S(2)}, u32[]{:S(2)}) %all-to-all-start) | async-done | bytes 294944 | tf_op jit(solution)/shard_map/all_to_all | solution.py:231
  102.9 4.1 %all-to-all-start.1 = ((bf16[4,2,6144]{2,1,0:T(2,128)(2,1)}), bf16[4,2,6144]{2,1,0:T(2,128)(2,1)}, u32[]{:S(2)}, u32[]{:S(2)}) async-start(bf16[4,2,6144]{2,1,0:T(2,128)(2,1)} %copy.193), calls=%async_computation.1 | async-start | bytes 196608 | tf_op jit(solution)/shard_map/all_to_all | solution.py:253
  108.7 4.0 %all-to-all-done.1 = bf16[4,2,6144]{2,1,0:T(2,128)(2,1)} async-done(((bf16[4,2,6144]{2,1,0:T(2,128)(2,1)}), bf16[4,2,6144]{2,1,0:T(2,128)(2,1)}, u32[]{:S(2)}, u32[]{:S(2)}) %all-to-all-start.1) | async-done | bytes 98336 | tf_op jit(solution)/shard_map/all_to_all | solution.py:253
  112.7 1.0 reshape.243
  114.4 1.3 collective-permute-done.21
  118.1 1.0 reduce.7
  119.8 3.3 %all-to-all-start.2 = ((bf16[4,2,3072]{2,1,0:T(2,128)(2,1)}), bf16[4,2,3072]{2,1,0:T(2,128)(2,1)S(1)}, u32[]{:S(2)}, u32[]{:S(2)}) async-start(bf16[4,2,3072]{2,1,0:T(2,128)(2,1)} %reshape.263), calls=%async_computation.2 | async-start | bytes 98304 | tf_op jit(solution)/shard_map/all_to_all | solution.py:327
  123.3 5.4 %all-to-all-done.2 = bf16[4,2,3072]{2,1,0:T(2,128)(2,1)S(1)} async-done(((bf16[4,2,3072]{2,1,0:T(2,128)(2,1)}), bf16[4,2,3072]{2,1,0:T(2,128)(2,1)S(1)}, u32[]{:S(2)}, u32[]{:S(2)}) %all-to-all-start.2) | async-done | bytes 49184 | tf_op jit(solution)/shard_map/all_to_all | solution.py:327
  130.4 1.1 fusion.7
  131.7 1.0 fusion.12
  135.1 4.0 %all-to-all-start.3 = ((bf16[4,2,9216]{2,1,0:T(2,128)(2,1)}), bf16[4,2,9216]{2,1,0:T(2,128)(2,1)}, u32[]{:S(2)}, u32[]{:S(2)}) async-start(bf16[4,2,9216]{2,1,0:T(2,128)(2,1)} %reshape.265), calls=%async_computation.3 | async-start | bytes 294912 | tf_op jit(solution)/shard_map/all_to_all | solution.py:338
  139.3 5.9 %all-to-all-done.3 = bf16[4,2,9216]{2,1,0:T(2,128)(2,1)} async-done(((bf16[4,2,9216]{2,1,0:T(2,128)(2,1)}), bf16[4,2,9216]{2,1,0:T(2,128)(2,1)}, u32[]{:S(2)}, u32[]{:S(2)}) %all-to-all-start.3) | async-done | bytes 147488 | tf_op jit(solution)/shard_map/all_to_all | solution.py:338
  145.2 1.0 reshape.266
  148.2 1.2 collective-permute-done.23
  149.7 1.0 collective-permute-done.24
  151.3 3.1 %collective-permute-start.26 = (bf16[2,384]{1,0:T(2,128)(2,1)S(1)}, bf16[2,384]{1,0:T(2,128)(2,1)S(1)}, u32[]{:S(2)}, u32[]{:S(2)}) collective-permute-start(bf16[2,384]{1,0:T(2,128)(2,1)S(1)} %get-tuple-element.113), channel_id=1, source_target_pairs={{0,4},{4,8},{8,12},{1,5},{5,9},{9,13},{2,6},{6,10},{10,14},{3,7},{... | collective-permute-start | bytes 4616 | tf_op jit(solution)/shard_map/ppermute | solution.py:23
  154.7 1.3 collective-permute-start.25
  156.5 3.7 %collective-permute-done.25 = bf16[2,384]{1,0:T(2,128)(2,1)S(1)} collective-permute-done((bf16[2,384]{1,0:T(2,128)(2,1)S(1)}, bf16[2,384]{1,0:T(2,128)(2,1)S(1)}, u32[]{:S(2)}, u32[]{:S(2)}) %collective-permute-start.25) | collective-permute-done | bytes 1568 | tf_op jit(solution)/shard_map/ppermute | solution.py:25
  (223 shorter events, 37.0 us)
Async XLA Ops:
  0.6 20.1 %copy-start.13 = (bf16[1,128,384]{2,1,0:T(8,128)(2,1)S(1)}, bf16[1,128,384]{2,1,0:T(8,128)(2,1)}, u32[]{:S(2)}) copy-start(bf16[1,128,384]{2,1,0:T(8,128)(2,1)} %param.7) | copy-start | bytes 294916
  1.6 37.0 %collective-permute-start = (bf16[144,384]{1,0:T(8,128)(2,1)S(1)}, bf16[144,384]{1,0:T(8,128)(2,1)S(1)}, u32[]{:S(2)}, u32[]{:S(2)}) collective-permute-start(bf16[144,384]{1,0:T(8,128)(2,1)S(1)} %get-tuple-element.80), channel_id=1, source_target_pairs={{0,4},{4,8},{8,12},{12,0},{1,5},{5,9},{9,13},{13,1},{2,6},{6,10},{... | collective-permute-start | bytes 331784 | tf_op jit(solution)/shard_map/ppermute | solution.py:48
  4.7 35.5 %collective-permute-start.1 = (bf16[144,384]{1,0:T(8,128)(2,1)S(1)}, bf16[144,384]{1,0:T(8,128)(2,1)S(1)}, u32[]{:S(2)}, u32[]{:S(2)}) collective-permute-start(bf16[144,384]{1,0:T(8,128)(2,1)S(1)} %get-tuple-element.80), channel_id=1, source_target_pairs={{0,8},{4,12},{8,0},{12,4},{1,9},{5,13},{9,1},{13,5},{2,10},{6,14},... | collective-permute-start | bytes 331784 | tf_op jit(solution)/shard_map/ppermute | solution.py:48
  7.3 33.5 %collective-permute-start.2 = (bf16[144,384]{1,0:T(8,128)(2,1)S(1)}, bf16[144,384]{1,0:T(8,128)(2,1)S(1)}, u32[]{:S(2)}, u32[]{:S(2)}) collective-permute-start(bf16[144,384]{1,0:T(8,128)(2,1)S(1)} %get-tuple-element.80), channel_id=1, source_target_pairs={{0,12},{4,0},{8,4},{12,8},{1,13},{5,1},{9,5},{13,9},{2,14},{6,2},{... | collective-permute-start | bytes 331784 | tf_op jit(solution)/shard_map/ppermute | solution.py:48
  10.4 7.4 %collective-permute-start.6 = (bf16[2,2,384]{2,1,0:T(2,128)(2,1)S(1)}, bf16[2,2,384]{2,1,0:T(2,128)(2,1)S(1)}, u32[]{:S(2)}, u32[]{:S(2)}) collective-permute-start(bf16[2,2,384]{2,1,0:T(2,128)(2,1)S(1)} %get-tuple-element.108), channel_id=1, source_target_pairs={{0,4},{4,8},{8,12},{1,5},{5,9},{9,13},{2,6},{6,10},{10,14},{3,7},{... | collective-permute-start | bytes 9224 | tf_op jit(solution)/shard_map/ppermute | solution.py:23
  13.0 7.4 %collective-permute-start.13 = (bf16[2,2,384]{2,1,0:T(2,128)(2,1)S(1)}, bf16[2,2,384]{2,1,0:T(2,128)(2,1)S(1)}, u32[]{:S(2)}, u32[]{:S(2)}) collective-permute-start(bf16[2,2,384]{2,1,0:T(2,128)(2,1)S(1)} %get-tuple-element.109), channel_id=1, source_target_pairs={{4,0},{8,4},{12,8},{5,1},{9,5},{13,9},{6,2},{10,6},{14,10},{7,3},{... | collective-permute-start | bytes 9224 | tf_op jit(solution)/shard_map/ppermute | solution.py:25
  17.8 5.8 %collective-permute-start.15 = (bf16[48,384]{1,0:T(8,128)(2,1)S(1)}, bf16[48,384]{1,0:T(8,128)(2,1)S(1)}, u32[]{:S(2)}, u32[]{:S(2)}) collective-permute-start(bf16[48,384]{1,0:T(8,128)(2,1)S(1)} %get-tuple-element.76), channel_id=1, source_target_pairs={{0,4},{4,8},{8,12},{12,0},{1,5},{5,9},{9,13},{13,1},{2,6},{6,10},{... | collective-permute-start | bytes 110600 | tf_op jit(solution)/shard_map/ppermute | solution.py:48
  20.4 4.9 %collective-permute-start.16 = (bf16[48,384]{1,0:T(8,128)(2,1)S(1)}, bf16[48,384]{1,0:T(8,128)(2,1)S(1)}, u32[]{:S(2)}, u32[]{:S(2)}) collective-permute-start(bf16[48,384]{1,0:T(8,128)(2,1)S(1)} %get-tuple-element.76), channel_id=1, source_target_pairs={{0,8},{4,12},{8,0},{12,4},{1,9},{5,13},{9,1},{13,5},{2,10},{6,14},... | collective-permute-start | bytes 110600 | tf_op jit(solution)/shard_map/ppermute | solution.py:48
  23.6 5.0 %collective-permute-start.17 = (bf16[48,384]{1,0:T(8,128)(2,1)S(1)}, bf16[48,384]{1,0:T(8,128)(2,1)S(1)}, u32[]{:S(2)}, u32[]{:S(2)}) collective-permute-start(bf16[48,384]{1,0:T(8,128)(2,1)S(1)} %get-tuple-element.76), channel_id=1, source_target_pairs={{0,12},{4,0},{8,4},{12,8},{1,13},{5,1},{9,5},{13,9},{2,14},{6,2},{... | collective-permute-start | bytes 110600 | tf_op jit(solution)/shard_map/ppermute | solution.py:48
  25.3 7.1 %collective-permute-start.7 = (bf16[120,384]{1,0:T(8,128)(2,1)S(1)}, bf16[120,384]{1,0:T(8,128)(2,1)S(1)}, u32[]{:S(2)}, u32[]{:S(2)}) collective-permute-start(bf16[120,384]{1,0:T(8,128)(2,1)S(1)} %get-tuple-element.78), channel_id=1, source_target_pairs={{0,4},{4,8},{8,12},{12,0},{1,5},{5,9},{9,13},{13,1},{2,6},{6,10},{... | collective-permute-start | bytes 276488 | tf_op jit(solution)/shard_map/ppermute | solution.py:48
  28.6 6.1 %collective-permute-start.8 = (bf16[120,384]{1,0:T(8,128)(2,1)S(1)}, bf16[120,384]{1,0:T(8,128)(2,1)S(1)}, u32[]{:S(2)}, u32[]{:S(2)}) collective-permute-start(bf16[120,384]{1,0:T(8,128)(2,1)S(1)} %get-tuple-element.78), channel_id=1, source_target_pairs={{0,8},{4,12},{8,0},{12,4},{1,9},{5,13},{9,1},{13,5},{2,10},{6,14},... | collective-permute-start | bytes 276488 | tf_op jit(solution)/shard_map/ppermute | solution.py:48
  31.1 7.3 %copy-start.10 = (bf16[4,4,48,384]{3,2,0,1:T(8,128)(2,1)}, bf16[4,4,48,384]{3,2,0,1:T(8,128)(2,1)S(1)}, u32[]{:S(2)}) copy-start(bf16[4,4,48,384]{3,2,0,1:T(8,128)(2,1)S(1)} %bitcast_dynamic-update-slice_fusion.10) | copy-start | bytes 1769476
  32.4 4.6 %collective-permute-start.9 = (bf16[120,384]{1,0:T(8,128)(2,1)S(1)}, bf16[120,384]{1,0:T(8,128)(2,1)S(1)}, u32[]{:S(2)}, u32[]{:S(2)}) collective-permute-start(bf16[120,384]{1,0:T(8,128)(2,1)S(1)} %get-tuple-element.78), channel_id=1, source_target_pairs={{0,12},{4,0},{8,4},{12,8},{1,13},{5,1},{9,5},{13,9},{2,14},{6,2},{... | collective-permute-start | bytes 276488 | tf_op jit(solution)/shard_map/ppermute | solution.py:48
  34.7 53.7 %collective-permute-start.18 = (bf16[4,48,384]{2,1,0:T(8,128)(2,1)}, bf16[4,48,384]{2,1,0:T(8,128)(2,1)}, u32[]{:S(2)}, u32[]{:S(2)}) collective-permute-start(bf16[4,48,384]{2,1,0:T(8,128)(2,1)} %bitcast_dynamic-update-slice_fusion.20), channel_id=1, source_target_pairs={{0,2},{2,0},{16,18},{18,16},{1,3},{3,1},{17,19},{19,17},{4,6},{6,4... | collective-permute-start | bytes 442376 | tf_op jit(solution)/shard_map/ppermute | solution.py:59
  36.9 52.5 %collective-permute-start.19 = (bf16[4,48,384]{2,1,0:T(8,128)(2,1)}, bf16[4,48,384]{2,1,0:T(8,128)(2,1)}, u32[]{:S(2)}, u32[]{:S(2)}) collective-permute-start(bf16[4,48,384]{2,1,0:T(8,128)(2,1)} %bitcast_dynamic-update-slice_fusion.20), channel_id=1, source_target_pairs={{0,16},{2,18},{16,0},{18,2},{1,17},{3,19},{17,1},{19,3},{4,20},{6,... | collective-permute-start | bytes 442376 | tf_op jit(solution)/shard_map/ppermute | solution.py:59
  38.7 68.3 %collective-permute-start.20 = (bf16[4,48,384]{2,1,0:T(8,128)(2,1)}, bf16[4,48,384]{2,1,0:T(8,128)(2,1)}, u32[]{:S(2)}, u32[]{:S(2)}) collective-permute-start(bf16[4,48,384]{2,1,0:T(8,128)(2,1)} %bitcast_dynamic-update-slice_fusion.20), channel_id=1, source_target_pairs={{0,18},{2,16},{16,2},{18,0},{1,19},{3,17},{17,3},{19,1},{4,22},{6,... | collective-permute-start | bytes 442376 | tf_op jit(solution)/shard_map/ppermute | solution.py:59
  40.2 9.6 %collective-permute-start.10 = (bf16[4,120,384]{2,1,0:T(8,128)(2,1)S(1)}, bf16[4,120,384]{2,1,0:T(8,128)(2,1)S(1)}, u32[]{:S(2)}, u32[]{:S(2)}) collective-permute-start(bf16[4,120,384]{2,1,0:T(8,128)(2,1)S(1)} %bitcast_dynamic-update-slice_fusion.16), channel_id=1, source_target_pairs={{0,2},{2,0},{16,18},{18,16},{1,3},{3,1},{17,19},{19,17},{4,6},{6,4... | collective-permute-start | bytes 1105928 | tf_op jit(solution)/shard_map/ppermute | solution.py:59
  40.8 12.3 %collective-permute-start.11 = (bf16[4,120,384]{2,1,0:T(8,128)(2,1)S(1)}, bf16[4,120,384]{2,1,0:T(8,128)(2,1)S(1)}, u32[]{:S(2)}, u32[]{:S(2)}) collective-permute-start(bf16[4,120,384]{2,1,0:T(8,128)(2,1)S(1)} %bitcast_dynamic-update-slice_fusion.16), channel_id=1, source_target_pairs={{0,16},{2,18},{16,0},{18,2},{1,17},{3,19},{17,1},{19,3},{4,20},{6,... | collective-permute-start | bytes 1105928 | tf_op jit(solution)/shard_map/ppermute | solution.py:59
  49.8 12.7 %collective-permute-start.12 = (bf16[4,120,384]{2,1,0:T(8,128)(2,1)S(1)}, bf16[4,120,384]{2,1,0:T(8,128)(2,1)S(1)}, u32[]{:S(2)}, u32[]{:S(2)}) collective-permute-start(bf16[4,120,384]{2,1,0:T(8,128)(2,1)S(1)} %bitcast_dynamic-update-slice_fusion.16), channel_id=1, source_target_pairs={{0,18},{2,16},{16,2},{18,0},{1,19},{3,17},{17,3},{19,1},{4,22},{6,... | collective-permute-start | bytes 1105928 | tf_op jit(solution)/shard_map/ppermute | solution.py:59
  53.2 15.0 %collective-permute-start.3 = (bf16[4,144,384]{2,1,0:T(8,128)(2,1)S(1)}, bf16[4,144,384]{2,1,0:T(8,128)(2,1)}, u32[]{:S(2)}, u32[]{:S(2)}) collective-permute-start(bf16[4,144,384]{2,1,0:T(8,128)(2,1)S(1)} %bitcast_dynamic-update-slice_fusion.12), channel_id=1, source_target_pairs={{0,2},{2,0},{16,18},{18,16},{1,3},{3,1},{17,19},{19,17},{4,6},{6,4... | collective-permute-start | bytes 1327112 | tf_op jit(solution)/shard_map/ppermute | solution.py:59
  62.5 17.9 %collective-permute-start.4 = (bf16[4,144,384]{2,1,0:T(8,128)(2,1)S(1)}, bf16[4,144,384]{2,1,0:T(8,128)(2,1)}, u32[]{:S(2)}, u32[]{:S(2)}) collective-permute-start(bf16[4,144,384]{2,1,0:T(8,128)(2,1)S(1)} %bitcast_dynamic-update-slice_fusion.12), channel_id=1, source_target_pairs={{0,16},{2,18},{16,0},{18,2},{1,17},{3,19},{17,1},{19,3},{4,20},{6,... | collective-permute-start | bytes 1327112 | tf_op jit(solution)/shard_map/ppermute | solution.py:59
  68.1 13.9 %copy-start.14 = (bf16[2,64,384]{2,1,0:T(8,128)(2,1)}, bf16[2,64,384]{2,1,0:T(8,128)(2,1)S(1)}, u32[]{:S(2)}) copy-start(bf16[2,64,384]{2,1,0:T(8,128)(2,1)S(1)} %fusion.75) | copy-start | bytes 294916
  68.1 13.4 %collective-permute-start.5 = (bf16[4,144,384]{2,1,0:T(8,128)(2,1)S(1)}, bf16[4,144,384]{2,1,0:T(8,128)(2,1)S(1)}, u32[]{:S(2)}, u32[]{:S(2)}) collective-permute-start(bf16[4,144,384]{2,1,0:T(8,128)(2,1)S(1)} %bitcast_dynamic-update-slice_fusion.12), channel_id=1, source_target_pairs={{0,18},{2,16},{16,2},{18,0},{1,19},{3,17},{17,3},{19,1},{4,22},{6,... | collective-permute-start | bytes 1327112 | tf_op jit(solution)/shard_map/ppermute | solution.py:59
  80.4 1.4 collective-permute-start.14
  82.9 5.5 %copy-start.11 = (bf16[4,4,48,384]{3,2,0,1:T(8,128)(2,1)S(1)}, bf16[4,4,48,384]{3,2,0,1:T(8,128)(2,1)}, u32[]{:S(2)}) copy-start(bf16[4,4,48,384]{3,2,0,1:T(8,128)(2,1)} %copy-done.10) | copy-start | bytes 1769476
  85.0 13.9 %all-to-all-start = ((bf16[4,2,18432]{2,1,0:T(2,128)(2,1)}), bf16[4,2,18432]{2,1,0:T(2,128)(2,1)S(1)}, u32[]{:S(2)}, u32[]{:S(2)}) async-start(bf16[4,2,18432]{2,1,0:T(2,128)(2,1)} %pad_maximum_fusion), calls=%async_computation | async-start | bytes 589824 | tf_op jit(solution)/shard_map/all_to_all | solution.py:231
  100.7 7.2 %copy-start.21 = (bf16[256,96]{0,1:T(8,128)(2,1)}, bf16[256,96]{0,1:T(8,128)(2,1)S(1)}, u32[]{:S(2)}) copy-start(bf16[256,96]{0,1:T(8,128)(2,1)S(1)} %convolution_convert_fusion.4) | copy-start | bytes 147460
  102.9 9.8 %all-to-all-start.1 = ((bf16[4,2,6144]{2,1,0:T(2,128)(2,1)}), bf16[4,2,6144]{2,1,0:T(2,128)(2,1)}, u32[]{:S(2)}, u32[]{:S(2)}) async-start(bf16[4,2,6144]{2,1,0:T(2,128)(2,1)} %copy.193), calls=%async_computation.1 | async-start | bytes 196608 | tf_op jit(solution)/shard_map/all_to_all | solution.py:253
  108.4 7.3 %copy-start.15 = (bf16[2,64,384]{2,1,0:T(8,128)(2,1)S(1)}, bf16[2,64,384]{2,1,0:T(8,128)(2,1)}, u32[]{:S(2)}) copy-start(bf16[2,64,384]{2,1,0:T(8,128)(2,1)} %copy-done.14) | copy-start | bytes 294916
  114.0 9.1 %copy-start.17 = (bf16[256,96]{1,0:T(8,128)(2,1)S(1)}, bf16[256,96]{1,0:T(8,128)(2,1)}, u32[]{:S(2)}) copy-start(bf16[256,96]{1,0:T(8,128)(2,1)} %copy-done.16) | copy-start | bytes 147460
  114.3 1.4 collective-permute-start.21
  115.8 1.3 collective-permute-start.22
  116.7 12.5 %copy-start.19 = (bf16[256,192]{1,0:T(8,128)(2,1)}, bf16[256,192]{1,0:T(8,128)(2,1)S(1)}, u32[]{:S(2)}) copy-start(bf16[256,192]{1,0:T(8,128)(2,1)S(1)} %squeeze.87) | copy-start | bytes 294916
  116.8 14.8 %copy-start.18 = (bf16[256,96]{1,0:T(8,128)(2,1)S(1)}, bf16[256,96]{1,0:T(8,128)(2,1)}, u32[]{:S(2)}) copy-start(bf16[256,96]{1,0:T(8,128)(2,1)} %copy-done.16) | copy-start | bytes 147460
  119.8 8.9 %all-to-all-start.2 = ((bf16[4,2,3072]{2,1,0:T(2,128)(2,1)}), bf16[4,2,3072]{2,1,0:T(2,128)(2,1)S(1)}, u32[]{:S(2)}, u32[]{:S(2)}) async-start(bf16[4,2,3072]{2,1,0:T(2,128)(2,1)} %reshape.263), calls=%async_computation.2 | async-start | bytes 98304 | tf_op jit(solution)/shard_map/all_to_all | solution.py:327
  129.5 9.7 %copy-start.12 = (f32[2,128,384]{2,1,0:T(8,128)S(1)}, f32[2,128,384]{2,1,0:T(8,128)}, u32[]{:S(2)}) copy-start(f32[2,128,384]{2,1,0:T(8,128)} %get-tuple-element.124) | copy-start | bytes 1179652
  135.1 10.1 %all-to-all-start.3 = ((bf16[4,2,9216]{2,1,0:T(2,128)(2,1)}), bf16[4,2,9216]{2,1,0:T(2,128)(2,1)}, u32[]{:S(2)}, u32[]{:S(2)}) async-start(bf16[4,2,9216]{2,1,0:T(2,128)(2,1)} %reshape.265), calls=%async_computation.3 | async-start | bytes 294912 | tf_op jit(solution)/shard_map/all_to_all | solution.py:338
  148.0 8.0 %copy-start.9 = (bf16[1,4,96,384]{3,2,0,1:T(8,128)(2,1)S(1)}, bf16[1,4,96,384]{3,2,0,1:T(8,128)(2,1)}, u32[]{:S(2)}) copy-start(bf16[1,4,96,384]{3,2,0,1:T(8,128)(2,1)} %copy-done.8) | copy-start | bytes 884740
  148.1 1.3 collective-permute-start.23
  149.5 6.8 %copy-start.7 = (bf16[1,4,96,384]{3,2,0,1:T(8,128)(2,1)S(1)}, bf16[1,4,96,384]{3,2,0,1:T(8,128)(2,1)}, u32[]{:S(2)}) copy-start(bf16[1,4,96,384]{3,2,0,1:T(8,128)(2,1)} %copy-done.6) | copy-start | bytes 884740
  149.5 1.2 collective-permute-start.24
  150.8 9.4 %copy-start.5 = (bf16[1,4,96,384]{3,2,0,1:T(8,128)(2,1)S(1)}, bf16[1,4,96,384]{3,2,0,1:T(8,128)(2,1)}, u32[]{:S(2)}) copy-start(bf16[1,4,96,384]{3,2,0,1:T(8,128)(2,1)} %copy-done.4) | copy-start | bytes 884740
  150.9 9.5 %copy-start.3 = (bf16[1,4,96,384]{3,2,0,1:T(8,128)(2,1)S(1)}, bf16[1,4,96,384]{3,2,0,1:T(8,128)(2,1)}, u32[]{:S(2)}) copy-start(bf16[1,4,96,384]{3,2,0,1:T(8,128)(2,1)} %copy-done.2) | copy-start | bytes 884740
  151.3 5.0 %collective-permute-start.26 = (bf16[2,384]{1,0:T(2,128)(2,1)S(1)}, bf16[2,384]{1,0:T(2,128)(2,1)S(1)}, u32[]{:S(2)}, u32[]{:S(2)}) collective-permute-start(bf16[2,384]{1,0:T(2,128)(2,1)S(1)} %get-tuple-element.113), channel_id=1, source_target_pairs={{0,4},{4,8},{8,12},{1,5},{5,9},{9,13},{2,6},{6,10},{10,14},{3,7},{... | collective-permute-start | bytes 4616 | tf_op jit(solution)/shard_map/ppermute | solution.py:23
  154.4 6.3 %copy-start.1 = (bf16[1,4,96,384]{3,2,0,1:T(8,128)(2,1)S(1)}, bf16[1,4,96,384]{3,2,0,1:T(8,128)(2,1)}, u32[]{:S(2)}) copy-start(bf16[1,4,96,384]{3,2,0,1:T(8,128)(2,1)} %copy-done) | copy-start | bytes 884740
  154.7 5.5 %collective-permute-start.25 = (bf16[2,384]{1,0:T(2,128)(2,1)S(1)}, bf16[2,384]{1,0:T(2,128)(2,1)S(1)}, u32[]{:S(2)}, u32[]{:S(2)}) collective-permute-start(bf16[2,384]{1,0:T(2,128)(2,1)S(1)} %get-tuple-element.112), channel_id=1, source_target_pairs={{4,0},{8,4},{12,8},{5,1},{9,5},{13,9},{6,2},{10,6},{14,10},{7,3},{... | collective-permute-start | bytes 4616 | tf_op jit(solution)/shard_map/ppermute | solution.py:25
  156.3 6.2 %copy-start.20 = (f32[1,128,384]{2,1,0:T(8,128)S(1)}, f32[1,128,384]{2,1,0:T(8,128)}, u32[]{:S(2)}) copy-start(f32[1,128,384]{2,1,0:T(8,128)} %param.8) | copy-start | bytes 589828
  160.9 1.4 collective-permute-start.27
  (8 other events, 9.9 us)

commit v13 on v8

--- a/solution.py
+++ b/solution.py
@@ -166,7 +166,7 @@
 
 
 def forward(stack, conv_weight, conv_bias, norm_gain, qkv_weight, out_weight):
-    pass_count, positions, channels = stack.shape
+    pass_count, positions, _ = stack.shape
     reach = KW // 2
     half_width = conv_weight.shape[2]
     padded_input = with_halo(stack, (("seq", 1),), reach)
@@ -285,7 +285,7 @@
     (
         pre_act,
         pooled_wide,
-        whole_wide,
+        _,
         row_scale,
         query_heads,
         keyval_heads,
@@ -365,7 +365,8 @@
     offset_mp = lax.axis_index("mp") * half_width
     gain_own = lax.dynamic_slice_in_dim(norm_gain, offset_mp, half_width, 0)
     normed_grad = add_halves(normed_terms.astype(jnp.bfloat16), 1)
-    weighted = lax.psum(jnp.sum(normed_grad * gain_own * pooled_wide, axis=1, keepdims=True), "mp")
+    weighted_own = jnp.sum(normed_grad * gain_own * pooled_wide, axis=1, keepdims=True)
+    weighted = weighted_own + swap_mp(weighted_own)
     pooled_grad = (
         difference + row_scale * gain_own * normed_grad - pooled_wide * row_scale**3 * weighted / F
     )

time: 163 us -> 162 us (level)
  blocking collectives: 6.43 us -> 3.82 us
    psum x1 -> x0, blocking collectives: 2.6 us -> none  [shards(): lax.psum(jnp.sum(normed_grad * gain_own * pooled_wide, axis=1, keepdims=T...]
    ppermute x3 -> x4, waiting for transfers between devices: 2.32 us -> 3.32 us  [swap_mp(): return lax.ppermute(cells, 'mp', [(0, 1), (1, 0)])]
  transfers between devices with their start and end apart: 29 -> 30, of which waited for: 16 -> 17; matrix products, arithmetic and copies ran while one was open for 17% -> 17% of each run, Pallas kernels for 0% -> 0%
where the time goes in v13:
time: 162 us; the launch traced here: 161 us
  waiting for transfers between devices  61.8 us (38%)
  starting transfers between devices  51.3 us (32%)
  local copies, waits for them, and re-layouts  27.3 us (17%)
  other arithmetic  7.8 us (5%)
  matrix products  7.19 us (4%)
  blocking collectives  3.82 us (2%)
  between operations  1.94 us (1%)
    ppermute x9, waiting for transfers between devices, gather_seq(): arrived = lax.ppermute(along, spread, [(i, i ^ mask) for i in range(count)])  25.4 us
    ppermute x9, starting transfers between devices, gather_seq(): lax.ppermute(piece, 'seq', [(i, (i + shift) % ring) for i in range(ring)])  14.7 us
    ppermute x9, starting transfers between devices, gather_seq(): arrived = lax.ppermute(along, spread, [(i, i ^ mask) for i in range(count)])  13.3 us
    all_to_all x1, waiting for transfers between devices, forward(): lax.all_to_all(jnp.concatenate([query_send, keyval_send], axis=2), 'seq',...  7.13 us
    ppermute x9, waiting for transfers between devices, gather_seq(): lax.ppermute(piece, 'seq', [(i, (i + shift) % ring) for i in range(ring)])  6.97 us
    all_to_all x1, waiting for transfers between devices, shards(): lax.all_to_all(jnp.concatenate([query_grad.reshape(devices, query_len).as...  5.96 us
    ppermute x2, starting transfers between devices, with_halo(): lax.ppermute(tail, axis, [(i, (i + 1) % count) for i in range(ends)])  5.72 us
    all_to_all x1, waiting for transfers between devices, shards(): lax.all_to_all(grad_send, 'seq', split_axis=0, concat_axis=1, tiled=True)  5.45 us
  transfers between devices with their start and end apart: 30, of which 17 were waited for; matrix products, arithmetic and copies ran while one was open for 17% of the time, Pallas kernels for 0%

profile of v13, /device:TPU:0, one launch (start us, length us, event | category | flops | bytes accessed | tf_op | source)
XLA Modules:
  0.0 161.1 jit_solution(15332009132457066759)
XLA Ops:
  0.7 0.9 bitcast_dynamic-update-slice_fusion.15
  1.6 3.1 %collective-permute-start = (bf16[144,384]{1,0:T(8,128)(2,1)S(1)}, bf16[144,384]{1,0:T(8,128)(2,1)S(1)}, u32[]{:S(2)}, u32[]{:S(2)}) collective-permute-start(bf16[144,384]{1,0:T(8,128)(2,1)S(1)} %get-tuple-element.80), channel_id=1, source_target_pairs={{0,4},{4,8},{8,12},{12,0},{1,5},{5,9},{9,13},{13,1},{2,6},{6,10},{... | collective-permute-start | bytes 331784 | tf_op jit(solution)/shard_map/ppermute | solution.py:48
  4.7 2.6 %collective-permute-start.1 = (bf16[144,384]{1,0:T(8,128)(2,1)S(1)}, bf16[144,384]{1,0:T(8,128)(2,1)S(1)}, u32[]{:S(2)}, u32[]{:S(2)}) collective-permute-start(bf16[144,384]{1,0:T(8,128)(2,1)S(1)} %get-tuple-element.80), channel_id=1, source_target_pairs={{0,8},{4,12},{8,0},{12,4},{1,9},{5,13},{9,1},{13,5},{2,10},{6,14},... | collective-permute-start | bytes 331784 | tf_op jit(solution)/shard_map/ppermute | solution.py:48
  7.3 1.3 collective-permute-start.2
  8.7 1.0 add_convert_fusion.2
  10.4 2.6 %collective-permute-start.6 = (bf16[2,2,384]{2,1,0:T(2,128)(2,1)S(1)}, bf16[2,2,384]{2,1,0:T(2,128)(2,1)S(1)}, u32[]{:S(2)}, u32[]{:S(2)}) collective-permute-start(bf16[2,2,384]{2,1,0:T(2,128)(2,1)S(1)} %get-tuple-element.108), channel_id=1, source_target_pairs={{0,4},{4,8},{8,12},{1,5},{5,9},{9,13},{2,6},{6,10},{10,14},{3,7},{... | collective-permute-start | bytes 9224 | tf_op jit(solution)/shard_map/ppermute | solution.py:23
  13.0 1.3 collective-permute-start.13
  14.3 1.0 copy.195
  17.8 2.6 %collective-permute-start.14 = (bf16[48,384]{1,0:T(8,128)(2,1)S(1)}, bf16[48,384]{1,0:T(8,128)(2,1)S(1)}, u32[]{:S(2)}, u32[]{:S(2)}) collective-permute-start(bf16[48,384]{1,0:T(8,128)(2,1)S(1)} %get-tuple-element.76), channel_id=1, source_target_pairs={{0,4},{4,8},{8,12},{12,0},{1,5},{5,9},{9,13},{13,1},{2,6},{6,10},{... | collective-permute-start | bytes 110600 | tf_op jit(solution)/shard_map/ppermute | solution.py:48
  20.8 2.7 %collective-permute-done.14 = bf16[48,384]{1,0:T(8,128)(2,1)S(1)} collective-permute-done((bf16[48,384]{1,0:T(8,128)(2,1)S(1)}, bf16[48,384]{1,0:T(8,128)(2,1)S(1)}, u32[]{:S(2)}, u32[]{:S(2)}) %collective-permute-start.14) | collective-permute-done | bytes 36896 | tf_op jit(solution)/shard_map/ppermute | solution.py:48
  25.3 0.9 collective-permute-start.7
  26.8 1.7 %collective-permute-done.16 = bf16[48,384]{1,0:T(8,128)(2,1)S(1)} collective-permute-done((bf16[48,384]{1,0:T(8,128)(2,1)S(1)}, bf16[48,384]{1,0:T(8,128)(2,1)S(1)}, u32[]{:S(2)}, u32[]{:S(2)}) %collective-permute-start.16) | collective-permute-done | bytes 36896 | tf_op jit(solution)/shard_map/ppermute | solution.py:48
  30.1 0.9 bitcast_dynamic-update-slice_fusion.10
  31.1 1.3 collective-permute-done.7
  32.4 2.3 %collective-permute-start.9 = (bf16[120,384]{1,0:T(8,128)(2,1)S(1)}, bf16[120,384]{1,0:T(8,128)(2,1)S(1)}, u32[]{:S(2)}, u32[]{:S(2)}) collective-permute-start(bf16[120,384]{1,0:T(8,128)(2,1)S(1)} %get-tuple-element.78), channel_id=1, source_target_pairs={{0,12},{4,0},{8,4},{12,8},{1,13},{5,1},{9,5},{13,9},{2,14},{6,2},{... | collective-permute-start | bytes 276488 | tf_op jit(solution)/shard_map/ppermute | solution.py:48
  34.7 1.5 collective-permute-start.17
  36.9 1.5 collective-permute-start.18
  38.7 1.5 collective-permute-start.19
  40.8 1.6 collective-permute-start.11
  42.7 7.1 %collective-permute-done.10 = bf16[4,120,384]{2,1,0:T(8,128)(2,1)S(1)} collective-permute-done((bf16[4,120,384]{2,1,0:T(8,128)(2,1)S(1)}, bf16[4,120,384]{2,1,0:T(8,128)(2,1)S(1)}, u32[]{:S(2)}, u32[]{:S(2)}) %collective-permute-start.10) | collective-permute-done | bytes 368672 | tf_op jit(solution)/shard_map/ppermute | solution.py:59
  49.8 3.3 %collective-permute-start.12 = (bf16[4,120,384]{2,1,0:T(8,128)(2,1)S(1)}, bf16[4,120,384]{2,1,0:T(8,128)(2,1)S(1)}, u32[]{:S(2)}, u32[]{:S(2)}) collective-permute-start(bf16[4,120,384]{2,1,0:T(8,128)(2,1)S(1)} %bitcast_dynamic-update-slice_fusion.16), channel_id=1, source_target_pairs={{0,18},{2,16},{16,2},{18,0},{1,19},{3,17},{17,3},{19,1},{4,22},{6,... | collective-permute-start | bytes 1105928 | tf_op jit(solution)/shard_map/ppermute | solution.py:59
  53.9 8.7 %collective-permute-done.12 = bf16[4,120,384]{2,1,0:T(8,128)(2,1)S(1)} collective-permute-done((bf16[4,120,384]{2,1,0:T(8,128)(2,1)S(1)}, bf16[4,120,384]{2,1,0:T(8,128)(2,1)S(1)}, u32[]{:S(2)}, u32[]{:S(2)}) %collective-permute-start.12) | collective-permute-done | bytes 368672 | tf_op jit(solution)/shard_map/ppermute | solution.py:59
  62.5 1.2 collective-permute-start.4
  65.3 1.3 fusion.23
  66.5 1.2 reshape.239
  68.1 1.9 %all-gather = bf16[2,64,1,768]{3,1,0,2:T(8,128)(2,1)S(1)} all-gather(bf16[2,64,1,384]{3,1,0,2:T(8,128)(2,1)S(1)} %fusion.54), channel_id=2, replica_groups=mesh['group'=2,'seq'=4,'batch'=2,'mp'=2] {'mp'}, dimensions={3}, use_global_device_ids=true | all-gather | bytes 294912 | tf_op jit(solution)/shard_map/all_gather | solution.py:186
  70.2 1.5 collective-permute-start.5
  71.7 1.1 bitcast_dynamic-update-slice_fusion.1
  72.7 1.1 bitcast_dynamic-update-slice_fusion
  73.8 9.5 %collective-permute-done.5 = bf16[4,144,384]{2,1,0:T(8,128)(2,1)S(1)} collective-permute-done((bf16[4,144,384]{2,1,0:T(8,128)(2,1)S(1)}, bf16[4,144,384]{2,1,0:T(8,128)(2,1)S(1)}, u32[]{:S(2)}, u32[]{:S(2)}) %collective-permute-start.5) | collective-permute-done | bytes 442400 | tf_op jit(solution)/shard_map/ppermute | solution.py:59
  85.9 1.0 pad_maximum_fusion
  86.8 3.8 %all-to-all-start = ((bf16[4,2,18432]{2,1,0:T(2,128)(2,1)}), bf16[4,2,18432]{2,1,0:T(2,128)(2,1)S(1)}, u32[]{:S(2)}, u32[]{:S(2)}) async-start(bf16[4,2,18432]{2,1,0:T(2,128)(2,1)} %pad_maximum_fusion), calls=%async_computation | async-start | bytes 589824 | tf_op jit(solution)/shard_map/all_to_all | solution.py:223
  90.7 0.9 bitcast_dynamic-update-slice_fusion.9
  91.6 0.9 bitcast_dynamic-update-slice_fusion.8
  92.6 7.1 %all-to-all-done = bf16[4,2,18432]{2,1,0:T(2,128)(2,1)S(1)} async-done(((bf16[4,2,18432]{2,1,0:T(2,128)(2,1)}), bf16[4,2,18432]{2,1,0:T(2,128)(2,1)S(1)}, u32[]{:S(2)}, u32[]{:S(2)}) %all-to-all-start) | async-done | bytes 294944 | tf_op jit(solution)/shard_map/all_to_all | solution.py:223
  103.6 4.1 %all-to-all-start.1 = ((bf16[4,2,6144]{2,1,0:T(2,128)(2,1)}), bf16[4,2,6144]{2,1,0:T(2,128)(2,1)}, u32[]{:S(2)}, u32[]{:S(2)}) async-start(bf16[4,2,6144]{2,1,0:T(2,128)(2,1)} %copy.193), calls=%async_computation.1 | async-start | bytes 196608 | tf_op jit(solution)/shard_map/all_to_all | solution.py:245
  107.7 0.9 bitcast_dynamic-update-slice_fusion.11
  109.4 4.0 %all-to-all-done.1 = bf16[4,2,6144]{2,1,0:T(2,128)(2,1)} async-done(((bf16[4,2,6144]{2,1,0:T(2,128)(2,1)}), bf16[4,2,6144]{2,1,0:T(2,128)(2,1)}, u32[]{:S(2)}, u32[]{:S(2)}) %all-to-all-start.1) | async-done | bytes 98336 | tf_op jit(solution)/shard_map/all_to_all | solution.py:245
  113.4 1.0 reshape.243
  117.5 1.9 %all_gather.7 = bf16[64,768]{1,0:T(8,128)(2,1)S(1)} all-gather(bf16[64,384]{1,0:T(8,128)(2,1)S(1)} %fusion.84), channel_id=1, replica_groups=mesh['group'=2,'seq'=4,'batch'=2,'mp'=2] {'mp'}, dimensions={1}, use_global_device_ids=true | all-gather | bytes 147456 | tf_op jit(solution)/shard_map/all_gather | solution.py:307
  122.0 3.3 %all-to-all-start.2 = ((bf16[4,2,3072]{2,1,0:T(2,128)(2,1)}), bf16[4,2,3072]{2,1,0:T(2,128)(2,1)S(1)}, u32[]{:S(2)}, u32[]{:S(2)}) async-start(bf16[4,2,3072]{2,1,0:T(2,128)(2,1)} %reshape.265), calls=%async_computation.2 | async-start | bytes 98304 | tf_op jit(solution)/shard_map/all_to_all | solution.py:319
  125.5 5.4 %all-to-all-done.2 = bf16[4,2,3072]{2,1,0:T(2,128)(2,1)S(1)} async-done(((bf16[4,2,3072]{2,1,0:T(2,128)(2,1)}), bf16[4,2,3072]{2,1,0:T(2,128)(2,1)S(1)}, u32[]{:S(2)}, u32[]{:S(2)}) %all-to-all-start.2) | async-done | bytes 49184 | tf_op jit(solution)/shard_map/all_to_all | solution.py:319
  134.6 3.3 %all-to-all-start.3 = ((bf16[4,2,9216]{2,1,0:T(2,128)(2,1)}), bf16[4,2,9216]{2,1,0:T(2,128)(2,1)S(1)}, u32[]{:S(2)}, u32[]{:S(2)}) async-start(bf16[4,2,9216]{2,1,0:T(2,128)(2,1)} %reshape.267), calls=%async_computation.3 | async-start | bytes 294912 | tf_op jit(solution)/shard_map/all_to_all | solution.py:330
  138.0 6.0 %all-to-all-done.3 = bf16[4,2,9216]{2,1,0:T(2,128)(2,1)S(1)} async-done(((bf16[4,2,9216]{2,1,0:T(2,128)(2,1)}), bf16[4,2,9216]{2,1,0:T(2,128)(2,1)S(1)}, u32[]{:S(2)}, u32[]{:S(2)}) %all-to-all-start.3) | async-done | bytes 147488 | tf_op jit(solution)/shard_map/all_to_all | solution.py:330
  146.1 1.2 collective-permute-done.21
  149.1 3.1 %collective-permute-start.24 = (bf16[2,384]{1,0:T(2,128)(2,1)S(1)}, bf16[2,384]{1,0:T(2,128)(2,1)S(1)}, u32[]{:S(2)}, u32[]{:S(2)}) collective-permute-start(bf16[2,384]{1,0:T(2,128)(2,1)S(1)} %get-tuple-element.113), channel_id=1, source_target_pairs={{0,4},{4,8},{8,12},{1,5},{5,9},{9,13},{2,6},{6,10},{10,14},{3,7},{... | collective-permute-start | bytes 4616 | tf_op jit(solution)/shard_map/ppermute | solution.py:23
  152.6 1.3 collective-permute-start.23
  154.4 3.7 %collective-permute-done.23 = bf16[2,384]{1,0:T(2,128)(2,1)S(1)} collective-permute-done((bf16[2,384]{1,0:T(2,128)(2,1)S(1)}, bf16[2,384]{1,0:T(2,128)(2,1)S(1)}, u32[]{:S(2)}, u32[]{:S(2)}) %collective-permute-start.23) | collective-permute-done | bytes 1568 | tf_op jit(solution)/shard_map/ppermute | solution.py:25
  (219 shorter events, 35.7 us)
Async XLA Ops:
  0.6 20.1 %copy-start.13 = (bf16[1,128,384]{2,1,0:T(8,128)(2,1)S(1)}, bf16[1,128,384]{2,1,0:T(8,128)(2,1)}, u32[]{:S(2)}) copy-start(bf16[1,128,384]{2,1,0:T(8,128)(2,1)} %param.7) | copy-start | bytes 294916
  1.6 37.0 %collective-permute-start = (bf16[144,384]{1,0:T(8,128)(2,1)S(1)}, bf16[144,384]{1,0:T(8,128)(2,1)S(1)}, u32[]{:S(2)}, u32[]{:S(2)}) collective-permute-start(bf16[144,384]{1,0:T(8,128)(2,1)S(1)} %get-tuple-element.80), channel_id=1, source_target_pairs={{0,4},{4,8},{8,12},{12,0},{1,5},{5,9},{9,13},{13,1},{2,6},{6,10},{... | collective-permute-start | bytes 331784 | tf_op jit(solution)/shard_map/ppermute | solution.py:48
  4.7 35.5 %collective-permute-start.1 = (bf16[144,384]{1,0:T(8,128)(2,1)S(1)}, bf16[144,384]{1,0:T(8,128)(2,1)S(1)}, u32[]{:S(2)}, u32[]{:S(2)}) collective-permute-start(bf16[144,384]{1,0:T(8,128)(2,1)S(1)} %get-tuple-element.80), channel_id=1, source_target_pairs={{0,8},{4,12},{8,0},{12,4},{1,9},{5,13},{9,1},{13,5},{2,10},{6,14},... | collective-permute-start | bytes 331784 | tf_op jit(solution)/shard_map/ppermute | solution.py:48
  7.3 33.5 %collective-permute-start.2 = (bf16[144,384]{1,0:T(8,128)(2,1)S(1)}, bf16[144,384]{1,0:T(8,128)(2,1)S(1)}, u32[]{:S(2)}, u32[]{:S(2)}) collective-permute-start(bf16[144,384]{1,0:T(8,128)(2,1)S(1)} %get-tuple-element.80), channel_id=1, source_target_pairs={{0,12},{4,0},{8,4},{12,8},{1,13},{5,1},{9,5},{13,9},{2,14},{6,2},{... | collective-permute-start | bytes 331784 | tf_op jit(solution)/shard_map/ppermute | solution.py:48
  10.4 7.4 %collective-permute-start.6 = (bf16[2,2,384]{2,1,0:T(2,128)(2,1)S(1)}, bf16[2,2,384]{2,1,0:T(2,128)(2,1)S(1)}, u32[]{:S(2)}, u32[]{:S(2)}) collective-permute-start(bf16[2,2,384]{2,1,0:T(2,128)(2,1)S(1)} %get-tuple-element.108), channel_id=1, source_target_pairs={{0,4},{4,8},{8,12},{1,5},{5,9},{9,13},{2,6},{6,10},{10,14},{3,7},{... | collective-permute-start | bytes 9224 | tf_op jit(solution)/shard_map/ppermute | solution.py:23
  13.0 7.4 %collective-permute-start.13 = (bf16[2,2,384]{2,1,0:T(2,128)(2,1)S(1)}, bf16[2,2,384]{2,1,0:T(2,128)(2,1)S(1)}, u32[]{:S(2)}, u32[]{:S(2)}) collective-permute-start(bf16[2,2,384]{2,1,0:T(2,128)(2,1)S(1)} %get-tuple-element.109), channel_id=1, source_target_pairs={{4,0},{8,4},{12,8},{5,1},{9,5},{13,9},{6,2},{10,6},{14,10},{7,3},{... | collective-permute-start | bytes 9224 | tf_op jit(solution)/shard_map/ppermute | solution.py:25
  17.8 5.8 %collective-permute-start.14 = (bf16[48,384]{1,0:T(8,128)(2,1)S(1)}, bf16[48,384]{1,0:T(8,128)(2,1)S(1)}, u32[]{:S(2)}, u32[]{:S(2)}) collective-permute-start(bf16[48,384]{1,0:T(8,128)(2,1)S(1)} %get-tuple-element.76), channel_id=1, source_target_pairs={{0,4},{4,8},{8,12},{12,0},{1,5},{5,9},{9,13},{13,1},{2,6},{6,10},{... | collective-permute-start | bytes 110600 | tf_op jit(solution)/shard_map/ppermute | solution.py:48
  20.4 4.9 %collective-permute-start.15 = (bf16[48,384]{1,0:T(8,128)(2,1)S(1)}, bf16[48,384]{1,0:T(8,128)(2,1)S(1)}, u32[]{:S(2)}, u32[]{:S(2)}) collective-permute-start(bf16[48,384]{1,0:T(8,128)(2,1)S(1)} %get-tuple-element.76), channel_id=1, source_target_pairs={{0,8},{4,12},{8,0},{12,4},{1,9},{5,13},{9,1},{13,5},{2,10},{6,14},... | collective-permute-start | bytes 110600 | tf_op jit(solution)/shard_map/ppermute | solution.py:48
  23.6 5.0 %collective-permute-start.16 = (bf16[48,384]{1,0:T(8,128)(2,1)S(1)}, bf16[48,384]{1,0:T(8,128)(2,1)S(1)}, u32[]{:S(2)}, u32[]{:S(2)}) collective-permute-start(bf16[48,384]{1,0:T(8,128)(2,1)S(1)} %get-tuple-element.76), channel_id=1, source_target_pairs={{0,12},{4,0},{8,4},{12,8},{1,13},{5,1},{9,5},{13,9},{2,14},{6,2},{... | collective-permute-start | bytes 110600 | tf_op jit(solution)/shard_map/ppermute | solution.py:48
  25.3 7.1 %collective-permute-start.7 = (bf16[120,384]{1,0:T(8,128)(2,1)S(1)}, bf16[120,384]{1,0:T(8,128)(2,1)S(1)}, u32[]{:S(2)}, u32[]{:S(2)}) collective-permute-start(bf16[120,384]{1,0:T(8,128)(2,1)S(1)} %get-tuple-element.78), channel_id=1, source_target_pairs={{0,4},{4,8},{8,12},{12,0},{1,5},{5,9},{9,13},{13,1},{2,6},{6,10},{... | collective-permute-start | bytes 276488 | tf_op jit(solution)/shard_map/ppermute | solution.py:48
  28.6 6.1 %collective-permute-start.8 = (bf16[120,384]{1,0:T(8,128)(2,1)S(1)}, bf16[120,384]{1,0:T(8,128)(2,1)S(1)}, u32[]{:S(2)}, u32[]{:S(2)}) collective-permute-start(bf16[120,384]{1,0:T(8,128)(2,1)S(1)} %get-tuple-element.78), channel_id=1, source_target_pairs={{0,8},{4,12},{8,0},{12,4},{1,9},{5,13},{9,1},{13,5},{2,10},{6,14},... | collective-permute-start | bytes 276488 | tf_op jit(solution)/shard_map/ppermute | solution.py:48
  31.1 7.3 %copy-start.10 = (bf16[4,4,48,384]{3,2,0,1:T(8,128)(2,1)}, bf16[4,4,48,384]{3,2,0,1:T(8,128)(2,1)S(1)}, u32[]{:S(2)}) copy-start(bf16[4,4,48,384]{3,2,0,1:T(8,128)(2,1)S(1)} %bitcast_dynamic-update-slice_fusion.10) | copy-start | bytes 1769476
  32.4 4.6 %collective-permute-start.9 = (bf16[120,384]{1,0:T(8,128)(2,1)S(1)}, bf16[120,384]{1,0:T(8,128)(2,1)S(1)}, u32[]{:S(2)}, u32[]{:S(2)}) collective-permute-start(bf16[120,384]{1,0:T(8,128)(2,1)S(1)} %get-tuple-element.78), channel_id=1, source_target_pairs={{0,12},{4,0},{8,4},{12,8},{1,13},{5,1},{9,5},{13,9},{2,14},{6,2},{... | collective-permute-start | bytes 276488 | tf_op jit(solution)/shard_map/ppermute | solution.py:48
  34.7 55.9 %collective-permute-start.17 = (bf16[4,48,384]{2,1,0:T(8,128)(2,1)}, bf16[4,48,384]{2,1,0:T(8,128)(2,1)}, u32[]{:S(2)}, u32[]{:S(2)}) collective-permute-start(bf16[4,48,384]{2,1,0:T(8,128)(2,1)} %bitcast_dynamic-update-slice_fusion.20), channel_id=1, source_target_pairs={{0,2},{2,0},{16,18},{18,16},{1,3},{3,1},{17,19},{19,17},{4,6},{6,4... | collective-permute-start | bytes 442376 | tf_op jit(solution)/shard_map/ppermute | solution.py:59
  36.9 54.7 %collective-permute-start.18 = (bf16[4,48,384]{2,1,0:T(8,128)(2,1)}, bf16[4,48,384]{2,1,0:T(8,128)(2,1)}, u32[]{:S(2)}, u32[]{:S(2)}) collective-permute-start(bf16[4,48,384]{2,1,0:T(8,128)(2,1)} %bitcast_dynamic-update-slice_fusion.20), channel_id=1, source_target_pairs={{0,16},{2,18},{16,0},{18,2},{1,17},{3,19},{17,1},{19,3},{4,20},{6,... | collective-permute-start | bytes 442376 | tf_op jit(solution)/shard_map/ppermute | solution.py:59
  38.7 69.0 %collective-permute-start.19 = (bf16[4,48,384]{2,1,0:T(8,128)(2,1)}, bf16[4,48,384]{2,1,0:T(8,128)(2,1)}, u32[]{:S(2)}, u32[]{:S(2)}) collective-permute-start(bf16[4,48,384]{2,1,0:T(8,128)(2,1)} %bitcast_dynamic-update-slice_fusion.20), channel_id=1, source_target_pairs={{0,18},{2,16},{16,2},{18,0},{1,19},{3,17},{17,3},{19,1},{4,22},{6,... | collective-permute-start | bytes 442376 | tf_op jit(solution)/shard_map/ppermute | solution.py:59
  40.2 9.6 %collective-permute-start.10 = (bf16[4,120,384]{2,1,0:T(8,128)(2,1)S(1)}, bf16[4,120,384]{2,1,0:T(8,128)(2,1)S(1)}, u32[]{:S(2)}, u32[]{:S(2)}) collective-permute-start(bf16[4,120,384]{2,1,0:T(8,128)(2,1)S(1)} %bitcast_dynamic-update-slice_fusion.16), channel_id=1, source_target_pairs={{0,2},{2,0},{16,18},{18,16},{1,3},{3,1},{17,19},{19,17},{4,6},{6,4... | collective-permute-start | bytes 1105928 | tf_op jit(solution)/shard_map/ppermute | solution.py:59
  40.8 12.3 %collective-permute-start.11 = (bf16[4,120,384]{2,1,0:T(8,128)(2,1)S(1)}, bf16[4,120,384]{2,1,0:T(8,128)(2,1)S(1)}, u32[]{:S(2)}, u32[]{:S(2)}) collective-permute-start(bf16[4,120,384]{2,1,0:T(8,128)(2,1)S(1)} %bitcast_dynamic-update-slice_fusion.16), channel_id=1, source_target_pairs={{0,16},{2,18},{16,0},{18,2},{1,17},{3,19},{17,1},{19,3},{4,20},{6,... | collective-permute-start | bytes 1105928 | tf_op jit(solution)/shard_map/ppermute | solution.py:59
  49.8 12.7 %collective-permute-start.12 = (bf16[4,120,384]{2,1,0:T(8,128)(2,1)S(1)}, bf16[4,120,384]{2,1,0:T(8,128)(2,1)S(1)}, u32[]{:S(2)}, u32[]{:S(2)}) collective-permute-start(bf16[4,120,384]{2,1,0:T(8,128)(2,1)S(1)} %bitcast_dynamic-update-slice_fusion.16), channel_id=1, source_target_pairs={{0,18},{2,16},{16,2},{18,0},{1,19},{3,17},{17,3},{19,1},{4,22},{6,... | collective-permute-start | bytes 1105928 | tf_op jit(solution)/shard_map/ppermute | solution.py:59
  53.2 17.0 %collective-permute-start.3 = (bf16[4,144,384]{2,1,0:T(8,128)(2,1)S(1)}, bf16[4,144,384]{2,1,0:T(8,128)(2,1)}, u32[]{:S(2)}, u32[]{:S(2)}) collective-permute-start(bf16[4,144,384]{2,1,0:T(8,128)(2,1)S(1)} %bitcast_dynamic-update-slice_fusion.12), channel_id=1, source_target_pairs={{0,2},{2,0},{16,18},{18,16},{1,3},{3,1},{17,19},{19,17},{4,6},{6,4... | collective-permute-start | bytes 1327112 | tf_op jit(solution)/shard_map/ppermute | solution.py:59
  62.5 10.2 %collective-permute-start.4 = (bf16[4,144,384]{2,1,0:T(8,128)(2,1)S(1)}, bf16[4,144,384]{2,1,0:T(8,128)(2,1)}, u32[]{:S(2)}, u32[]{:S(2)}) collective-permute-start(bf16[4,144,384]{2,1,0:T(8,128)(2,1)S(1)} %bitcast_dynamic-update-slice_fusion.12), channel_id=1, source_target_pairs={{0,16},{2,18},{16,0},{18,2},{1,17},{3,19},{17,1},{19,3},{4,20},{6,... | collective-permute-start | bytes 1327112 | tf_op jit(solution)/shard_map/ppermute | solution.py:59
  64.0 1.2 copy-start.2
  64.0 1.2 copy-start.4
  68.1 15.4 %copy-start.14 = (bf16[2,64,1,384]{3,1,0,2:T(8,128)(2,1)}, bf16[2,64,1,384]{3,1,0,2:T(8,128)(2,1)S(1)}, u32[]{:S(2)}) copy-start(bf16[2,64,1,384]{3,1,0,2:T(8,128)(2,1)S(1)} %fusion.54) | copy-start | bytes 294916
  70.2 13.2 %collective-permute-start.5 = (bf16[4,144,384]{2,1,0:T(8,128)(2,1)S(1)}, bf16[4,144,384]{2,1,0:T(8,128)(2,1)S(1)}, u32[]{:S(2)}, u32[]{:S(2)}) collective-permute-start(bf16[4,144,384]{2,1,0:T(8,128)(2,1)S(1)} %bitcast_dynamic-update-slice_fusion.12), channel_id=1, source_target_pairs={{0,18},{2,16},{16,2},{18,0},{1,19},{3,17},{17,3},{19,1},{4,22},{6,... | collective-permute-start | bytes 1327112 | tf_op jit(solution)/shard_map/ppermute | solution.py:59
  84.8 5.9 %copy-start.11 = (bf16[4,4,48,384]{3,2,0,1:T(8,128)(2,1)S(1)}, bf16[4,4,48,384]{3,2,0,1:T(8,128)(2,1)}, u32[]{:S(2)}) copy-start(bf16[4,4,48,384]{3,2,0,1:T(8,128)(2,1)} %copy-done.10) | copy-start | bytes 1769476
  86.8 12.8 %all-to-all-start = ((bf16[4,2,18432]{2,1,0:T(2,128)(2,1)}), bf16[4,2,18432]{2,1,0:T(2,128)(2,1)S(1)}, u32[]{:S(2)}, u32[]{:S(2)}) async-start(bf16[4,2,18432]{2,1,0:T(2,128)(2,1)} %pad_maximum_fusion), calls=%async_computation | async-start | bytes 589824 | tf_op jit(solution)/shard_map/all_to_all | solution.py:223
  100.4 2.4 %copy-start.16 = (bf16[256,96]{1,0:T(8,128)(2,1)}, bf16[256,96]{1,0:T(8,128)(2,1)S(1)}, u32[]{:S(2)}) copy-start(bf16[256,96]{1,0:T(8,128)(2,1)S(1)} %squeeze.83) | copy-start | bytes 147460
  101.5 7.2 %copy-start.19 = (bf16[256,96]{0,1:T(8,128)(2,1)}, bf16[256,96]{0,1:T(8,128)(2,1)S(1)}, u32[]{:S(2)}) copy-start(bf16[256,96]{0,1:T(8,128)(2,1)S(1)} %convolution_convert_fusion.4) | copy-start | bytes 147460
  103.6 9.8 %all-to-all-start.1 = ((bf16[4,2,6144]{2,1,0:T(2,128)(2,1)}), bf16[4,2,6144]{2,1,0:T(2,128)(2,1)}, u32[]{:S(2)}, u32[]{:S(2)}) async-start(bf16[4,2,6144]{2,1,0:T(2,128)(2,1)} %copy.193), calls=%async_computation.1 | async-start | bytes 196608 | tf_op jit(solution)/shard_map/all_to_all | solution.py:245
  109.1 7.5 %copy-start.15 = (bf16[2,64,1,384]{3,1,0,2:T(8,128)(2,1)S(1)}, bf16[2,64,1,384]{3,1,0,2:T(8,128)(2,1)}, u32[]{:S(2)}) copy-start(bf16[2,64,1,384]{3,1,0,2:T(8,128)(2,1)} %copy-done.14) | copy-start | bytes 294916
  115.0 10.2 %copy-start.17 = (bf16[256,96]{1,0:T(8,128)(2,1)S(1)}, bf16[256,96]{1,0:T(8,128)(2,1)}, u32[]{:S(2)}) copy-start(bf16[256,96]{1,0:T(8,128)(2,1)} %copy-done.16) | copy-start | bytes 147460
  115.0 1.5 collective-permute-start.20
  115.9 15.8 %copy-start.20 = (bf16[256,96]{0,1:T(8,128)(2,1)S(1)}, bf16[256,96]{0,1:T(8,128)(2,1)}, u32[]{:S(2)}) copy-start(bf16[256,96]{0,1:T(8,128)(2,1)} %copy-done.19) | copy-start | bytes 147460
  122.0 8.9 %all-to-all-start.2 = ((bf16[4,2,3072]{2,1,0:T(2,128)(2,1)}), bf16[4,2,3072]{2,1,0:T(2,128)(2,1)S(1)}, u32[]{:S(2)}, u32[]{:S(2)}) async-start(bf16[4,2,3072]{2,1,0:T(2,128)(2,1)} %reshape.265), calls=%async_computation.2 | async-start | bytes 98304 | tf_op jit(solution)/shard_map/all_to_all | solution.py:319
  134.6 9.4 %all-to-all-start.3 = ((bf16[4,2,9216]{2,1,0:T(2,128)(2,1)}), bf16[4,2,9216]{2,1,0:T(2,128)(2,1)S(1)}, u32[]{:S(2)}, u32[]{:S(2)}) async-start(bf16[4,2,9216]{2,1,0:T(2,128)(2,1)} %reshape.267), calls=%async_computation.3 | async-start | bytes 294912 | tf_op jit(solution)/shard_map/all_to_all | solution.py:330
  144.7 3.0 %copy-start.12 = (f32[2,128,384]{2,1,0:T(8,128)S(1)}, f32[2,128,384]{2,1,0:T(8,128)}, u32[]{:S(2)}) copy-start(f32[2,128,384]{2,1,0:T(8,128)} %get-tuple-element.124) | copy-start | bytes 1179652
  146.0 1.3 collective-permute-start.21
  147.4 1.2 collective-permute-start.22
  147.6 6.3 %copy-start.9 = (bf16[1,4,96,384]{3,2,0,1:T(8,128)(2,1)S(1)}, bf16[1,4,96,384]{3,2,0,1:T(8,128)(2,1)}, u32[]{:S(2)}) copy-start(bf16[1,4,96,384]{3,2,0,1:T(8,128)(2,1)} %copy-done.8) | copy-start | bytes 884740
  147.8 6.4 %copy-start.7 = (bf16[1,4,96,384]{3,2,0,1:T(8,128)(2,1)S(1)}, bf16[1,4,96,384]{3,2,0,1:T(8,128)(2,1)}, u32[]{:S(2)}) copy-start(bf16[1,4,96,384]{3,2,0,1:T(8,128)(2,1)} %copy-done.6) | copy-start | bytes 884740
  148.7 9.4 %copy-start.5 = (bf16[1,4,96,384]{3,2,0,1:T(8,128)(2,1)S(1)}, bf16[1,4,96,384]{3,2,0,1:T(8,128)(2,1)}, u32[]{:S(2)}) copy-start(bf16[1,4,96,384]{3,2,0,1:T(8,128)(2,1)} %copy-done.4) | copy-start | bytes 884740
  148.8 9.5 %copy-start.3 = (bf16[1,4,96,384]{3,2,0,1:T(8,128)(2,1)S(1)}, bf16[1,4,96,384]{3,2,0,1:T(8,128)(2,1)}, u32[]{:S(2)}) copy-start(bf16[1,4,96,384]{3,2,0,1:T(8,128)(2,1)} %copy-done.2) | copy-start | bytes 884740
  149.1 5.0 %collective-permute-start.24 = (bf16[2,384]{1,0:T(2,128)(2,1)S(1)}, bf16[2,384]{1,0:T(2,128)(2,1)S(1)}, u32[]{:S(2)}, u32[]{:S(2)}) collective-permute-start(bf16[2,384]{1,0:T(2,128)(2,1)S(1)} %get-tuple-element.113), channel_id=1, source_target_pairs={{0,4},{4,8},{8,12},{1,5},{5,9},{9,13},{2,6},{6,10},{10,14},{3,7},{... | collective-permute-start | bytes 4616 | tf_op jit(solution)/shard_map/ppermute | solution.py:23
  152.3 6.3 %copy-start.1 = (bf16[1,4,96,384]{3,2,0,1:T(8,128)(2,1)S(1)}, bf16[1,4,96,384]{3,2,0,1:T(8,128)(2,1)}, u32[]{:S(2)}) copy-start(bf16[1,4,96,384]{3,2,0,1:T(8,128)(2,1)} %copy-done) | copy-start | bytes 884740
  152.6 5.5 %collective-permute-start.23 = (bf16[2,384]{1,0:T(2,128)(2,1)S(1)}, bf16[2,384]{1,0:T(2,128)(2,1)S(1)}, u32[]{:S(2)}, u32[]{:S(2)}) collective-permute-start(bf16[2,384]{1,0:T(2,128)(2,1)S(1)} %get-tuple-element.112), channel_id=1, source_target_pairs={{4,0},{8,4},{12,8},{5,1},{9,5},{13,9},{6,2},{10,6},{14,10},{7,3},{... | collective-permute-start | bytes 4616 | tf_op jit(solution)/shard_map/ppermute | solution.py:25
  154.2 6.2 %copy-start.18 = (f32[1,128,384]{2,1,0:T(8,128)S(1)}, f32[1,128,384]{2,1,0:T(8,128)}, u32[]{:S(2)}) copy-start(f32[1,128,384]{2,1,0:T(8,128)} %param.8) | copy-start | bytes 589828
  158.8 1.4 collective-permute-start.25
  (5 other events, 5.1 us)

commit v14 on v12

--- a/solution.py
+++ b/solution.py
@@ -174,7 +174,7 @@
 
 
 def forward(stack, conv_weight, conv_bias, norm_gain, qkv_weight, out_weight):
-    pass_count, positions, channels = stack.shape
+    pass_count, positions, _ = stack.shape
     reach = KW // 2
     half_width = conv_weight.shape[2]
     padded_input = with_halo(stack, (("seq", 1),), reach)
@@ -191,7 +191,7 @@
     paired = jax.nn.gelu(pre_act).reshape(pass_count, positions // 2, 2, half_width)
     pooled = (0.5 * (paired[:, :, 0] + paired[:, :, 1])).astype(jnp.bfloat16)
     pooled_wide = lax.optimization_barrier(pooled).astype(jnp.float32)
-    whole = join_mp(pooled, 2)
+    whole = lax.all_gather(pooled, "mp", axis=2, tiled=True)
     whole_wide = whole.astype(jnp.float32)
     row_scale = lax.rsqrt(jnp.mean(whole_wide * whole_wide, axis=2, keepdims=True) + epsilon)
     normed = (whole_wide * row_scale * norm_gain).astype(jnp.bfloat16)
@@ -293,7 +293,7 @@
     (
         pre_act,
         pooled_wide,
-        whole_wide,
+        _,
         row_scale,
         query_heads,
         keyval_heads,

time: 164 us -> 161 us (0.982)
  starting transfers between devices: 54.2 us -> 51.5 us
  blocking collectives: 0 us -> 1.95 us
  matrix products: 8.97 us -> 7.2 us
    ppermute x9, starting transfers between devices: 15.7 us -> 13.3 us  [gather_seq(): arrived = lax.ppermute(along, spread, [(i, i ^ mask) for i in range(count)])]
    ppermute x9, waiting for transfers between devices: 23.1 us -> 25.4 us  [gather_seq(): arrived = lax.ppermute(along, spread, [(i, i ^ mask) for i in range(count)])]
    all_gather x0 -> x1, blocking collectives: none -> 1.95 us  [forward(): whole = lax.all_gather(pooled, 'mp', axis=2, tiled=True)]
    unnamed x54 -> x52, local copies, waits for them, and re-layouts: 4.08 us -> 3.32 us
    ppermute x6 -> x5, waiting for transfers between devices: 4.43 us -> 4.27 us  [swap_mp(): return lax.ppermute(cells, 'mp', [(0, 1), (1, 0)])]
  transfers between devices with their start and end apart: 32 -> 31, of which waited for: 18 -> 18; matrix products, arithmetic and copies ran while one was open for 17% -> 18% of each run, Pallas kernels for 0% -> 0%
where the time goes in v14:
time: 161 us; the launch traced here: 160 us
  waiting for transfers between devices  62.8 us (39%)
  starting transfers between devices  51.5 us (32%)
  local copies, waits for them, and re-layouts  27.3 us (17%)
  matrix products  7.2 us (4%)
  other arithmetic  6.91 us (4%)
  blocking collectives  1.95 us (1%)
  between operations  1.94 us (1%)
    ppermute x9, waiting for transfers between devices, gather_seq(): arrived = lax.ppermute(along, spread, [(i, i ^ mask) for i in range(count)])  25.4 us
    ppermute x9, starting transfers between devices, gather_seq(): lax.ppermute(piece, 'seq', [(i, (i + shift) % ring) for i in range(ring)])  14.7 us
    ppermute x9, starting transfers between devices, gather_seq(): arrived = lax.ppermute(along, spread, [(i, i ^ mask) for i in range(count)])  13.3 us
    all_to_all x1, waiting for transfers between devices, forward(): lax.all_to_all(jnp.concatenate([query_send, keyval_send], axis=2), 'seq',...  7.13 us
    ppermute x9, waiting for transfers between devices, gather_seq(): lax.ppermute(piece, 'seq', [(i, (i + shift) % ring) for i in range(ring)])  6.97 us
    all_to_all x1, waiting for transfers between devices, shards(): lax.all_to_all(jnp.concatenate([query_grad.reshape(devices, query_len).as...  5.97 us
    ppermute x2, starting transfers between devices, with_halo(): lax.ppermute(tail, axis, [(i, (i + 1) % count) for i in range(ends)])  5.72 us
    all_to_all x1, waiting for transfers between devices, shards(): lax.all_to_all(grad_send, 'seq', split_axis=0, concat_axis=1, tiled=True)  5.45 us
  transfers between devices with their start and end apart: 31, of which 18 were waited for; matrix products, arithmetic and copies ran while one was open for 18% of the time, Pallas kernels for 0%

profile of v14, /device:TPU:0, one launch (start us, length us, event | category | flops | bytes accessed | tf_op | source)
XLA Modules:
  0.0 159.5 jit_solution(16975732356587971135)
XLA Ops:
  0.7 0.9 bitcast_dynamic-update-slice_fusion.15
  1.6 3.1 %collective-permute-start = (bf16[144,384]{1,0:T(8,128)(2,1)S(1)}, bf16[144,384]{1,0:T(8,128)(2,1)S(1)}, u32[]{:S(2)}, u32[]{:S(2)}) collective-permute-start(bf16[144,384]{1,0:T(8,128)(2,1)S(1)} %get-tuple-element.80), channel_id=1, source_target_pairs={{0,4},{4,8},{8,12},{12,0},{1,5},{5,9},{9,13},{13,1},{2,6},{6,10},{... | collective-permute-start | bytes 331784 | tf_op jit(solution)/shard_map/ppermute | solution.py:48
  4.7 2.6 %collective-permute-start.1 = (bf16[144,384]{1,0:T(8,128)(2,1)S(1)}, bf16[144,384]{1,0:T(8,128)(2,1)S(1)}, u32[]{:S(2)}, u32[]{:S(2)}) collective-permute-start(bf16[144,384]{1,0:T(8,128)(2,1)S(1)} %get-tuple-element.80), channel_id=1, source_target_pairs={{0,8},{4,12},{8,0},{12,4},{1,9},{5,13},{9,1},{13,5},{2,10},{6,14},... | collective-permute-start | bytes 331784 | tf_op jit(solution)/shard_map/ppermute | solution.py:48
  7.3 1.3 collective-permute-start.2
  8.7 1.0 add_convert_fusion.2
  10.4 2.6 %collective-permute-start.6 = (bf16[2,2,384]{2,1,0:T(2,128)(2,1)S(1)}, bf16[2,2,384]{2,1,0:T(2,128)(2,1)S(1)}, u32[]{:S(2)}, u32[]{:S(2)}) collective-permute-start(bf16[2,2,384]{2,1,0:T(2,128)(2,1)S(1)} %get-tuple-element.108), channel_id=1, source_target_pairs={{0,4},{4,8},{8,12},{1,5},{5,9},{9,13},{2,6},{6,10},{10,14},{3,7},{... | collective-permute-start | bytes 9224 | tf_op jit(solution)/shard_map/ppermute | solution.py:23
  13.0 1.3 collective-permute-start.13
  14.3 1.0 copy.195
  17.8 2.6 %collective-permute-start.14 = (bf16[48,384]{1,0:T(8,128)(2,1)S(1)}, bf16[48,384]{1,0:T(8,128)(2,1)S(1)}, u32[]{:S(2)}, u32[]{:S(2)}) collective-permute-start(bf16[48,384]{1,0:T(8,128)(2,1)S(1)} %get-tuple-element.76), channel_id=1, source_target_pairs={{0,4},{4,8},{8,12},{12,0},{1,5},{5,9},{9,13},{13,1},{2,6},{6,10},{... | collective-permute-start | bytes 110600 | tf_op jit(solution)/shard_map/ppermute | solution.py:48
  20.8 2.7 %collective-permute-done.14 = bf16[48,384]{1,0:T(8,128)(2,1)S(1)} collective-permute-done((bf16[48,384]{1,0:T(8,128)(2,1)S(1)}, bf16[48,384]{1,0:T(8,128)(2,1)S(1)}, u32[]{:S(2)}, u32[]{:S(2)}) %collective-permute-start.14) | collective-permute-done | bytes 36896 | tf_op jit(solution)/shard_map/ppermute | solution.py:48
  25.3 0.9 collective-permute-start.7
  26.8 1.7 %collective-permute-done.16 = bf16[48,384]{1,0:T(8,128)(2,1)S(1)} collective-permute-done((bf16[48,384]{1,0:T(8,128)(2,1)S(1)}, bf16[48,384]{1,0:T(8,128)(2,1)S(1)}, u32[]{:S(2)}, u32[]{:S(2)}) %collective-permute-start.16) | collective-permute-done | bytes 36896 | tf_op jit(solution)/shard_map/ppermute | solution.py:48
  30.1 0.9 bitcast_dynamic-update-slice_fusion.10
  31.1 1.3 collective-permute-done.7
  32.4 2.3 %collective-permute-start.9 = (bf16[120,384]{1,0:T(8,128)(2,1)S(1)}, bf16[120,384]{1,0:T(8,128)(2,1)S(1)}, u32[]{:S(2)}, u32[]{:S(2)}) collective-permute-start(bf16[120,384]{1,0:T(8,128)(2,1)S(1)} %get-tuple-element.78), channel_id=1, source_target_pairs={{0,12},{4,0},{8,4},{12,8},{1,13},{5,1},{9,5},{13,9},{2,14},{6,2},{... | collective-permute-start | bytes 276488 | tf_op jit(solution)/shard_map/ppermute | solution.py:48
  34.7 1.5 collective-permute-start.17
  36.9 1.5 collective-permute-start.18
  38.7 1.5 collective-permute-start.19
  40.8 1.6 collective-permute-start.11
  42.7 7.1 %collective-permute-done.10 = bf16[4,120,384]{2,1,0:T(8,128)(2,1)S(1)} collective-permute-done((bf16[4,120,384]{2,1,0:T(8,128)(2,1)S(1)}, bf16[4,120,384]{2,1,0:T(8,128)(2,1)S(1)}, u32[]{:S(2)}, u32[]{:S(2)}) %collective-permute-start.10) | collective-permute-done | bytes 368672 | tf_op jit(solution)/shard_map/ppermute | solution.py:59
  49.8 3.3 %collective-permute-start.12 = (bf16[4,120,384]{2,1,0:T(8,128)(2,1)S(1)}, bf16[4,120,384]{2,1,0:T(8,128)(2,1)S(1)}, u32[]{:S(2)}, u32[]{:S(2)}) collective-permute-start(bf16[4,120,384]{2,1,0:T(8,128)(2,1)S(1)} %bitcast_dynamic-update-slice_fusion.16), channel_id=1, source_target_pairs={{0,18},{2,16},{16,2},{18,0},{1,19},{3,17},{17,3},{19,1},{4,22},{6,... | collective-permute-start | bytes 1105928 | tf_op jit(solution)/shard_map/ppermute | solution.py:59
  53.9 8.7 %collective-permute-done.12 = bf16[4,120,384]{2,1,0:T(8,128)(2,1)S(1)} collective-permute-done((bf16[4,120,384]{2,1,0:T(8,128)(2,1)S(1)}, bf16[4,120,384]{2,1,0:T(8,128)(2,1)S(1)}, u32[]{:S(2)}, u32[]{:S(2)}) %collective-permute-start.12) | collective-permute-done | bytes 368672 | tf_op jit(solution)/shard_map/ppermute | solution.py:59
  62.5 1.2 collective-permute-start.4
  65.3 1.3 fusion.23
  66.5 1.2 reshape.239
  68.1 1.9 %all-gather = bf16[2,64,1,768]{3,1,0,2:T(8,128)(2,1)S(1)} all-gather(bf16[2,64,1,384]{3,1,0,2:T(8,128)(2,1)S(1)} %fusion.54), channel_id=2, replica_groups=mesh['group'=2,'seq'=4,'batch'=2,'mp'=2] {'mp'}, dimensions={3}, use_global_device_ids=true | all-gather | bytes 294912 | tf_op jit(solution)/shard_map/all_gather | solution.py:194
  70.2 1.5 collective-permute-start.5
  71.6 1.1 bitcast_dynamic-update-slice_fusion.1
  72.7 1.1 bitcast_dynamic-update-slice_fusion
  73.8 9.5 %collective-permute-done.5 = bf16[4,144,384]{2,1,0:T(8,128)(2,1)S(1)} collective-permute-done((bf16[4,144,384]{2,1,0:T(8,128)(2,1)S(1)}, bf16[4,144,384]{2,1,0:T(8,128)(2,1)S(1)}, u32[]{:S(2)}, u32[]{:S(2)}) %collective-permute-start.5) | collective-permute-done | bytes 442400 | tf_op jit(solution)/shard_map/ppermute | solution.py:59
  85.9 1.0 pad_maximum_fusion
  86.8 3.8 %all-to-all-start = ((bf16[4,2,18432]{2,1,0:T(2,128)(2,1)}), bf16[4,2,18432]{2,1,0:T(2,128)(2,1)S(1)}, u32[]{:S(2)}, u32[]{:S(2)}) async-start(bf16[4,2,18432]{2,1,0:T(2,128)(2,1)} %pad_maximum_fusion), calls=%async_computation | async-start | bytes 589824 | tf_op jit(solution)/shard_map/all_to_all | solution.py:231
  90.6 0.9 bitcast_dynamic-update-slice_fusion.9
  91.6 0.9 bitcast_dynamic-update-slice_fusion.8
  92.5 7.1 %all-to-all-done = bf16[4,2,18432]{2,1,0:T(2,128)(2,1)S(1)} async-done(((bf16[4,2,18432]{2,1,0:T(2,128)(2,1)}), bf16[4,2,18432]{2,1,0:T(2,128)(2,1)S(1)}, u32[]{:S(2)}, u32[]{:S(2)}) %all-to-all-start) | async-done | bytes 294944 | tf_op jit(solution)/shard_map/all_to_all | solution.py:231
  103.6 4.1 %all-to-all-start.1 = ((bf16[4,2,6144]{2,1,0:T(2,128)(2,1)}), bf16[4,2,6144]{2,1,0:T(2,128)(2,1)}, u32[]{:S(2)}, u32[]{:S(2)}) async-start(bf16[4,2,6144]{2,1,0:T(2,128)(2,1)} %copy.193), calls=%async_computation.1 | async-start | bytes 196608 | tf_op jit(solution)/shard_map/all_to_all | solution.py:253
  107.7 0.9 bitcast_dynamic-update-slice_fusion.11
  109.4 4.0 %all-to-all-done.1 = bf16[4,2,6144]{2,1,0:T(2,128)(2,1)} async-done(((bf16[4,2,6144]{2,1,0:T(2,128)(2,1)}), bf16[4,2,6144]{2,1,0:T(2,128)(2,1)}, u32[]{:S(2)}, u32[]{:S(2)}) %all-to-all-start.1) | async-done | bytes 98336 | tf_op jit(solution)/shard_map/all_to_all | solution.py:253
  113.4 1.0 reshape.243
  115.1 1.3 collective-permute-done.20
  120.4 3.3 %all-to-all-start.2 = ((bf16[4,2,3072]{2,1,0:T(2,128)(2,1)}), bf16[4,2,3072]{2,1,0:T(2,128)(2,1)S(1)}, u32[]{:S(2)}, u32[]{:S(2)}) async-start(bf16[4,2,3072]{2,1,0:T(2,128)(2,1)} %reshape.265), calls=%async_computation.2 | async-start | bytes 98304 | tf_op jit(solution)/shard_map/all_to_all | solution.py:327
  123.9 5.4 %all-to-all-done.2 = bf16[4,2,3072]{2,1,0:T(2,128)(2,1)S(1)} async-done(((bf16[4,2,3072]{2,1,0:T(2,128)(2,1)}), bf16[4,2,3072]{2,1,0:T(2,128)(2,1)S(1)}, u32[]{:S(2)}, u32[]{:S(2)}) %all-to-all-start.2) | async-done | bytes 49184 | tf_op jit(solution)/shard_map/all_to_all | solution.py:327
  133.0 3.3 %all-to-all-start.3 = ((bf16[4,2,9216]{2,1,0:T(2,128)(2,1)}), bf16[4,2,9216]{2,1,0:T(2,128)(2,1)S(1)}, u32[]{:S(2)}, u32[]{:S(2)}) async-start(bf16[4,2,9216]{2,1,0:T(2,128)(2,1)} %reshape.267), calls=%async_computation.3 | async-start | bytes 294912 | tf_op jit(solution)/shard_map/all_to_all | solution.py:338
  136.5 6.0 %all-to-all-done.3 = bf16[4,2,9216]{2,1,0:T(2,128)(2,1)S(1)} async-done(((bf16[4,2,9216]{2,1,0:T(2,128)(2,1)}), bf16[4,2,9216]{2,1,0:T(2,128)(2,1)S(1)}, u32[]{:S(2)}, u32[]{:S(2)}) %all-to-all-start.3) | async-done | bytes 147488 | tf_op jit(solution)/shard_map/all_to_all | solution.py:338
  144.5 1.2 collective-permute-done.22
  147.6 3.1 %collective-permute-start.25 = (bf16[2,384]{1,0:T(2,128)(2,1)S(1)}, bf16[2,384]{1,0:T(2,128)(2,1)S(1)}, u32[]{:S(2)}, u32[]{:S(2)}) collective-permute-start(bf16[2,384]{1,0:T(2,128)(2,1)S(1)} %get-tuple-element.113), channel_id=1, source_target_pairs={{0,4},{4,8},{8,12},{1,5},{5,9},{9,13},{2,6},{6,10},{10,14},{3,7},{... | collective-permute-start | bytes 4616 | tf_op jit(solution)/shard_map/ppermute | solution.py:23
  151.0 1.3 collective-permute-start.24
  152.8 3.7 %collective-permute-done.24 = bf16[2,384]{1,0:T(2,128)(2,1)S(1)} collective-permute-done((bf16[2,384]{1,0:T(2,128)(2,1)S(1)}, bf16[2,384]{1,0:T(2,128)(2,1)S(1)}, u32[]{:S(2)}, u32[]{:S(2)}) %collective-permute-start.24) | collective-permute-done | bytes 1568 | tf_op jit(solution)/shard_map/ppermute | solution.py:25
  (220 shorter events, 34.7 us)
Async XLA Ops:
  0.6 20.1 %copy-start.13 = (bf16[1,128,384]{2,1,0:T(8,128)(2,1)S(1)}, bf16[1,128,384]{2,1,0:T(8,128)(2,1)}, u32[]{:S(2)}) copy-start(bf16[1,128,384]{2,1,0:T(8,128)(2,1)} %param.7) | copy-start | bytes 294916
  1.6 37.0 %collective-permute-start = (bf16[144,384]{1,0:T(8,128)(2,1)S(1)}, bf16[144,384]{1,0:T(8,128)(2,1)S(1)}, u32[]{:S(2)}, u32[]{:S(2)}) collective-permute-start(bf16[144,384]{1,0:T(8,128)(2,1)S(1)} %get-tuple-element.80), channel_id=1, source_target_pairs={{0,4},{4,8},{8,12},{12,0},{1,5},{5,9},{9,13},{13,1},{2,6},{6,10},{... | collective-permute-start | bytes 331784 | tf_op jit(solution)/shard_map/ppermute | solution.py:48
  4.7 35.5 %collective-permute-start.1 = (bf16[144,384]{1,0:T(8,128)(2,1)S(1)}, bf16[144,384]{1,0:T(8,128)(2,1)S(1)}, u32[]{:S(2)}, u32[]{:S(2)}) collective-permute-start(bf16[144,384]{1,0:T(8,128)(2,1)S(1)} %get-tuple-element.80), channel_id=1, source_target_pairs={{0,8},{4,12},{8,0},{12,4},{1,9},{5,13},{9,1},{13,5},{2,10},{6,14},... | collective-permute-start | bytes 331784 | tf_op jit(solution)/shard_map/ppermute | solution.py:48
  7.3 33.5 %collective-permute-start.2 = (bf16[144,384]{1,0:T(8,128)(2,1)S(1)}, bf16[144,384]{1,0:T(8,128)(2,1)S(1)}, u32[]{:S(2)}, u32[]{:S(2)}) collective-permute-start(bf16[144,384]{1,0:T(8,128)(2,1)S(1)} %get-tuple-element.80), channel_id=1, source_target_pairs={{0,12},{4,0},{8,4},{12,8},{1,13},{5,1},{9,5},{13,9},{2,14},{6,2},{... | collective-permute-start | bytes 331784 | tf_op jit(solution)/shard_map/ppermute | solution.py:48
  10.4 7.4 %collective-permute-start.6 = (bf16[2,2,384]{2,1,0:T(2,128)(2,1)S(1)}, bf16[2,2,384]{2,1,0:T(2,128)(2,1)S(1)}, u32[]{:S(2)}, u32[]{:S(2)}) collective-permute-start(bf16[2,2,384]{2,1,0:T(2,128)(2,1)S(1)} %get-tuple-element.108), channel_id=1, source_target_pairs={{0,4},{4,8},{8,12},{1,5},{5,9},{9,13},{2,6},{6,10},{10,14},{3,7},{... | collective-permute-start | bytes 9224 | tf_op jit(solution)/shard_map/ppermute | solution.py:23
  13.0 7.4 %collective-permute-start.13 = (bf16[2,2,384]{2,1,0:T(2,128)(2,1)S(1)}, bf16[2,2,384]{2,1,0:T(2,128)(2,1)S(1)}, u32[]{:S(2)}, u32[]{:S(2)}) collective-permute-start(bf16[2,2,384]{2,1,0:T(2,128)(2,1)S(1)} %get-tuple-element.109), channel_id=1, source_target_pairs={{4,0},{8,4},{12,8},{5,1},{9,5},{13,9},{6,2},{10,6},{14,10},{7,3},{... | collective-permute-start | bytes 9224 | tf_op jit(solution)/shard_map/ppermute | solution.py:25
  17.8 5.8 %collective-permute-start.14 = (bf16[48,384]{1,0:T(8,128)(2,1)S(1)}, bf16[48,384]{1,0:T(8,128)(2,1)S(1)}, u32[]{:S(2)}, u32[]{:S(2)}) collective-permute-start(bf16[48,384]{1,0:T(8,128)(2,1)S(1)} %get-tuple-element.76), channel_id=1, source_target_pairs={{0,4},{4,8},{8,12},{12,0},{1,5},{5,9},{9,13},{13,1},{2,6},{6,10},{... | collective-permute-start | bytes 110600 | tf_op jit(solution)/shard_map/ppermute | solution.py:48
  20.4 4.9 %collective-permute-start.15 = (bf16[48,384]{1,0:T(8,128)(2,1)S(1)}, bf16[48,384]{1,0:T(8,128)(2,1)S(1)}, u32[]{:S(2)}, u32[]{:S(2)}) collective-permute-start(bf16[48,384]{1,0:T(8,128)(2,1)S(1)} %get-tuple-element.76), channel_id=1, source_target_pairs={{0,8},{4,12},{8,0},{12,4},{1,9},{5,13},{9,1},{13,5},{2,10},{6,14},... | collective-permute-start | bytes 110600 | tf_op jit(solution)/shard_map/ppermute | solution.py:48
  23.6 5.0 %collective-permute-start.16 = (bf16[48,384]{1,0:T(8,128)(2,1)S(1)}, bf16[48,384]{1,0:T(8,128)(2,1)S(1)}, u32[]{:S(2)}, u32[]{:S(2)}) collective-permute-start(bf16[48,384]{1,0:T(8,128)(2,1)S(1)} %get-tuple-element.76), channel_id=1, source_target_pairs={{0,12},{4,0},{8,4},{12,8},{1,13},{5,1},{9,5},{13,9},{2,14},{6,2},{... | collective-permute-start | bytes 110600 | tf_op jit(solution)/shard_map/ppermute | solution.py:48
  25.3 7.1 %collective-permute-start.7 = (bf16[120,384]{1,0:T(8,128)(2,1)S(1)}, bf16[120,384]{1,0:T(8,128)(2,1)S(1)}, u32[]{:S(2)}, u32[]{:S(2)}) collective-permute-start(bf16[120,384]{1,0:T(8,128)(2,1)S(1)} %get-tuple-element.78), channel_id=1, source_target_pairs={{0,4},{4,8},{8,12},{12,0},{1,5},{5,9},{9,13},{13,1},{2,6},{6,10},{... | collective-permute-start | bytes 276488 | tf_op jit(solution)/shard_map/ppermute | solution.py:48
  28.6 6.1 %collective-permute-start.8 = (bf16[120,384]{1,0:T(8,128)(2,1)S(1)}, bf16[120,384]{1,0:T(8,128)(2,1)S(1)}, u32[]{:S(2)}, u32[]{:S(2)}) collective-permute-start(bf16[120,384]{1,0:T(8,128)(2,1)S(1)} %get-tuple-element.78), channel_id=1, source_target_pairs={{0,8},{4,12},{8,0},{12,4},{1,9},{5,13},{9,1},{13,5},{2,10},{6,14},... | collective-permute-start | bytes 276488 | tf_op jit(solution)/shard_map/ppermute | solution.py:48
  31.1 7.3 %copy-start.10 = (bf16[4,4,48,384]{3,2,0,1:T(8,128)(2,1)}, bf16[4,4,48,384]{3,2,0,1:T(8,128)(2,1)S(1)}, u32[]{:S(2)}) copy-start(bf16[4,4,48,384]{3,2,0,1:T(8,128)(2,1)S(1)} %bitcast_dynamic-update-slice_fusion.10) | copy-start | bytes 1769476
  32.4 4.6 %collective-permute-start.9 = (bf16[120,384]{1,0:T(8,128)(2,1)S(1)}, bf16[120,384]{1,0:T(8,128)(2,1)S(1)}, u32[]{:S(2)}, u32[]{:S(2)}) collective-permute-start(bf16[120,384]{1,0:T(8,128)(2,1)S(1)} %get-tuple-element.78), channel_id=1, source_target_pairs={{0,12},{4,0},{8,4},{12,8},{1,13},{5,1},{9,5},{13,9},{2,14},{6,2},{... | collective-permute-start | bytes 276488 | tf_op jit(solution)/shard_map/ppermute | solution.py:48
  34.7 55.9 %collective-permute-start.17 = (bf16[4,48,384]{2,1,0:T(8,128)(2,1)}, bf16[4,48,384]{2,1,0:T(8,128)(2,1)}, u32[]{:S(2)}, u32[]{:S(2)}) collective-permute-start(bf16[4,48,384]{2,1,0:T(8,128)(2,1)} %bitcast_dynamic-update-slice_fusion.20), channel_id=1, source_target_pairs={{0,2},{2,0},{16,18},{18,16},{1,3},{3,1},{17,19},{19,17},{4,6},{6,4... | collective-permute-start | bytes 442376 | tf_op jit(solution)/shard_map/ppermute | solution.py:59
  36.9 54.7 %collective-permute-start.18 = (bf16[4,48,384]{2,1,0:T(8,128)(2,1)}, bf16[4,48,384]{2,1,0:T(8,128)(2,1)}, u32[]{:S(2)}, u32[]{:S(2)}) collective-permute-start(bf16[4,48,384]{2,1,0:T(8,128)(2,1)} %bitcast_dynamic-update-slice_fusion.20), channel_id=1, source_target_pairs={{0,16},{2,18},{16,0},{18,2},{1,17},{3,19},{17,1},{19,3},{4,20},{6,... | collective-permute-start | bytes 442376 | tf_op jit(solution)/shard_map/ppermute | solution.py:59
  38.7 69.0 %collective-permute-start.19 = (bf16[4,48,384]{2,1,0:T(8,128)(2,1)}, bf16[4,48,384]{2,1,0:T(8,128)(2,1)}, u32[]{:S(2)}, u32[]{:S(2)}) collective-permute-start(bf16[4,48,384]{2,1,0:T(8,128)(2,1)} %bitcast_dynamic-update-slice_fusion.20), channel_id=1, source_target_pairs={{0,18},{2,16},{16,2},{18,0},{1,19},{3,17},{17,3},{19,1},{4,22},{6,... | collective-permute-start | bytes 442376 | tf_op jit(solution)/shard_map/ppermute | solution.py:59
  40.2 9.6 %collective-permute-start.10 = (bf16[4,120,384]{2,1,0:T(8,128)(2,1)S(1)}, bf16[4,120,384]{2,1,0:T(8,128)(2,1)S(1)}, u32[]{:S(2)}, u32[]{:S(2)}) collective-permute-start(bf16[4,120,384]{2,1,0:T(8,128)(2,1)S(1)} %bitcast_dynamic-update-slice_fusion.16), channel_id=1, source_target_pairs={{0,2},{2,0},{16,18},{18,16},{1,3},{3,1},{17,19},{19,17},{4,6},{6,4... | collective-permute-start | bytes 1105928 | tf_op jit(solution)/shard_map/ppermute | solution.py:59
  40.8 12.3 %collective-permute-start.11 = (bf16[4,120,384]{2,1,0:T(8,128)(2,1)S(1)}, bf16[4,120,384]{2,1,0:T(8,128)(2,1)S(1)}, u32[]{:S(2)}, u32[]{:S(2)}) collective-permute-start(bf16[4,120,384]{2,1,0:T(8,128)(2,1)S(1)} %bitcast_dynamic-update-slice_fusion.16), channel_id=1, source_target_pairs={{0,16},{2,18},{16,0},{18,2},{1,17},{3,19},{17,1},{19,3},{4,20},{6,... | collective-permute-start | bytes 1105928 | tf_op jit(solution)/shard_map/ppermute | solution.py:59
  49.8 12.7 %collective-permute-start.12 = (bf16[4,120,384]{2,1,0:T(8,128)(2,1)S(1)}, bf16[4,120,384]{2,1,0:T(8,128)(2,1)S(1)}, u32[]{:S(2)}, u32[]{:S(2)}) collective-permute-start(bf16[4,120,384]{2,1,0:T(8,128)(2,1)S(1)} %bitcast_dynamic-update-slice_fusion.16), channel_id=1, source_target_pairs={{0,18},{2,16},{16,2},{18,0},{1,19},{3,17},{17,3},{19,1},{4,22},{6,... | collective-permute-start | bytes 1105928 | tf_op jit(solution)/shard_map/ppermute | solution.py:59
  53.2 17.0 %collective-permute-start.3 = (bf16[4,144,384]{2,1,0:T(8,128)(2,1)S(1)}, bf16[4,144,384]{2,1,0:T(8,128)(2,1)}, u32[]{:S(2)}, u32[]{:S(2)}) collective-permute-start(bf16[4,144,384]{2,1,0:T(8,128)(2,1)S(1)} %bitcast_dynamic-update-slice_fusion.12), channel_id=1, source_target_pairs={{0,2},{2,0},{16,18},{18,16},{1,3},{3,1},{17,19},{19,17},{4,6},{6,4... | collective-permute-start | bytes 1327112 | tf_op jit(solution)/shard_map/ppermute | solution.py:59
  62.5 10.2 %collective-permute-start.4 = (bf16[4,144,384]{2,1,0:T(8,128)(2,1)S(1)}, bf16[4,144,384]{2,1,0:T(8,128)(2,1)}, u32[]{:S(2)}, u32[]{:S(2)}) collective-permute-start(bf16[4,144,384]{2,1,0:T(8,128)(2,1)S(1)} %bitcast_dynamic-update-slice_fusion.12), channel_id=1, source_target_pairs={{0,16},{2,18},{16,0},{18,2},{1,17},{3,19},{17,1},{19,3},{4,20},{6,... | collective-permute-start | bytes 1327112 | tf_op jit(solution)/shard_map/ppermute | solution.py:59
  64.0 1.2 copy-start.2
  68.1 15.4 %copy-start.14 = (bf16[2,64,1,384]{3,1,0,2:T(8,128)(2,1)}, bf16[2,64,1,384]{3,1,0,2:T(8,128)(2,1)S(1)}, u32[]{:S(2)}) copy-start(bf16[2,64,1,384]{3,1,0,2:T(8,128)(2,1)S(1)} %fusion.54) | copy-start | bytes 294916
  70.2 13.2 %collective-permute-start.5 = (bf16[4,144,384]{2,1,0:T(8,128)(2,1)S(1)}, bf16[4,144,384]{2,1,0:T(8,128)(2,1)S(1)}, u32[]{:S(2)}, u32[]{:S(2)}) collective-permute-start(bf16[4,144,384]{2,1,0:T(8,128)(2,1)S(1)} %bitcast_dynamic-update-slice_fusion.12), channel_id=1, source_target_pairs={{0,18},{2,16},{16,2},{18,0},{1,19},{3,17},{17,3},{19,1},{4,22},{6,... | collective-permute-start | bytes 1327112 | tf_op jit(solution)/shard_map/ppermute | solution.py:59
  84.8 5.9 %copy-start.11 = (bf16[4,4,48,384]{3,2,0,1:T(8,128)(2,1)S(1)}, bf16[4,4,48,384]{3,2,0,1:T(8,128)(2,1)}, u32[]{:S(2)}) copy-start(bf16[4,4,48,384]{3,2,0,1:T(8,128)(2,1)} %copy-done.10) | copy-start | bytes 1769476
  86.8 12.8 %all-to-all-start = ((bf16[4,2,18432]{2,1,0:T(2,128)(2,1)}), bf16[4,2,18432]{2,1,0:T(2,128)(2,1)S(1)}, u32[]{:S(2)}, u32[]{:S(2)}) async-start(bf16[4,2,18432]{2,1,0:T(2,128)(2,1)} %pad_maximum_fusion), calls=%async_computation | async-start | bytes 589824 | tf_op jit(solution)/shard_map/all_to_all | solution.py:231
  100.4 2.4 %copy-start.16 = (bf16[256,96]{1,0:T(8,128)(2,1)}, bf16[256,96]{1,0:T(8,128)(2,1)S(1)}, u32[]{:S(2)}) copy-start(bf16[256,96]{1,0:T(8,128)(2,1)S(1)} %squeeze.83) | copy-start | bytes 147460
  101.4 7.2 %copy-start.19 = (bf16[256,96]{0,1:T(8,128)(2,1)}, bf16[256,96]{0,1:T(8,128)(2,1)S(1)}, u32[]{:S(2)}) copy-start(bf16[256,96]{0,1:T(8,128)(2,1)S(1)} %convolution_convert_fusion.4) | copy-start | bytes 147460
  103.6 9.8 %all-to-all-start.1 = ((bf16[4,2,6144]{2,1,0:T(2,128)(2,1)}), bf16[4,2,6144]{2,1,0:T(2,128)(2,1)}, u32[]{:S(2)}, u32[]{:S(2)}) async-start(bf16[4,2,6144]{2,1,0:T(2,128)(2,1)} %copy.193), calls=%async_computation.1 | async-start | bytes 196608 | tf_op jit(solution)/shard_map/all_to_all | solution.py:253
  109.1 7.3 %copy-start.15 = (bf16[2,64,1,384]{3,1,0,2:T(8,128)(2,1)S(1)}, bf16[2,64,1,384]{3,1,0,2:T(8,128)(2,1)}, u32[]{:S(2)}) copy-start(bf16[2,64,1,384]{3,1,0,2:T(8,128)(2,1)} %copy-done.14) | copy-start | bytes 294916
  114.7 9.0 %copy-start.17 = (bf16[256,96]{1,0:T(8,128)(2,1)S(1)}, bf16[256,96]{1,0:T(8,128)(2,1)}, u32[]{:S(2)}) copy-start(bf16[256,96]{1,0:T(8,128)(2,1)} %copy-done.16) | copy-start | bytes 147460
  115.1 1.4 collective-permute-start.20
  116.5 13.6 %copy-start.20 = (bf16[256,96]{0,1:T(8,128)(2,1)S(1)}, bf16[256,96]{0,1:T(8,128)(2,1)}, u32[]{:S(2)}) copy-start(bf16[256,96]{0,1:T(8,128)(2,1)} %copy-done.19) | copy-start | bytes 147460
  116.5 1.3 collective-permute-start.21
  120.4 8.9 %all-to-all-start.2 = ((bf16[4,2,3072]{2,1,0:T(2,128)(2,1)}), bf16[4,2,3072]{2,1,0:T(2,128)(2,1)S(1)}, u32[]{:S(2)}, u32[]{:S(2)}) async-start(bf16[4,2,3072]{2,1,0:T(2,128)(2,1)} %reshape.265), calls=%async_computation.2 | async-start | bytes 98304 | tf_op jit(solution)/shard_map/all_to_all | solution.py:327
  133.0 9.4 %all-to-all-start.3 = ((bf16[4,2,9216]{2,1,0:T(2,128)(2,1)}), bf16[4,2,9216]{2,1,0:T(2,128)(2,1)S(1)}, u32[]{:S(2)}, u32[]{:S(2)}) async-start(bf16[4,2,9216]{2,1,0:T(2,128)(2,1)} %reshape.267), calls=%async_computation.3 | async-start | bytes 294912 | tf_op jit(solution)/shard_map/all_to_all | solution.py:338
  143.1 2.9 %copy-start.12 = (f32[2,128,384]{2,1,0:T(8,128)S(1)}, f32[2,128,384]{2,1,0:T(8,128)}, u32[]{:S(2)}) copy-start(f32[2,128,384]{2,1,0:T(8,128)} %get-tuple-element.124) | copy-start | bytes 1179652
  144.4 1.3 collective-permute-start.22
  145.8 1.2 collective-permute-start.23
  146.0 6.3 %copy-start.9 = (bf16[1,4,96,384]{3,2,0,1:T(8,128)(2,1)S(1)}, bf16[1,4,96,384]{3,2,0,1:T(8,128)(2,1)}, u32[]{:S(2)}) copy-start(bf16[1,4,96,384]{3,2,0,1:T(8,128)(2,1)} %copy-done.8) | copy-start | bytes 884740
  146.2 6.4 %copy-start.7 = (bf16[1,4,96,384]{3,2,0,1:T(8,128)(2,1)S(1)}, bf16[1,4,96,384]{3,2,0,1:T(8,128)(2,1)}, u32[]{:S(2)}) copy-start(bf16[1,4,96,384]{3,2,0,1:T(8,128)(2,1)} %copy-done.6) | copy-start | bytes 884740
  147.1 9.4 %copy-start.5 = (bf16[1,4,96,384]{3,2,0,1:T(8,128)(2,1)S(1)}, bf16[1,4,96,384]{3,2,0,1:T(8,128)(2,1)}, u32[]{:S(2)}) copy-start(bf16[1,4,96,384]{3,2,0,1:T(8,128)(2,1)} %copy-done.4) | copy-start | bytes 884740
  147.3 9.5 %copy-start.3 = (bf16[1,4,96,384]{3,2,0,1:T(8,128)(2,1)S(1)}, bf16[1,4,96,384]{3,2,0,1:T(8,128)(2,1)}, u32[]{:S(2)}) copy-start(bf16[1,4,96,384]{3,2,0,1:T(8,128)(2,1)} %copy-done.2) | copy-start | bytes 884740
  147.6 5.0 %collective-permute-start.25 = (bf16[2,384]{1,0:T(2,128)(2,1)S(1)}, bf16[2,384]{1,0:T(2,128)(2,1)S(1)}, u32[]{:S(2)}, u32[]{:S(2)}) collective-permute-start(bf16[2,384]{1,0:T(2,128)(2,1)S(1)} %get-tuple-element.113), channel_id=1, source_target_pairs={{0,4},{4,8},{8,12},{1,5},{5,9},{9,13},{2,6},{6,10},{10,14},{3,7},{... | collective-permute-start | bytes 4616 | tf_op jit(solution)/shard_map/ppermute | solution.py:23
  150.7 6.3 %copy-start.1 = (bf16[1,4,96,384]{3,2,0,1:T(8,128)(2,1)S(1)}, bf16[1,4,96,384]{3,2,0,1:T(8,128)(2,1)}, u32[]{:S(2)}) copy-start(bf16[1,4,96,384]{3,2,0,1:T(8,128)(2,1)} %copy-done) | copy-start | bytes 884740
  151.0 5.5 %collective-permute-start.24 = (bf16[2,384]{1,0:T(2,128)(2,1)S(1)}, bf16[2,384]{1,0:T(2,128)(2,1)S(1)}, u32[]{:S(2)}, u32[]{:S(2)}) collective-permute-start(bf16[2,384]{1,0:T(2,128)(2,1)S(1)} %get-tuple-element.112), channel_id=1, source_target_pairs={{4,0},{8,4},{12,8},{5,1},{9,5},{13,9},{6,2},{10,6},{14,10},{7,3},{... | collective-permute-start | bytes 4616 | tf_op jit(solution)/shard_map/ppermute | solution.py:25
  152.6 6.2 %copy-start.18 = (f32[1,128,384]{2,1,0:T(8,128)S(1)}, f32[1,128,384]{2,1,0:T(8,128)}, u32[]{:S(2)}) copy-start(f32[1,128,384]{2,1,0:T(8,128)} %param.8) | copy-start | bytes 589828
  157.3 1.4 collective-permute-start.26
  (6 other events, 6.3 us)
